TPU v7x, 32 devices: a whole 2x2x4 slice. The times are simulated.
32 devices in a mesh: heads: 4 (over y, core), seq: 8 (over z, x).
Axes of the slice: x: 2, y: 2, z: 4, core: 2. Of those that a mesh axis runs over, the one named last changes fastest.
Arguments:
- hidden: bfloat16 [8, 256, 2048], P('seq', 'heads'), may hold values from -6 to 6
- norm_gain: bfloat16 [2048], replicated, may hold values from 0.099609375 to 1.8984375
- router_weight: bfloat16 [2048, 4], replicated, may hold values from -0.125 to 0.125
- att_experts: int32 [8, 256, 2], P('seq'), may hold values from 0 to 3, all different within a row
- q_weight: bfloat16 [4, 2048, 1024], P(None, None, 'heads'), may hold values from -0.125 to 0.125
- kv_weight: bfloat16 [2, 2048, 1024], P(None, None, 'heads'), may hold values from -0.125 to 0.125
- o_weight: bfloat16 [4, 1024, 2048], P(None, 'heads'), may hold values from -1 to 1
- kv_cache: bfloat16 [2, 128, 128, 1024], P(None, 'seq', None, 'heads'), may hold values from -200 to 200
- cached_blocks: int32 [8], replicated, may hold values from 1 to 32, 128 in all
- tail_trim: int32 [8], replicated, may hold values from 0 to 127
- block_pool: int32 [128], replicated, may hold values from 0 to 127, each once
Outputs:
- attn_out: bfloat16 [8, 256, 2048], P('seq', 'heads')
Inputs may be any that keep to these rules, and one draw needn't show every extreme that they name: `block_pool`: the cached_blocks sum to 128, so every block belongs to one request.
All inputs are finite; a program needn't handle non-finite values.
Results may differ from a plain program's by a relative error of at most 0.019.
The roundings to bfloat16 on the way count: a program that leaves them out, or rounds other values in their place, can miss the bound.
Values may be sent and summed in bfloat16 or wider, within the bound.
No kernel may reach another device: no remote copies, remote signals or barrier semaphores. Data moves between devices by JAX's collectives and lax.ppermute only.
A program may use at most 128 MiB of HBM per device.

v0:
```python
import jax
import jax.numpy as jnp
from jax import lax
from jax.sharding import PartitionSpec as P

HD = 128


NEG_FILL = -1e30


def rotate(values, positions):
    half_dim = values.shape[-1] // 2
    inverse = 10000.0 ** (-2.0 * jnp.arange(half_dim, dtype=jnp.float32) / values.shape[-1])
    angles = positions.astype(jnp.float32)[:, None] * inverse[None, :]
    target = (values.shape[0],) + (1,) * (values.ndim - 2) + (half_dim,)
    cosine = jnp.cos(angles).reshape(target)
    sine_part = jnp.sin(angles).reshape(target)
    leading_part = values[..., :half_dim]
    trailing_part = values[..., half_dim:]
    return jnp.concatenate(
        [
            leading_part * cosine - trailing_part * sine_part,
            trailing_part * cosine + leading_part * sine_part,
        ],
        axis=-1,
    )


def normalize(rows, norm_gain):
    wide_rows = rows.astype(jnp.float32)
    scaled = wide_rows * lax.rsqrt(jnp.mean(wide_rows * wide_rows, axis=-1, keepdims=True) + 1e-05)
    return (scaled * norm_gain.astype(jnp.float32)).astype(jnp.bfloat16)


def route(normed, router_weight, chosen):
    logits = jnp.dot(normed, router_weight, preferred_element_type=jnp.float32)
    experts_all = router_weight.shape[1]
    onehot = (chosen[:, :, None] == jnp.arange(experts_all, dtype=jnp.int32)[None, None, :]).astype(
        jnp.float32
    )
    picked = jnp.sum(onehot * logits[:, None, :], axis=-1)
    return (onehot, jax.nn.softmax(picked, axis=-1))


def per_device(
    hidden,
    norm_gain,
    router_weight,
    att_experts,
    q_weight,
    kv_weight,
    o_weight,
    kv_cache,
    cached_blocks,
    tail_trim,
    block_pool,
):
    head_count = lax.axis_size("heads")
    seq_rank = lax.axis_index("seq")
    block_size = kv_cache.shape[2]
    local_blocks = kv_cache.shape[1]
    local_heads = q_weight.shape[2] // HD
    scale_q = HD ** (-0.5)
    normed = normalize(hidden[0], norm_gain)
    gathered = lax.all_gather(normed, "heads", axis=0, tiled=True)
    new_count = gathered.shape[0]
    chosen = att_experts[0]
    cached_len = cached_blocks * block_size - tail_trim
    positions = cached_len[seq_rank] + jnp.arange(new_count, dtype=jnp.int32)
    onehot, gates = route(gathered, router_weight, chosen)
    every_q = jnp.einsum("nd,edc->nec", gathered, q_weight, preferred_element_type=jnp.float32)
    chosen_q = jnp.sum(onehot[:, :, :, None] * every_q[:, None, :, :], axis=2).reshape(
        new_count, 2, local_heads, HD
    )
    queries = rotate(chosen_q, positions).astype(jnp.bfloat16)
    fresh = jnp.einsum("nd,sdc->snc", gathered, kv_weight, preferred_element_type=jnp.float32)
    new_keys = rotate(fresh[0].reshape(new_count, local_heads, HD), positions).astype(jnp.bfloat16)
    new_values = fresh[1].reshape(new_count, local_heads, HD).astype(jnp.bfloat16)
    all_queries = lax.all_gather(queries[None], "seq", axis=0, tiled=True)
    request_count = all_queries.shape[0]
    pool_size = block_pool.shape[0]
    global_ids = seq_rank * local_blocks + jnp.arange(local_blocks, dtype=jnp.int32)
    matches = block_pool[None, :] == global_ids[:, None]
    slot_of = jnp.sum(
        jnp.where(matches, jnp.arange(pool_size, dtype=jnp.int32)[None, :], 0), axis=1
    )
    starts = jnp.cumsum(cached_blocks) - cached_blocks
    owner = jnp.sum((starts[None, :] <= slot_of[:, None]).astype(jnp.int32), axis=1) - 1
    ordinal = slot_of - starts[owner]
    stat_shape = (request_count, new_count, 2, local_heads)
    initial = (
        jnp.full(stat_shape, NEG_FILL, jnp.float32),
        jnp.zeros(stat_shape, jnp.float32),
        jnp.zeros(stat_shape + (HD,), jnp.float32),
    )

    def visit(carry, block):
        best, totals, accum = carry
        request = owner[block]
        query_rows = lax.dynamic_index_in_dim(all_queries, request, 0, keepdims=False)
        pair_kv = lax.dynamic_index_in_dim(kv_cache, block, 1, keepdims=False)
        keys_here = pair_kv[0].reshape(block_size, local_heads, HD)
        values_here = pair_kv[1].reshape(block_size, local_heads, HD)
        scores = (
            jnp.einsum("nkhc,thc->nkht", query_rows, keys_here, preferred_element_type=jnp.float32)
            * scale_q
        )
        key_pos = ordinal[block] * block_size + jnp.arange(block_size, dtype=jnp.int32)
        scores = jnp.where((key_pos < cached_len[request])[None, None, None, :], scores, NEG_FILL)
        old_best = lax.dynamic_index_in_dim(best, request, 0, keepdims=False)
        new_best = jnp.maximum(old_best, jnp.max(scores, axis=-1))
        weights = jnp.exp(scores - new_best[..., None])
        rescale = jnp.exp(old_best - new_best)
        new_total = lax.dynamic_index_in_dim(
            totals, request, 0, keepdims=False
        ) * rescale + jnp.sum(weights, axis=-1)
        product = jnp.einsum(
            "nkht,thc->nkhc",
            weights.astype(jnp.bfloat16),
            values_here,
            preferred_element_type=jnp.float32,
        )
        new_accum = (
            lax.dynamic_index_in_dim(accum, request, 0, keepdims=False) * rescale[..., None]
            + product
        )
        best = lax.dynamic_update_index_in_dim(best, new_best, request, 0)
        totals = lax.dynamic_update_index_in_dim(totals, new_total, request, 0)
        accum = lax.dynamic_update_index_in_dim(accum, new_accum, request, 0)
        return ((best, totals, accum), None)

    scanned = lax.scan(visit, initial, jnp.arange(local_blocks, dtype=jnp.int32))
    best, totals, accum = scanned[0]
    self_scores = (
        jnp.einsum("nkhc,thc->nkht", queries, new_keys, preferred_element_type=jnp.float32)
        * scale_q
    )
    causal = (
        jnp.arange(new_count, dtype=jnp.int32)[None, :]
        <= jnp.arange(new_count, dtype=jnp.int32)[:, None]
    )
    self_scores = jnp.where(causal[:, None, None, :], self_scores, NEG_FILL)
    self_best = jnp.max(self_scores, axis=-1)
    self_weights = jnp.exp(self_scores - self_best[..., None])
    self_total = jnp.sum(self_weights, axis=-1)
    self_accum = jnp.einsum(
        "nkht,thc->nkhc",
        self_weights.astype(jnp.bfloat16),
        new_values,
        preferred_element_type=jnp.float32,
    )
    global_best = lax.pmax(best.astype(jnp.bfloat16), "seq").astype(best.dtype)
    factor = jnp.exp(best - global_best)
    cache_accum, cache_total = (
        lax.psum_scatter(
            (accum * factor[..., None]).astype(jnp.bfloat16), "seq", scatter_dimension=0, tiled=True
        ).astype(jnp.float32),
        lax.psum_scatter(
            (totals * factor).astype(jnp.bfloat16), "seq", scatter_dimension=0, tiled=True
        ).astype(jnp.float32),
    )
    cache_best = lax.dynamic_index_in_dim(global_best, seq_rank, 0, keepdims=True)
    peak = jnp.maximum(cache_best[0], self_best)
    cache_share = jnp.exp(cache_best[0] - peak)
    self_share = jnp.exp(self_best - peak)
    numerator = cache_accum[0] * cache_share[..., None] + self_accum * self_share[..., None]
    denominator = cache_total[0] * cache_share + self_total * self_share
    attended = (
        (numerator / denominator[..., None])
        .astype(jnp.bfloat16)
        .reshape(new_count, 2, local_heads * HD)
    )
    rows_each = new_count // head_count
    output = jnp.zeros((rows_each * lax.axis_size("heads"), o_weight.shape[2]), jnp.float32)
    for expert in range(o_weight.shape[0]):
        weight_expert = jnp.sum(onehot[:, :, expert] * gates, axis=1)
        picked = jnp.where(
            chosen[:, 0:1] == expert,
            attended[:, 0],
            jnp.where(chosen[:, 1:2] == expert, attended[:, 1], jnp.zeros_like(attended[:, 0])),
        )
        output = output + weight_expert[:, None] * jnp.dot(
            picked, o_weight[expert], preferred_element_type=jnp.float32
        )
    summed = lax.psum_scatter(
        output.astype(jnp.bfloat16), "heads", scatter_dimension=0, tiled=True
    ).astype(jnp.float32)
    return summed[None].astype(jnp.bfloat16)


def solution(mesh):
    return jax.shard_map(
        per_device,
        mesh=mesh,
        in_specs=(
            P("seq", "heads", None),
            P(),
            P(),
            P("seq", None, None),
            P(None, None, "heads"),
            P(None, None, "heads"),
            P(None, "heads", None),
            P(None, "seq", None, "heads"),
            P(),
            P(),
            P(),
        ),
        out_specs=P("seq", "heads", None),
        check_vma=False,
    )
```

profile of v0, /device:TPU:0, one launch (start us, length us, event | category | flops | bytes accessed | tf_op | source)
XLA Modules:
  0.0 433.7 jit_solution(16295591473125909563)
XLA Ops:
  8.5 1.8 fusion.37
  15.1 14.8 %all-gather.3.cloned.1.call-done = bf16[256,2048]{1,0:T(8,128)(2,1)} async-done(((bf16[64,2048]{1,0:T(8,128)(2,1)}), bf16[256,2048]{1,0:T(8,128)(2,1)}) %all-gather.3.cloned.1.call-update) | async-done | bytes 1048592 | tf_op jit(solution)/shard_map/all_gather | solution.py:66
  29.9 3.8 fusion.27
  38.4 48.4 %all-gather.5.cloned.1.call-done = bf16[8,256,2,2,128]{4,1,3,2,0:T(8,128)(2,1)} async-done(((bf16[1,256,2,2,128]{4,1,3,2,0:T(8,128)(2,1)}), bf16[8,256,2,2,128]{4,1,3,2,0:T(8,128)(2,1)}) %all-gather.5.cloned.1.call-update) | async-done | bytes 2097168 | tf_op jit(solution)/shard_map/all_gather | solution.py:80
  86.8 2.4 broadcast_in_dim.133
  89.2 202.3 %while.14 = (s32[]{:T(128)}, f32[8,256,2,2]{1,2,3,0:T(2,128)S(1)}, f32[8,256,2,2]{1,2,3,0:T(2,128)S(1)}, f32[8,256,2,2,128]{1,4,2,3,0:T(8,128)}, s32[16]{0:T(128...) while((s32[]{:T(128)}, f32[8,256,2,2]{1,2,3,0:T(2,128)S(1)}, ...), condition=%wide.region_12.13_spmd, body=%wide.region_9.12_spmd.sunk | while | flops 68292872 | bytes 4649549 | solution.py:133
  98.2 1.2 fusion.122
  110.9 1.2 fusion.122
  123.5 1.2 fusion.122
  136.1 1.2 fusion.122
  148.8 1.2 fusion.122
  161.4 1.2 fusion.122
  174.1 1.2 fusion.122
  186.7 1.2 fusion.122
  199.4 1.2 fusion.122
  224.6 1.2 fusion.122
  237.3 1.2 fusion.122
  262.6 1.2 fusion.122
  275.2 1.2 fusion.122
  287.9 1.2 fusion.122
  291.5 34.6 %pmax.7 = bf16[8,256,2,2]{1,2,3,0:T(2,128)(2,1)S(1)} all-reduce(bf16[8,256,2,2]{1,2,3,0:T(2,128)(2,1)S(1)} %convert_element_type.81), channel_id=1, replica_groups=mesh['heads'=4,'seq'=8] {'seq'}, use_global_device_ids=true, to_apply=%region_13.14 | all-reduce | flops 8192 | bytes 32768 | tf_op jit(solution)/shard_map/pmax | solution.py:153
  326.8 4.0 multiply_convert_fusion
  330.9 1.3 dynamic-slice
  332.2 1.4 compare_reduce_fusion.1
  336.2 1.6 fusion.103
  338.6 1.4 fusion.102
  340.2 33.7 %all-reduce = bf16[8,256,2,2]{1,2,3,0:T(2,128)(2,1)S(1)} all-reduce(bf16[8,256,2,2]{1,2,3,0:T(2,128)(2,1)} %get-tuple-element.139), channel_id=3, replica_groups=mesh['heads'=4,'seq'=8] {'seq'}, use_global_device_ids=true, to_apply=%region_16.17.clone | all-reduce | flops 8192 | bytes 32768
  374.5 22.4 %reduce-scatter.3.cloned.1.call-done = bf16[1,256,2,2,128]{1,4,2,3,0:T(8,128)(2,1)} async-done(((bf16[8,256,2,2,128]{1,4,2,3,0:T(8,128)(2,1)}), bf16[1,256,2,2,128]{1,4,2,3,0:T(8,128)(2,1)}) %reduce-scatter.3.cloned.1.call-update) | async-done | bytes 262160 | tf_op jit(solution)/shard_map/reduce_scatter | solution.py:156
  397.0 1.5 fusion.21
  398.5 1.7 convolution_multiply_fusion.4
  401.6 1.5 fusion.15
  403.1 24.0 %reduce-scatter.5.cloned.1.call-done = bf16[64,2048]{1,0:T(8,128)(2,1)} async-done(((bf16[256,2048]{1,0:T(8,128)(2,1)}), bf16[64,2048]{1,0:T(8,128)(2,1)}) %reduce-scatter.5.cloned.1.call-update) | async-done | bytes 262160 | tf_op jit(solution)/shard_map/reduce_scatter | solution.py:186
  (312 shorter events, 126.5 us)
Async XLA Ops:
  6.5 327.7 %copy-start = (bf16[2,2048,256]{2,1,0:T(8,128)(2,1)S(1)}, bf16[2,2048,256]{2,1,0:T(8,128)(2,1)}, u32[]{:S(2)}) copy-start(bf16[2,2048,256]{2,1,0:T(8,128)(2,1)} %param.18) | copy-start | bytes 6291460
  6.5 23.4 %all-gather.3.cloned.1.call-start = ((), (), s32[]{:S(2)}) async-start(), calls=%async_computation.2 | async-start | bytes 1310720 | tf_op jit(solution)/shard_map/all_gather | solution.py:66
  10.3 76.5 %all-gather.5.cloned.1.call-start = ((), (), s32[]{:S(2)}) async-start(), calls=%async_computation.3 | async-start | bytes 2359296 | tf_op jit(solution)/shard_map/all_gather | solution.py:80
  11.1 2.2 copy-start.5
  34.4 2.9 copy-start.21
  35.7 0.7 copy-start.2
  37.3 359.6 %reduce-scatter.3.cloned.1.call-start = ((), (), s32[]{:S(2)}) async-start(), calls=%async_computation.4 | async-start | bytes 2359296 | tf_op jit(solution)/shard_map/reduce_scatter | solution.py:156
  330.8 3.4 copy-start.4
  330.9 96.3 %reduce-scatter.5.cloned.1.call-start = ((), (), s32[]{:S(2)}) async-start(), calls=%async_computation.5 | async-start | bytes 1310720 | tf_op jit(solution)/shard_map/reduce_scatter | solution.py:186
  335.2 1.0 copy-start.8
  335.2 2.6 copy-start.7
  335.2 2.7 copy-start.6
  335.2 3.3 copy-start.3
  340.2 58.3 %copy-start.11 = (f32[256]{0:T(256)S(1)}, f32[256]{0:T(256)}, u32[]{:S(2)}) copy-start(f32[256]{0:T(256)} %get-tuple-element.105) | copy-start | bytes 3076
  340.2 58.3 %copy-start.17 = (pred[256]{0:T(512)(128)(4,1)S(1)}, pred[256]{0:T(512)(128)(4,1)}, u32[]{:S(2)}) copy-start(pred[256]{0:T(512)(128)(4,1)} %get-tuple-element.112) | copy-start | bytes 772
  340.2 58.3 %copy-start.18 = (pred[256]{0:T(512)(128)(4,1)S(1)}, pred[256]{0:T(512)(128)(4,1)}, u32[]{:S(2)}) copy-start(pred[256]{0:T(512)(128)(4,1)} %get-tuple-element.113) | copy-start | bytes 772
  396.9 3.3 copy-start.1
  398.4 1.8 copy-start.10
  398.5 1.8 copy-start.15
  398.5 1.8 copy-start.16
  400.3 0.7 copy-start.9
  400.3 0.7 copy-start.13
  400.3 0.6 copy-start.14
  400.9 0.6 copy-start.12
  400.9 0.7 copy-start.19
  400.9 0.7 copy-start.20
Sparse Core Ops, SparseCore 0:
  10.4 19.4 all-gather.2
  37.4 49.2 all-gather.4
  331.0 65.9 reduce-scatter.2
  403.2 23.8 reduce-scatter.4
where the time goes:
time: 438 us; the launch traced here: 434 us
  waiting for transfers between devices  110 us (25%)
  local copies, waits for them, and re-layouts  84.8 us (19%)
  loops' own time  76 us (17%)
  blocking collectives  68.3 us (16%)
  matrix products  49.9 us (11%)
  other arithmetic  31.2 us (7%)
  between operations  13.6 us (3%)
    another operation x1, loops' own time, per_device(): lax.scan(visit, initial, jnp.arange(local_blocks, dtype=jnp.int32))  76 us
    all_gather x1, waiting for transfers between devices, per_device(): all_queries = lax.all_gather(queries[None], 'seq', axis=0, tiled=True)  48.4 us
    pmax x1, blocking collectives, per_device(): global_best = lax.pmax(best.astype(jnp.bfloat16), 'seq').astype(best.dtype)  34.6 us
    unnamed x1, blocking collectives  33.7 us
    reduce_scatter x1, waiting for transfers between devices, per_device(): lax.psum_scatter(output.astype(jnp.bfloat16), 'heads', scatter_dimension=...  24 us
    reduce_scatter x1, waiting for transfers between devices, per_device(): lax.psum_scatter((accum * factor[..., None]).astype(jnp.bfloat16), 'seq',...  22.4 us
    dot_general x16, matrix products, visit(): jnp.einsum('nkhc,thc->nkht', query_rows, keys_here, preferred_element_typ...  19.8 us
    dynamic_slice x16, local copies, waits for them, and re-layouts, visit(): lax.dynamic_index_in_dim(accum, request, 0, keepdims=False)  17.3 us
  transfers between devices with their start and end apart: 4, of which 4 were waited for; matrix products, arithmetic and copies ran while one was open for 4% of the time, Pallas kernels for 0%

commit v1 on v0

--- a/solution.py
+++ b/solution.py
@@ -41,6 +41,12 @@
     )
     picked = jnp.sum(onehot * logits[:, None, :], axis=-1)
     return (onehot, jax.nn.softmax(picked, axis=-1))
+
+
+def split_bf16(x):
+    hi = lax.reduce_precision(x, exponent_bits=8, mantissa_bits=7)
+    lo = lax.reduce_precision(x - hi, exponent_bits=8, mantissa_bits=7)
+    return hi, lo
 
 
 def per_device(
@@ -80,6 +86,7 @@
     all_queries = lax.all_gather(queries[None], "seq", axis=0, tiled=True)
     request_count = all_queries.shape[0]
     pool_size = block_pool.shape[0]
+
     global_ids = seq_rank * local_blocks + jnp.arange(local_blocks, dtype=jnp.int32)
     matches = block_pool[None, :] == global_ids[:, None]
     slot_of = jnp.sum(
@@ -88,87 +95,88 @@
     starts = jnp.cumsum(cached_blocks) - cached_blocks
     owner = jnp.sum((starts[None, :] <= slot_of[:, None]).astype(jnp.int32), axis=1) - 1
     ordinal = slot_of - starts[owner]
-    stat_shape = (request_count, new_count, 2, local_heads)
-    initial = (
-        jnp.full(stat_shape, NEG_FILL, jnp.float32),
-        jnp.zeros(stat_shape, jnp.float32),
-        jnp.zeros(stat_shape + (HD,), jnp.float32),
-    )
-
-    def visit(carry, block):
-        best, totals, accum = carry
-        request = owner[block]
-        query_rows = lax.dynamic_index_in_dim(all_queries, request, 0, keepdims=False)
-        pair_kv = lax.dynamic_index_in_dim(kv_cache, block, 1, keepdims=False)
-        keys_here = pair_kv[0].reshape(block_size, local_heads, HD)
-        values_here = pair_kv[1].reshape(block_size, local_heads, HD)
-        scores = (
-            jnp.einsum("nkhc,thc->nkht", query_rows, keys_here, preferred_element_type=jnp.float32)
-            * scale_q
+    owns = owner[None, :] == jnp.arange(request_count, dtype=jnp.int32)[:, None]
+
+    block_queries = jnp.take(all_queries, owner, axis=0)
+    keys_here = kv_cache[0].reshape(local_blocks, block_size, local_heads, HD)
+    values_here = kv_cache[1].reshape(local_blocks, block_size, local_heads, HD)
+    scores = (
+        jnp.einsum(
+            "bnkhc,bthc->bhnkt", block_queries, keys_here, preferred_element_type=jnp.float32
         )
-        key_pos = ordinal[block] * block_size + jnp.arange(block_size, dtype=jnp.int32)
-        scores = jnp.where((key_pos < cached_len[request])[None, None, None, :], scores, NEG_FILL)
-        old_best = lax.dynamic_index_in_dim(best, request, 0, keepdims=False)
-        new_best = jnp.maximum(old_best, jnp.max(scores, axis=-1))
-        weights = jnp.exp(scores - new_best[..., None])
-        rescale = jnp.exp(old_best - new_best)
-        new_total = lax.dynamic_index_in_dim(
-            totals, request, 0, keepdims=False
-        ) * rescale + jnp.sum(weights, axis=-1)
-        product = jnp.einsum(
-            "nkht,thc->nkhc",
-            weights.astype(jnp.bfloat16),
-            values_here,
-            preferred_element_type=jnp.float32,
-        )
-        new_accum = (
-            lax.dynamic_index_in_dim(accum, request, 0, keepdims=False) * rescale[..., None]
-            + product
-        )
-        best = lax.dynamic_update_index_in_dim(best, new_best, request, 0)
-        totals = lax.dynamic_update_index_in_dim(totals, new_total, request, 0)
-        accum = lax.dynamic_update_index_in_dim(accum, new_accum, request, 0)
-        return ((best, totals, accum), None)
-
-    scanned = lax.scan(visit, initial, jnp.arange(local_blocks, dtype=jnp.int32))
-    best, totals, accum = scanned[0]
+        * scale_q
+    )
+    key_pos = ordinal[:, None] * block_size + jnp.arange(block_size, dtype=jnp.int32)[None, :]
+    key_ok = key_pos < cached_len[owner][:, None]
+    scores = jnp.where(key_ok[:, None, None, None, :], scores, NEG_FILL)
+    block_best = jnp.max(scores, axis=-1)
+    request_best = jnp.max(
+        jnp.where(owns[:, :, None, None, None], block_best[None], NEG_FILL), axis=1
+    )
+    best_hi, best_lo = split_bf16(request_best)
+    request_ref = best_hi + best_lo
+    weights = jnp.exp(scores - jnp.take(request_ref, owner, axis=0)[..., None])
+    block_totals = jnp.sum(weights, axis=-1)
+    block_accum = jnp.einsum(
+        "bhnkt,bthc->bhnkc",
+        weights.astype(jnp.bfloat16),
+        values_here,
+        preferred_element_type=jnp.float32,
+    )
+    owns_f = owns.astype(jnp.float32)
+    accum = jnp.einsum("rb,bhnkc->rhnkc", owns_f, block_accum, precision=lax.Precision.HIGHEST)
+    totals = jnp.einsum("rb,bhnk->rhnk", owns_f, block_totals, precision=lax.Precision.HIGHEST)
+    totals_hi, totals_lo = split_bf16(totals)
+    stats = jnp.stack([best_hi, best_lo, totals_hi, totals_lo], axis=1).astype(jnp.bfloat16)
+    stat_rows = stats.size // (request_count * HD)
+    payload = jnp.concatenate(
+        [
+            accum.astype(jnp.bfloat16).reshape(request_count, -1, HD),
+            stats.reshape(request_count, stat_rows, HD),
+        ],
+        axis=1,
+    )
+    received = lax.all_to_all(payload, "seq", 0, 0, tiled=True)
+    acc_rows = local_heads * new_count * 2
+    sources = received.shape[0]
+    part_accum = received[:, :acc_rows].astype(jnp.float32).reshape(
+        sources, local_heads, new_count, 2, HD
+    )
+    part_stats = received[:, acc_rows:].astype(jnp.float32).reshape(
+        sources, 4, local_heads, new_count, 2
+    )
+    part_best = part_stats[:, 0] + part_stats[:, 1]
+    part_totals = part_stats[:, 2] + part_stats[:, 3]
+    cache_best = jnp.max(part_best, axis=0)
+    factor = jnp.exp(part_best - cache_best[None])
+    cache_total = jnp.sum(part_totals * factor, axis=0)
+    cache_accum = jnp.sum(part_accum * factor[..., None], axis=0)
+
     self_scores = (
-        jnp.einsum("nkhc,thc->nkht", queries, new_keys, preferred_element_type=jnp.float32)
+        jnp.einsum("nkhc,thc->hnkt", queries, new_keys, preferred_element_type=jnp.float32)
         * scale_q
     )
     causal = (
         jnp.arange(new_count, dtype=jnp.int32)[None, :]
         <= jnp.arange(new_count, dtype=jnp.int32)[:, None]
     )
-    self_scores = jnp.where(causal[:, None, None, :], self_scores, NEG_FILL)
+    self_scores = jnp.where(causal[None, :, None, :], self_scores, NEG_FILL)
     self_best = jnp.max(self_scores, axis=-1)
     self_weights = jnp.exp(self_scores - self_best[..., None])
     self_total = jnp.sum(self_weights, axis=-1)
     self_accum = jnp.einsum(
-        "nkht,thc->nkhc",
+        "hnkt,thc->hnkc",
         self_weights.astype(jnp.bfloat16),
         new_values,
         preferred_element_type=jnp.float32,
     )
-    global_best = lax.pmax(best.astype(jnp.bfloat16), "seq").astype(best.dtype)
-    factor = jnp.exp(best - global_best)
-    cache_accum, cache_total = (
-        lax.psum_scatter(
-            (accum * factor[..., None]).astype(jnp.bfloat16), "seq", scatter_dimension=0, tiled=True
-        ).astype(jnp.float32),
-        lax.psum_scatter(
-            (totals * factor).astype(jnp.bfloat16), "seq", scatter_dimension=0, tiled=True
-        ).astype(jnp.float32),
-    )
-    cache_best = lax.dynamic_index_in_dim(global_best, seq_rank, 0, keepdims=True)
-    peak = jnp.maximum(cache_best[0], self_best)
-    cache_share = jnp.exp(cache_best[0] - peak)
+    peak = jnp.maximum(cache_best, self_best)
+    cache_share = jnp.exp(cache_best - peak)
     self_share = jnp.exp(self_best - peak)
-    numerator = cache_accum[0] * cache_share[..., None] + self_accum * self_share[..., None]
-    denominator = cache_total[0] * cache_share + self_total * self_share
+    numerator = cache_accum * cache_share[..., None] + self_accum * self_share[..., None]
+    denominator = cache_total * cache_share + self_total * self_share
     attended = (
-        (numerator / denominator[..., None])
-        .astype(jnp.bfloat16)
+        jnp.transpose((numerator / denominator[..., None]).astype(jnp.bfloat16), (1, 2, 0, 3))
         .reshape(new_count, 2, local_heads * HD)
     )
     rows_each = new_count // head_count

time: 438 us -> 226 us (0.52)
  loops' own time: 76 us -> 0 us
  blocking collectives: 68.3 us -> 0 us
  local copies, waits for them, and re-layouts: 84.8 us -> 26 us
  matrix products: 49.9 us -> 33.7 us
  waiting for transfers between devices: 110 us -> 121 us
  other arithmetic: 31.2 us -> 26.3 us
  starting transfers between devices: 0.13 us -> 4.79 us
    another operation x1 -> x0, loops' own time: 76 us -> none  [per_device(): lax.scan(visit, initial, jnp.arange(local_blocks, dtype=jnp.int32))]
    dynamic_slice x80 -> x0, local copies, waits for them, and re-layouts: 58.6 us -> none  [the longest x16 17.3 us: visit(): lax.dynamic_index_in_dim(accum, request, 0, keepdims=False)]
    all_to_all x0 -> x1, waiting for transfers between devices: none -> 39.8 us  [per_device(): received = lax.all_to_all(payload, 'seq', 0, 0, tiled=True)]
    pmax x1 -> x0, blocking collectives: 34.6 us -> none  [per_device(): global_best = lax.pmax(best.astype(jnp.bfloat16), 'seq').astype(best.dtype)]
    unnamed x1 -> x0, blocking collectives: 33.7 us -> none
    reduce_scatter x1 -> x0, waiting for transfers between devices: 22.4 us -> none  [per_device(): lax.psum_scatter((accum * factor[..., None]).astype(jnp.bfloat16), 'seq',...]
    dot_general x34 -> x6, matrix products: 39.6 us -> 22.1 us  [the longest x1 8.12 us: per_device(): jnp.einsum('bnkhc,bthc->bhnkt', block_queries, keys_here, preferred_eleme...]
    slice x16 -> x1, local copies, waits for them, and re-layouts: 14.2 us -> 2.72 us  [per_device(): values_here = kv_cache[1].reshape(local_blocks, block_size, local_heads, HD)]
  transfers between devices with their start and end apart: 4 -> 4, of which waited for: 4 -> 4; matrix products, arithmetic and copies ran while one was open for 4% -> 9% of each run, Pallas kernels for 0% -> 0%
where the time goes in v1:
time: 226 us; the launch traced here: 225 us
  waiting for transfers between devices  121 us (54%)
  matrix products  33.7 us (15%)
  other arithmetic  26.3 us (12%)
  local copies, waits for them, and re-layouts  26 us (12%)
  between operations  13.7 us (6%)
  starting transfers between devices  4.79 us (2%)
    all_gather x1, waiting for transfers between devices, per_device(): all_queries = lax.all_gather(queries[None], 'seq', axis=0, tiled=True)  42.2 us
    all_to_all x1, waiting for transfers between devices, per_device(): received = lax.all_to_all(payload, 'seq', 0, 0, tiled=True)  39.8 us
    reduce_scatter x1, waiting for transfers between devices, per_device(): lax.psum_scatter(output.astype(jnp.bfloat16), 'heads', scatter_dimension=...  24.1 us
    all_gather x1, waiting for transfers between devices, per_device(): gathered = lax.all_gather(normed, 'heads', axis=0, tiled=True)  14.7 us
    dot_general x1, matrix products, per_device(): jnp.einsum('bnkhc,bthc->bhnkt', block_queries, keys_here, preferred_eleme...  8.12 us
    dot_general x1, matrix products, per_device(): jnp.einsum('rb,bhnkc->rhnkc', owns_f, block_accum, precision=lax.Precisio...  6.32 us
    unnamed x40, local copies, waits for them, and re-layouts  6.3 us
    dot_general x1, matrix products, per_device(): jnp.einsum('bhnkt,bthc->bhnkc', weights.astype(jnp.bfloat16), values_here...  5.25 us
  transfers between devices with their start and end apart: 4, of which 4 were waited for; matrix products, arithmetic and copies ran while one was open for 9% of the time, Pallas kernels for 0%

profile of v1, /device:TPU:0, one launch (start us, length us, event | category | flops | bytes accessed | tf_op | source)
XLA Modules:
  0.0 225.4 jit_solution(2896448327227569336)
XLA Ops:
  7.4 1.1 fusion.38
  8.5 1.8 fusion.40
  13.9 1.2 multiply_cosine_fusion
  15.2 14.7 %all-gather.3.cloned.1.call-done = bf16[256,2048]{1,0:T(8,128)(2,1)} async-done(((bf16[64,2048]{1,0:T(8,128)(2,1)}), bf16[256,2048]{1,0:T(8,128)(2,1)}) %all-gather.3.cloned.1.call-update) | async-done | bytes 1048592 | tf_op jit(solution)/shard_map/all_gather | solution.py:72
  29.9 3.8 %fusion.30 = f32[256,4,256]{2,0,1:T(8,128)S(1)} fusion(bf16[4,2048,256]{2,1,0:T(8,128)(2,1)} %param.15, bf16[256,2048]{1,0:T(8,128)(2,1)} %all-gather.3.cloned.1.call-done), kind=kOutput, calls=%fused_computation.44 | convolution fusion | flops 1073741824 | bytes 6291456 | tf_op jit(solution)/shard_map/nd,edc->nec/dot_general | solution.py:78
  34.5 1.0 copy.272
  35.5 1.3 subtract_convert_fusion
  39.3 2.7 %fusion.122 = (bf16[1,16,128,256]{3,2,1,0:T(8,128)(2,1)}, bf16[1,16,128,256]{3,2,1,0:T(8,128)(2,1)S(1)}) fusion(bf16[2,16,128,256]{3,2,1,0:T(8,128)(2,1)} %param.18), kind=kLoop, calls=%fused_computation.196 | loop fusion | bytes 4194304 | tf_op jit(solution)/shard_map/slice | solution.py:102
  42.1 1.3 copy.274
  43.4 1.6 copy.275
  45.1 42.2 %all-gather.5.cloned.1.call-done = bf16[8,256,2,2,128]{4,1,3,2,0:T(8,128)(2,1)} async-done(((bf16[1,256,2,2,128]{4,1,3,2,0:T(8,128)(2,1)}), bf16[8,256,2,2,128]{4,1,3,2,0:T(8,128)(2,1)}) %all-gather.5.cloned.1.call-update) | async-done | bytes 2097168 | tf_op jit(solution)/shard_map/all_gather | solution.py:86
  87.4 4.6 %gather_fusion.2 = bf16[16,256,2,2,128]{4,1,3,2,0:T(8,128)(2,1)} fusion(bf16[8,256,2,2,128]{4,1,3,2,0:T(8,128)(2,1)} %all-gather.5.cloned.1.call-done, s32[1024]{0:T(1024)S(1)} %pad_clamp_fusion), kind=kCustom, calls=%fused_computation.2 | custom fusion | bytes 8388672 | tf_op jit(solution)/shard_map/jit(_take)/gather | solution.py:100
  92.0 8.1 %fusion.2 = (f32[16,2,256,2]{2,3,1,0:T(2,128)S(1)}, f32[16,2,256,2,128]{2,4,3,1,0:T(8,128)}) fusion(pred[16,128]{1,0:T(8,128)(4,1)S(1)} %add_compare_fusion, bf16[16,128,2,128,1]{1,3,4,2,0:T(8,128)(2,1)} %bitcast.191, bf16[16,256,2,2,128]{4,1,3,2,0:T(8,128)(2,1)} %gather_fusion.2, pred[16]{0:T(512)(128)(4,1)S(1)} %compare_and_fusion), kind=kOutput, calls=%fused_computation.8 | convolution fusion | flops 545243136 | bytes 13699088 | tf_op jit(solution)/shard_map/bnkhc,bthc->bhnkt/dot_general | solution.py:104
  101.8 4.7 %fusion.3 = f32[16,2,256,2]{2,3,1,0:T(2,128)S(1)} fusion(f32[16,2,256,2,128]{2,4,3,1,0:T(8,128)} %get-tuple-element.41, f32[16,2,256,2]{2,3,1,0:T(2,128)S(1)} %broadcast_select_fusion.1, pred[16,128]{1,0:T(8,128)(4,1)S(1)} %add_compare_fusion), kind=kLoop, calls=%fused_computation.9 | loop fusion | flops 8372224 | bytes 8521728 | tf_op jit(solution)/shard_map/reduce_sum | solution.py:119
  106.7 2.0 copy.237
  108.7 1.6 copy.239
  110.3 5.2 %fusion.5 = f32[16,2,256,2,128]{4,2,3,1,0:T(8,128)S(1)} fusion(bf16[16,128,2,128,1]{1,3,4,2,0:T(8,128)(2,1)S(1)} %bitcast.181, f32[16,2,256,2,128]{2,4,3,1,0:T(8,128)} %get-tuple-element.41, f32[16,2,256,2]{2,3,1,0:T(2,128)} %copy-done.7, pred[16,128]{1,0:T(8,128)(4,1)S(1)} %add_compare_fusion), kind=kOutput, calls=%fused_computation.11 | convolution fusion | flops 545259520 | bytes 17893376 | tf_op jit(solution)/shard_map/bhnkt,bthc->bhnkc/dot_general | solution.py:120
  115.5 6.3 %fusion.17 = bf16[8,2,256,2,128]{4,0,3,2,1:T(8,128)(2,1)S(1)} fusion(f32[16,2,256,2,128]{4,2,3,1,0:T(8,128)S(1)} %fusion.5, s32[16]{0:T(128)S(1)} %copy-done.14), kind=kOutput, calls=%fused_computation.30 | convolution fusion | flops 202375296 | bytes 10485824 | tf_op jit(solution)/shard_map/rb,bhnkc->rhnkc/dot_general | solution.py:127
  122.1 1.5 pad_maximum_fusion
  123.6 4.5 %all-to-all-start = ((bf16[8,1056,128]{2,1,0:T(8,128)(2,1)}), bf16[8,1056,128]{2,1,0:T(8,128)(2,1)}, u32[]{:S(2)}, u32[]{:S(2)}) async-start(bf16[8,1056,128]{2,1,0:T(8,128)(2,1)} %pad_maximum_fusion), calls=%async_computation | async-start | bytes 4325376 | tf_op jit(solution)/shard_map/all_to_all | solution.py:139
  129.0 2.2 convolution_bitcast_fusion.1
  132.6 1.0 copy.276
  133.7 1.6 fusion.130
  137.1 39.8 %all-to-all-done = bf16[8,1056,128]{2,1,0:T(8,128)(2,1)} async-done(((bf16[8,1056,128]{2,1,0:T(8,128)(2,1)}), bf16[8,1056,128]{2,1,0:T(8,128)(2,1)}, u32[]{:S(2)}, u32[]{:S(2)}) %all-to-all-start) | async-done | bytes 2162720 | tf_op jit(solution)/shard_map/all_to_all | solution.py:139
  177.8 1.9 copy.240
  179.7 1.9 fusion.121
  181.9 2.4 %fusion.44 = f32[2,256,2]{2,1,0:T(8,128)S(1)} fusion(f32[8,4,2,256,2]{0,4,3,2,1:T(2,128)} %bitcast.178, f32[8,1,2,256,2]{0,4,3,2,1:T(2,128)S(1)} %get-tuple-element.21, f32[2,256,2]{2,1,0:T(8,128)S(1)} %get-tuple-element.20), kind=kLoop, calls=%fused_computation.61 | loop fusion | flops 31744 | bytes 106496 | tf_op jit(solution)/shard_map/reduce_sum | solution.py:152
  184.4 3.1 %multiply_reduce_fusion = f32[1024,128]{1,0:T(8,128)S(1)} fusion(bf16[8,1056,128]{2,1,0:T(8,128)(2,1)} %all-to-all-done, f32[8,1024]{1,0:T(8,128)S(1)} %subtract_exponential_fusion.2), kind=kLoop, calls=%fused_computation.14 | loop fusion | flops 3014656 | bytes 2654208 | tf_op jit(solution)/shard_map/reduce_sum | solution.py:153
  188.7 1.8 fusion.24
  190.6 1.7 convolution_multiply_fusion.3
  193.3 1.5 fusion.16
  194.8 24.1 %reduce-scatter.2.cloned.1.call-done = bf16[64,2048]{1,0:T(8,128)(2,1)} async-done(((bf16[256,2048]{1,0:T(8,128)(2,1)}), bf16[64,2048]{1,0:T(8,128)(2,1)}) %reduce-scatter.2.cloned.1.call-update) | async-done | bytes 262160 | tf_op jit(solution)/shard_map/reduce_scatter | solution.py:194
  (104 shorter events, 17.4 us)
Async XLA Ops:
  6.5 122.4 %copy-start = (bf16[2,2048,256]{2,1,0:T(8,128)(2,1)S(1)}, bf16[2,2048,256]{2,1,0:T(8,128)(2,1)}, u32[]{:S(2)}) copy-start(bf16[2,2048,256]{2,1,0:T(8,128)(2,1)} %param.16) | copy-start | bytes 6291460
  6.5 23.4 %all-gather.3.cloned.1.call-start = ((), (), s32[]{:S(2)}) async-start(), calls=%async_computation.2 | async-start | bytes 1310720 | tf_op jit(solution)/shard_map/all_gather | solution.py:72
  10.3 77.1 %all-gather.5.cloned.1.call-start = ((), (), s32[]{:S(2)}) async-start(), calls=%async_computation.3 | async-start | bytes 2359296 | tf_op jit(solution)/shard_map/all_gather | solution.py:86
  33.7 4.0 %copy-start.16 = (s32[128]{0:T(128)S(1)}, s32[128]{0:T(128)}, u32[]{:S(2)}) copy-start(s32[128]{0:T(128)} %param.21) | copy-start | bytes 1540
  36.8 1.9 copy-start.3
  45.0 47.0 %copy-start.15 = (pred[16]{0:T(512)(128)(4,1)}, pred[16]{0:T(512)(128)(4,1)S(1)}, u32[]{:S(2)}) copy-start(pred[16]{0:T(512)(128)(4,1)S(1)} %compare_and_fusion) | copy-start | bytes 52
  45.0 47.0 %copy-start.13 = (s32[16]{0:T(128)}, s32[16]{0:T(128)S(1)}, u32[]{:S(2)}) copy-start(s32[16]{0:T(128)S(1)} %broadcast_add_fusion) | copy-start | bytes 196
  101.8 4.7 %copy-start.7 = (f32[16,2,256,2]{2,3,1,0:T(2,128)}, f32[16,2,256,2]{2,3,1,0:T(2,128)S(1)}, u32[]{:S(2)}) copy-start(f32[16,2,256,2]{2,3,1,0:T(2,128)S(1)} %broadcast_select_fusion.1) | copy-start | bytes 196612
  101.8 4.7 %copy-start.14 = (s32[16]{0:T(128)S(1)}, s32[16]{0:T(128)}, u32[]{:S(2)}) copy-start(s32[16]{0:T(128)} %copy-done.13) | copy-start | bytes 196
  122.1 6.3 %copy-start.9 = (s32[1,256,2]{1,2,0:T(2,128)S(1)}, s32[1,256,2]{1,2,0:T(2,128)}, u32[]{:S(2)}) copy-start(s32[1,256,2]{1,2,0:T(2,128)} %param.14) | copy-start | bytes 6148
  123.6 10.1 %copy-start.10 = (bf16[2048,4]{0,1:T(4,128)(2,1)S(1)}, bf16[2048,4]{0,1:T(4,128)(2,1)}, u32[]{:S(2)}) copy-start(bf16[2048,4]{0,1:T(4,128)(2,1)} %param.13) | copy-start | bytes 49156
  123.6 53.3 %all-to-all-start = ((bf16[8,1056,128]{2,1,0:T(8,128)(2,1)}), bf16[8,1056,128]{2,1,0:T(8,128)(2,1)}, u32[]{:S(2)}, u32[]{:S(2)}) async-start(bf16[8,1056,128]{2,1,0:T(8,128)(2,1)} %pad_maximum_fusion), calls=%async_computation | async-start | bytes 4325376 | tf_op jit(solution)/shard_map/all_to_all | solution.py:139
  128.1 7.3 %copy-start.5 = (f32[256,64]{1,0:T(8,128)S(1)}, f32[256,64]{1,0:T(8,128)}, u32[]{:S(2)}) copy-start(f32[256,64]{1,0:T(8,128)} %get-tuple-element.36) | copy-start | bytes 196612
  128.1 7.3 %copy-start.6 = (f32[256,64]{1,0:T(8,128)S(1)}, f32[256,64]{1,0:T(8,128)}, u32[]{:S(2)}) copy-start(f32[256,64]{1,0:T(8,128)} %get-tuple-element.37) | copy-start | bytes 196612
  128.1 7.4 %copy-start.4 = (bf16[256,2,2,64]{3,0,1,2:T(8,128)(2,1)S(1)}, bf16[256,2,2,64]{3,0,1,2:T(8,128)(2,1)}, u32[]{:S(2)}) copy-start(bf16[256,2,2,64]{3,0,1,2:T(8,128)(2,1)} %copy-done.3) | copy-start | bytes 393220
  128.1 90.8 %reduce-scatter.2.cloned.1.call-start = ((), (), s32[]{:S(2)}) async-start(), calls=%async_computation.4 | async-start | bytes 1310720 | tf_op jit(solution)/shard_map/reduce_scatter | solution.py:194
  136.0 1.0 copy-start.2
  179.7 9.0 %copy-start.8 = (bf16[1,256,256]{1,2,0:T(8,128)(2,1)S(1)}, bf16[1,256,256]{1,2,0:T(8,128)(2,1)}, u32[]{:S(2)}) copy-start(bf16[1,256,256]{1,2,0:T(8,128)(2,1)} %slice.234) | copy-start | bytes 393220
  188.7 3.6 %copy-start.1 = (bf16[4,256,2048]{2,1,0:T(8,128)(2,1)S(1)}, bf16[4,256,2048]{2,1,0:T(8,128)(2,1)}, u32[]{:S(2)}) copy-start(bf16[4,256,2048]{2,1,0:T(8,128)(2,1)} %param.17) | copy-start | bytes 12582916
  192.3 1.0 copy-start.11
  192.3 1.0 copy-start.12
Sparse Core Ops, SparseCore 0:
  10.4 19.4 all-gather.2
  37.8 49.5 all-gather.4
  194.9 23.9 reduce-scatter.1

commit v2 on v1

v2 whole, which is shorter than its diff:
```python
import jax
import jax.numpy as jnp
from jax import lax
from jax.sharding import PartitionSpec as P

HD = 128


NEG_FILL = -1e30


def rotate(values, positions):
    half_dim = values.shape[-1] // 2
    inverse = 10000.0 ** (-2.0 * jnp.arange(half_dim, dtype=jnp.float32) / values.shape[-1])
    angles = positions.astype(jnp.float32)[:, None] * inverse[None, :]
    target = (values.shape[0],) + (1,) * (values.ndim - 2) + (half_dim,)
    cosine = jnp.cos(angles).reshape(target)
    sine_part = jnp.sin(angles).reshape(target)
    leading_part = values[..., :half_dim]
    trailing_part = values[..., half_dim:]
    return jnp.concatenate(
        [
            leading_part * cosine - trailing_part * sine_part,
            trailing_part * cosine + leading_part * sine_part,
        ],
        axis=-1,
    )


def normalize(rows, norm_gain):
    wide_rows = rows.astype(jnp.float32)
    scaled = wide_rows * lax.rsqrt(jnp.mean(wide_rows * wide_rows, axis=-1, keepdims=True) + 1e-05)
    return (scaled * norm_gain.astype(jnp.float32)).astype(jnp.bfloat16)


def route(normed, router_weight, chosen):
    logits = jnp.dot(normed, router_weight, preferred_element_type=jnp.float32)
    experts_all = router_weight.shape[1]
    onehot = (chosen[:, :, None] == jnp.arange(experts_all, dtype=jnp.int32)[None, None, :]).astype(
        jnp.float32
    )
    picked = jnp.sum(onehot * logits[:, None, :], axis=-1)
    return (onehot, jax.nn.softmax(picked, axis=-1))


def split_bf16(x):
    hi = lax.reduce_precision(x, exponent_bits=8, mantissa_bits=7)
    lo = lax.reduce_precision(x - hi, exponent_bits=8, mantissa_bits=7)
    return hi, lo


def per_device(
    hidden,
    norm_gain,
    router_weight,
    att_experts,
    q_weight,
    kv_weight,
    o_weight,
    kv_cache,
    cached_blocks,
    tail_trim,
    block_pool,
):
    head_count = lax.axis_size("heads")
    seq_rank = lax.axis_index("seq")
    block_size = kv_cache.shape[2]
    local_blocks = kv_cache.shape[1]
    local_heads = q_weight.shape[2] // HD
    scale_q = HD ** (-0.5)
    normed = normalize(hidden[0], norm_gain)
    gathered = lax.all_gather(normed, "heads", axis=0, tiled=True)
    new_count = gathered.shape[0]
    chosen = att_experts[0]
    cached_len = cached_blocks * block_size - tail_trim
    positions = cached_len[seq_rank] + jnp.arange(new_count, dtype=jnp.int32)
    onehot, gates = route(gathered, router_weight, chosen)
    every_q = jnp.einsum("nd,edc->nec", gathered, q_weight, preferred_element_type=jnp.float32)
    chosen_q = jnp.sum(onehot[:, :, :, None] * every_q[:, None, :, :], axis=2).reshape(
        new_count, 2, local_heads, HD
    )
    queries = rotate(chosen_q, positions).astype(jnp.bfloat16)
    fresh = jnp.einsum("nd,sdc->snc", gathered, kv_weight, preferred_element_type=jnp.float32)
    new_keys = rotate(fresh[0].reshape(new_count, local_heads, HD), positions).astype(jnp.bfloat16)
    new_values = fresh[1].reshape(new_count, local_heads, HD).astype(jnp.bfloat16)
    pool_size = block_pool.shape[0]

    global_ids = seq_rank * local_blocks + jnp.arange(local_blocks, dtype=jnp.int32)
    matches = block_pool[None, :] == global_ids[:, None]
    slot_of = jnp.sum(
        jnp.where(matches, jnp.arange(pool_size, dtype=jnp.int32)[None, :], 0), axis=1
    )
    starts = jnp.cumsum(cached_blocks) - cached_blocks
    owner = jnp.sum((starts[None, :] <= slot_of[:, None]).astype(jnp.int32), axis=1) - 1
    ordinal = slot_of - starts[owner]
    request_count = cached_blocks.shape[0]
    owns = owner[None, :] == jnp.arange(request_count, dtype=jnp.int32)[:, None]
    owns_f = owns.astype(jnp.float32)
    key_pos = ordinal[:, None] * block_size + jnp.arange(block_size, dtype=jnp.int32)[None, :]
    key_ok = key_pos < cached_len[owner][:, None]
    keys_here = kv_cache[0].reshape(local_blocks, block_size, local_heads, HD)
    values_here = kv_cache[1].reshape(local_blocks, block_size, local_heads, HD)
    slots = queries.shape[1]

    gathered_q = [
        lax.all_gather(queries[None, :, slot], "seq", axis=0, tiled=True) for slot in range(slots)
    ]

    self_scores = (
        jnp.einsum("nkhc,thc->khnt", queries, new_keys, preferred_element_type=jnp.float32)
        * scale_q
    )
    causal = (
        jnp.arange(new_count, dtype=jnp.int32)[None, :]
        <= jnp.arange(new_count, dtype=jnp.int32)[:, None]
    )
    self_scores = jnp.where(causal[None, None], self_scores, NEG_FILL)
    self_best = jnp.max(self_scores, axis=-1)
    self_weights = jnp.exp(self_scores - self_best[..., None])
    self_total = jnp.sum(self_weights, axis=-1)
    self_accum = jnp.einsum(
        "khnt,thc->khnc",
        self_weights.astype(jnp.bfloat16),
        new_values,
        preferred_element_type=jnp.float32,
    )
    self_parts = (self_best, self_total, self_accum)

    def cache_payload(slot_queries):
        block_queries = jnp.take(slot_queries, owner, axis=0)
        scores = (
            jnp.einsum(
                "bnhc,bthc->bhnt", block_queries, keys_here, preferred_element_type=jnp.float32
            )
            * scale_q
        )
        scores = jnp.where(key_ok[:, None, None, :], scores, NEG_FILL)
        block_best = jnp.max(scores, axis=-1)
        request_best = jnp.max(
            jnp.where(owns[:, :, None, None], block_best[None], NEG_FILL), axis=1
        )
        best_hi, best_lo = split_bf16(request_best)
        request_ref = best_hi + best_lo
        weights = jnp.exp(scores - jnp.take(request_ref, owner, axis=0)[..., None])
        block_totals = jnp.sum(weights, axis=-1)
        block_accum = jnp.einsum(
            "bhnt,bthc->bhnc",
            weights.astype(jnp.bfloat16),
            values_here,
            preferred_element_type=jnp.float32,
        )
        accum = jnp.einsum("rb,bhnc->rhnc", owns_f, block_accum, precision=lax.Precision.HIGHEST)
        totals = jnp.einsum("rb,bhn->rhn", owns_f, block_totals, precision=lax.Precision.HIGHEST)
        totals_hi, totals_lo = split_bf16(totals)
        stats = jnp.stack([best_hi, best_lo, totals_hi, totals_lo], axis=1).astype(jnp.bfloat16)
        stat_rows = stats.size // (request_count * HD)
        return jnp.concatenate(
            [
                accum.astype(jnp.bfloat16).reshape(request_count, -1, HD),
                stats.reshape(request_count, stat_rows, HD),
            ],
            axis=1,
        )

    def finish(received, slot):
        acc_rows = local_heads * new_count
        sources = received.shape[0]
        part_accum = received[:, :acc_rows].astype(jnp.float32).reshape(
            sources, local_heads, new_count, HD
        )
        part_stats = received[:, acc_rows:].astype(jnp.float32).reshape(
            sources, 4, local_heads, new_count
        )
        part_best = part_stats[:, 0] + part_stats[:, 1]
        part_totals = part_stats[:, 2] + part_stats[:, 3]
        cache_best = jnp.max(part_best, axis=0)
        factor = jnp.exp(part_best - cache_best[None])
        cache_total = jnp.sum(part_totals * factor, axis=0)
        cache_accum = jnp.sum(part_accum * factor[..., None], axis=0)
        slot_best, slot_total, slot_accum = (part[slot] for part in self_parts)
        peak = jnp.maximum(cache_best, slot_best)
        cache_share = jnp.exp(cache_best - peak)
        self_share = jnp.exp(slot_best - peak)
        numerator = cache_accum * cache_share[..., None] + slot_accum * self_share[..., None]
        denominator = cache_total * cache_share + slot_total * self_share
        attended = jnp.transpose(
            (numerator / denominator[..., None]).astype(jnp.bfloat16), (1, 0, 2)
        ).reshape(new_count, local_heads * HD)
        experts_all = o_weight.shape[0]
        picked = jnp.where(
            chosen[:, slot, None, None] == jnp.arange(experts_all, dtype=jnp.int32)[None, :, None],
            attended[:, None, :],
            jnp.zeros_like(attended[:, None, :]),
        )
        projected = jnp.einsum(
            "nec,ecd->nd", picked, o_weight, preferred_element_type=jnp.float32
        )
        return gates[:, slot, None] * projected

    first_queries, self_parts = lax.optimization_barrier((gathered_q[0], self_parts))
    payloads = [cache_payload(first_queries)]
    second_queries, first_payload = lax.optimization_barrier((gathered_q[1], payloads[0]))
    first_received = lax.all_to_all(first_payload, "seq", 0, 0, tiled=True)
    second_payload = cache_payload(second_queries)
    second_received = lax.all_to_all(second_payload, "seq", 0, 0, tiled=True)
    first_out = finish(first_received, 0)
    second_received, first_out = lax.optimization_barrier((second_received, first_out))
    output = first_out + finish(second_received, 1)
    summed = lax.psum_scatter(
        output.astype(jnp.bfloat16), "heads", scatter_dimension=0, tiled=True
    ).astype(jnp.float32)
    return summed[None].astype(jnp.bfloat16)


def solution(mesh):
    return jax.shard_map(
        per_device,
        mesh=mesh,
        in_specs=(
            P("seq", "heads", None),
            P(),
            P(),
            P("seq", None, None),
            P(None, None, "heads"),
            P(None, None, "heads"),
            P(None, "heads", None),
            P(None, "seq", None, "heads"),
            P(),
            P(),
            P(),
        ),
        out_specs=P("seq", "heads", None),
        check_vma=False,
    )
```

time: 226 us -> 233 us (1.031)
  waiting for transfers between devices: 121 us -> 99.8 us
  matrix products: 33.7 us -> 45.3 us
  local copies, waits for them, and re-layouts: 26 us -> 33.8 us
  other arithmetic: 26.3 us -> 31.4 us
  starting transfers between devices: 4.79 us -> 8.35 us
    all_to_all x1 -> x2, waiting for transfers between devices: 39.8 us -> 19.1 us  [the longest x1 14.6 us: per_device(): second_received = lax.all_to_all(second_payload, 'seq', 0, 0, tiled=True)]
    all_gather x1, waiting for transfers between devices: 14.7 us -> 2.57 us  [per_device(): gathered = lax.all_gather(normed, 'heads', axis=0, tiled=True)]
    dot_general x10 -> x12, matrix products: 26.2 us -> 38 us  [the longest x2 10 us: finish(): jnp.einsum('nec,ecd->nd', picked, o_weight, preferred_element_type=jnp.fl...]
    all_gather x1 -> x2, waiting for transfers between devices: 42.2 us -> 53.9 us  [per_device(): lax.all_gather(queries[None, :, slot], 'seq', axis=0, tiled=True)]
    unnamed x40 -> x30, local copies, waits for them, and re-layouts: 6.3 us -> 12.1 us
    all_to_all x1 -> x2, starting transfers between devices: 4.48 us -> 8.04 us  [the longest x1 4.47 us: per_device(): first_received = lax.all_to_all(first_payload, 'seq', 0, 0, tiled=True)]
    gather x2 -> x4, local copies, waits for them, and re-layouts: 5.27 us -> 8.41 us  [the longest x2 6.98 us: cache_payload(): block_queries = jnp.take(slot_queries, owner, axis=0)]
    convert_element_type x0 -> x2, other arithmetic: none -> 2.66 us  [finish(): (numerator / denominator[..., None]).astype(jnp.bfloat16)]
  transfers between devices with their start and end apart: 4 -> 6, of which waited for: 4 -> 6; matrix products, arithmetic and copies ran while one was open for 9% -> 33% of each run, Pallas kernels for 0% -> 0%
where the time goes in v2:
time: 233 us; the launch traced here: 232 us
  waiting for transfers between devices  99.8 us (43%)
  matrix products  45.3 us (19%)
  local copies, waits for them, and re-layouts  33.8 us (15%)
  other arithmetic  31.4 us (13%)
  between operations  13.7 us (6%)
  starting transfers between devices  8.35 us (4%)
    all_gather x2, waiting for transfers between devices, per_device(): lax.all_gather(queries[None, :, slot], 'seq', axis=0, tiled=True)  53.9 us
    reduce_scatter x1, waiting for transfers between devices, per_device(): lax.psum_scatter(output.astype(jnp.bfloat16), 'heads', scatter_dimension=...  24.1 us
    all_to_all x1, waiting for transfers between devices, per_device(): second_received = lax.all_to_all(second_payload, 'seq', 0, 0, tiled=True)  14.6 us
    unnamed x30, local copies, waits for them, and re-layouts  12.1 us
    dot_general x2, matrix products, finish(): jnp.einsum('nec,ecd->nd', picked, o_weight, preferred_element_type=jnp.fl...  10 us
    dot_general x2, matrix products, cache_payload(): jnp.einsum('bnhc,bthc->bhnt', block_queries, keys_here, preferred_element...  9.94 us
    dot_general x2, matrix products, cache_payload(): jnp.einsum('rb,bhnc->rhnc', owns_f, block_accum, precision=lax.Precision....  7.8 us
    gather x2, local copies, waits for them, and re-layouts, cache_payload(): block_queries = jnp.take(slot_queries, owner, axis=0)  6.98 us
  transfers between devices with their start and end apart: 6, of which 6 were waited for; matrix products, arithmetic and copies ran while one was open for 33% of the time, Pallas kernels for 0%

profile of v2, /device:TPU:0, one launch (start us, length us, event | category | flops | bytes accessed | tf_op | source)
XLA Modules:
  0.0 232.3 jit_solution(21598897990954414)
XLA Ops:
  8.5 1.8 fusion.49
  17.9 3.2 %fusion.138 = (bf16[1,16,128,256]{3,2,1,0:T(8,128)(2,1)}, bf16[1,16,128,256]{3,2,1,0:T(8,128)(2,1)}) fusion(bf16[2,16,128,256]{3,2,1,0:T(8,128)(2,1)} %param.22), kind=kLoop, calls=%fused_computation.221 | loop fusion | bytes 4194304 | tf_op jit(solution)/shard_map/slice | solution.py:102
  22.7 2.3 copy.320
  27.4 2.6 %all-gather.6.cloned.1.call-done = bf16[256,2048]{1,0:T(8,128)(2,1)} async-done(((bf16[64,2048]{1,0:T(8,128)(2,1)}), bf16[256,2048]{1,0:T(8,128)(2,1)}) %all-gather.6.cloned.1.call-update) | async-done | bytes 1048592 | tf_op jit(solution)/shard_map/all_gather | solution.py:72
  30.0 2.2 convolution_bitcast_fusion.3
  32.9 3.5 %fusion.41 = f32[256,4,256]{2,0,1:T(8,128)S(1)} fusion(bf16[4,2048,256]{2,1,0:T(8,128)(2,1)} %param.19, bf16[256,2048]{1,0:T(8,128)(2,1)S(1)} %copy-done.2), kind=kOutput, calls=%fused_computation.55 | convolution fusion | flops 1073741824 | bytes 6291456 | tf_op jit(solution)/shard_map/nd,edc->nec/dot_general | solution.py:78
  37.5 2.1 copy.260
  39.6 1.8 fusion.139
  42.1 1.7 copy.319
  45.6 2.0 copy.316
  47.6 2.0 copy.317
  57.1 2.0 convolution_bitcast_fusion.2
  59.2 33.8 %all-gather.10.cloned.1.call-done = bf16[2048,1,2,128]{3,0,1,2:T(8,128)(2,1)} async-done(((bf16[256,1,2,128]{3,0,1,2:T(8,128)(2,1)}), bf16[2048,1,2,128]{3,0,1,2:T(8,128)(2,1)}) %all-gather.10.cloned.1.call-update) | async-done | bytes 1048592 | tf_op jit(solution)/shard_map/all_gather | solution.py:106
  93.0 3.5 %gather_fusion.2 = bf16[16,256,2,128]{3,1,2,0:T(8,128)(2,1)} fusion(bf16[8,256,2,128]{3,1,0,2:T(8,128)(2,1)} %bitcast.215, s32[1024]{0:T(1024)} %pad_clamp_fusion), kind=kCustom, calls=%fused_computation.clone | custom fusion | bytes 4194368 | tf_op jit(solution)/shard_map/jit(_take)/gather | solution.py:130
  96.5 5.0 %fusion.4 = (f32[16,2,256]{2,1,0:T(2,128)S(1)}, f32[16,2,256,128]{2,3,1,0:T(8,128)}) fusion(pred[16,128]{1,0:T(8,128)(4,1)S(1)} %add_compare_fusion, bf16[16,128,2,128]{1,3,2,0:T(8,128)(2,1)} %bitcast.219, bf16[16,256,2,128]{3,1,2,0:T(8,128)(2,1)} %gather_fusion.2, pred[16]{0:T(512)(128)(4,1)S(1)} %copy-done.7), kind=kOutput, calls=%fused_computation.14 | convolution fusion | flops 272621568 | bytes 7374864 | tf_op jit(solution)/shard_map/bnhc,bthc->bhnt/dot_general | solution.py:132
  102.4 2.8 %fusion.6 = f32[16,2,256]{2,1,0:T(2,128)S(1)} fusion(f32[16,2,256,128]{2,3,1,0:T(8,128)} %get-tuple-element.68, f32[16,2,256]{2,1,0:T(2,128)S(1)} %broadcast_select_fusion.1, pred[16,128]{1,0:T(8,128)(4,1)S(1)} %add_compare_fusion), kind=kLoop, calls=%fused_computation.16 | loop fusion | flops 4186112 | bytes 4261888 | tf_op jit(solution)/shard_map/reduce_sum | solution.py:145
  105.5 3.3 %fusion.16 = f32[16,2,256,128]{3,2,1,0:T(8,128)S(1)} fusion(bf16[16,128,2,128]{1,3,2,0:T(8,128)(2,1)S(1)} %bitcast.212, f32[16,2,256,128]{2,3,1,0:T(8,128)} %get-tuple-element.68, f32[16,2,256]{2,1,0:T(2,128)S(1)} %broadcast_select_fusion.1, pred[16,128]{1,0:T(8,128)(4,1)S(1)} %add_compare_fusion), kind=kOutput, calls=%fused_computation.27 | convolution fusion | flops 272629760 | bytes 9472000 | tf_op jit(solution)/shard_map/bhnt,bthc->bhnc/dot_general | solution.py:146
  108.8 3.9 %fusion.32 = bf16[8,2,256,128]{3,0,2,1:T(8,128)(2,1)S(1)} fusion(f32[16,2,256,128]{3,2,1,0:T(8,128)S(1)} %fusion.16, s32[16]{0:T(128)S(1)} %copy-done.5), kind=kOutput, calls=%fused_computation.45 | convolution fusion | flops 101187712 | bytes 5242944 | tf_op jit(solution)/shard_map/rb,bhnc->rhnc/dot_general | solution.py:152
  114.0 20.2 %all-gather.8.cloned.1.call-done = bf16[2048,1,2,128]{3,0,1,2:T(8,128)(2,1)} async-done(((bf16[256,1,2,128]{3,0,1,2:T(8,128)(2,1)}), bf16[2048,1,2,128]{3,0,1,2:T(8,128)(2,1)}) %all-gather.8.cloned.1.call-update) | async-done | bytes 1048592 | tf_op jit(solution)/shard_map/all_gather | solution.py:106
  134.1 4.5 %all-to-all-start.1 = ((bf16[8,528,128]{2,1,0:T(8,128)(2,1)}), bf16[8,528,128]{2,1,0:T(8,128)(2,1)}, u32[]{:S(2)}, u32[]{:S(2)}) async-start(bf16[8,528,128]{2,1,0:T(8,128)(2,1)} %pad_maximum_fusion), calls=%async_computation.1 | async-start | bytes 2162688 | tf_op jit(solution)/shard_map/all_to_all | solution.py:203
  138.6 3.5 %gather_fusion.4 = bf16[16,256,2,128]{3,1,2,0:T(8,128)(2,1)} fusion(bf16[8,256,2,128]{3,1,0,2:T(8,128)(2,1)} %bitcast.214, s32[1024]{0:T(1024)} %pad_clamp_fusion), kind=kCustom, calls=%fused_computation.2.clone | custom fusion | bytes 4194368 | tf_op jit(solution)/shard_map/jit(_take)/gather | solution.py:130
  142.1 5.0 %fusion.5 = (f32[16,2,256]{2,1,0:T(2,128)S(1)}, f32[16,2,256,128]{2,3,1,0:T(8,128)}) fusion(pred[16,128]{1,0:T(8,128)(4,1)S(1)} %add_compare_fusion, bf16[16,128,2,128]{1,3,2,0:T(8,128)(2,1)} %bitcast.220, bf16[16,256,2,128]{3,1,2,0:T(8,128)(2,1)} %gather_fusion.4, pred[16]{0:T(512)(128)(4,1)S(1)} %copy-done.7), kind=kOutput, calls=%fused_computation.15 | convolution fusion | flops 272621568 | bytes 7374864 | tf_op jit(solution)/shard_map/bnhc,bthc->bhnt/dot_general | solution.py:132
  148.1 2.8 %fusion.8 = f32[16,2,256]{2,1,0:T(2,128)S(1)} fusion(f32[16,2,256,128]{2,3,1,0:T(8,128)} %get-tuple-element.70, f32[16,2,256]{2,1,0:T(2,128)S(1)} %broadcast_select_fusion, pred[16,128]{1,0:T(8,128)(4,1)S(1)} %add_compare_fusion), kind=kLoop, calls=%fused_computation.18 | loop fusion | flops 4186112 | bytes 4261888 | tf_op jit(solution)/shard_map/reduce_sum | solution.py:145
  151.2 3.3 %fusion.14 = f32[16,2,256,128]{3,2,1,0:T(8,128)S(1)} fusion(bf16[16,128,2,128]{1,3,2,0:T(8,128)(2,1)S(1)} %bitcast.213, f32[16,2,256,128]{2,3,1,0:T(8,128)} %get-tuple-element.70, f32[16,2,256]{2,1,0:T(2,128)S(1)} %broadcast_select_fusion, pred[16,128]{1,0:T(8,128)(4,1)S(1)} %add_compare_fusion), kind=kOutput, calls=%fused_computation.26 | convolution fusion | flops 272629760 | bytes 9472000 | tf_op jit(solution)/shard_map/bhnt,bthc->bhnc/dot_general | solution.py:146
  154.5 3.9 %fusion.35 = bf16[8,2,256,128]{3,0,2,1:T(8,128)(2,1)S(1)} fusion(f32[16,2,256,128]{3,2,1,0:T(8,128)S(1)} %fusion.14, s32[16]{0:T(128)S(1)} %copy-done.5), kind=kOutput, calls=%fused_computation.46 | convolution fusion | flops 101187712 | bytes 5242944 | tf_op jit(solution)/shard_map/rb,bhnc->rhnc/dot_general | solution.py:152
  159.6 4.5 %all-to-all-done.1 = bf16[8,528,128]{2,1,0:T(8,128)(2,1)} async-done(((bf16[8,528,128]{2,1,0:T(8,128)(2,1)}), bf16[8,528,128]{2,1,0:T(8,128)(2,1)}, u32[]{:S(2)}, u32[]{:S(2)}) %all-to-all-start.1) | async-done | bytes 1081376 | tf_op jit(solution)/shard_map/all_to_all | solution.py:203
  164.1 3.6 %all-to-all-start = ((bf16[8,528,128]{2,1,0:T(8,128)(2,1)}), bf16[8,528,128]{2,1,0:T(8,128)(2,1)S(1)}, u32[]{:S(2)}, u32[]{:S(2)}) async-start(bf16[8,528,128]{2,1,0:T(8,128)(2,1)} %pad_maximum_fusion.1), calls=%async_computation | async-start | bytes 2162688 | tf_op jit(solution)/shard_map/all_to_all | solution.py:205
  168.7 2.5 %multiply_reduce_fusion.1 = f32[512,128]{1,0:T(8,128)} fusion(bf16[8,528,128]{2,1,0:T(8,128)(2,1)} %all-to-all-done.1, f32[8,512]{1,0:T(8,128)S(1)} %subtract_exponential_fusion.4), kind=kLoop, calls=%fused_computation.33 | loop fusion | flops 1507328 | bytes 1327104 | tf_op jit(solution)/shard_map/reduce_sum | solution.py:179
  175.0 4.8 %fusion.11 = f32[256,2048]{1,0:T(8,128)} fusion(bf16[4,256,2048]{2,1,0:T(8,128)(2,1)} %param.21, f32[256]{0:T(256)S(1)} %bitcast.241, pred[256,4]{0,1:T(4,128)(4,1)S(1)} %copy-done.9, bf16[256,256]{1,0:T(8,128)(2,1)S(1)} %copy.297), kind=kOutput, calls=%fused_computation.23 | convolution fusion | flops 1074528256 | bytes 6424576 | tf_op jit(solution)/shard_map/nec,ecd->nd/dot_general | solution.py:195
  179.8 14.6 %all-to-all-done = bf16[8,528,128]{2,1,0:T(8,128)(2,1)S(1)} async-done(((bf16[8,528,128]{2,1,0:T(8,128)(2,1)}), bf16[8,528,128]{2,1,0:T(8,128)(2,1)S(1)}, u32[]{:S(2)}, u32[]{:S(2)}) %all-to-all-start) | async-done | bytes 1081376 | tf_op jit(solution)/shard_map/all_to_all | solution.py:205
  196.5 5.2 %fusion.13 = bf16[256,2048]{1,0:T(8,128)(2,1)} fusion(f32[256,2048]{1,0:T(8,128)} %fusion.11, bf16[4,256,2048]{2,1,0:T(8,128)(2,1)} %param.21, f32[256]{0:T(256)S(1)} %bitcast.240, pred[256,4]{0,1:T(4,128)(4,1)S(1)} %copy-done.8, bf16[256,256]{1,0:T(8,128)(2,1)S(1)} %copy.302), kind=kOutput, calls=%fused_computation.25 | convolution fusion | flops 1075576832 | bytes 7473152 | tf_op jit(solution)/shard_map/nec,ecd->nd/dot_general | solution.py:195
  201.7 24.1 %reduce-scatter.2.cloned.1.call-done = bf16[64,2048]{1,0:T(8,128)(2,1)} async-done(((bf16[256,2048]{1,0:T(8,128)(2,1)}), bf16[64,2048]{1,0:T(8,128)(2,1)}) %reduce-scatter.2.cloned.1.call-update) | async-done | bytes 262160 | tf_op jit(solution)/shard_map/reduce_scatter | solution.py:209
  (123 shorter events, 36.8 us)
Async XLA Ops:
  6.5 23.4 %copy-start = (bf16[2,2048,256]{2,1,0:T(8,128)(2,1)S(1)}, bf16[2,2048,256]{2,1,0:T(8,128)(2,1)}, u32[]{:S(2)}) copy-start(bf16[2,2048,256]{2,1,0:T(8,128)(2,1)} %param.20) | copy-start | bytes 6291460
  6.5 23.4 %all-gather.6.cloned.1.call-start = ((), (), s32[]{:S(2)}) async-start(), calls=%async_computation.3 | async-start | bytes 1310720 | tf_op jit(solution)/shard_map/all_gather | solution.py:72
  10.3 82.7 %all-gather.10.cloned.1.call-start = ((), (), s32[]{:S(2)}) async-start(), calls=%async_computation.6 | async-start | bytes 1179648 | tf_op jit(solution)/shard_map/all_gather | solution.py:106
  12.8 8.2 %copy-start.4 = (s32[16]{0:T(128)}, s32[16]{0:T(128)S(1)}, u32[]{:S(2)}) copy-start(s32[16]{0:T(128)S(1)} %broadcast_add_fusion) | copy-start | bytes 196
  17.9 7.2 %copy-start.3 = (s32[1,256,2]{1,2,0:T(2,128)S(1)}, s32[1,256,2]{1,2,0:T(2,128)}, u32[]{:S(2)}) copy-start(s32[1,256,2]{1,2,0:T(2,128)} %param.18) | copy-start | bytes 6148
  30.0 2.9 %copy-start.2 = (bf16[256,2048]{1,0:T(8,128)(2,1)S(1)}, bf16[256,2048]{1,0:T(8,128)(2,1)}, u32[]{:S(2)}) copy-start(bf16[256,2048]{1,0:T(8,128)(2,1)} %all-gather.6.cloned.1.call-done) | copy-start | bytes 3145732
  50.9 0.7 copy-start.1
  52.5 81.7 %all-gather.8.cloned.1.call-start = ((), (), s32[]{:S(2)}) async-start(), calls=%async_computation.5 | async-start | bytes 1179648 | tf_op jit(solution)/shard_map/all_gather | solution.py:106
  55.5 40.9 %copy-start.7 = (pred[16]{0:T(512)(128)(4,1)S(1)}, pred[16]{0:T(512)(128)(4,1)}, u32[]{:S(2)}) copy-start(pred[16]{0:T(512)(128)(4,1)} %get-tuple-element.33) | copy-start | bytes 52
  96.5 5.0 %copy-start.6 = (pred[8,16]{1,0:T(8,128)(4,1)S(1)}, pred[8,16]{1,0:T(8,128)(4,1)}, u32[]{:S(2)}) copy-start(pred[8,16]{1,0:T(8,128)(4,1)} %iota_compare_fusion.4) | copy-start | bytes 388
  101.4 3.9 %copy-start.5 = (s32[16]{0:T(128)S(1)}, s32[16]{0:T(128)}, u32[]{:S(2)}) copy-start(s32[16]{0:T(128)} %copy-done.4) | copy-start | bytes 196
  134.1 30.0 %all-to-all-start.1 = ((bf16[8,528,128]{2,1,0:T(8,128)(2,1)}), bf16[8,528,128]{2,1,0:T(8,128)(2,1)}, u32[]{:S(2)}, u32[]{:S(2)}) async-start(bf16[8,528,128]{2,1,0:T(8,128)(2,1)} %pad_maximum_fusion), calls=%async_computation.1 | async-start | bytes 2162688 | tf_op jit(solution)/shard_map/all_to_all | solution.py:203
  158.5 16.4 %copy-start.9 = (pred[256,4]{0,1:T(4,128)(4,1)S(1)}, pred[256,4]{0,1:T(4,128)(4,1)}, u32[]{:S(2)}) copy-start(pred[256,4]{0,1:T(4,128)(4,1)} %iota_compare_fusion.3) | copy-start | bytes 3076
  164.1 30.2 %all-to-all-start = ((bf16[8,528,128]{2,1,0:T(8,128)(2,1)}), bf16[8,528,128]{2,1,0:T(8,128)(2,1)S(1)}, u32[]{:S(2)}, u32[]{:S(2)}) async-start(bf16[8,528,128]{2,1,0:T(8,128)(2,1)} %pad_maximum_fusion.1), calls=%async_computation | async-start | bytes 2162688 | tf_op jit(solution)/shard_map/all_to_all | solution.py:205
  167.7 58.1 %reduce-scatter.2.cloned.1.call-start = ((), (), s32[]{:S(2)}) async-start(), calls=%async_computation.4 | async-start | bytes 1310720 | tf_op jit(solution)/shard_map/reduce_scatter | solution.py:209
  174.9 21.6 %copy-start.8 = (pred[256,4]{0,1:T(4,128)(4,1)S(1)}, pred[256,4]{0,1:T(4,128)(4,1)}, u32[]{:S(2)}) copy-start(pred[256,4]{0,1:T(4,128)(4,1)} %iota_compare_fusion.2) | copy-start | bytes 3076
Sparse Core Ops, SparseCore 0:
  10.4 19.4 all-gather.5
  52.6 40.3 all-gather.9
  95.2 38.9 all-gather.7
  201.8 23.9 reduce-scatter.1

commit v3 on v1

--- a/solution.py
+++ b/solution.py
@@ -1,3 +1,6 @@
+import functools
+
+import numpy as np
 import jax
 import jax.numpy as jnp
 from jax import lax
@@ -43,13 +46,114 @@
     return (onehot, jax.nn.softmax(picked, axis=-1))
 
 
-def split_bf16(x):
-    hi = lax.reduce_precision(x, exponent_bits=8, mantissa_bits=7)
-    lo = lax.reduce_precision(x - hi, exponent_bits=8, mantissa_bits=7)
-    return hi, lo
+def seq_cycle(mesh):
+    size = mesh.shape["seq"]
+    plain = list(range(size))
+    try:
+        devices = np.moveaxis(np.asarray(mesh.devices), mesh.axis_names.index("seq"), -1)
+        line = devices.reshape(-1, size)[0]
+        coords = np.array([list(d.coords) for d in line])
+    except Exception:
+        return plain
+    varying = [k for k in range(coords.shape[1]) if len(set(coords[:, k])) > 1]
+    if len(varying) == 1:
+        order = sorted(plain, key=lambda j: coords[j, varying[0]])
+        return order[0::2] + order[1::2][::-1]
+    if len(varying) != 2:
+        return plain
+    dim_a, dim_b = varying
+    values_a = sorted(set(coords[:, dim_a]))
+    values_b = sorted(set(coords[:, dim_b]))
+    if len(values_a) % 2:
+        dim_a, dim_b, values_a, values_b = dim_b, dim_a, values_b, values_a
+    if len(values_a) % 2 or len(values_a) * len(values_b) != size:
+        return plain
+    at = {(coords[j, dim_a], coords[j, dim_b]): j for j in plain}
+    cycle = [at[(a, values_b[0])] for a in values_a]
+    for row, a in enumerate(reversed(values_a)):
+        columns = values_b[1:] if row % 2 == 0 else values_b[1:][::-1]
+        cycle += [at[(a, b)] for b in columns]
+    if sorted(cycle) != plain:
+        return plain
+    return cycle
+
+
+def shift_all_gather(piece, axis_name):
+    size = lax.axis_size(axis_name)
+    rank = lax.axis_index(axis_name)
+    by_offset = [piece] + [
+        lax.ppermute(piece, axis_name, [(i, (i + s) % size) for i in range(size)])
+        for s in range(1, size)
+    ]
+    by_offset = jnp.stack(by_offset[:1] + by_offset[1:][::-1], axis=0)
+    return jnp.take(by_offset, (jnp.arange(size, dtype=jnp.int32) - rank) % size, axis=0)
+
+
+def shift_reduce_scatter(rows, axis_name):
+    size = lax.axis_size(axis_name)
+    rank = lax.axis_index(axis_name)
+    share = rows.shape[0] // size
+    total = lax.dynamic_slice_in_dim(rows, rank * share, share, 0).astype(jnp.float32)
+    for s in range(1, size):
+        piece = lax.dynamic_slice_in_dim(rows, ((rank + s) % size) * share, share, 0)
+        moved = lax.ppermute(piece, axis_name, [(i, (i + s) % size) for i in range(size)])
+        total = total + moved.astype(jnp.float32)
+    return total
+
+
+def ring_all_gather(piece, axis_name, cycle):
+    size = len(cycle)
+    forward = [(cycle[i], cycle[(i + 1) % size]) for i in range(size)]
+    backward = [(cycle[(i + 1) % size], cycle[i]) for i in range(size)]
+    ahead = size // 2
+    behind = size - 1 - ahead
+    from_behind, from_ahead = [], []
+    moving = piece
+    for _ in range(ahead):
+        moving = lax.ppermute(moving, axis_name, forward)
+        from_behind.append(moving)
+    moving = piece
+    for _ in range(behind):
+        moving = lax.ppermute(moving, axis_name, backward)
+        from_ahead.append(moving)
+    return jnp.stack([piece] + from_ahead + from_behind[::-1], axis=0)
+
+
+def merge_parts(first, second):
+    best_a, total_a, accum_a = first
+    best_b, total_b, accum_b = second
+    best = jnp.maximum(best_a, best_b)
+    share_a = jnp.exp(best_a - best)
+    share_b = jnp.exp(best_b - best)
+    return (
+        best,
+        total_a * share_a + total_b * share_b,
+        accum_a * share_a[..., None] + accum_b * share_b[..., None],
+    )
+
+
+def ring_reduce_scatter(parts, axis_name, cycle, position, forward_dir):
+    size = len(cycle)
+    cycle_arr = jnp.asarray(cycle, dtype=jnp.int32)
+    step_sign = 1 if forward_dir else -1
+    if forward_dir:
+        pairs = [(cycle[i], cycle[(i + 1) % size]) for i in range(size)]
+    else:
+        pairs = [(cycle[(i + 1) % size], cycle[i]) for i in range(size)]
+
+    def own(step):
+        request = cycle_arr[(position - step_sign * (1 + step)) % size]
+        return tuple(lax.dynamic_index_in_dim(p, request, 0, keepdims=False) for p in parts)
+
+    carried = own(0)
+    for step in range(1, size):
+        arrived = lax.ppermute(carried, axis_name, pairs)
+        carried = merge_parts(arrived, own(step))
+    return carried
 
 
 def per_device(
+    cycle,
     hidden,
     norm_gain,
     router_weight,
@@ -69,7 +173,7 @@
     local_heads = q_weight.shape[2] // HD
     scale_q = HD ** (-0.5)
     normed = normalize(hidden[0], norm_gain)
-    gathered = lax.all_gather(normed, "heads", axis=0, tiled=True)
+    gathered = shift_all_gather(normed, "heads").reshape(-1, normed.shape[1])
     new_count = gathered.shape[0]
     chosen = att_experts[0]
     cached_len = cached_blocks * block_size - tail_trim
@@ -83,8 +187,11 @@
     fresh = jnp.einsum("nd,sdc->snc", gathered, kv_weight, preferred_element_type=jnp.float32)
     new_keys = rotate(fresh[0].reshape(new_count, local_heads, HD), positions).astype(jnp.bfloat16)
     new_values = fresh[1].reshape(new_count, local_heads, HD).astype(jnp.bfloat16)
-    all_queries = lax.all_gather(queries[None], "seq", axis=0, tiled=True)
-    request_count = all_queries.shape[0]
+    ring_queries = ring_all_gather(queries, "seq", cycle)
+    request_count = ring_queries.shape[0]
+    ring_size = len(cycle)
+    position_of = np.argsort(np.asarray(cycle))
+    position = jnp.asarray(position_of, dtype=jnp.int32)[seq_rank]
     pool_size = block_pool.shape[0]
 
     global_ids = seq_rank * local_blocks + jnp.arange(local_blocks, dtype=jnp.int32)
@@ -97,7 +204,8 @@
     ordinal = slot_of - starts[owner]
     owns = owner[None, :] == jnp.arange(request_count, dtype=jnp.int32)[:, None]
 
-    block_queries = jnp.take(all_queries, owner, axis=0)
+    owner_offset = (jnp.asarray(position_of, dtype=jnp.int32)[owner] - position) % ring_size
+    block_queries = jnp.take(ring_queries, owner_offset, axis=0)
     keys_here = kv_cache[0].reshape(local_blocks, block_size, local_heads, HD)
     values_here = kv_cache[1].reshape(local_blocks, block_size, local_heads, HD)
     scores = (
@@ -113,9 +221,7 @@
     request_best = jnp.max(
         jnp.where(owns[:, :, None, None, None], block_best[None], NEG_FILL), axis=1
     )
-    best_hi, best_lo = split_bf16(request_best)
-    request_ref = best_hi + best_lo
-    weights = jnp.exp(scores - jnp.take(request_ref, owner, axis=0)[..., None])
+    weights = jnp.exp(scores - jnp.take(request_best, owner, axis=0)[..., None])
     block_totals = jnp.sum(weights, axis=-1)
     block_accum = jnp.einsum(
         "bhnkt,bthc->bhnkc",
@@ -126,31 +232,15 @@
     owns_f = owns.astype(jnp.float32)
     accum = jnp.einsum("rb,bhnkc->rhnkc", owns_f, block_accum, precision=lax.Precision.HIGHEST)
     totals = jnp.einsum("rb,bhnk->rhnk", owns_f, block_totals, precision=lax.Precision.HIGHEST)
-    totals_hi, totals_lo = split_bf16(totals)
-    stats = jnp.stack([best_hi, best_lo, totals_hi, totals_lo], axis=1).astype(jnp.bfloat16)
-    stat_rows = stats.size // (request_count * HD)
-    payload = jnp.concatenate(
-        [
-            accum.astype(jnp.bfloat16).reshape(request_count, -1, HD),
-            stats.reshape(request_count, stat_rows, HD),
-        ],
-        axis=1,
-    )
-    received = lax.all_to_all(payload, "seq", 0, 0, tiled=True)
-    acc_rows = local_heads * new_count * 2
-    sources = received.shape[0]
-    part_accum = received[:, :acc_rows].astype(jnp.float32).reshape(
-        sources, local_heads, new_count, 2, HD
-    )
-    part_stats = received[:, acc_rows:].astype(jnp.float32).reshape(
-        sources, 4, local_heads, new_count, 2
-    )
-    part_best = part_stats[:, 0] + part_stats[:, 1]
-    part_totals = part_stats[:, 2] + part_stats[:, 3]
-    cache_best = jnp.max(part_best, axis=0)
-    factor = jnp.exp(part_best - cache_best[None])
-    cache_total = jnp.sum(part_totals * factor, axis=0)
-    cache_accum = jnp.sum(part_accum * factor[..., None], axis=0)
+    half = new_count // 2
+    halves = []
+    for index, forward_dir in enumerate((True, False)):
+        cut = slice(index * half, (index + 1) * half)
+        parts = (request_best[:, :, cut], totals[:, :, cut], accum[:, :, cut])
+        halves.append(ring_reduce_scatter(parts, "seq", cycle, position, forward_dir))
+    cache_best, cache_total, cache_accum = (
+        jnp.concatenate([first, second], axis=1) for first, second in zip(*halves)
+    )
 
     self_scores = (
         jnp.einsum("nkhc,thc->hnkt", queries, new_keys, preferred_element_type=jnp.float32)
@@ -191,15 +281,13 @@
         output = output + weight_expert[:, None] * jnp.dot(
             picked, o_weight[expert], preferred_element_type=jnp.float32
         )
-    summed = lax.psum_scatter(
-        output.astype(jnp.bfloat16), "heads", scatter_dimension=0, tiled=True
-    ).astype(jnp.float32)
+    summed = shift_reduce_scatter(output.astype(jnp.bfloat16), "heads")
     return summed[None].astype(jnp.bfloat16)
 
 
 def solution(mesh):
     return jax.shard_map(
-        per_device,
+        functools.partial(per_device, tuple(seq_cycle(mesh))),
         mesh=mesh,
         in_specs=(
             P("seq", "heads", None),

time: 226 us -> 279 us (1.23)
  waiting for transfers between devices: 121 us -> 50.5 us
  starting transfers between devices: 4.79 us -> 59.9 us
  between operations: 13.7 us -> 40.8 us
  local copies, waits for them, and re-layouts: 26 us -> 50.9 us
  other arithmetic: 26.3 us -> 44.3 us
    ppermute x0 -> x55, starting transfers between devices: none -> 59.9 us  [the longest x42 45 us: ring_reduce_scatter(): arrived = lax.ppermute(carried, axis_name, pairs)]
    all_gather x2 -> x0, waiting for transfers between devices: 57 us -> none  [the longest x1 42.2 us: per_device(): all_queries = lax.all_gather(queries[None], 'seq', axis=0, tiled=True)]
    ppermute x0 -> x55, waiting for transfers between devices: none -> 50.5 us  [the longest x42 28.4 us: ring_reduce_scatter(): arrived = lax.ppermute(carried, axis_name, pairs)]
    all_to_all x1 -> x0, waiting for transfers between devices: 39.8 us -> none  [per_device(): received = lax.all_to_all(payload, 'seq', 0, 0, tiled=True)]
    reduce_scatter x1 -> x0, waiting for transfers between devices: 24.1 us -> none  [per_device(): lax.psum_scatter(output.astype(jnp.bfloat16), 'heads', scatter_dimension=...]
    squeeze x0 -> x18, local copies, waits for them, and re-layouts: none -> 11.2 us  [own(): lax.dynamic_index_in_dim(p, request, 0, keepdims=False)]
    add x1 -> x28, other arithmetic: 0.01 us -> 9.74 us  [the longest x14 8.26 us: merge_parts(): total_a * share_a + total_b * share_b]
    dynamic_slice x0 -> x7, local copies, waits for them, and re-layouts: none -> 9.53 us  [the longest x4 6.62 us: own(): lax.dynamic_index_in_dim(p, request, 0, keepdims=False)]
  transfers between devices with their start and end apart: 4 -> 55, of which waited for: 4 -> 20; matrix products, arithmetic and copies ran while one was open for 9% -> 29% of each run, Pallas kernels for 0% -> 0%
where the time goes in v3:
time: 279 us; the launch traced here: 278 us
  starting transfers between devices  59.9 us (21%)
  local copies, waits for them, and re-layouts  50.9 us (18%)
  waiting for transfers between devices  50.5 us (18%)
  other arithmetic  44.3 us (16%)
  between operations  40.8 us (15%)
  matrix products  31.2 us (11%)
    ppermute x42, starting transfers between devices, ring_reduce_scatter(): arrived = lax.ppermute(carried, axis_name, pairs)  45 us
    ppermute x42, waiting for transfers between devices, ring_reduce_scatter(): arrived = lax.ppermute(carried, axis_name, pairs)  28.4 us
    ppermute x3, waiting for transfers between devices, shift_reduce_scatter(): lax.ppermute(piece, axis_name, [(i, (i + s) % size) for i in range(size)])  11.9 us
    squeeze x18, local copies, waits for them, and re-layouts, own(): lax.dynamic_index_in_dim(p, request, 0, keepdims=False)  11.2 us
    unnamed x108, local copies, waits for them, and re-layouts  11 us
    ppermute x4, waiting for transfers between devices, ring_all_gather(): moving = lax.ppermute(moving, axis_name, forward)  9.5 us
    add x14, other arithmetic, merge_parts(): total_a * share_a + total_b * share_b  8.26 us
    dot_general x1, matrix products, per_device(): jnp.einsum('bnkhc,bthc->bhnkt', block_queries, keys_here, preferred_eleme...  8.08 us
  transfers between devices with their start and end apart: 55, of which 20 were waited for; matrix products, arithmetic and copies ran while one was open for 29% of the time, Pallas kernels for 0%

profile of v3, /device:TPU:0, one launch (start us, length us, event | category | flops | bytes accessed | tf_op | source)
XLA Modules:
  0.0 277.5 jit_solution(4065270182120429772)
XLA Ops:
  2.0 1.8 fusion.37
  4.2 2.5 collective-permute-start.1
  21.1 2.8 fusion.169
  69.2 1.9 multiply_cosine_fusion
  71.1 2.3 pad_maximum_fusion
  73.4 2.9 %gather_fusion = bf16[4,64,2048]{2,1,0:T(8,128)(2,1)} fusion(bf16[4,64,2048]{2,1,0:T(8,128)(2,1)} %pad_maximum_fusion, s32[1024]{0:T(1024)} %pad_clamp_fusion.2), kind=kCustom, calls=%fused_computation | custom fusion | bytes 2097168 | tf_op jit(solution)/shard_map/jit(_take)/gather | solution.py:89
  77.7 3.8 %fusion.25 = f32[256,4,256]{2,0,1:T(8,128)S(1)} fusion(bf16[4,2048,256]{2,1,0:T(8,128)(2,1)} %param.19, bf16[256,2048]{1,0:T(8,128)(2,1)S(1)} %bitcast_select_fusion), kind=kOutput, calls=%fused_computation.41 | convolution fusion | flops 1073741824 | bytes 6291456 | tf_op jit(solution)/shard_map/nd,edc->nec/dot_general | solution.py:182
  82.7 2.1 copy.178
  86.5 2.0 copy.276
  97.6 2.3 fusion.175
  103.6 2.0 fusion.31
  105.6 2.9 %collective-permute-done.7 = bf16[256,2,2,128]{3,0,1,2:T(8,128)(2,1)S(1)} collective-permute-done((bf16[256,2,2,128]{3,0,1,2:T(8,128)(2,1)}, bf16[256,2,2,128]{3,0,1,2:T(8,128)(2,1)S(1)}, u32[]{:S(2)}, u32[]{:S(2)}) %collective-permute-start.7) | collective-permute-done | bytes 262176 | tf_op jit(solution)/shard_map/ppermute | solution.py:113
  113.1 2.6 collective-permute-done.8
  118.0 4.1 %collective-permute-done.9 = bf16[256,2,2,128]{3,0,1,2:T(8,128)(2,1)S(1)} collective-permute-done((bf16[256,2,2,128]{3,0,1,2:T(8,128)(2,1)S(1)}, bf16[256,2,2,128]{3,0,1,2:T(8,128)(2,1)S(1)}, u32[]{:S(2)}, u32[]{:S(2)}) %collective-permute-start.9) | collective-permute-done | bytes 262176 | tf_op jit(solution)/shard_map/ppermute | solution.py:113
  123.2 3.3 %gather_fusion.4 = bf16[16,256,2,2,128]{4,1,2,3,0:T(8,128)(2,1)} fusion(bf16[8,256,2,2,128]{4,1,2,3,0:T(8,128)(2,1)S(1)} %bitcast_dynamic-update-slice_fusion, s32[1024]{0:T(1024)} %pad_clamp_fusion), kind=kCustom, calls=%fused_computation.4 | custom fusion | bytes 8388672 | tf_op jit(solution)/shard_map/jit(_take)/gather | solution.py:208
  126.5 8.1 %fusion.2 = (f32[16,2,256,2]{2,3,1,0:T(2,128)S(1)}, f32[16,2,256,2,128]{2,4,3,1,0:T(8,128)}) fusion(pred[16,128]{1,0:T(8,128)(4,1)S(1)} %copy-done.20, bf16[16,128,2,128,1]{1,3,4,2,0:T(8,128)(2,1)} %bitcast.345, bf16[16,256,2,2,128]{4,1,2,3,0:T(8,128)(2,1)} %gather_fusion.4, pred[16]{0:T(512)(128)(4,1)S(1)} %copy-done.47), kind=kOutput, calls=%fused_computation.10 | convolution fusion | flops 545243136 | bytes 13699088 | tf_op jit(solution)/shard_map/bnkhc,bthc->bhnkt/dot_general | solution.py:212
  138.9 4.7 %fusion.3 = f32[16,2,256,2]{2,3,1,0:T(2,128)S(1)} fusion(f32[16,2,256,2,128]{2,4,3,1,0:T(8,128)} %get-tuple-element.148, f32[16,2,256,2]{2,3,1,0:T(2,128)S(1)} %broadcast_select_fusion, pred[16,128]{1,0:T(8,128)(4,1)S(1)} %copy-done.20), kind=kLoop, calls=%fused_computation.11 | loop fusion | flops 8372224 | bytes 8521728 | tf_op jit(solution)/shard_map/reduce_sum | solution.py:225
  143.6 5.4 %fusion.5 = f32[16,2,256,2,128]{4,2,3,1,0:T(8,128)S(1)} fusion(bf16[16,128,2,128,1]{1,3,4,2,0:T(8,128)(2,1)S(1)} %bitcast.321, f32[16,2,256,2,128]{2,4,3,1,0:T(8,128)} %get-tuple-element.148, f32[16,2,256,2]{2,3,1,0:T(2,128)S(1)} %broadcast_select_fusion, pred[16,128]{1,0:T(8,128)(4,1)S(1)} %copy-done.20), kind=kOutput, calls=%fused_computation.13 | convolution fusion | flops 545259520 | bytes 17893376 | tf_op jit(solution)/shard_map/bhnkt,bthc->bhnkc/dot_general | solution.py:226
  149.1 7.9 %fusion = f32[8,2,256,2,128]{4,0,3,2,1:T(8,128)S(1)} fusion(f32[16,2,256,2,128]{4,2,3,1,0:T(8,128)S(1)} %fusion.5, s32[16]{0:T(128)S(1)} %copy-done.35), kind=kOutput, calls=%fused_computation.6 | convolution fusion | flops 201326720 | bytes 12582976 | tf_op jit(solution)/shard_map/rb,bhnkc->rhnkc/dot_general | solution.py:233
  158.0 2.6 constant_dynamic-slice_fusion.50
  161.7 1.8 collective-permute-start.38
  164.1 2.7 constant_dynamic-slice_fusion.34
  166.8 1.9 copy.205
  211.3 4.6 %collective-permute-done.26 = f32[2,128,2,128]{1,3,2,0:T(8,128)S(1)} collective-permute-done((f32[2,128,2,128]{1,3,2,0:T(8,128)S(1)}, f32[2,128,2,128]{1,3,2,0:T(8,128)S(1)}, u32[]{:S(2)}, u32[]{:S(2)}) %collective-permute-start.26) | collective-permute-done | bytes 262176 | tf_op jit(solution)/shard_map/ppermute | solution.py:150
  221.1 4.8 %collective-permute-done.28 = f32[2,128,2,128]{1,3,2,0:T(8,128)S(1)} collective-permute-done((f32[2,128,2,128]{1,3,2,0:T(8,128)S(1)}, f32[2,128,2,128]{1,3,2,0:T(8,128)S(1)}, u32[]{:S(2)}, u32[]{:S(2)}) %collective-permute-start.28) | collective-permute-done | bytes 262176 | tf_op jit(solution)/shard_map/ppermute | solution.py:150
  230.2 3.4 %collective-permute-done.30 = f32[2,128,2,128]{1,3,2,0:T(8,128)S(1)} collective-permute-done((f32[2,128,2,128]{1,3,2,0:T(8,128)S(1)}, f32[2,128,2,128]{1,3,2,0:T(8,128)S(1)}, u32[]{:S(2)}, u32[]{:S(2)}) %collective-permute-start.30) | collective-permute-done | bytes 262176 | tf_op jit(solution)/shard_map/ppermute | solution.py:150
  237.8 3.5 %collective-permute-done.32 = f32[2,128,2,128]{1,3,2,0:T(8,128)S(1)} collective-permute-done((f32[2,128,2,128]{1,3,2,0:T(8,128)S(1)}, f32[2,128,2,128]{1,3,2,0:T(8,128)S(1)}, u32[]{:S(2)}, u32[]{:S(2)}) %collective-permute-start.32) | collective-permute-done | bytes 262176 | tf_op jit(solution)/shard_map/ppermute | solution.py:150
  243.6 4.2 %collective-permute-done.34 = f32[2,128,2,128]{1,3,2,0:T(8,128)S(1)} collective-permute-done((f32[2,128,2,128]{1,3,2,0:T(8,128)S(1)}, f32[2,128,2,128]{1,3,2,0:T(8,128)S(1)}, u32[]{:S(2)}, u32[]{:S(2)}) %collective-permute-start.34) | collective-permute-done | bytes 262176 | tf_op jit(solution)/shard_map/ppermute | solution.py:150
  250.0 4.2 %collective-permute-done.36 = f32[2,128,2,128]{1,3,2,0:T(8,128)S(1)} collective-permute-done((f32[2,128,2,128]{1,3,2,0:T(8,128)S(1)}, f32[2,128,2,128]{1,3,2,0:T(8,128)S(1)}, u32[]{:S(2)}, u32[]{:S(2)}) %collective-permute-start.36) | collective-permute-done | bytes 262176 | tf_op jit(solution)/shard_map/ppermute | solution.py:150
  263.7 5.0 %collective-permute-done.52 = bf16[64,2048]{1,0:T(8,128)(2,1)} collective-permute-done((bf16[64,2048]{1,0:T(8,128)(2,1)}, bf16[64,2048]{1,0:T(8,128)(2,1)}, u32[]{:S(2)}, u32[]{:S(2)}) %collective-permute-start.52) | collective-permute-done | bytes 262176 | tf_op jit(solution)/shard_map/ppermute | solution.py:99
  269.8 5.7 %collective-permute-done.53 = bf16[64,2048]{1,0:T(8,128)(2,1)} collective-permute-done((bf16[64,2048]{1,0:T(8,128)(2,1)S(1)}, bf16[64,2048]{1,0:T(8,128)(2,1)}, u32[]{:S(2)}, u32[]{:S(2)}) %collective-permute-start.53) | collective-permute-done | bytes 262176 | tf_op jit(solution)/shard_map/ppermute | solution.py:99
  275.6 1.9 fusion.52
  (320 shorter events, 125.2 us)
Async XLA Ops:
  3.8 67.3 %collective-permute-start.2 = (bf16[64,2048]{1,0:T(8,128)(2,1)}, bf16[64,2048]{1,0:T(8,128)(2,1)}, u32[]{:S(2)}, u32[]{:S(2)}) collective-permute-start(bf16[64,2048]{1,0:T(8,128)(2,1)} %fusion.37), channel_id=1, source_target_pairs={{0,8},{8,16},{16,24},{24,0},{1,9},{9,17},{17,25},{25,1},{2,10},{10... | collective-permute-start | bytes 786440 | tf_op jit(solution)/shard_map/ppermute | solution.py:85
  4.2 66.9 %collective-permute-start.1 = (bf16[64,2048]{1,0:T(8,128)(2,1)}, bf16[64,2048]{1,0:T(8,128)(2,1)}, u32[]{:S(2)}, u32[]{:S(2)}) collective-permute-start(bf16[64,2048]{1,0:T(8,128)(2,1)} %fusion.37), channel_id=1, source_target_pairs={{0,16},{8,24},{16,0},{24,8},{1,17},{9,25},{17,1},{25,9},{2,18},{10... | collective-permute-start | bytes 786440 | tf_op jit(solution)/shard_map/ppermute | solution.py:85
  6.8 64.3 %collective-permute-start = (bf16[64,2048]{1,0:T(8,128)(2,1)}, bf16[64,2048]{1,0:T(8,128)(2,1)}, u32[]{:S(2)}, u32[]{:S(2)}) collective-permute-start(bf16[64,2048]{1,0:T(8,128)(2,1)} %fusion.37), channel_id=1, source_target_pairs={{0,24},{8,0},{16,8},{24,16},{1,25},{9,1},{17,9},{25,17},{2,26},{10... | collective-permute-start | bytes 786440 | tf_op jit(solution)/shard_map/ppermute | solution.py:85
  92.5 8.9 %collective-permute-start.6 = (bf16[256,2,2,128]{3,0,1,2:T(8,128)(2,1)}, bf16[256,2,2,128]{3,0,1,2:T(8,128)(2,1)}, u32[]{:S(2)}, u32[]{:S(2)}) collective-permute-start(bf16[256,2,2,128]{3,0,1,2:T(8,128)(2,1)} %pad_maximum_fusion.1), channel_id=1, source_target_pairs={{0,1},{1,3},{3,5},{5,7},{7,6},{6,4},{4,2},{2,0},{8,9},{9,11},{11,1... | collective-permute-start | bytes 786440 | tf_op jit(solution)/shard_map/ppermute | solution.py:113
  94.0 9.0 %collective-permute-start.3 = (bf16[256,2,2,128]{3,0,1,2:T(8,128)(2,1)}, bf16[256,2,2,128]{3,0,1,2:T(8,128)(2,1)}, u32[]{:S(2)}, u32[]{:S(2)}) collective-permute-start(bf16[256,2,2,128]{3,0,1,2:T(8,128)(2,1)} %pad_maximum_fusion.1), channel_id=1, source_target_pairs={{1,0},{3,1},{5,3},{7,5},{6,7},{4,6},{2,4},{0,2},{9,8},{11,9},{13,1... | collective-permute-start | bytes 786440 | tf_op jit(solution)/shard_map/ppermute | solution.py:117
  101.4 7.0 %collective-permute-start.7 = (bf16[256,2,2,128]{3,0,1,2:T(8,128)(2,1)}, bf16[256,2,2,128]{3,0,1,2:T(8,128)(2,1)S(1)}, u32[]{:S(2)}, u32[]{:S(2)}) collective-permute-start(bf16[256,2,2,128]{3,0,1,2:T(8,128)(2,1)} %collective-permute-done.6), channel_id=1, source_target_pairs={{0,1},{1,3},{3,5},{5,7},{7,6},{6,4},{4,2},{2,0},{8,9},{9,11},{11,1... | collective-permute-start | bytes 786440 | tf_op jit(solution)/shard_map/ppermute | solution.py:113
  103.0 8.5 %collective-permute-start.4 = (bf16[256,2,2,128]{3,0,1,2:T(8,128)(2,1)}, bf16[256,2,2,128]{3,0,1,2:T(8,128)(2,1)S(1)}, u32[]{:S(2)}, u32[]{:S(2)}) collective-permute-start(bf16[256,2,2,128]{3,0,1,2:T(8,128)(2,1)} %collective-permute-done.3), channel_id=1, source_target_pairs={{1,0},{3,1},{5,3},{7,5},{6,7},{4,6},{2,4},{0,2},{9,8},{11,9},{13,1... | collective-permute-start | bytes 786440 | tf_op jit(solution)/shard_map/ppermute | solution.py:117
  108.4 7.3 %collective-permute-start.8 = (bf16[256,2,2,128]{3,0,1,2:T(8,128)(2,1)S(1)}, bf16[256,2,2,128]{3,0,1,2:T(8,128)(2,1)S(1)}, u32[]{:S(2)}, u32[]{:S(2)}) collective-permute-start(bf16[256,2,2,128]{3,0,1,2:T(8,128)(2,1)S(1)} %collective-permute-done.7), channel_id=1, source_target_pairs={{0,1},{1,3},{3,5},{5,7},{7,6},{6,4},{4,2},{2,0},{8,9},{9,11},{11,1... | collective-permute-start | bytes 786440 | tf_op jit(solution)/shard_map/ppermute | solution.py:113
  136.2 44.8 %collective-permute-start.25 = (f32[2,128,2]{1,2,0:T(2,128)}, f32[2,128,2]{1,2,0:T(2,128)}, u32[]{:S(2)}, u32[]{:S(2)}) collective-permute-start(f32[2,128,2]{1,2,0:T(2,128)} %fusion.103), channel_id=1, source_target_pairs={{1,0},{3,1},{5,3},{7,5},{6,7},{4,6},{2,4},{0,2},{9,8},{11,9},{13,1... | collective-permute-start | bytes 6152 | tf_op jit(solution)/shard_map/ppermute | solution.py:150
  138.3 39.9 %collective-permute-start.11 = (f32[2,128,2]{1,2,0:T(2,128)}, f32[2,128,2]{1,2,0:T(2,128)}, u32[]{:S(2)}, u32[]{:S(2)}) collective-permute-start(f32[2,128,2]{1,2,0:T(2,128)} %fusion.95), channel_id=1, source_target_pairs={{0,1},{1,3},{3,5},{5,7},{7,6},{6,4},{4,2},{2,0},{8,9},{9,11},{11,1... | collective-permute-start | bytes 6152 | tf_op jit(solution)/shard_map/ppermute | solution.py:150
  161.7 17.0 %collective-permute-start.38 = (f32[2,128,2]{1,2,0:T(2,128)}, f32[2,128,2]{1,2,0:T(2,128)}, u32[]{:S(2)}, u32[]{:S(2)}) collective-permute-start(f32[2,128,2]{1,2,0:T(2,128)} %bitcast.91), channel_id=1, source_target_pairs={{0,1},{1,3},{3,5},{5,7},{7,6},{6,4},{4,2},{2,0},{8,9},{9,11},{11,1... | collective-permute-start | bytes 6152 | tf_op jit(solution)/shard_map/ppermute | solution.py:150
  169.8 12.7 %collective-permute-start.45 = (f32[2,128,2]{1,2,0:T(2,128)}, f32[2,128,2]{1,2,0:T(2,128)}, u32[]{:S(2)}, u32[]{:S(2)}) collective-permute-start(f32[2,128,2]{1,2,0:T(2,128)} %bitcast.365), channel_id=1, source_target_pairs={{1,0},{3,1},{5,3},{7,5},{6,7},{4,6},{2,4},{0,2},{9,8},{11,9},{13,1... | collective-permute-start | bytes 6152 | tf_op jit(solution)/shard_map/ppermute | solution.py:150
  176.6 28.8 %collective-permute-start.24 = (f32[2,128,2,128]{1,3,2,0:T(8,128)}, f32[2,128,2,128]{1,3,2,0:T(8,128)S(1)}, u32[]{:S(2)}, u32[]{:S(2)}) collective-permute-start(f32[2,128,2,128]{1,3,2,0:T(8,128)} %copy.205), channel_id=1, source_target_pairs={{1,0},{3,1},{5,3},{7,5},{6,7},{4,6},{2,4},{0,2},{9,8},{11,9},{13,1... | collective-permute-start | bytes 786440 | tf_op jit(solution)/shard_map/ppermute | solution.py:150
  178.2 28.7 %collective-permute-start.10 = (f32[2,128,2,128]{1,3,2,0:T(8,128)}, f32[2,128,2,128]{1,3,2,0:T(8,128)S(1)}, u32[]{:S(2)}, u32[]{:S(2)}) collective-permute-start(f32[2,128,2,128]{1,3,2,0:T(8,128)} %copy.189), channel_id=1, source_target_pairs={{0,1},{1,3},{3,5},{5,7},{7,6},{6,4},{4,2},{2,0},{8,9},{9,11},{11,1... | collective-permute-start | bytes 786440 | tf_op jit(solution)/shard_map/ppermute | solution.py:150
  201.1 7.4 %collective-permute-start.49 = (f32[2,128,2]{1,2,0:T(2,128)S(1)}, f32[2,128,2]{1,2,0:T(2,128)S(1)}, u32[]{:S(2)}, u32[]{:S(2)}) collective-permute-start(f32[2,128,2]{1,2,0:T(2,128)S(1)} %get-tuple-element.60), channel_id=1, source_target_pairs={{1,0},{3,1},{5,3},{7,5},{6,7},{4,6},{2,4},{0,2},{9,8},{11,9},{13,1... | collective-permute-start | bytes 6152 | tf_op jit(solution)/shard_map/ppermute | solution.py:150
  204.5 14.4 %collective-permute-start.43 = (f32[2,128,2]{1,2,0:T(2,128)S(1)}, f32[2,128,2]{1,2,0:T(2,128)S(1)}, u32[]{:S(2)}, u32[]{:S(2)}) collective-permute-start(f32[2,128,2]{1,2,0:T(2,128)S(1)} %get-tuple-element.28), channel_id=1, source_target_pairs={{0,1},{1,3},{3,5},{5,7},{7,6},{6,4},{4,2},{2,0},{8,9},{9,11},{11,1... | collective-permute-start | bytes 6152 | tf_op jit(solution)/shard_map/ppermute | solution.py:150
  205.4 14.4 %collective-permute-start.21 = (f32[2,128,2]{1,2,0:T(2,128)S(1)}, f32[2,128,2]{1,2,0:T(2,128)S(1)}, u32[]{:S(2)}, u32[]{:S(2)}) collective-permute-start(f32[2,128,2]{1,2,0:T(2,128)S(1)} %get-tuple-element.31), channel_id=1, source_target_pairs={{0,1},{1,3},{3,5},{5,7},{7,6},{6,4},{4,2},{2,0},{8,9},{9,11},{11,1... | collective-permute-start | bytes 6152 | tf_op jit(solution)/shard_map/ppermute | solution.py:150
  207.0 9.0 %collective-permute-start.26 = (f32[2,128,2,128]{1,3,2,0:T(8,128)S(1)}, f32[2,128,2,128]{1,3,2,0:T(8,128)S(1)}, u32[]{:S(2)}, u32[]{:S(2)}) collective-permute-start(f32[2,128,2,128]{1,3,2,0:T(8,128)S(1)} %multiply_add_fusion.6), channel_id=1, source_target_pairs={{1,0},{3,1},{5,3},{7,5},{6,7},{4,6},{2,4},{0,2},{9,8},{11,9},{13,1... | collective-permute-start | bytes 786440 | tf_op jit(solution)/shard_map/ppermute | solution.py:150
  208.5 9.1 %collective-permute-start.12 = (f32[2,128,2,128]{1,3,2,0:T(8,128)S(1)}, f32[2,128,2,128]{1,3,2,0:T(8,128)S(1)}, u32[]{:S(2)}, u32[]{:S(2)}) collective-permute-start(f32[2,128,2,128]{1,3,2,0:T(8,128)S(1)} %multiply_add_fusion.13), channel_id=1, source_target_pairs={{0,1},{1,3},{3,5},{5,7},{7,6},{6,4},{4,2},{2,0},{8,9},{9,11},{11,1... | collective-permute-start | bytes 786440 | tf_op jit(solution)/shard_map/ppermute | solution.py:150
  209.8 18.2 %collective-permute-start.50 = (f32[2,128,2]{1,2,0:T(2,128)S(1)}, f32[2,128,2]{1,2,0:T(2,128)S(1)}, u32[]{:S(2)}, u32[]{:S(2)}) collective-permute-start(f32[2,128,2]{1,2,0:T(2,128)S(1)} %get-tuple-element.56), channel_id=1, source_target_pairs={{1,0},{3,1},{5,3},{7,5},{6,7},{4,6},{2,4},{0,2},{9,8},{11,9},{13,1... | collective-permute-start | bytes 6152 | tf_op jit(solution)/shard_map/ppermute | solution.py:150
  215.9 13.2 %collective-permute-start.35 = (f32[2,128,2]{1,2,0:T(2,128)S(1)}, f32[2,128,2]{1,2,0:T(2,128)S(1)}, u32[]{:S(2)}, u32[]{:S(2)}) collective-permute-start(f32[2,128,2]{1,2,0:T(2,128)S(1)} %get-tuple-element.59), channel_id=1, source_target_pairs={{1,0},{3,1},{5,3},{7,5},{6,7},{4,6},{2,4},{0,2},{9,8},{11,9},{13,1... | collective-permute-start | bytes 6152 | tf_op jit(solution)/shard_map/ppermute | solution.py:150
  217.7 8.2 %collective-permute-start.28 = (f32[2,128,2,128]{1,3,2,0:T(8,128)S(1)}, f32[2,128,2,128]{1,3,2,0:T(8,128)S(1)}, u32[]{:S(2)}, u32[]{:S(2)}) collective-permute-start(f32[2,128,2,128]{1,3,2,0:T(8,128)S(1)} %multiply_add_fusion.5), channel_id=1, source_target_pairs={{1,0},{3,1},{5,3},{7,5},{6,7},{4,6},{2,4},{0,2},{9,8},{11,9},{13,1... | collective-permute-start | bytes 786440 | tf_op jit(solution)/shard_map/ppermute | solution.py:150
  218.9 8.1 %collective-permute-start.14 = (f32[2,128,2,128]{1,3,2,0:T(8,128)S(1)}, f32[2,128,2,128]{1,3,2,0:T(8,128)S(1)}, u32[]{:S(2)}, u32[]{:S(2)}) collective-permute-start(f32[2,128,2,128]{1,3,2,0:T(8,128)S(1)} %multiply_add_fusion.12), channel_id=1, source_target_pairs={{0,1},{1,3},{3,5},{5,7},{7,6},{6,4},{4,2},{2,0},{8,9},{9,11},{11,1... | collective-permute-start | bytes 786440 | tf_op jit(solution)/shard_map/ppermute | solution.py:150
  220.5 15.7 %collective-permute-start.44 = (f32[2,128,2]{1,2,0:T(2,128)S(1)}, f32[2,128,2]{1,2,0:T(2,128)S(1)}, u32[]{:S(2)}, u32[]{:S(2)}) collective-permute-start(f32[2,128,2]{1,2,0:T(2,128)S(1)} %get-tuple-element.24), channel_id=1, source_target_pairs={{0,1},{1,3},{3,5},{5,7},{7,6},{6,4},{4,2},{2,0},{8,9},{9,11},{11,1... | collective-permute-start | bytes 6152 | tf_op jit(solution)/shard_map/ppermute | solution.py:150
  225.9 11.2 %collective-permute-start.23 = (f32[2,128,2]{1,2,0:T(2,128)S(1)}, f32[2,128,2]{1,2,0:T(2,128)S(1)}, u32[]{:S(2)}, u32[]{:S(2)}) collective-permute-start(f32[2,128,2]{1,2,0:T(2,128)S(1)} %get-tuple-element.27), channel_id=1, source_target_pairs={{0,1},{1,3},{3,5},{5,7},{7,6},{6,4},{4,2},{2,0},{8,9},{9,11},{11,1... | collective-permute-start | bytes 6152 | tf_op jit(solution)/shard_map/ppermute | solution.py:150
  227.0 6.6 %collective-permute-start.30 = (f32[2,128,2,128]{1,3,2,0:T(8,128)S(1)}, f32[2,128,2,128]{1,3,2,0:T(8,128)S(1)}, u32[]{:S(2)}, u32[]{:S(2)}) collective-permute-start(f32[2,128,2,128]{1,3,2,0:T(8,128)S(1)} %multiply_add_fusion.4), channel_id=1, source_target_pairs={{1,0},{3,1},{5,3},{7,5},{6,7},{4,6},{2,4},{0,2},{9,8},{11,9},{13,1... | collective-permute-start | bytes 786440 | tf_op jit(solution)/shard_map/ppermute | solution.py:150
  228.1 6.8 %collective-permute-start.16 = (f32[2,128,2,128]{1,3,2,0:T(8,128)S(1)}, f32[2,128,2,128]{1,3,2,0:T(8,128)S(1)}, u32[]{:S(2)}, u32[]{:S(2)}) collective-permute-start(f32[2,128,2,128]{1,3,2,0:T(8,128)S(1)} %multiply_add_fusion.11), channel_id=1, source_target_pairs={{0,1},{1,3},{3,5},{5,7},{7,6},{6,4},{4,2},{2,0},{8,9},{9,11},{11,1... | collective-permute-start | bytes 786440 | tf_op jit(solution)/shard_map/ppermute | solution.py:150
  229.2 14.3 %collective-permute-start.51 = (f32[2,128,2]{1,2,0:T(2,128)S(1)}, f32[2,128,2]{1,2,0:T(2,128)S(1)}, u32[]{:S(2)}, u32[]{:S(2)}) collective-permute-start(f32[2,128,2]{1,2,0:T(2,128)S(1)} %get-tuple-element.52), channel_id=1, source_target_pairs={{1,0},{3,1},{5,3},{7,5},{6,7},{4,6},{2,4},{0,2},{9,8},{11,9},{13,1... | collective-permute-start | bytes 6152 | tf_op jit(solution)/shard_map/ppermute | solution.py:150
  233.7 9.9 %collective-permute-start.37 = (f32[2,128,2]{1,2,0:T(2,128)S(1)}, f32[2,128,2]{1,2,0:T(2,128)S(1)}, u32[]{:S(2)}, u32[]{:S(2)}) collective-permute-start(f32[2,128,2]{1,2,0:T(2,128)S(1)} %get-tuple-element.55), channel_id=1, source_target_pairs={{1,0},{3,1},{5,3},{7,5},{6,7},{4,6},{2,4},{0,2},{9,8},{11,9},{13,1... | collective-permute-start | bytes 6152 | tf_op jit(solution)/shard_map/ppermute | solution.py:150
  261.0 7.7 %collective-permute-start.52 = (bf16[64,2048]{1,0:T(8,128)(2,1)}, bf16[64,2048]{1,0:T(8,128)(2,1)}, u32[]{:S(2)}, u32[]{:S(2)}) collective-permute-start(bf16[64,2048]{1,0:T(8,128)(2,1)} %get-tuple-element.98), channel_id=1, source_target_pairs={{0,8},{8,16},{16,24},{24,0},{1,9},{9,17},{17,25},{25,1},{2,10},{10... | collective-permute-start | bytes 786440 | tf_op jit(solution)/shard_map/ppermute | solution.py:99
  261.0 8.8 %collective-permute-start.54 = (bf16[64,2048]{1,0:T(8,128)(2,1)}, bf16[64,2048]{1,0:T(8,128)(2,1)}, u32[]{:S(2)}, u32[]{:S(2)}) collective-permute-start(bf16[64,2048]{1,0:T(8,128)(2,1)} %get-tuple-element.99), channel_id=1, source_target_pairs={{0,24},{8,0},{16,8},{24,16},{1,25},{9,1},{17,9},{25,17},{2,26},{10... | collective-permute-start | bytes 786440 | tf_op jit(solution)/shard_map/ppermute | solution.py:99
  262.8 12.8 %collective-permute-start.53 = (bf16[64,2048]{1,0:T(8,128)(2,1)S(1)}, bf16[64,2048]{1,0:T(8,128)(2,1)}, u32[]{:S(2)}, u32[]{:S(2)}) collective-permute-start(bf16[64,2048]{1,0:T(8,128)(2,1)S(1)} %get-tuple-element.100), channel_id=1, source_target_pairs={{0,16},{8,24},{16,0},{24,8},{1,17},{9,25},{17,1},{25,9},{2,18},{10... | collective-permute-start | bytes 786440 | tf_op jit(solution)/shard_map/ppermute | solution.py:99
  (71 other events, 569.5 us)

commit v4 on v1

--- a/solution.py
+++ b/solution.py
@@ -1,3 +1,6 @@
+import functools
+
+import numpy as np
 import jax
 import jax.numpy as jnp
 from jax import lax
@@ -49,7 +52,81 @@
     return hi, lo
 
 
+def seq_cycle(mesh):
+    size = mesh.shape["seq"]
+    plain = list(range(size))
+    try:
+        devices = np.moveaxis(np.asarray(mesh.devices), mesh.axis_names.index("seq"), -1)
+        line = devices.reshape(-1, size)[0]
+        coords = np.array([list(d.coords) for d in line])
+    except Exception:
+        return plain
+    varying = [k for k in range(coords.shape[1]) if len(set(coords[:, k])) > 1]
+    if len(varying) == 1:
+        order = sorted(plain, key=lambda j: coords[j, varying[0]])
+        return order[0::2] + order[1::2][::-1]
+    if len(varying) != 2:
+        return plain
+    dim_a, dim_b = varying
+    values_a = sorted(set(coords[:, dim_a]))
+    values_b = sorted(set(coords[:, dim_b]))
+    if len(values_a) % 2:
+        dim_a, dim_b, values_a, values_b = dim_b, dim_a, values_b, values_a
+    if len(values_a) % 2 or len(values_a) * len(values_b) != size:
+        return plain
+    at = {(coords[j, dim_a], coords[j, dim_b]): j for j in plain}
+    cycle = [at[(a, values_b[0])] for a in values_a]
+    for row, a in enumerate(reversed(values_a)):
+        columns = values_b[1:] if row % 2 == 0 else values_b[1:][::-1]
+        cycle += [at[(a, b)] for b in columns]
+    if sorted(cycle) != plain:
+        return plain
+    return cycle
+
+
+def shift_all_gather(piece, axis_name):
+    size = lax.axis_size(axis_name)
+    rank = lax.axis_index(axis_name)
+    by_offset = [piece] + [
+        lax.ppermute(piece, axis_name, [(i, (i + s) % size) for i in range(size)])
+        for s in range(1, size)
+    ]
+    by_offset = jnp.stack(by_offset[:1] + by_offset[1:][::-1], axis=0)
+    return jnp.take(by_offset, (jnp.arange(size, dtype=jnp.int32) - rank) % size, axis=0)
+
+
+def shift_reduce_scatter(rows, axis_name):
+    size = lax.axis_size(axis_name)
+    rank = lax.axis_index(axis_name)
+    share = rows.shape[0] // size
+    total = lax.dynamic_slice_in_dim(rows, rank * share, share, 0).astype(jnp.float32)
+    for s in range(1, size):
+        piece = lax.dynamic_slice_in_dim(rows, ((rank + s) % size) * share, share, 0)
+        moved = lax.ppermute(piece, axis_name, [(i, (i + s) % size) for i in range(size)])
+        total = total + moved.astype(jnp.float32)
+    return total
+
+
+def ring_all_gather(piece, axis_name, cycle):
+    size = len(cycle)
+    forward = [(cycle[i], cycle[(i + 1) % size]) for i in range(size)]
+    backward = [(cycle[(i + 1) % size], cycle[i]) for i in range(size)]
+    ahead = size // 2
+    behind = size - 1 - ahead
+    from_behind, from_ahead = [], []
+    moving = piece
+    for _ in range(ahead):
+        moving = lax.ppermute(moving, axis_name, forward)
+        from_behind.append(moving)
+    moving = piece
+    for _ in range(behind):
+        moving = lax.ppermute(moving, axis_name, backward)
+        from_ahead.append(moving)
+    return jnp.stack([piece] + from_ahead + from_behind[::-1], axis=0)
+
+
 def per_device(
+    cycle,
     hidden,
     norm_gain,
     router_weight,
@@ -83,8 +160,11 @@
     fresh = jnp.einsum("nd,sdc->snc", gathered, kv_weight, preferred_element_type=jnp.float32)
     new_keys = rotate(fresh[0].reshape(new_count, local_heads, HD), positions).astype(jnp.bfloat16)
     new_values = fresh[1].reshape(new_count, local_heads, HD).astype(jnp.bfloat16)
-    all_queries = lax.all_gather(queries[None], "seq", axis=0, tiled=True)
-    request_count = all_queries.shape[0]
+    ring_queries = ring_all_gather(queries, "seq", cycle)
+    request_count = ring_queries.shape[0]
+    ring_size = len(cycle)
+    position_of = np.argsort(np.asarray(cycle))
+    position = jnp.asarray(position_of, dtype=jnp.int32)[seq_rank]
     pool_size = block_pool.shape[0]
 
     global_ids = seq_rank * local_blocks + jnp.arange(local_blocks, dtype=jnp.int32)
@@ -97,7 +177,29 @@
     ordinal = slot_of - starts[owner]
     owns = owner[None, :] == jnp.arange(request_count, dtype=jnp.int32)[:, None]
 
-    block_queries = jnp.take(all_queries, owner, axis=0)
+    self_scores = (
+        jnp.einsum("nkhc,thc->hnkt", queries, new_keys, preferred_element_type=jnp.float32)
+        * scale_q
+    )
+    causal = (
+        jnp.arange(new_count, dtype=jnp.int32)[None, :]
+        <= jnp.arange(new_count, dtype=jnp.int32)[:, None]
+    )
+    self_scores = jnp.where(causal[None, :, None, :], self_scores, NEG_FILL)
+    self_best = jnp.max(self_scores, axis=-1)
+    self_weights = jnp.exp(self_scores - self_best[..., None])
+    self_total = jnp.sum(self_weights, axis=-1)
+    self_accum = jnp.einsum(
+        "hnkt,thc->hnkc",
+        self_weights.astype(jnp.bfloat16),
+        new_values,
+        preferred_element_type=jnp.float32,
+    )
+    ring_queries, self_best, self_total, self_accum = lax.optimization_barrier(
+        (ring_queries, self_best, self_total, self_accum)
+    )
+    owner_offset = (jnp.asarray(position_of, dtype=jnp.int32)[owner] - position) % ring_size
+    block_queries = jnp.take(ring_queries, owner_offset, axis=0)
     keys_here = kv_cache[0].reshape(local_blocks, block_size, local_heads, HD)
     values_here = kv_cache[1].reshape(local_blocks, block_size, local_heads, HD)
     scores = (
@@ -152,24 +254,6 @@
     cache_total = jnp.sum(part_totals * factor, axis=0)
     cache_accum = jnp.sum(part_accum * factor[..., None], axis=0)
 
-    self_scores = (
-        jnp.einsum("nkhc,thc->hnkt", queries, new_keys, preferred_element_type=jnp.float32)
-        * scale_q
-    )
-    causal = (
-        jnp.arange(new_count, dtype=jnp.int32)[None, :]
-        <= jnp.arange(new_count, dtype=jnp.int32)[:, None]
-    )
-    self_scores = jnp.where(causal[None, :, None, :], self_scores, NEG_FILL)
-    self_best = jnp.max(self_scores, axis=-1)
-    self_weights = jnp.exp(self_scores - self_best[..., None])
-    self_total = jnp.sum(self_weights, axis=-1)
-    self_accum = jnp.einsum(
-        "hnkt,thc->hnkc",
-        self_weights.astype(jnp.bfloat16),
-        new_values,
-        preferred_element_type=jnp.float32,
-    )
     peak = jnp.maximum(cache_best, self_best)
     cache_share = jnp.exp(cache_best - peak)
     self_share = jnp.exp(self_best - peak)
@@ -191,15 +275,13 @@
         output = output + weight_expert[:, None] * jnp.dot(
             picked, o_weight[expert], preferred_element_type=jnp.float32
         )
-    summed = lax.psum_scatter(
-        output.astype(jnp.bfloat16), "heads", scatter_dimension=0, tiled=True
-    ).astype(jnp.float32)
+    summed = shift_reduce_scatter(output.astype(jnp.bfloat16), "heads")
     return summed[None].astype(jnp.bfloat16)
 
 
 def solution(mesh):
     return jax.shard_map(
-        per_device,
+        functools.partial(per_device, tuple(seq_cycle(mesh))),
         mesh=mesh,
         in_specs=(
             P("seq", "heads", None),

time: 226 us -> 195 us (0.86)
  waiting for transfers between devices: 121 us -> 76.4 us
  starting transfers between devices: 4.79 us -> 11.9 us
  other arithmetic: 26.3 us -> 31.7 us
  local copies, waits for them, and re-layouts: 26 us -> 28.7 us
    all_gather x1 -> x0, waiting for transfers between devices: 42.2 us -> none  [per_device(): all_queries = lax.all_gather(queries[None], 'seq', axis=0, tiled=True)]
    ppermute x0 -> x10, waiting for transfers between devices: none -> 28.8 us  [the longest x4 14.7 us: ring_all_gather(): moving = lax.ppermute(moving, axis_name, forward)]
    reduce_scatter x1 -> x0, waiting for transfers between devices: 24.1 us -> none  [per_device(): lax.psum_scatter(output.astype(jnp.bfloat16), 'heads', scatter_dimension=...]
    all_gather x1, waiting for transfers between devices: 14.7 us -> 2.35 us  [per_device(): gathered = lax.all_gather(normed, 'heads', axis=0, tiled=True)]
    ppermute x0 -> x10, starting transfers between devices: none -> 7.13 us  [the longest x3 4.46 us: ring_all_gather(): moving = lax.ppermute(moving, axis_name, backward)]
    all_to_all x1, waiting for transfers between devices: 39.8 us -> 45.3 us  [per_device(): received = lax.all_to_all(payload, 'seq', 0, 0, tiled=True)]
    unnamed x40 -> x50, local copies, waits for them, and re-layouts: 6.3 us -> 9.4 us
    gather x1 -> x2, local copies, waits for them, and re-layouts: 4.65 us -> 3.84 us  [the longest x1 3.18 us: per_device(): block_queries = jnp.take(ring_queries, owner_offset, axis=0)]
  transfers between devices with their start and end apart: 4 -> 12, of which waited for: 4 -> 11; matrix products, arithmetic and copies ran while one was open for 9% -> 13% of each run, Pallas kernels for 0% -> 0%
where the time goes in v4:
time: 195 us; the launch traced here: 194 us
  waiting for transfers between devices  76.4 us (39%)
  matrix products  31.8 us (16%)
  other arithmetic  31.7 us (16%)
  local copies, waits for them, and re-layouts  28.7 us (15%)
  between operations  14 us (7%)
  starting transfers between devices  11.9 us (6%)
    all_to_all x1, waiting for transfers between devices, per_device(): received = lax.all_to_all(payload, 'seq', 0, 0, tiled=True)  45.3 us
    ppermute x4, waiting for transfers between devices, ring_all_gather(): moving = lax.ppermute(moving, axis_name, forward)  14.7 us
    ppermute x3, waiting for transfers between devices, shift_reduce_scatter(): lax.ppermute(piece, axis_name, [(i, (i + s) % size) for i in range(size)])  12.8 us
    unnamed x50, local copies, waits for them, and re-layouts  9.4 us
    dot_general x1, matrix products, per_device(): jnp.einsum('bnkhc,bthc->bhnkt', block_queries, keys_here, preferred_eleme...  7.99 us
    dot_general x1, matrix products, per_device(): jnp.einsum('rb,bhnkc->rhnkc', owns_f, block_accum, precision=lax.Precisio...  6.32 us
    dot_general x1, matrix products, per_device(): jnp.einsum('bhnkt,bthc->bhnkc', weights.astype(jnp.bfloat16), values_here...  5.22 us
    all_to_all x1, starting transfers between devices, per_device(): received = lax.all_to_all(payload, 'seq', 0, 0, tiled=True)  4.72 us
  transfers between devices with their start and end apart: 12, of which 11 were waited for; matrix products, arithmetic and copies ran while one was open for 13% of the time, Pallas kernels for 0%

profile of v4, /device:TPU:0, one launch (start us, length us, event | category | flops | bytes accessed | tf_op | source)
XLA Modules:
  0.0 194.5 jit_solution(13304430576117952579)
XLA Ops:
  8.5 1.8 fusion.38
  16.8 2.7 %fusion.126 = (bf16[1,16,128,256]{3,2,1,0:T(8,128)(2,1)}, bf16[1,16,128,256]{3,2,1,0:T(8,128)(2,1)S(1)}) fusion(bf16[2,16,128,256]{3,2,1,0:T(8,128)(2,1)} %param.20), kind=kLoop, calls=%fused_computation.220 | loop fusion | bytes 4194304 | tf_op jit(solution)/shard_map/slice | solution.py:204
  22.2 1.6 copy.265
  27.5 2.4 %all-gather.2.cloned.1.call-done = bf16[256,2048]{1,0:T(8,128)(2,1)} async-done(((bf16[64,2048]{1,0:T(8,128)(2,1)}), bf16[256,2048]{1,0:T(8,128)(2,1)}) %all-gather.2.cloned.1.call-update) | async-done | bytes 1048592 | tf_op jit(solution)/shard_map/all_gather | solution.py:149
  29.9 3.8 %fusion.28 = f32[256,4,256]{2,0,1:T(8,128)S(1)} fusion(bf16[4,2048,256]{2,1,0:T(8,128)(2,1)} %param.17, bf16[256,2048]{1,0:T(8,128)(2,1)} %all-gather.2.cloned.1.call-done), kind=kOutput, calls=%fused_computation.41 | convolution fusion | flops 1073741824 | bytes 6291456 | tf_op jit(solution)/shard_map/nd,edc->nec/dot_general | solution.py:155
  34.8 2.1 %copy.211 = f32[256,2,256]{0,2,1:T(8,128)} copy(f32[256,2,256]{2,0,1:T(8,128)} %multiply_reduce_fusion.1) | data formatting | bytes 1048576 | tf_op jit(solution)/shard_map/reduce_sum | solution.py:156
  36.9 1.8 fusion.127
  38.6 1.9 copy.261
  41.6 1.4 subtract_convert_fusion
  44.6 1.5 collective-permute-start
  50.6 1.4 fusion.129
  52.0 2.6 %collective-permute-done.3 = bf16[256,2,2,128]{3,0,1,2:T(8,128)(2,1)} collective-permute-done((bf16[256,2,2,128]{3,0,1,2:T(8,128)(2,1)}, bf16[256,2,2,128]{3,0,1,2:T(8,128)(2,1)}, u32[]{:S(2)}, u32[]{:S(2)}) %collective-permute-start.3) | collective-permute-done | bytes 262176 | tf_op jit(solution)/shard_map/ppermute | solution.py:119
  56.3 1.5 collective-permute-start.1
  57.9 4.1 %collective-permute-done.4 = bf16[256,2,2,128]{3,0,1,2:T(8,128)(2,1)S(1)} collective-permute-done((bf16[256,2,2,128]{3,0,1,2:T(8,128)(2,1)}, bf16[256,2,2,128]{3,0,1,2:T(8,128)(2,1)S(1)}, u32[]{:S(2)}, u32[]{:S(2)}) %collective-permute-start.4) | collective-permute-done | bytes 262176 | tf_op jit(solution)/shard_map/ppermute | solution.py:119
  63.5 1.5 collective-permute-start.2
  66.0 2.8 %collective-permute-done.5 = bf16[256,2,2,128]{3,0,1,2:T(8,128)(2,1)S(1)} collective-permute-done((bf16[256,2,2,128]{3,0,1,2:T(8,128)(2,1)S(1)}, bf16[256,2,2,128]{3,0,1,2:T(8,128)(2,1)S(1)}, u32[]{:S(2)}, u32[]{:S(2)}) %collective-permute-start.5) | collective-permute-done | bytes 262176 | tf_op jit(solution)/shard_map/ppermute | solution.py:119
  69.9 5.2 %collective-permute-done.6 = bf16[256,2,2,128]{3,0,1,2:T(8,128)(2,1)S(1)} collective-permute-done((bf16[256,2,2,128]{3,0,1,2:T(8,128)(2,1)S(1)}, bf16[256,2,2,128]{3,0,1,2:T(8,128)(2,1)S(1)}, u32[]{:S(2)}, u32[]{:S(2)}) %collective-permute-start.6) | collective-permute-done | bytes 262176 | tf_op jit(solution)/shard_map/ppermute | solution.py:119
  76.3 3.2 %gather_fusion.3 = bf16[16,256,2,2,128]{4,1,2,3,0:T(8,128)(2,1)} fusion(bf16[8,256,2,2,128]{4,1,2,3,0:T(8,128)(2,1)S(1)} %bitcast_dynamic-update-slice_fusion, s32[1024]{0:T(1024)} %pad_clamp_fusion), kind=kCustom, calls=%fused_computation.3 | custom fusion | bytes 8388672 | tf_op jit(solution)/shard_map/jit(_take)/gather | solution.py:202
  79.5 8.0 %fusion.2 = (f32[16,2,256,2]{2,3,1,0:T(2,128)S(1)}, f32[16,2,256,2,128]{2,4,3,1,0:T(8,128)}) fusion(pred[16,128]{1,0:T(8,128)(4,1)S(1)} %add_compare_fusion, bf16[16,128,2,128,1]{1,3,4,2,0:T(8,128)(2,1)} %bitcast.182, bf16[16,256,2,2,128]{4,1,2,3,0:T(8,128)(2,1)} %gather_fusion.3, pred[16]{0:T(512)(128)(4,1)S(1)} %copy-done.18), kind=kOutput, calls=%fused_computation.9 | convolution fusion | flops 545243136 | bytes 13699088 | tf_op jit(solution)/shard_map/bnkhc,bthc->bhnkt/dot_general | solution.py:206
  88.6 4.7 %fusion.3 = f32[16,2,256,2]{2,3,1,0:T(2,128)S(1)} fusion(f32[16,2,256,2,128]{2,4,3,1,0:T(8,128)} %get-tuple-element.54, f32[16,2,256,2]{2,3,1,0:T(2,128)S(1)} %broadcast_select_fusion, pred[16,128]{1,0:T(8,128)(4,1)S(1)} %add_compare_fusion), kind=kLoop, calls=%fused_computation.10 | loop fusion | flops 8372224 | bytes 8521728 | tf_op jit(solution)/shard_map/reduce_sum | solution.py:221
  94.6 5.2 %fusion.5 = f32[16,2,256,2,128]{4,2,3,1,0:T(8,128)S(1)} fusion(bf16[16,128,2,128,1]{1,3,4,2,0:T(8,128)(2,1)S(1)} %bitcast.172, f32[16,2,256,2,128]{2,4,3,1,0:T(8,128)} %get-tuple-element.54, f32[16,2,256,2]{2,3,1,0:T(2,128)S(1)} %broadcast_select_fusion, pred[16,128]{1,0:T(8,128)(4,1)S(1)} %add_compare_fusion), kind=kOutput, calls=%fused_computation.12 | convolution fusion | flops 545259520 | bytes 17893376 | tf_op jit(solution)/shard_map/bhnkt,bthc->bhnkc/dot_general | solution.py:222
  99.8 6.3 %fusion.19 = bf16[8,2,256,2,128]{4,0,3,2,1:T(8,128)(2,1)S(1)} fusion(f32[16,2,256,2,128]{4,2,3,1,0:T(8,128)S(1)} %fusion.5, s32[16]{0:T(128)S(1)} %copy-done.16), kind=kOutput, calls=%fused_computation.32 | convolution fusion | flops 202375296 | bytes 10485824 | tf_op jit(solution)/shard_map/rb,bhnkc->rhnkc/dot_general | solution.py:229
  106.4 1.5 pad_maximum_fusion
  107.9 4.7 %all-to-all-start = ((bf16[8,1056,128]{2,1,0:T(8,128)(2,1)}), bf16[8,1056,128]{2,1,0:T(8,128)(2,1)}, u32[]{:S(2)}, u32[]{:S(2)}) async-start(bf16[8,1056,128]{2,1,0:T(8,128)(2,1)} %pad_maximum_fusion), calls=%async_computation | async-start | bytes 4325376 | tf_op jit(solution)/shard_map/all_to_all | solution.py:241
  113.2 45.3 %all-to-all-done = bf16[8,1056,128]{2,1,0:T(8,128)(2,1)} async-done(((bf16[8,1056,128]{2,1,0:T(8,128)(2,1)}), bf16[8,1056,128]{2,1,0:T(8,128)(2,1)}, u32[]{:S(2)}, u32[]{:S(2)}) %all-to-all-start) | async-done | bytes 2162720 | tf_op jit(solution)/shard_map/all_to_all | solution.py:241
  160.9 1.3 fusion.43
  162.6 3.1 %multiply_reduce_fusion = f32[1024,128]{1,0:T(8,128)S(1)} fusion(bf16[8,1056,128]{2,1,0:T(8,128)(2,1)} %all-to-all-done, f32[8,1024]{1,0:T(8,128)S(1)} %subtract_exponential_fusion.2), kind=kLoop, calls=%fused_computation.13 | loop fusion | flops 3014656 | bytes 2654208 | tf_op jit(solution)/shard_map/reduce_sum | solution.py:255
  166.4 1.7 convolution_multiply_fusion.3
  168.1 1.9 fusion.16
  172.9 6.5 %collective-permute-done.9 = bf16[64,2048]{1,0:T(8,128)(2,1)} collective-permute-done((bf16[64,2048]{1,0:T(8,128)(2,1)}, bf16[64,2048]{1,0:T(8,128)(2,1)}, u32[]{:S(2)}, u32[]{:S(2)}) %collective-permute-start.9) | collective-permute-done | bytes 262176 | tf_op jit(solution)/shard_map/ppermute | solution.py:105
  179.4 5.4 %collective-permute-done.8 = bf16[64,2048]{1,0:T(8,128)(2,1)} collective-permute-done((bf16[64,2048]{1,0:T(8,128)(2,1)}, bf16[64,2048]{1,0:T(8,128)(2,1)}, u32[]{:S(2)}, u32[]{:S(2)}) %collective-permute-start.8) | collective-permute-done | bytes 262176 | tf_op jit(solution)/shard_map/ppermute | solution.py:105
  185.7 1.9 fusion.49
  (132 shorter events, 39.7 us)
Async XLA Ops:
  6.5 40.1 %copy-start = (bf16[2,2048,256]{2,1,0:T(8,128)(2,1)S(1)}, bf16[2,2048,256]{2,1,0:T(8,128)(2,1)}, u32[]{:S(2)}) copy-start(bf16[2,2048,256]{2,1,0:T(8,128)(2,1)} %param.18) | copy-start | bytes 6291460
  6.5 8.2 %copy-start.2 = (s32[8]{0:T(128)S(1)}, s32[8]{0:T(128)}, u32[]{:S(2)}) copy-start(s32[8]{0:T(128)} %constant.127.clone) | copy-start | bytes 100
  6.5 9.6 %copy-start.11 = (s32[1,256,2]{1,2,0:T(2,128)S(1)}, s32[1,256,2]{1,2,0:T(2,128)}, u32[]{:S(2)}) copy-start(s32[1,256,2]{1,2,0:T(2,128)} %param.16) | copy-start | bytes 6148
  6.5 23.4 %all-gather.2.cloned.1.call-start = ((), (), s32[]{:S(2)}) async-start(), calls=%async_computation.1 | async-start | bytes 1310720 | tf_op jit(solution)/shard_map/all_gather | solution.py:149
  12.8 3.4 %copy-start.13 = (s32[1024]{0:T(1024)}, s32[1024]{0:T(1024)S(1)}, u32[]{:S(2)}) copy-start(s32[1024]{0:T(1024)S(1)} %pad_clamp_fusion.1) | copy-start | bytes 12292
  24.4 9.2 %copy-start.15 = (s32[16]{0:T(128)}, s32[16]{0:T(128)S(1)}, u32[]{:S(2)}) copy-start(s32[16]{0:T(128)S(1)} %broadcast_add_fusion) | copy-start | bytes 196
  41.6 5.0 %copy-start.7 = (bf16[256,2048]{1,0:T(8,128)(2,1)S(1)}, bf16[256,2048]{1,0:T(8,128)(2,1)}, u32[]{:S(2)}) copy-start(bf16[256,2048]{1,0:T(8,128)(2,1)} %all-gather.2.cloned.1.call-done) | copy-start | bytes 3145732
  43.0 0.7 copy-start.4
  44.6 11.7 %collective-permute-start = (bf16[256,2,2,128]{3,0,1,2:T(8,128)(2,1)}, bf16[256,2,2,128]{3,0,1,2:T(8,128)(2,1)}, u32[]{:S(2)}, u32[]{:S(2)}) collective-permute-start(bf16[256,2,2,128]{3,0,1,2:T(8,128)(2,1)} %pad_maximum_fusion.1), channel_id=1, source_target_pairs={{1,0},{3,1},{5,3},{7,5},{6,7},{4,6},{2,4},{0,2},{9,8},{11,9},{13,1... | collective-permute-start | bytes 786440 | tf_op jit(solution)/shard_map/ppermute | solution.py:123
  46.1 8.5 %collective-permute-start.3 = (bf16[256,2,2,128]{3,0,1,2:T(8,128)(2,1)}, bf16[256,2,2,128]{3,0,1,2:T(8,128)(2,1)}, u32[]{:S(2)}, u32[]{:S(2)}) collective-permute-start(bf16[256,2,2,128]{3,0,1,2:T(8,128)(2,1)} %pad_maximum_fusion.1), channel_id=1, source_target_pairs={{0,1},{1,3},{3,5},{5,7},{7,6},{6,4},{4,2},{2,0},{8,9},{9,11},{11,1... | collective-permute-start | bytes 786440 | tf_op jit(solution)/shard_map/ppermute | solution.py:119
  47.6 0.8 copy-start.9
  47.6 3.0 %copy-start.10 = (pred[256,256]{0,1:T(8,128)(4,1)S(1)}, pred[256,256]{0,1:T(8,128)(4,1)}, u32[]{:S(2)}) copy-start(pred[256,256]{0,1:T(8,128)(4,1)} %iota_compare_fusion) | copy-start | bytes 196612
  50.6 12.0 %copy-start.5 = (bf16[256,2,2,64]{3,0,1,2:T(8,128)(2,1)S(1)}, bf16[256,2,2,64]{3,0,1,2:T(8,128)(2,1)}, u32[]{:S(2)}) copy-start(bf16[256,2,2,64]{3,0,1,2:T(8,128)(2,1)} %copy-done.4) | copy-start | bytes 393220
  54.6 7.5 %collective-permute-start.4 = (bf16[256,2,2,128]{3,0,1,2:T(8,128)(2,1)}, bf16[256,2,2,128]{3,0,1,2:T(8,128)(2,1)S(1)}, u32[]{:S(2)}, u32[]{:S(2)}) collective-permute-start(bf16[256,2,2,128]{3,0,1,2:T(8,128)(2,1)} %collective-permute-done.3), channel_id=1, source_target_pairs={{0,1},{1,3},{3,5},{5,7},{7,6},{6,4},{4,2},{2,0},{8,9},{9,11},{11,1... | collective-permute-start | bytes 786440 | tf_op jit(solution)/shard_map/ppermute | solution.py:119
  56.3 7.2 %collective-permute-start.1 = (bf16[256,2,2,128]{3,0,1,2:T(8,128)(2,1)}, bf16[256,2,2,128]{3,0,1,2:T(8,128)(2,1)S(1)}, u32[]{:S(2)}, u32[]{:S(2)}) collective-permute-start(bf16[256,2,2,128]{3,0,1,2:T(8,128)(2,1)} %collective-permute-done), channel_id=1, source_target_pairs={{1,0},{3,1},{5,3},{7,5},{6,7},{4,6},{2,4},{0,2},{9,8},{11,9},{13,1... | collective-permute-start | bytes 786440 | tf_op jit(solution)/shard_map/ppermute | solution.py:123
  62.1 6.7 %collective-permute-start.5 = (bf16[256,2,2,128]{3,0,1,2:T(8,128)(2,1)S(1)}, bf16[256,2,2,128]{3,0,1,2:T(8,128)(2,1)S(1)}, u32[]{:S(2)}, u32[]{:S(2)}) collective-permute-start(bf16[256,2,2,128]{3,0,1,2:T(8,128)(2,1)S(1)} %collective-permute-done.4), channel_id=1, source_target_pairs={{0,1},{1,3},{3,5},{5,7},{7,6},{6,4},{4,2},{2,0},{8,9},{9,11},{11,1... | collective-permute-start | bytes 786440 | tf_op jit(solution)/shard_map/ppermute | solution.py:119
  63.5 6.4 %collective-permute-start.2 = (bf16[256,2,2,128]{3,0,1,2:T(8,128)(2,1)S(1)}, bf16[256,2,2,128]{3,0,1,2:T(8,128)(2,1)S(1)}, u32[]{:S(2)}, u32[]{:S(2)}) collective-permute-start(bf16[256,2,2,128]{3,0,1,2:T(8,128)(2,1)S(1)} %collective-permute-done.1), channel_id=1, source_target_pairs={{1,0},{3,1},{5,3},{7,5},{6,7},{4,6},{2,4},{0,2},{9,8},{11,9},{13,1... | collective-permute-start | bytes 786440 | tf_op jit(solution)/shard_map/ppermute | solution.py:123
  68.8 6.4 %collective-permute-start.6 = (bf16[256,2,2,128]{3,0,1,2:T(8,128)(2,1)S(1)}, bf16[256,2,2,128]{3,0,1,2:T(8,128)(2,1)S(1)}, u32[]{:S(2)}, u32[]{:S(2)}) collective-permute-start(bf16[256,2,2,128]{3,0,1,2:T(8,128)(2,1)S(1)} %collective-permute-done.5), channel_id=1, source_target_pairs={{0,1},{1,3},{3,5},{5,7},{7,6},{6,4},{4,2},{2,0},{8,9},{9,11},{11,1... | collective-permute-start | bytes 786440 | tf_op jit(solution)/shard_map/ppermute | solution.py:119
  76.3 3.2 %copy-start.18 = (pred[16]{0:T(512)(128)(4,1)S(1)}, pred[16]{0:T(512)(128)(4,1)}, u32[]{:S(2)}) copy-start(pred[16]{0:T(512)(128)(4,1)} %get-tuple-element.56) | copy-start | bytes 52
  79.5 8.0 %copy-start.17 = (pred[8,16]{1,0:T(8,128)(4,1)S(1)}, pred[8,16]{1,0:T(8,128)(4,1)}, u32[]{:S(2)}) copy-start(pred[8,16]{1,0:T(8,128)(4,1)} %iota_compare_fusion.2) | copy-start | bytes 388
  87.8 0.8 copy-start.14
  88.6 4.7 %copy-start.16 = (s32[16]{0:T(128)S(1)}, s32[16]{0:T(128)}, u32[]{:S(2)}) copy-start(s32[16]{0:T(128)} %copy-done.15) | copy-start | bytes 196
  107.9 4.8 %copy-start.8 = (bf16[256,2048]{1,0:T(8,128)(2,1)S(1)}, bf16[256,2048]{1,0:T(8,128)(2,1)}, u32[]{:S(2)}) copy-start(bf16[256,2048]{1,0:T(8,128)(2,1)} %all-gather.2.cloned.1.call-done) | copy-start | bytes 3145732
  107.9 4.8 %copy-start.12 = (bf16[2048,4]{0,1:T(4,128)(2,1)S(1)}, bf16[2048,4]{0,1:T(4,128)(2,1)}, u32[]{:S(2)}) copy-start(bf16[2048,4]{0,1:T(4,128)(2,1)} %param.15) | copy-start | bytes 49156
  107.9 50.6 %all-to-all-start = ((bf16[8,1056,128]{2,1,0:T(8,128)(2,1)}), bf16[8,1056,128]{2,1,0:T(8,128)(2,1)}, u32[]{:S(2)}, u32[]{:S(2)}) async-start(bf16[8,1056,128]{2,1,0:T(8,128)(2,1)} %pad_maximum_fusion), calls=%async_computation | async-start | bytes 4325376 | tf_op jit(solution)/shard_map/all_to_all | solution.py:241
  162.2 3.5 %copy-start.6 = (f32[2,256,2,128]{3,1,2,0:T(8,128)S(1)}, f32[2,256,2,128]{3,1,2,0:T(8,128)}, u32[]{:S(2)}) copy-start(f32[2,256,2,128]{3,1,2,0:T(8,128)} %fusion.39) | copy-start | bytes 1572868
  168.1 2.5 %copy-start.3 = (bf16[4,256,2048]{2,1,0:T(8,128)(2,1)S(1)}, bf16[4,256,2048]{2,1,0:T(8,128)(2,1)}, u32[]{:S(2)}) copy-start(bf16[4,256,2048]{2,1,0:T(8,128)(2,1)} %param.19) | copy-start | bytes 12582916
  171.1 16.6 %copy-start.1 = (bf16[2,2048,256]{2,1,0:T(8,128)(2,1)S(1)}, bf16[2,2048,256]{2,1,0:T(8,128)(2,1)}, u32[]{:S(2)}) copy-start(bf16[2,2048,256]{2,1,0:T(8,128)(2,1)} %param.18) | copy-start | bytes 6291460
  172.4 7.0 %collective-permute-start.9 = (bf16[64,2048]{1,0:T(8,128)(2,1)}, bf16[64,2048]{1,0:T(8,128)(2,1)}, u32[]{:S(2)}, u32[]{:S(2)}) collective-permute-start(bf16[64,2048]{1,0:T(8,128)(2,1)} %get-tuple-element.35), channel_id=1, source_target_pairs={{0,24},{8,0},{16,8},{24,16},{1,25},{9,1},{17,9},{25,17},{2,26},{10... | collective-permute-start | bytes 786440 | tf_op jit(solution)/shard_map/ppermute | solution.py:105
  172.4 12.5 %collective-permute-start.8 = (bf16[64,2048]{1,0:T(8,128)(2,1)}, bf16[64,2048]{1,0:T(8,128)(2,1)}, u32[]{:S(2)}, u32[]{:S(2)}) collective-permute-start(bf16[64,2048]{1,0:T(8,128)(2,1)} %get-tuple-element.36), channel_id=1, source_target_pairs={{0,16},{8,24},{16,0},{24,8},{1,17},{9,25},{17,1},{25,9},{2,18},{10... | collective-permute-start | bytes 786440 | tf_op jit(solution)/shard_map/ppermute | solution.py:105
  172.6 13.1 %collective-permute-start.7 = (bf16[64,2048]{1,0:T(8,128)(2,1)S(1)}, bf16[64,2048]{1,0:T(8,128)(2,1)}, u32[]{:S(2)}, u32[]{:S(2)}) collective-permute-start(bf16[64,2048]{1,0:T(8,128)(2,1)S(1)} %get-tuple-element.34), channel_id=1, source_target_pairs={{0,8},{8,16},{16,24},{24,0},{1,9},{9,17},{17,25},{25,1},{2,10},{10... | collective-permute-start | bytes 786440 | tf_op jit(solution)/shard_map/ppermute | solution.py:105
Sparse Core Ops, SparseCore 0:
  10.4 19.4 all-gather.1

commit v5 on v4

--- a/solution.py
+++ b/solution.py
@@ -146,7 +146,7 @@
     local_heads = q_weight.shape[2] // HD
     scale_q = HD ** (-0.5)
     normed = normalize(hidden[0], norm_gain)
-    gathered = lax.all_gather(normed, "heads", axis=0, tiled=True)
+    gathered = shift_all_gather(normed, "heads").reshape(-1, normed.shape[1])
     new_count = gathered.shape[0]
     chosen = att_experts[0]
     cached_len = cached_blocks * block_size - tail_trim

time: 195 us -> 196 us (level)
  between operations: 14 us -> 0.59 us
  other arithmetic: 31.7 us -> 39.4 us
  starting transfers between devices: 11.9 us -> 16.9 us
  local copies, waits for them, and re-layouts: 28.7 us -> 32.4 us
  waiting for transfers between devices: 76.4 us -> 73.5 us
    ppermute x0 -> x3, starting transfers between devices: none -> 4.44 us  [shift_all_gather(): lax.ppermute(piece, axis_name, [(i, (i + s) % size) for i in range(size)])]
    gather x0 -> x1, local copies, waits for them, and re-layouts: none -> 2.99 us  [shift_all_gather(): jnp.take(by_offset, (jnp.arange(size, dtype=jnp.int32) - rank) % size, ax...]
    all_gather x1 -> x0, waiting for transfers between devices: 2.35 us -> none  [per_device(): gathered = lax.all_gather(normed, 'heads', axis=0, tiled=True)]
    another operation x4 -> x5, other arithmetic: 3.27 us -> 5.5 us
    unnamed x50 -> x56, local copies, waits for them, and re-layouts: 9.4 us -> 9.47 us
  transfers between devices with their start and end apart: 12 -> 14, of which waited for: 11 -> 9; matrix products, arithmetic and copies ran while one was open for 13% -> 15% of each run, Pallas kernels for 0% -> 0%
where the time goes in v5:
time: 196 us; the launch traced here: 195 us
  waiting for transfers between devices  73.5 us (38%)
  other arithmetic  39.4 us (20%)
  local copies, waits for them, and re-layouts  32.4 us (17%)
  matrix products  31.9 us (16%)
  starting transfers between devices  16.9 us (9%)
    all_to_all x1, waiting for transfers between devices, per_device(): received = lax.all_to_all(payload, 'seq', 0, 0, tiled=True)  44.1 us
    ppermute x4, waiting for transfers between devices, ring_all_gather(): moving = lax.ppermute(moving, axis_name, forward)  15.6 us
    ppermute x3, waiting for transfers between devices, shift_reduce_scatter(): lax.ppermute(piece, axis_name, [(i, (i + s) % size) for i in range(size)])  12.9 us
    unnamed x56, local copies, waits for them, and re-layouts  9.47 us
    dot_general x1, matrix products, per_device(): jnp.einsum('bnkhc,bthc->bhnkt', block_queries, keys_here, preferred_eleme...  7.99 us
    dot_general x1, matrix products, per_device(): jnp.einsum('rb,bhnkc->rhnkc', owns_f, block_accum, precision=lax.Precisio...  6.31 us
    dot_general x1, matrix products, per_device(): jnp.einsum('bhnkt,bthc->bhnkc', weights.astype(jnp.bfloat16), values_here...  5.22 us
    ppermute x3, starting transfers between devices, ring_all_gather(): moving = lax.ppermute(moving, axis_name, backward)  4.97 us
  transfers between devices with their start and end apart: 14, of which 9 were waited for; matrix products, arithmetic and copies ran while one was open for 15% of the time, Pallas kernels for 0%

profile of v5, /device:TPU:0, one launch (start us, length us, event | category | flops | bytes accessed | tf_op | source)
XLA Modules:
  0.0 194.7 jit_solution(2813713152433117136)
XLA Ops:
  2.0 1.8 fusion.40
  4.2 2.5 %collective-permute-start.1 = (bf16[64,2048]{1,0:T(8,128)(2,1)}, bf16[64,2048]{1,0:T(8,128)(2,1)}, u32[]{:S(2)}, u32[]{:S(2)}) collective-permute-start(bf16[64,2048]{1,0:T(8,128)(2,1)} %fusion.40), channel_id=1, source_target_pairs={{0,16},{8,24},{16,0},{24,8},{1,17},{9,25},{17,1},{25,9},{2,18},{10... | collective-permute-start | bytes 786440 | tf_op jit(solution)/shard_map/ppermute | solution.py:91
  19.5 2.7 %fusion.133 = (bf16[1,16,128,256]{3,2,1,0:T(8,128)(2,1)}, bf16[1,16,128,256]{3,2,1,0:T(8,128)(2,1)S(1)}) fusion(bf16[2,16,128,256]{3,2,1,0:T(8,128)(2,1)} %param.20), kind=kLoop, calls=%fused_computation.240 | loop fusion | bytes 4194304 | tf_op jit(solution)/shard_map/slice | solution.py:204
  26.7 1.6 copy.265
  28.3 1.9 multiply_cosine_fusion
  30.2 2.2 %pad_maximum_fusion.1 = bf16[4,64,2048]{2,1,0:T(8,128)(2,1)} fusion(bf16[1,64,2048]{2,1,0:T(8,128)(2,1)} %bitcast.5, bf16[1,64,2048]{2,1,0:T(8,128)(2,1)} %bitcast.4, bf16[1,64,2048]{2,1,0:T(8,128)(2,1)} %bitcast.3, bf16[1,64,2048]{2,1,0:T(8,128)(2,1)S(1)} %fusion.42), kind=kLoop, calls=%fused_computation.37 | loop fusion | flops 1572864 | bytes 2097152 | tf_op jit(solution)/shard_map/stack | solution.py:94
  32.4 3.0 %gather_fusion = bf16[4,64,2048]{2,1,0:T(8,128)(2,1)} fusion(bf16[4,64,2048]{2,1,0:T(8,128)(2,1)} %pad_maximum_fusion.1, s32[1024]{0:T(1024)} %pad_clamp_fusion.2), kind=kCustom, calls=%fused_computation | custom fusion | bytes 2097168 | tf_op jit(solution)/shard_map/jit(_take)/gather | solution.py:95
  36.8 3.8 %fusion.28 = f32[256,4,256]{2,0,1:T(8,128)S(1)} fusion(bf16[4,2048,256]{2,1,0:T(8,128)(2,1)} %param.17, bf16[256,2048]{1,0:T(8,128)(2,1)S(1)} %bitcast_select_fusion), kind=kOutput, calls=%fused_computation.43 | convolution fusion | flops 1073741824 | bytes 6291456 | tf_op jit(solution)/shard_map/nd,edc->nec/dot_general | solution.py:155
  41.8 2.1 %copy.211 = f32[256,2,256]{0,2,1:T(8,128)} copy(f32[256,2,256]{2,0,1:T(8,128)} %multiply_reduce_fusion.1) | data formatting | bytes 1048576 | tf_op jit(solution)/shard_map/reduce_sum | solution.py:156
  43.8 1.8 fusion.134
  45.6 1.9 copy.261
  51.6 1.6 collective-permute-start.3
  59.0 1.5 collective-permute-done.6
  62.1 1.6 collective-permute-start.4
  63.9 3.8 %collective-permute-done.7 = bf16[256,2,2,128]{3,0,1,2:T(8,128)(2,1)S(1)} collective-permute-done((bf16[256,2,2,128]{3,0,1,2:T(8,128)(2,1)}, bf16[256,2,2,128]{3,0,1,2:T(8,128)(2,1)S(1)}, u32[]{:S(2)}, u32[]{:S(2)}) %collective-permute-start.7) | collective-permute-done | bytes 262176 | tf_op jit(solution)/shard_map/ppermute | solution.py:119
  69.1 1.8 collective-permute-start.5
  71.9 3.9 %collective-permute-done.8 = bf16[256,2,2,128]{3,0,1,2:T(8,128)(2,1)S(1)} collective-permute-done((bf16[256,2,2,128]{3,0,1,2:T(8,128)(2,1)S(1)}, bf16[256,2,2,128]{3,0,1,2:T(8,128)(2,1)S(1)}, u32[]{:S(2)}, u32[]{:S(2)}) %collective-permute-start.8) | collective-permute-done | bytes 262176 | tf_op jit(solution)/shard_map/ppermute | solution.py:119
  75.9 6.3 %collective-permute-done.9 = bf16[256,2,2,128]{3,0,1,2:T(8,128)(2,1)S(1)} collective-permute-done((bf16[256,2,2,128]{3,0,1,2:T(8,128)(2,1)S(1)}, bf16[256,2,2,128]{3,0,1,2:T(8,128)(2,1)S(1)}, u32[]{:S(2)}, u32[]{:S(2)}) %collective-permute-start.9) | collective-permute-done | bytes 262176 | tf_op jit(solution)/shard_map/ppermute | solution.py:119
  83.3 3.2 %gather_fusion.4 = bf16[16,256,2,2,128]{4,1,2,3,0:T(8,128)(2,1)} fusion(bf16[8,256,2,2,128]{4,1,2,3,0:T(8,128)(2,1)S(1)} %bitcast_dynamic-update-slice_fusion, s32[1024]{0:T(1024)} %pad_clamp_fusion), kind=kCustom, calls=%fused_computation.4 | custom fusion | bytes 8388672 | tf_op jit(solution)/shard_map/jit(_take)/gather | solution.py:202
  86.5 8.0 %fusion.2 = (f32[16,2,256,2]{2,3,1,0:T(2,128)S(1)}, f32[16,2,256,2,128]{2,4,3,1,0:T(8,128)}) fusion(pred[16,128]{1,0:T(8,128)(4,1)S(1)} %copy-done.12, bf16[16,128,2,128,1]{1,3,4,2,0:T(8,128)(2,1)} %bitcast.197, bf16[16,256,2,2,128]{4,1,2,3,0:T(8,128)(2,1)} %gather_fusion.4, pred[16]{0:T(512)(128)(4,1)S(1)} %copy-done.21), kind=kOutput, calls=%fused_computation.10 | convolution fusion | flops 545243136 | bytes 13699088 | tf_op jit(solution)/shard_map/bnkhc,bthc->bhnkt/dot_general | solution.py:206
  95.7 4.7 %fusion.3 = f32[16,2,256,2]{2,3,1,0:T(2,128)S(1)} fusion(f32[16,2,256,2,128]{2,4,3,1,0:T(8,128)} %get-tuple-element.54, f32[16,2,256,2]{2,3,1,0:T(2,128)S(1)} %broadcast_select_fusion, pred[16,128]{1,0:T(8,128)(4,1)S(1)} %copy-done.12), kind=kLoop, calls=%fused_computation.11 | loop fusion | flops 8372224 | bytes 8521728 | tf_op jit(solution)/shard_map/reduce_sum | solution.py:221
  101.6 5.2 %fusion.5 = f32[16,2,256,2,128]{4,2,3,1,0:T(8,128)S(1)} fusion(bf16[16,128,2,128,1]{1,3,4,2,0:T(8,128)(2,1)S(1)} %bitcast.187, f32[16,2,256,2,128]{2,4,3,1,0:T(8,128)} %get-tuple-element.54, f32[16,2,256,2]{2,3,1,0:T(2,128)S(1)} %broadcast_select_fusion, pred[16,128]{1,0:T(8,128)(4,1)S(1)} %copy-done.12), kind=kOutput, calls=%fused_computation.13 | convolution fusion | flops 545259520 | bytes 17893376 | tf_op jit(solution)/shard_map/bhnkt,bthc->bhnkc/dot_general | solution.py:222
  106.9 6.3 %fusion.19 = bf16[8,2,256,2,128]{4,0,3,2,1:T(8,128)(2,1)S(1)} fusion(f32[16,2,256,2,128]{4,2,3,1,0:T(8,128)S(1)} %fusion.5, s32[16]{0:T(128)S(1)} %copy-done.19), kind=kOutput, calls=%fused_computation.33 | convolution fusion | flops 202375296 | bytes 10485824 | tf_op jit(solution)/shard_map/rb,bhnkc->rhnkc/dot_general | solution.py:229
  113.5 1.5 pad_maximum_fusion
  115.0 4.9 %all-to-all-start = ((bf16[8,1056,128]{2,1,0:T(8,128)(2,1)}), bf16[8,1056,128]{2,1,0:T(8,128)(2,1)}, u32[]{:S(2)}, u32[]{:S(2)}) async-start(bf16[8,1056,128]{2,1,0:T(8,128)(2,1)} %pad_maximum_fusion), calls=%async_computation | async-start | bytes 4325376 | tf_op jit(solution)/shard_map/all_to_all | solution.py:241
  120.4 44.1 %all-to-all-done = bf16[8,1056,128]{2,1,0:T(8,128)(2,1)} async-done(((bf16[8,1056,128]{2,1,0:T(8,128)(2,1)}), bf16[8,1056,128]{2,1,0:T(8,128)(2,1)}, u32[]{:S(2)}, u32[]{:S(2)}) %all-to-all-start) | async-done | bytes 2162720 | tf_op jit(solution)/shard_map/all_to_all | solution.py:241
  168.6 3.1 %multiply_reduce_fusion = f32[1024,128]{1,0:T(8,128)S(1)} fusion(bf16[8,1056,128]{2,1,0:T(8,128)(2,1)} %all-to-all-done, f32[8,1024]{1,0:T(8,128)S(1)} %subtract_exponential_fusion.2), kind=kLoop, calls=%fused_computation.14 | loop fusion | flops 3014656 | bytes 2654208 | tf_op jit(solution)/shard_map/reduce_sum | solution.py:255
  172.4 1.7 convolution_multiply_fusion.3
  174.1 1.9 fusion.16
  179.9 4.8 %collective-permute-done.12 = bf16[64,2048]{1,0:T(8,128)(2,1)} collective-permute-done((bf16[64,2048]{1,0:T(8,128)(2,1)}, bf16[64,2048]{1,0:T(8,128)(2,1)}, u32[]{:S(2)}, u32[]{:S(2)}) %collective-permute-start.12) | collective-permute-done | bytes 262176 | tf_op jit(solution)/shard_map/ppermute | solution.py:105
  184.7 7.7 %collective-permute-done.11 = bf16[64,2048]{1,0:T(8,128)(2,1)} collective-permute-done((bf16[64,2048]{1,0:T(8,128)(2,1)}, bf16[64,2048]{1,0:T(8,128)(2,1)}, u32[]{:S(2)}, u32[]{:S(2)}) %collective-permute-start.11) | collective-permute-done | bytes 262176 | tf_op jit(solution)/shard_map/ppermute | solution.py:105
  192.7 1.9 fusion.53
  (150 shorter events, 49.2 us)
Async XLA Ops:
  0.0 53.6 %copy-start = (bf16[2,2048,256]{2,1,0:T(8,128)(2,1)S(1)}, bf16[2,2048,256]{2,1,0:T(8,128)(2,1)}, u32[]{:S(2)}) copy-start(bf16[2,2048,256]{2,1,0:T(8,128)(2,1)} %param.18) | copy-start | bytes 6291460
  0.0 14.4 %copy-start.2 = (s32[8]{0:T(128)S(1)}, s32[8]{0:T(128)}, u32[]{:S(2)}) copy-start(s32[8]{0:T(128)} %constant.149.clone) | copy-start | bytes 100
  0.0 17.6 %copy-start.13 = (s32[1,256,2]{1,2,0:T(2,128)S(1)}, s32[1,256,2]{1,2,0:T(2,128)}, u32[]{:S(2)}) copy-start(s32[1,256,2]{1,2,0:T(2,128)} %param.16) | copy-start | bytes 6148
  3.8 26.4 %collective-permute-start.2 = (bf16[64,2048]{1,0:T(8,128)(2,1)}, bf16[64,2048]{1,0:T(8,128)(2,1)}, u32[]{:S(2)}, u32[]{:S(2)}) collective-permute-start(bf16[64,2048]{1,0:T(8,128)(2,1)} %fusion.40), channel_id=1, source_target_pairs={{0,8},{8,16},{16,24},{24,0},{1,9},{9,17},{17,25},{25,1},{2,10},{10... | collective-permute-start | bytes 786440 | tf_op jit(solution)/shard_map/ppermute | solution.py:91
  4.2 26.0 %collective-permute-start.1 = (bf16[64,2048]{1,0:T(8,128)(2,1)}, bf16[64,2048]{1,0:T(8,128)(2,1)}, u32[]{:S(2)}, u32[]{:S(2)}) collective-permute-start(bf16[64,2048]{1,0:T(8,128)(2,1)} %fusion.40), channel_id=1, source_target_pairs={{0,16},{8,24},{16,0},{24,8},{1,17},{9,25},{17,1},{25,9},{2,18},{10... | collective-permute-start | bytes 786440 | tf_op jit(solution)/shard_map/ppermute | solution.py:91
  6.8 23.4 %collective-permute-start = (bf16[64,2048]{1,0:T(8,128)(2,1)}, bf16[64,2048]{1,0:T(8,128)(2,1)}, u32[]{:S(2)}, u32[]{:S(2)}) collective-permute-start(bf16[64,2048]{1,0:T(8,128)(2,1)} %fusion.40), channel_id=1, source_target_pairs={{0,24},{8,0},{16,8},{24,16},{1,25},{9,1},{17,9},{25,17},{2,26},{10... | collective-permute-start | bytes 786440 | tf_op jit(solution)/shard_map/ppermute | solution.py:91
  12.4 7.1 %copy-start.16 = (s32[1024]{0:T(1024)}, s32[1024]{0:T(1024)S(1)}, u32[]{:S(2)}) copy-start(s32[1024]{0:T(1024)S(1)} %pad_clamp_fusion.1) | copy-start | bytes 12292
  17.6 9.0 %copy-start.18 = (s32[16]{0:T(128)}, s32[16]{0:T(128)S(1)}, u32[]{:S(2)}) copy-start(s32[16]{0:T(128)S(1)} %broadcast_add_fusion) | copy-start | bytes 196
  36.8 3.8 %copy-start.3 = (bf16[256,2048]{1,0:T(8,128)(2,1)}, bf16[256,2048]{1,0:T(8,128)(2,1)S(1)}, u32[]{:S(2)}) copy-start(bf16[256,2048]{1,0:T(8,128)(2,1)S(1)} %bitcast_select_fusion) | copy-start | bytes 3145732
  48.6 5.0 %copy-start.4 = (bf16[256,2048]{1,0:T(8,128)(2,1)S(1)}, bf16[256,2048]{1,0:T(8,128)(2,1)}, u32[]{:S(2)}) copy-start(bf16[256,2048]{1,0:T(8,128)(2,1)} %copy-done.3) | copy-start | bytes 3145732
  51.6 10.5 %collective-permute-start.3 = (bf16[256,2,2,128]{3,0,1,2:T(8,128)(2,1)}, bf16[256,2,2,128]{3,0,1,2:T(8,128)(2,1)}, u32[]{:S(2)}, u32[]{:S(2)}) collective-permute-start(bf16[256,2,2,128]{3,0,1,2:T(8,128)(2,1)} %pad_maximum_fusion.2), channel_id=1, source_target_pairs={{1,0},{3,1},{5,3},{7,5},{6,7},{4,6},{2,4},{0,2},{9,8},{11,9},{13,1... | collective-permute-start | bytes 786440 | tf_op jit(solution)/shard_map/ppermute | solution.py:123
  53.2 7.3 %collective-permute-start.6 = (bf16[256,2,2,128]{3,0,1,2:T(8,128)(2,1)}, bf16[256,2,2,128]{3,0,1,2:T(8,128)(2,1)}, u32[]{:S(2)}, u32[]{:S(2)}) collective-permute-start(bf16[256,2,2,128]{3,0,1,2:T(8,128)(2,1)} %pad_maximum_fusion.2), channel_id=1, source_target_pairs={{0,1},{1,3},{3,5},{5,7},{7,6},{6,4},{4,2},{2,0},{8,9},{9,11},{11,1... | collective-permute-start | bytes 786440 | tf_op jit(solution)/shard_map/ppermute | solution.py:119
  54.6 3.0 %copy-start.11 = (pred[256,256]{0,1:T(8,128)(4,1)S(1)}, pred[256,256]{0,1:T(8,128)(4,1)}, u32[]{:S(2)}) copy-start(pred[256,256]{0,1:T(8,128)(4,1)} %iota_compare_fusion) | copy-start | bytes 196612
  57.6 10.3 %copy-start.8 = (bf16[256,2,2,64]{3,0,1,2:T(8,128)(2,1)S(1)}, bf16[256,2,2,64]{3,0,1,2:T(8,128)(2,1)}, u32[]{:S(2)}) copy-start(bf16[256,2,2,64]{3,0,1,2:T(8,128)(2,1)} %copy-done.7) | copy-start | bytes 393220
  60.5 7.2 %collective-permute-start.7 = (bf16[256,2,2,128]{3,0,1,2:T(8,128)(2,1)}, bf16[256,2,2,128]{3,0,1,2:T(8,128)(2,1)S(1)}, u32[]{:S(2)}, u32[]{:S(2)}) collective-permute-start(bf16[256,2,2,128]{3,0,1,2:T(8,128)(2,1)} %collective-permute-done.6), channel_id=1, source_target_pairs={{0,1},{1,3},{3,5},{5,7},{7,6},{6,4},{4,2},{2,0},{8,9},{9,11},{11,1... | collective-permute-start | bytes 786440 | tf_op jit(solution)/shard_map/ppermute | solution.py:119
  62.1 6.9 %collective-permute-start.4 = (bf16[256,2,2,128]{3,0,1,2:T(8,128)(2,1)}, bf16[256,2,2,128]{3,0,1,2:T(8,128)(2,1)S(1)}, u32[]{:S(2)}, u32[]{:S(2)}) collective-permute-start(bf16[256,2,2,128]{3,0,1,2:T(8,128)(2,1)} %collective-permute-done.3), channel_id=1, source_target_pairs={{1,0},{3,1},{5,3},{7,5},{6,7},{4,6},{2,4},{0,2},{9,8},{11,9},{13,1... | collective-permute-start | bytes 786440 | tf_op jit(solution)/shard_map/ppermute | solution.py:123
  67.7 8.1 %collective-permute-start.8 = (bf16[256,2,2,128]{3,0,1,2:T(8,128)(2,1)S(1)}, bf16[256,2,2,128]{3,0,1,2:T(8,128)(2,1)S(1)}, u32[]{:S(2)}, u32[]{:S(2)}) collective-permute-start(bf16[256,2,2,128]{3,0,1,2:T(8,128)(2,1)S(1)} %collective-permute-done.7), channel_id=1, source_target_pairs={{0,1},{1,3},{3,5},{5,7},{7,6},{6,4},{4,2},{2,0},{8,9},{9,11},{11,1... | collective-permute-start | bytes 786440 | tf_op jit(solution)/shard_map/ppermute | solution.py:119
  69.1 6.8 %collective-permute-start.5 = (bf16[256,2,2,128]{3,0,1,2:T(8,128)(2,1)S(1)}, bf16[256,2,2,128]{3,0,1,2:T(8,128)(2,1)S(1)}, u32[]{:S(2)}, u32[]{:S(2)}) collective-permute-start(bf16[256,2,2,128]{3,0,1,2:T(8,128)(2,1)S(1)} %collective-permute-done.4), channel_id=1, source_target_pairs={{1,0},{3,1},{5,3},{7,5},{6,7},{4,6},{2,4},{0,2},{9,8},{11,9},{13,1... | collective-permute-start | bytes 786440 | tf_op jit(solution)/shard_map/ppermute | solution.py:123
  75.8 6.4 %collective-permute-start.9 = (bf16[256,2,2,128]{3,0,1,2:T(8,128)(2,1)S(1)}, bf16[256,2,2,128]{3,0,1,2:T(8,128)(2,1)S(1)}, u32[]{:S(2)}, u32[]{:S(2)}) collective-permute-start(bf16[256,2,2,128]{3,0,1,2:T(8,128)(2,1)S(1)} %collective-permute-done.8), channel_id=1, source_target_pairs={{0,1},{1,3},{3,5},{5,7},{7,6},{6,4},{4,2},{2,0},{8,9},{9,11},{11,1... | collective-permute-start | bytes 786440 | tf_op jit(solution)/shard_map/ppermute | solution.py:119
  83.3 3.2 %copy-start.12 = (pred[16,128]{1,0:T(8,128)(4,1)S(1)}, pred[16,128]{1,0:T(8,128)(4,1)}, u32[]{:S(2)}) copy-start(pred[16,128]{1,0:T(8,128)(4,1)} %add_compare_fusion) | copy-start | bytes 6148
  83.3 3.2 %copy-start.21 = (pred[16]{0:T(512)(128)(4,1)S(1)}, pred[16]{0:T(512)(128)(4,1)}, u32[]{:S(2)}) copy-start(pred[16]{0:T(512)(128)(4,1)} %get-tuple-element.56) | copy-start | bytes 52
  86.5 8.0 %copy-start.20 = (pred[8,16]{1,0:T(8,128)(4,1)S(1)}, pred[8,16]{1,0:T(8,128)(4,1)}, u32[]{:S(2)}) copy-start(pred[8,16]{1,0:T(8,128)(4,1)} %iota_compare_fusion.2) | copy-start | bytes 388
  95.7 4.7 %copy-start.19 = (s32[16]{0:T(128)S(1)}, s32[16]{0:T(128)}, u32[]{:S(2)}) copy-start(s32[16]{0:T(128)} %copy-done.18) | copy-start | bytes 196
  114.9 4.9 %copy-start.14 = (s32[1,256,2]{1,2,0:T(2,128)S(1)}, s32[1,256,2]{1,2,0:T(2,128)}, u32[]{:S(2)}) copy-start(s32[1,256,2]{1,2,0:T(2,128)} %param.16) | copy-start | bytes 6148
  114.9 5.0 %copy-start.5 = (bf16[256,2048]{1,0:T(8,128)(2,1)S(1)}, bf16[256,2048]{1,0:T(8,128)(2,1)}, u32[]{:S(2)}) copy-start(bf16[256,2048]{1,0:T(8,128)(2,1)} %copy-done.3) | copy-start | bytes 3145732
  114.9 5.0 %copy-start.15 = (bf16[2048,4]{0,1:T(4,128)(2,1)S(1)}, bf16[2048,4]{0,1:T(4,128)(2,1)}, u32[]{:S(2)}) copy-start(bf16[2048,4]{0,1:T(4,128)(2,1)} %param.15) | copy-start | bytes 49156
  115.0 49.6 %all-to-all-start = ((bf16[8,1056,128]{2,1,0:T(8,128)(2,1)}), bf16[8,1056,128]{2,1,0:T(8,128)(2,1)}, u32[]{:S(2)}, u32[]{:S(2)}) async-start(bf16[8,1056,128]{2,1,0:T(8,128)(2,1)} %pad_maximum_fusion), calls=%async_computation | async-start | bytes 4325376 | tf_op jit(solution)/shard_map/all_to_all | solution.py:241
  168.2 3.5 %copy-start.9 = (f32[2,256,2,128]{3,1,2,0:T(8,128)S(1)}, f32[2,256,2,128]{3,1,2,0:T(8,128)}, u32[]{:S(2)}) copy-start(f32[2,256,2,128]{3,1,2,0:T(8,128)} %fusion.43) | copy-start | bytes 1572868
  177.1 17.6 %copy-start.1 = (bf16[2,2048,256]{2,1,0:T(8,128)(2,1)S(1)}, bf16[2,2048,256]{2,1,0:T(8,128)(2,1)}, u32[]{:S(2)}) copy-start(bf16[2,2048,256]{2,1,0:T(8,128)(2,1)} %param.18) | copy-start | bytes 6291460
  178.4 6.3 %collective-permute-start.12 = (bf16[64,2048]{1,0:T(8,128)(2,1)}, bf16[64,2048]{1,0:T(8,128)(2,1)}, u32[]{:S(2)}, u32[]{:S(2)}) collective-permute-start(bf16[64,2048]{1,0:T(8,128)(2,1)} %get-tuple-element.35), channel_id=1, source_target_pairs={{0,24},{8,0},{16,8},{24,16},{1,25},{9,1},{17,9},{25,17},{2,26},{10... | collective-permute-start | bytes 786440 | tf_op jit(solution)/shard_map/ppermute | solution.py:105
  178.4 14.0 %collective-permute-start.11 = (bf16[64,2048]{1,0:T(8,128)(2,1)}, bf16[64,2048]{1,0:T(8,128)(2,1)}, u32[]{:S(2)}, u32[]{:S(2)}) collective-permute-start(bf16[64,2048]{1,0:T(8,128)(2,1)} %get-tuple-element.36), channel_id=1, source_target_pairs={{0,16},{8,24},{16,0},{24,8},{1,17},{9,25},{17,1},{25,9},{2,18},{10... | collective-permute-start | bytes 786440 | tf_op jit(solution)/shard_map/ppermute | solution.py:105
  179.7 13.1 %collective-permute-start.10 = (bf16[64,2048]{1,0:T(8,128)(2,1)S(1)}, bf16[64,2048]{1,0:T(8,128)(2,1)}, u32[]{:S(2)}, u32[]{:S(2)}) collective-permute-start(bf16[64,2048]{1,0:T(8,128)(2,1)S(1)} %get-tuple-element.34), channel_id=1, source_target_pairs={{0,8},{8,16},{16,24},{24,0},{1,9},{9,17},{17,25},{25,1},{2,10},{10... | collective-permute-start | bytes 786440 | tf_op jit(solution)/shard_map/ppermute | solution.py:105
  (4 other events, 4.8 us)

commit v6 on v5

--- a/solution.py
+++ b/solution.py
@@ -4,6 +4,8 @@
 import jax
 import jax.numpy as jnp
 from jax import lax
+from jax.experimental import pallas as pl
+from jax.experimental.pallas import tpu as pltpu
 from jax.sharding import PartitionSpec as P
 
 HD = 128
@@ -125,6 +127,57 @@
     return jnp.stack([piece] + from_ahead + from_behind[::-1], axis=0)
 
 
+def block_attention(ring_queries, keys, values_t, owner_offset, valid):
+    blocks, block_size, width = keys.shape
+    query_rows = ring_queries.shape[1]
+    heads = width // HD
+    scale = HD ** (-0.5)
+
+    def kernel(offset_ref, valid_ref, q_ref, k_ref, v_ref, best_ref, total_ref, accum_ref):
+        b = pl.program_id(0)
+        limit = valid_ref[b]
+        row = lax.broadcasted_iota(jnp.int32, (block_size, query_rows), 0)
+        for h in range(heads):
+            q = q_ref[0, :, h * HD:(h + 1) * HD]
+            k = k_ref[0, :, h * HD:(h + 1) * HD]
+            scores = lax.dot_general(
+                k, q, (((1,), (1,)), ((), ())), preferred_element_type=jnp.float32
+            ) * scale
+            scores = jnp.where(row < limit, scores, NEG_FILL)
+            best = jnp.max(scores, axis=0, keepdims=True)
+            weights = jnp.exp(scores - best)
+            best_ref[0, h] = best
+            total_ref[0, h] = jnp.sum(weights, axis=0, keepdims=True)
+            v_t = v_ref[0, h * HD:(h + 1) * HD, :]
+            accum_ref[0, h] = jnp.dot(
+                v_t, weights.astype(jnp.bfloat16), preferred_element_type=jnp.float32
+            )
+
+    grid_spec = pltpu.PrefetchScalarGridSpec(
+        num_scalar_prefetch=2,
+        grid=(blocks,),
+        in_specs=[
+            pl.BlockSpec((1, query_rows, width), lambda b, off, val: (off[b], 0, 0)),
+            pl.BlockSpec((1, block_size, width), lambda b, off, val: (b, 0, 0)),
+            pl.BlockSpec((1, width, block_size), lambda b, off, val: (b, 0, 0)),
+        ],
+        out_specs=[
+            pl.BlockSpec((1, heads, 1, query_rows), lambda b, off, val: (b, 0, 0, 0)),
+            pl.BlockSpec((1, heads, 1, query_rows), lambda b, off, val: (b, 0, 0, 0)),
+            pl.BlockSpec((1, heads, HD, query_rows), lambda b, off, val: (b, 0, 0, 0)),
+        ],
+    )
+    return pl.pallas_call(
+        kernel,
+        grid_spec=grid_spec,
+        out_shape=[
+            jax.ShapeDtypeStruct((blocks, heads, 1, query_rows), jnp.float32),
+            jax.ShapeDtypeStruct((blocks, heads, 1, query_rows), jnp.float32),
+            jax.ShapeDtypeStruct((blocks, heads, HD, query_rows), jnp.float32),
+        ],
+    )(owner_offset, valid, ring_queries, keys, values_t)
+
+
 def per_device(
     cycle,
     hidden,
@@ -199,60 +252,58 @@
         (ring_queries, self_best, self_total, self_accum)
     )
     owner_offset = (jnp.asarray(position_of, dtype=jnp.int32)[owner] - position) % ring_size
-    block_queries = jnp.take(ring_queries, owner_offset, axis=0)
-    keys_here = kv_cache[0].reshape(local_blocks, block_size, local_heads, HD)
-    values_here = kv_cache[1].reshape(local_blocks, block_size, local_heads, HD)
-    scores = (
-        jnp.einsum(
-            "bnkhc,bthc->bhnkt", block_queries, keys_here, preferred_element_type=jnp.float32
-        )
-        * scale_q
-    )
-    key_pos = ordinal[:, None] * block_size + jnp.arange(block_size, dtype=jnp.int32)[None, :]
-    key_ok = key_pos < cached_len[owner][:, None]
-    scores = jnp.where(key_ok[:, None, None, None, :], scores, NEG_FILL)
-    block_best = jnp.max(scores, axis=-1)
-    request_best = jnp.max(
-        jnp.where(owns[:, :, None, None, None], block_best[None], NEG_FILL), axis=1
-    )
+    valid = jnp.clip(cached_len[owner] - ordinal * block_size, 0, block_size).astype(jnp.int32)
+    query_rows = new_count * 2
+    block_best, block_totals, block_accum = block_attention(
+        ring_queries.reshape(request_count, query_rows, local_heads * HD),
+        kv_cache[0],
+        jnp.swapaxes(kv_cache[1], 1, 2),
+        owner_offset,
+        valid,
+    )
+    block_best = block_best[:, :, 0]
+    block_totals = block_totals[:, :, 0]
+    request_best = jnp.max(jnp.where(owns[:, :, None, None], block_best[None], NEG_FILL), axis=1)
     best_hi, best_lo = split_bf16(request_best)
     request_ref = best_hi + best_lo
-    weights = jnp.exp(scores - jnp.take(request_ref, owner, axis=0)[..., None])
-    block_totals = jnp.sum(weights, axis=-1)
-    block_accum = jnp.einsum(
-        "bhnkt,bthc->bhnkc",
-        weights.astype(jnp.bfloat16),
-        values_here,
-        preferred_element_type=jnp.float32,
-    )
+    factor = jnp.exp(block_best - jnp.take(request_ref, owner, axis=0))
     owns_f = owns.astype(jnp.float32)
-    accum = jnp.einsum("rb,bhnkc->rhnkc", owns_f, block_accum, precision=lax.Precision.HIGHEST)
-    totals = jnp.einsum("rb,bhnk->rhnk", owns_f, block_totals, precision=lax.Precision.HIGHEST)
+    totals = jnp.einsum(
+        "rb,bhq->rhq", owns_f, block_totals * factor, precision=lax.Precision.HIGHEST
+    )
+    accum = jnp.einsum(
+        "rb,bhcq->rhcq",
+        owns_f,
+        block_accum * factor[:, :, None, :],
+        precision=lax.Precision.HIGHEST,
+    )
     totals_hi, totals_lo = split_bf16(totals)
     stats = jnp.stack([best_hi, best_lo, totals_hi, totals_lo], axis=1).astype(jnp.bfloat16)
-    stat_rows = stats.size // (request_count * HD)
     payload = jnp.concatenate(
         [
-            accum.astype(jnp.bfloat16).reshape(request_count, -1, HD),
-            stats.reshape(request_count, stat_rows, HD),
+            accum.astype(jnp.bfloat16).reshape(request_count, -1, query_rows),
+            stats.reshape(request_count, -1, query_rows),
         ],
         axis=1,
     )
     received = lax.all_to_all(payload, "seq", 0, 0, tiled=True)
-    acc_rows = local_heads * new_count * 2
+    acc_rows = local_heads * HD
     sources = received.shape[0]
     part_accum = received[:, :acc_rows].astype(jnp.float32).reshape(
-        sources, local_heads, new_count, 2, HD
+        sources, local_heads, HD, query_rows
     )
     part_stats = received[:, acc_rows:].astype(jnp.float32).reshape(
-        sources, 4, local_heads, new_count, 2
+        sources, 4, local_heads, query_rows
     )
     part_best = part_stats[:, 0] + part_stats[:, 1]
     part_totals = part_stats[:, 2] + part_stats[:, 3]
     cache_best = jnp.max(part_best, axis=0)
-    factor = jnp.exp(part_best - cache_best[None])
-    cache_total = jnp.sum(part_totals * factor, axis=0)
-    cache_accum = jnp.sum(part_accum * factor[..., None], axis=0)
+    share = jnp.exp(part_best - cache_best[None])
+    cache_total = jnp.sum(part_totals * share, axis=0).reshape(local_heads, new_count, 2)
+    cache_accum = jnp.transpose(
+        jnp.sum(part_accum * share[:, :, None, :], axis=0), (0, 2, 1)
+    ).reshape(local_heads, new_count, 2, HD)
+    cache_best = cache_best.reshape(local_heads, new_count, 2)
 
     peak = jnp.maximum(cache_best, self_best)
     cache_share = jnp.exp(cache_best - peak)

time: 196 us -> 187 us (0.954)
  Pallas kernels: 0 us -> 17.1 us
  matrix products: 31.9 us -> 18.6 us
  other arithmetic: 39.4 us -> 29.4 us
  local copies, waits for them, and re-layouts: 32.4 us -> 29.5 us
    pallas_call x0 -> x1, Pallas kernels: none -> 17.1 us  [block_attention(): pl.pallas_call(kernel, grid_spec=grid_spec, out_shape=[jax.ShapeDtypeStru...]
    dot_general x4 -> x2, matrix products: 19.7 us -> 6.4 us  [the longest x1 6.25 us: per_device(): jnp.einsum('rb,bhcq->rhcq', owns_f, block_accum * factor[:, :, None, :],...]
    reduce_sum x3 -> x2, other arithmetic: 9.14 us -> 0.48 us  [the longest x1 0.43 us: per_device(): jnp.sum(part_accum * share[:, :, None, :], axis=0)]
    mul x1 -> x2, other arithmetic: 0.01 us -> 5.53 us  [the longest x1 4.51 us: per_device(): block_accum * factor[:, :, None, :]]
    reshape x1 -> x6, local copies, waits for them, and re-layouts: 0.27 us -> 3.99 us  [the longest x1 2.69 us: per_device(): ring_queries.reshape(request_count, query_rows, local_heads * HD)]
    gather x3 -> x2, local copies, waits for them, and re-layouts: 4.59 us -> 1.41 us  [the longest x1 0.74 us: per_device(): factor = jnp.exp(block_best - jnp.take(request_ref, owner, axis=0))]
    optimization_barrier x0 -> x1, local copies, waits for them, and re-layouts: none -> 2.16 us  [per_device(): lax.optimization_barrier((ring_queries, self_best, self_total, self_accum))]
    unnamed x56 -> x45, local copies, waits for them, and re-layouts: 9.47 us -> 8.99 us
  transfers between devices with their start and end apart: 14 -> 14, of which waited for: 9 -> 9; matrix products, arithmetic and copies ran while one was open for 15% -> 13% of each run, Pallas kernels for 0% -> 0%
where the time goes in v6:
time: 187 us; the launch traced here: 186 us
  waiting for transfers between devices  73.4 us (39%)
  local copies, waits for them, and re-layouts  29.5 us (16%)
  other arithmetic  29.4 us (16%)
  matrix products  18.6 us (10%)
  starting transfers between devices  17.1 us (9%)
  Pallas kernels  17.1 us (9%)
    all_to_all x1, waiting for transfers between devices, per_device(): received = lax.all_to_all(payload, 'seq', 0, 0, tiled=True)  44 us
    pallas_call x1, Pallas kernels, block_attention(): pl.pallas_call(kernel, grid_spec=grid_spec, out_shape=[jax.ShapeDtypeStru...  17.1 us
    ppermute x4, waiting for transfers between devices, ring_all_gather(): moving = lax.ppermute(moving, axis_name, forward)  15.5 us
    ppermute x3, waiting for transfers between devices, shift_reduce_scatter(): lax.ppermute(piece, axis_name, [(i, (i + s) % size) for i in range(size)])  12.9 us
    unnamed x45, local copies, waits for them, and re-layouts  8.99 us
    dot_general x1, matrix products, per_device(): jnp.einsum('rb,bhcq->rhcq', owns_f, block_accum * factor[:, :, None, :],...  6.25 us
    all_to_all x1, starting transfers between devices, per_device(): received = lax.all_to_all(payload, 'seq', 0, 0, tiled=True)  5.11 us
    ppermute x3, starting transfers between devices, ring_all_gather(): moving = lax.ppermute(moving, axis_name, backward)  5 us
  transfers between devices with their start and end apart: 14, of which 9 were waited for; matrix products, arithmetic and copies ran while one was open for 13% of the time, Pallas kernels for 0%

profile of v6, /device:TPU:0, one launch (start us, length us, event | category | flops | bytes accessed | tf_op | source)
XLA Modules:
  0.0 185.6 jit_solution(13276827294309463591)
XLA Ops:
  2.0 1.8 fusion.28
  4.2 2.5 %collective-permute-start.1 = (bf16[64,2048]{1,0:T(8,128)(2,1)}, bf16[64,2048]{1,0:T(8,128)(2,1)}, u32[]{:S(2)}, u32[]{:S(2)}) collective-permute-start(bf16[64,2048]{1,0:T(8,128)(2,1)} %fusion.28), channel_id=1, source_target_pairs={{0,16},{8,24},{16,0},{24,8},{1,17},{9,25},{17,1},{25,9},{2,18},{10... | collective-permute-start | bytes 786440 | tf_op jit(solution)/shard_map/ppermute | solution.py:93
  6.8 1.4 collective-permute-start
  12.5 1.3 dynamic_slice.18
  17.7 2.7 %fusion.120 = (bf16[1,16,128,256]{3,2,1,0:T(8,128)(2,1)S(1)}, bf16[16,128,256]{2,1,0:T(8,128)(2,1)}) fusion(bf16[2,16,128,256]{3,2,1,0:T(8,128)(2,1)} %param.20), kind=kLoop, calls=%fused_computation.221 | loop fusion | bytes 4194304 | tf_op jit(solution)/shard_map/slice | solution.py:260
  22.4 1.3 copy.182
  25.0 2.2 %pad_maximum_fusion.1 = bf16[4,64,2048]{2,1,0:T(8,128)(2,1)} fusion(bf16[1,64,2048]{2,1,0:T(8,128)(2,1)} %bitcast.5, bf16[1,64,2048]{2,1,0:T(8,128)(2,1)} %bitcast.4, bf16[1,64,2048]{2,1,0:T(8,128)(2,1)} %bitcast.3, bf16[1,64,2048]{2,1,0:T(8,128)(2,1)S(1)} %fusion.30), kind=kLoop, calls=%fused_computation.24 | loop fusion | flops 1572864 | bytes 2097152 | tf_op jit(solution)/shard_map/stack | solution.py:96
  27.2 1.8 gather_fusion
  29.3 3.8 %fusion.16 = f32[256,4,256]{2,0,1:T(8,128)S(1)} fusion(bf16[4,2048,256]{2,1,0:T(8,128)(2,1)} %param.17, bf16[256,2048]{1,0:T(8,128)(2,1)S(1)} %bitcast_select_fusion), kind=kOutput, calls=%fused_computation.30 | convolution fusion | flops 1073741824 | bytes 6291456 | tf_op jit(solution)/shard_map/nd,edc->nec/dot_general | solution.py:208
  34.4 2.1 %copy.179 = f32[256,2,2,64]{3,0,1,2:T(8,128)} copy(f32[256,2,2,64]{0,3,2,1:T(8,128)} %get-tuple-element.45) | data formatting | bytes 524288
  37.5 1.4 subtract_convert_fusion
  40.5 1.6 collective-permute-start.3
  46.5 1.4 fusion.123
  47.9 1.5 collective-permute-done.6
  51.0 1.6 collective-permute-start.4
  52.8 3.8 %collective-permute-done.7 = bf16[256,2,2,128]{3,0,1,2:T(8,128)(2,1)S(1)} collective-permute-done((bf16[256,2,2,128]{3,0,1,2:T(8,128)(2,1)}, bf16[256,2,2,128]{3,0,1,2:T(8,128)(2,1)S(1)}, u32[]{:S(2)}, u32[]{:S(2)}) %collective-permute-start.7) | collective-permute-done | bytes 262176 | tf_op jit(solution)/shard_map/ppermute | solution.py:121
  57.9 1.9 collective-permute-start.5
  60.8 3.9 %collective-permute-done.8 = bf16[256,2,2,128]{3,0,1,2:T(8,128)(2,1)S(1)} collective-permute-done((bf16[256,2,2,128]{3,0,1,2:T(8,128)(2,1)S(1)}, bf16[256,2,2,128]{3,0,1,2:T(8,128)(2,1)S(1)}, u32[]{:S(2)}, u32[]{:S(2)}) %collective-permute-start.8) | collective-permute-done | bytes 262176 | tf_op jit(solution)/shard_map/ppermute | solution.py:121
  64.8 6.3 %collective-permute-done.9 = bf16[256,2,2,128]{3,0,1,2:T(8,128)(2,1)S(1)} collective-permute-done((bf16[256,2,2,128]{3,0,1,2:T(8,128)(2,1)S(1)}, bf16[256,2,2,128]{3,0,1,2:T(8,128)(2,1)S(1)}, u32[]{:S(2)}, u32[]{:S(2)}) %collective-permute-start.9) | collective-permute-done | bytes 262176 | tf_op jit(solution)/shard_map/ppermute | solution.py:121
  72.2 2.2 %copy.145 = bf16[8,256,2,2,128]{4,3,2,1,0:T(2,128)(2,1)S(1)} copy(bf16[8,256,2,2,128]{4,1,2,3,0:T(8,128)(2,1)S(1)} %bitcast_dynamic-update-slice_fusion) | data formatting | bytes 4194304 | tf_op jit(solution)/shard_map/optimization_barrier | solution.py:251
  74.4 2.7 %reshape.458.q_ref = bf16[8,512,256]{2,1,0:T(8,128)(2,1)} reshape(bf16[8,256,2,2,128]{4,3,2,1,0:T(2,128)(2,1)S(1)} %copy.145) | data formatting | bytes 4194304 | tf_op jit(solution)/shard_map/reshape | solution.py:258
  77.1 17.1 %shard_map.127 = (f32[16,2,1,512]{3,2,1,0:T(1,128)}, f32[16,2,1,512]{3,2,1,0:T(1,128)}, f32[16,2,128,512]{3,2,1,0:T(8,128)}) custom-call(s32[16]{0:T(128)} %get-tuple-element.59.offset_ref, s32[16]{0:T(128)} %get-tuple-element.60.valid_ref, bf16[8,512,256]{2,1,0:T(8,128)(2,1)} %reshape.458.q_ref, bf16[16,128,256]{2,1,0:T(8,128)(2,1)} %get-tuple-element.37.k_ref, ...), custom_call_target="tpu_custom_call" | custom-call | tf_op jit(solution)/shard_map/pallas_call | solution.py:170
  98.4 4.5 %broadcast_multiply_fusion = f32[16,2,128,512]{3,2,1,0:T(8,128)S(1)} fusion(f32[16,2,128,512]{3,2,1,0:T(8,128)} %get-tuple-element.13, f32[16,2,512]{2,1,0:T(2,128)S(1)} %bitcast.215), kind=kLoop, calls=%fused_computation.9 | loop fusion | flops 2097152 | bytes 16842752 | tf_op jit(solution)/shard_map/mul | solution.py:277
  103.0 6.3 %fusion.7 = bf16[8,2,128,512]{3,0,2,1:T(8,128)(2,1)S(1)} fusion(f32[16,2,128,512]{3,2,1,0:T(8,128)S(1)} %broadcast_multiply_fusion, s32[16]{0:T(128)S(1)} %copy-done.14), kind=kOutput, calls=%fused_computation.20 | convolution fusion | flops 202375296 | bytes 10485824 | tf_op jit(solution)/shard_map/rb,bhcq->rhcq/dot_general | solution.py:274
  109.9 1.5 pad_maximum_fusion
  111.4 5.1 %all-to-all-start = ((bf16[8,264,512]{2,1,0:T(8,128)(2,1)}), bf16[8,264,512]{2,1,0:T(8,128)(2,1)S(1)}, u32[]{:S(2)}, u32[]{:S(2)}) async-start(bf16[8,264,512]{2,1,0:T(8,128)(2,1)} %pad_maximum_fusion), calls=%async_computation | async-start | bytes 4325376 | tf_op jit(solution)/shard_map/all_to_all | solution.py:289
  117.0 44.0 %all-to-all-done = bf16[8,264,512]{2,1,0:T(8,128)(2,1)S(1)} async-done(((bf16[8,264,512]{2,1,0:T(8,128)(2,1)}), bf16[8,264,512]{2,1,0:T(8,128)(2,1)S(1)}, u32[]{:S(2)}, u32[]{:S(2)}) %all-to-all-start) | async-done | bytes 2162720 | tf_op jit(solution)/shard_map/all_to_all | solution.py:289
  163.3 1.7 convolution_multiply_fusion.3
  165.0 1.9 fusion.5
  170.8 4.8 %collective-permute-done.12 = bf16[64,2048]{1,0:T(8,128)(2,1)} collective-permute-done((bf16[64,2048]{1,0:T(8,128)(2,1)}, bf16[64,2048]{1,0:T(8,128)(2,1)}, u32[]{:S(2)}, u32[]{:S(2)}) %collective-permute-start.12) | collective-permute-done | bytes 262176 | tf_op jit(solution)/shard_map/ppermute | solution.py:107
  175.6 7.8 %collective-permute-done.11 = bf16[64,2048]{1,0:T(8,128)(2,1)} collective-permute-done((bf16[64,2048]{1,0:T(8,128)(2,1)}, bf16[64,2048]{1,0:T(8,128)(2,1)}, u32[]{:S(2)}, u32[]{:S(2)}) %collective-permute-start.11) | collective-permute-done | bytes 262176 | tf_op jit(solution)/shard_map/ppermute | solution.py:107
  183.7 1.9 %fusion.37 = bf16[1,64,2048]{2,1,0:T(8,128)(2,1)} fusion(bf16[64,2048]{1,0:T(8,128)(2,1)} %collective-permute-done.12, bf16[64,2048]{1,0:T(8,128)(2,1)} %collective-permute-done.11, bf16[64,2048]{1,0:T(8,128)(2,1)} %collective-permute-done.10, bf16[256,2048]{1,0:T(8,128)(2,1)S(1)} %fusion.6, s32[]{:T(128)S(6)} %select_n.186), kind=kLoop, calls=%fused_computation.60 | loop fusion | flops 1048576 | bytes 1310724 | tf_op jit(solution)/shard_map/convert_element_type | solution.py:330
  (136 shorter events, 39.3 us)
Async XLA Ops:
  0.0 42.5 %copy-start = (bf16[2,2048,256]{2,1,0:T(8,128)(2,1)S(1)}, bf16[2,2048,256]{2,1,0:T(8,128)(2,1)}, u32[]{:S(2)}) copy-start(bf16[2,2048,256]{2,1,0:T(8,128)(2,1)} %param.18) | copy-start | bytes 6291460
  0.0 17.0 %copy-start.9 = (s32[1,256,2]{1,2,0:T(2,128)S(1)}, s32[1,256,2]{1,2,0:T(2,128)}, u32[]{:S(2)}) copy-start(s32[1,256,2]{1,2,0:T(2,128)} %param.16) | copy-start | bytes 6148
  3.8 21.2 %collective-permute-start.2 = (bf16[64,2048]{1,0:T(8,128)(2,1)}, bf16[64,2048]{1,0:T(8,128)(2,1)}, u32[]{:S(2)}, u32[]{:S(2)}) collective-permute-start(bf16[64,2048]{1,0:T(8,128)(2,1)} %fusion.28), channel_id=1, source_target_pairs={{0,8},{8,16},{16,24},{24,0},{1,9},{9,17},{17,25},{25,1},{2,10},{10... | collective-permute-start | bytes 786440 | tf_op jit(solution)/shard_map/ppermute | solution.py:93
  4.2 20.8 %collective-permute-start.1 = (bf16[64,2048]{1,0:T(8,128)(2,1)}, bf16[64,2048]{1,0:T(8,128)(2,1)}, u32[]{:S(2)}, u32[]{:S(2)}) collective-permute-start(bf16[64,2048]{1,0:T(8,128)(2,1)} %fusion.28), channel_id=1, source_target_pairs={{0,16},{8,24},{16,0},{24,8},{1,17},{9,25},{17,1},{25,9},{2,18},{10... | collective-permute-start | bytes 786440 | tf_op jit(solution)/shard_map/ppermute | solution.py:93
  6.8 18.2 %collective-permute-start = (bf16[64,2048]{1,0:T(8,128)(2,1)}, bf16[64,2048]{1,0:T(8,128)(2,1)}, u32[]{:S(2)}, u32[]{:S(2)}) collective-permute-start(bf16[64,2048]{1,0:T(8,128)(2,1)} %fusion.28), channel_id=1, source_target_pairs={{0,24},{8,0},{16,8},{24,16},{1,25},{9,1},{17,9},{25,17},{2,26},{10... | collective-permute-start | bytes 786440 | tf_op jit(solution)/shard_map/ppermute | solution.py:93
  11.8 5.2 %copy-start.11 = (s32[1024]{0:T(1024)}, s32[1024]{0:T(1024)S(1)}, u32[]{:S(2)}) copy-start(s32[1024]{0:T(1024)S(1)} %pad_clamp_fusion) | copy-start | bytes 12292
  16.4 4.0 %copy-start.13 = (s32[16]{0:T(128)}, s32[16]{0:T(128)S(1)}, u32[]{:S(2)}) copy-start(s32[16]{0:T(128)S(1)} %broadcast_add_fusion) | copy-start | bytes 196
  29.3 3.8 %copy-start.2 = (bf16[256,2048]{1,0:T(8,128)(2,1)}, bf16[256,2048]{1,0:T(8,128)(2,1)S(1)}, u32[]{:S(2)}) copy-start(bf16[256,2048]{1,0:T(8,128)(2,1)S(1)} %bitcast_select_fusion) | copy-start | bytes 3145732
  34.4 8.1 %copy-start.3 = (bf16[256,2048]{1,0:T(8,128)(2,1)S(1)}, bf16[256,2048]{1,0:T(8,128)(2,1)}, u32[]{:S(2)}) copy-start(bf16[256,2048]{1,0:T(8,128)(2,1)} %copy-done.2) | copy-start | bytes 3145732
  38.9 0.7 copy-start.5
  40.5 10.5 %collective-permute-start.3 = (bf16[256,2,2,128]{3,0,1,2:T(8,128)(2,1)}, bf16[256,2,2,128]{3,0,1,2:T(8,128)(2,1)}, u32[]{:S(2)}, u32[]{:S(2)}) collective-permute-start(bf16[256,2,2,128]{3,0,1,2:T(8,128)(2,1)} %pad_maximum_fusion.2), channel_id=1, source_target_pairs={{1,0},{3,1},{5,3},{7,5},{6,7},{4,6},{2,4},{0,2},{9,8},{11,9},{13,1... | collective-permute-start | bytes 786440 | tf_op jit(solution)/shard_map/ppermute | solution.py:125
  42.1 7.3 %collective-permute-start.6 = (bf16[256,2,2,128]{3,0,1,2:T(8,128)(2,1)}, bf16[256,2,2,128]{3,0,1,2:T(8,128)(2,1)}, u32[]{:S(2)}, u32[]{:S(2)}) collective-permute-start(bf16[256,2,2,128]{3,0,1,2:T(8,128)(2,1)} %pad_maximum_fusion.2), channel_id=1, source_target_pairs={{0,1},{1,3},{3,5},{5,7},{7,6},{6,4},{4,2},{2,0},{8,9},{9,11},{11,1... | collective-permute-start | bytes 786440 | tf_op jit(solution)/shard_map/ppermute | solution.py:121
  43.5 0.8 copy-start.8
  46.5 10.2 %copy-start.6 = (bf16[256,2,2,64]{3,0,1,2:T(8,128)(2,1)S(1)}, bf16[256,2,2,64]{3,0,1,2:T(8,128)(2,1)}, u32[]{:S(2)}) copy-start(bf16[256,2,2,64]{3,0,1,2:T(8,128)(2,1)} %copy-done.5) | copy-start | bytes 393220
  49.4 7.2 %collective-permute-start.7 = (bf16[256,2,2,128]{3,0,1,2:T(8,128)(2,1)}, bf16[256,2,2,128]{3,0,1,2:T(8,128)(2,1)S(1)}, u32[]{:S(2)}, u32[]{:S(2)}) collective-permute-start(bf16[256,2,2,128]{3,0,1,2:T(8,128)(2,1)} %collective-permute-done.6), channel_id=1, source_target_pairs={{0,1},{1,3},{3,5},{5,7},{7,6},{6,4},{4,2},{2,0},{8,9},{9,11},{11,1... | collective-permute-start | bytes 786440 | tf_op jit(solution)/shard_map/ppermute | solution.py:121
  51.0 6.9 %collective-permute-start.4 = (bf16[256,2,2,128]{3,0,1,2:T(8,128)(2,1)}, bf16[256,2,2,128]{3,0,1,2:T(8,128)(2,1)S(1)}, u32[]{:S(2)}, u32[]{:S(2)}) collective-permute-start(bf16[256,2,2,128]{3,0,1,2:T(8,128)(2,1)} %collective-permute-done.3), channel_id=1, source_target_pairs={{1,0},{3,1},{5,3},{7,5},{6,7},{4,6},{2,4},{0,2},{9,8},{11,9},{13,1... | collective-permute-start | bytes 786440 | tf_op jit(solution)/shard_map/ppermute | solution.py:125
  56.6 8.1 %collective-permute-start.8 = (bf16[256,2,2,128]{3,0,1,2:T(8,128)(2,1)S(1)}, bf16[256,2,2,128]{3,0,1,2:T(8,128)(2,1)S(1)}, u32[]{:S(2)}, u32[]{:S(2)}) collective-permute-start(bf16[256,2,2,128]{3,0,1,2:T(8,128)(2,1)S(1)} %collective-permute-done.7), channel_id=1, source_target_pairs={{0,1},{1,3},{3,5},{5,7},{7,6},{6,4},{4,2},{2,0},{8,9},{9,11},{11,1... | collective-permute-start | bytes 786440 | tf_op jit(solution)/shard_map/ppermute | solution.py:121
  57.9 6.8 %collective-permute-start.5 = (bf16[256,2,2,128]{3,0,1,2:T(8,128)(2,1)S(1)}, bf16[256,2,2,128]{3,0,1,2:T(8,128)(2,1)S(1)}, u32[]{:S(2)}, u32[]{:S(2)}) collective-permute-start(bf16[256,2,2,128]{3,0,1,2:T(8,128)(2,1)S(1)} %collective-permute-done.4), channel_id=1, source_target_pairs={{1,0},{3,1},{5,3},{7,5},{6,7},{4,6},{2,4},{0,2},{9,8},{11,9},{13,1... | collective-permute-start | bytes 786440 | tf_op jit(solution)/shard_map/ppermute | solution.py:125
  64.7 6.4 %collective-permute-start.9 = (bf16[256,2,2,128]{3,0,1,2:T(8,128)(2,1)S(1)}, bf16[256,2,2,128]{3,0,1,2:T(8,128)(2,1)S(1)}, u32[]{:S(2)}, u32[]{:S(2)}) collective-permute-start(bf16[256,2,2,128]{3,0,1,2:T(8,128)(2,1)S(1)} %collective-permute-done.8), channel_id=1, source_target_pairs={{0,1},{1,3},{3,5},{5,7},{7,6},{6,4},{4,2},{2,0},{8,9},{9,11},{11,1... | collective-permute-start | bytes 786440 | tf_op jit(solution)/shard_map/ppermute | solution.py:121
  77.1 18.0 %copy-start.15 = (pred[8,16]{1,0:T(8,128)(4,1)S(1)}, pred[8,16]{1,0:T(8,128)(4,1)}, u32[]{:S(2)}) copy-start(pred[8,16]{1,0:T(8,128)(4,1)} %iota_compare_fusion.2) | copy-start | bytes 388
  77.1 19.1 %copy-start.12 = (pred[16]{0:T(512)(128)(4,1)S(1)}, pred[16]{0:T(512)(128)(4,1)}, u32[]{:S(2)}) copy-start(pred[16]{0:T(512)(128)(4,1)} %compare_and_fusion) | copy-start | bytes 52
  77.1 21.1 %copy-start.14 = (s32[16]{0:T(128)S(1)}, s32[16]{0:T(128)}, u32[]{:S(2)}) copy-start(s32[16]{0:T(128)} %copy-done.13) | copy-start | bytes 196
  111.4 5.2 %copy-start.10 = (bf16[2048,4]{0,1:T(4,128)(2,1)S(1)}, bf16[2048,4]{0,1:T(4,128)(2,1)}, u32[]{:S(2)}) copy-start(bf16[2048,4]{0,1:T(4,128)(2,1)} %param.15) | copy-start | bytes 49156
  111.4 49.6 %all-to-all-start = ((bf16[8,264,512]{2,1,0:T(8,128)(2,1)}), bf16[8,264,512]{2,1,0:T(8,128)(2,1)S(1)}, u32[]{:S(2)}, u32[]{:S(2)}) async-start(bf16[8,264,512]{2,1,0:T(8,128)(2,1)} %pad_maximum_fusion), calls=%async_computation | async-start | bytes 4325376 | tf_op jit(solution)/shard_map/all_to_all | solution.py:289
  161.6 1.0 copy-start.7
  165.0 2.5 %copy-start.4 = (bf16[4,256,2048]{2,1,0:T(8,128)(2,1)S(1)}, bf16[4,256,2048]{2,1,0:T(8,128)(2,1)}, u32[]{:S(2)}) copy-start(bf16[4,256,2048]{2,1,0:T(8,128)(2,1)} %param.19) | copy-start | bytes 12582916
  168.0 17.6 %copy-start.1 = (bf16[2,2048,256]{2,1,0:T(8,128)(2,1)S(1)}, bf16[2,2048,256]{2,1,0:T(8,128)(2,1)}, u32[]{:S(2)}) copy-start(bf16[2,2048,256]{2,1,0:T(8,128)(2,1)} %param.18) | copy-start | bytes 6291460
  169.3 6.3 %collective-permute-start.12 = (bf16[64,2048]{1,0:T(8,128)(2,1)}, bf16[64,2048]{1,0:T(8,128)(2,1)}, u32[]{:S(2)}, u32[]{:S(2)}) collective-permute-start(bf16[64,2048]{1,0:T(8,128)(2,1)} %get-tuple-element.41), channel_id=1, source_target_pairs={{0,24},{8,0},{16,8},{24,16},{1,25},{9,1},{17,9},{25,17},{2,26},{10... | collective-permute-start | bytes 786440 | tf_op jit(solution)/shard_map/ppermute | solution.py:107
  169.3 14.0 %collective-permute-start.11 = (bf16[64,2048]{1,0:T(8,128)(2,1)}, bf16[64,2048]{1,0:T(8,128)(2,1)}, u32[]{:S(2)}, u32[]{:S(2)}) collective-permute-start(bf16[64,2048]{1,0:T(8,128)(2,1)} %get-tuple-element.42), channel_id=1, source_target_pairs={{0,16},{8,24},{16,0},{24,8},{1,17},{9,25},{17,1},{25,9},{2,18},{10... | collective-permute-start | bytes 786440 | tf_op jit(solution)/shard_map/ppermute | solution.py:107
  170.6 13.1 %collective-permute-start.10 = (bf16[64,2048]{1,0:T(8,128)(2,1)S(1)}, bf16[64,2048]{1,0:T(8,128)(2,1)}, u32[]{:S(2)}, u32[]{:S(2)}) collective-permute-start(bf16[64,2048]{1,0:T(8,128)(2,1)S(1)} %get-tuple-element.40), channel_id=1, source_target_pairs={{0,8},{8,16},{16,24},{24,0},{1,9},{9,17},{17,25},{25,1},{2,10},{10... | collective-permute-start | bytes 786440 | tf_op jit(solution)/shard_map/ppermute | solution.py:107

commit v7 on v6

--- a/solution.py
+++ b/solution.py
@@ -127,14 +127,22 @@
     return jnp.stack([piece] + from_ahead + from_behind[::-1], axis=0)
 
 
-def block_attention(ring_queries, keys, values_t, owner_offset, valid):
+def block_attention(ring_queries, keys, values_t, owner_offset, owner, valid, requests):
     blocks, block_size, width = keys.shape
     query_rows = ring_queries.shape[1]
     heads = width // HD
     scale = HD ** (-0.5)
 
-    def kernel(offset_ref, valid_ref, q_ref, k_ref, v_ref, best_ref, total_ref, accum_ref):
+    def kernel(offset_ref, owner_ref, valid_ref, q_ref, k_ref, v_ref, best_ref, total_ref, accum_ref):
         b = pl.program_id(0)
+
+        @pl.when(b == 0)
+        def _():
+            best_ref[...] = jnp.full(best_ref.shape, NEG_FILL, jnp.float32)
+            total_ref[...] = jnp.zeros(total_ref.shape, jnp.float32)
+            accum_ref[...] = jnp.zeros(accum_ref.shape, jnp.float32)
+
+        request = owner_ref[b]
         limit = valid_ref[b]
         row = lax.broadcasted_iota(jnp.int32, (block_size, query_rows), 0)
         for h in range(heads):
@@ -144,38 +152,47 @@
                 k, q, (((1,), (1,)), ((), ())), preferred_element_type=jnp.float32
             ) * scale
             scores = jnp.where(row < limit, scores, NEG_FILL)
-            best = jnp.max(scores, axis=0, keepdims=True)
-            weights = jnp.exp(scores - best)
-            best_ref[0, h] = best
-            total_ref[0, h] = jnp.sum(weights, axis=0, keepdims=True)
+            old_best = best_ref[request, h]
+            new_best = jnp.maximum(old_best, jnp.max(scores, axis=0, keepdims=True))
+            rescale = jnp.exp(old_best - new_best)
+            weights = jnp.exp(scores - new_best)
+            best_ref[request, h] = new_best
+            total_ref[request, h] = total_ref[request, h] * rescale + jnp.sum(
+                weights, axis=0, keepdims=True
+            )
             v_t = v_ref[0, h * HD:(h + 1) * HD, :]
-            accum_ref[0, h] = jnp.dot(
+            accum_ref[request, h] = accum_ref[request, h] * rescale + jnp.dot(
                 v_t, weights.astype(jnp.bfloat16), preferred_element_type=jnp.float32
             )
 
     grid_spec = pltpu.PrefetchScalarGridSpec(
-        num_scalar_prefetch=2,
+        num_scalar_prefetch=3,
         grid=(blocks,),
         in_specs=[
-            pl.BlockSpec((1, query_rows, width), lambda b, off, val: (off[b], 0, 0)),
-            pl.BlockSpec((1, block_size, width), lambda b, off, val: (b, 0, 0)),
-            pl.BlockSpec((1, width, block_size), lambda b, off, val: (b, 0, 0)),
+            pl.BlockSpec((1, query_rows, width), lambda b, off, own, val: (off[b], 0, 0)),
+            pl.BlockSpec((1, block_size, width), lambda b, off, own, val: (b, 0, 0)),
+            pl.BlockSpec((1, width, block_size), lambda b, off, own, val: (b, 0, 0)),
         ],
         out_specs=[
-            pl.BlockSpec((1, heads, 1, query_rows), lambda b, off, val: (b, 0, 0, 0)),
-            pl.BlockSpec((1, heads, 1, query_rows), lambda b, off, val: (b, 0, 0, 0)),
-            pl.BlockSpec((1, heads, HD, query_rows), lambda b, off, val: (b, 0, 0, 0)),
-        ],
-    )
+            pl.BlockSpec((requests, heads, 1, query_rows), lambda b, off, own, val: (0, 0, 0, 0)),
+            pl.BlockSpec((requests, heads, 1, query_rows), lambda b, off, own, val: (0, 0, 0, 0)),
+            pl.BlockSpec((requests, heads, HD, query_rows), lambda b, off, own, val: (0, 0, 0, 0)),
+        ],
+    )
+    resident = 2 * requests * heads * (HD + 16) * query_rows * 4
     return pl.pallas_call(
         kernel,
         grid_spec=grid_spec,
         out_shape=[
-            jax.ShapeDtypeStruct((blocks, heads, 1, query_rows), jnp.float32),
-            jax.ShapeDtypeStruct((blocks, heads, 1, query_rows), jnp.float32),
-            jax.ShapeDtypeStruct((blocks, heads, HD, query_rows), jnp.float32),
-        ],
-    )(owner_offset, valid, ring_queries, keys, values_t)
+            jax.ShapeDtypeStruct((requests, heads, 1, query_rows), jnp.float32),
+            jax.ShapeDtypeStruct((requests, heads, 1, query_rows), jnp.float32),
+            jax.ShapeDtypeStruct((requests, heads, HD, query_rows), jnp.float32),
+        ],
+        compiler_params=pltpu.CompilerParams(
+            dimension_semantics=("arbitrary",),
+            vmem_limit_bytes=resident + 24 * 1024 * 1024,
+        ),
+    )(owner_offset, owner, valid, ring_queries, keys, values_t)
 
 
 def per_device(
@@ -213,7 +230,9 @@
     fresh = jnp.einsum("nd,sdc->snc", gathered, kv_weight, preferred_element_type=jnp.float32)
     new_keys = rotate(fresh[0].reshape(new_count, local_heads, HD), positions).astype(jnp.bfloat16)
     new_values = fresh[1].reshape(new_count, local_heads, HD).astype(jnp.bfloat16)
-    ring_queries = ring_all_gather(queries, "seq", cycle)
+    ring_queries = ring_all_gather(
+        queries.reshape(new_count * 2, local_heads * HD), "seq", cycle
+    )
     request_count = ring_queries.shape[0]
     ring_size = len(cycle)
     position_of = np.argsort(np.asarray(cycle))
@@ -254,29 +273,22 @@
     owner_offset = (jnp.asarray(position_of, dtype=jnp.int32)[owner] - position) % ring_size
     valid = jnp.clip(cached_len[owner] - ordinal * block_size, 0, block_size).astype(jnp.int32)
     query_rows = new_count * 2
-    block_best, block_totals, block_accum = block_attention(
-        ring_queries.reshape(request_count, query_rows, local_heads * HD),
+    request_best, totals, accum = block_attention(
+        ring_queries,
         kv_cache[0],
         jnp.swapaxes(kv_cache[1], 1, 2),
         owner_offset,
+        owner,
         valid,
-    )
-    block_best = block_best[:, :, 0]
-    block_totals = block_totals[:, :, 0]
-    request_best = jnp.max(jnp.where(owns[:, :, None, None], block_best[None], NEG_FILL), axis=1)
+        request_count,
+    )
+    request_best = request_best[:, :, 0]
     best_hi, best_lo = split_bf16(request_best)
     request_ref = best_hi + best_lo
-    factor = jnp.exp(block_best - jnp.take(request_ref, owner, axis=0))
-    owns_f = owns.astype(jnp.float32)
-    totals = jnp.einsum(
-        "rb,bhq->rhq", owns_f, block_totals * factor, precision=lax.Precision.HIGHEST
-    )
-    accum = jnp.einsum(
-        "rb,bhcq->rhcq",
-        owns_f,
-        block_accum * factor[:, :, None, :],
-        precision=lax.Precision.HIGHEST,
-    )
+    present = request_best > 0.5 * NEG_FILL
+    adjust = jnp.exp(jnp.where(present, request_best - request_ref, 0.0))
+    totals = totals[:, :, 0] * adjust
+    accum = accum * adjust[:, :, None, :]
     totals_hi, totals_lo = split_bf16(totals)
     stats = jnp.stack([best_hi, best_lo, totals_hi, totals_lo], axis=1).astype(jnp.bfloat16)
     payload = jnp.concatenate(

time: 187 us -> 179 us (0.957)
  matrix products: 18.6 us -> 12 us
  local copies, waits for them, and re-layouts: 29.5 us -> 35.9 us
  waiting for transfers between devices: 73.4 us -> 67.3 us
  Pallas kernels: 17.1 us -> 11.8 us
  starting transfers between devices: 17.1 us -> 21.1 us
    ppermute x4, waiting for transfers between devices: 15.5 us -> 5.85 us  [ring_all_gather(): moving = lax.ppermute(moving, axis_name, forward)]
    dot_general x2 -> x0, matrix products: 6.4 us -> none  [the longest x1 6.25 us: per_device(): jnp.einsum('rb,bhcq->rhcq', owns_f, block_accum * factor[:, :, None, :],...]
    mul x2 -> x0, other arithmetic: 5.53 us -> none  [the longest x1 4.51 us: per_device(): block_accum * factor[:, :, None, :]]
    pallas_call x1, Pallas kernels: 17.1 us -> 11.8 us  [block_attention(): pl.pallas_call(kernel, grid_spec=grid_spec, out_shape=[jax.ShapeDtypeStru...]
    unnamed x45 -> x44, local copies, waits for them, and re-layouts: 8.99 us -> 13.3 us
    ppermute x4, starting transfers between devices: 1.08 us -> 4.97 us  [ring_all_gather(): moving = lax.ppermute(moving, axis_name, forward)]
    reshape x2 -> x0, local copies, waits for them, and re-layouts: 3.36 us -> none  [the longest x1 2.69 us: per_device(): ring_queries.reshape(request_count, query_rows, local_heads * HD)]
    reduce_sum x1, other arithmetic: 0.43 us -> 2.87 us  [per_device(): jnp.sum(part_accum * share[:, :, None, :], axis=0)]
  transfers between devices with their start and end apart: 14 -> 14, of which waited for: 9 -> 8; matrix products, arithmetic and copies ran while one was open for 13% -> 17% of each run, Pallas kernels for 0% -> 0%
where the time goes in v7:
time: 179 us; the launch traced here: 178 us
  waiting for transfers between devices  67.3 us (38%)
  local copies, waits for them, and re-layouts  35.9 us (20%)
  other arithmetic  29.1 us (16%)
  starting transfers between devices  21.1 us (12%)
  matrix products  12 us (7%)
  Pallas kernels  11.8 us (7%)
    all_to_all x1, waiting for transfers between devices, per_device(): received = lax.all_to_all(payload, 'seq', 0, 0, tiled=True)  45.5 us
    unnamed x44, local copies, waits for them, and re-layouts  13.3 us
    ppermute x3, waiting for transfers between devices, shift_reduce_scatter(): lax.ppermute(piece, axis_name, [(i, (i + s) % size) for i in range(size)])  12.8 us
    pallas_call x1, Pallas kernels, block_attention(): pl.pallas_call(kernel, grid_spec=grid_spec, out_shape=[jax.ShapeDtypeStru...  11.8 us
    all_to_all x1, starting transfers between devices, per_device(): received = lax.all_to_all(payload, 'seq', 0, 0, tiled=True)  5.9 us
    ppermute x4, waiting for transfers between devices, ring_all_gather(): moving = lax.ppermute(moving, axis_name, forward)  5.85 us
    ppermute x4, starting transfers between devices, ring_all_gather(): moving = lax.ppermute(moving, axis_name, forward)  4.97 us
    dot_general x4, matrix products, per_device(): jnp.dot(picked, o_weight[expert], preferred_element_type=jnp.float32)  4.49 us
  transfers between devices with their start and end apart: 14, of which 8 were waited for; matrix products, arithmetic and copies ran while one was open for 17% of the time, Pallas kernels for 0%

profile of v7, /device:TPU:0, one launch (start us, length us, event | category | flops | bytes accessed | tf_op | source)
XLA Modules:
  0.0 177.8 jit_solution(84210913617675226)
XLA Ops:
  2.0 1.8 %fusion.23 = bf16[64,2048]{1,0:T(8,128)(2,1)} fusion(bf16[1,64,2048]{2,1,0:T(8,128)(2,1)} %param.13, f32[2048]{0:T(1024)S(1)} %convert_element_type.101, f32[64]{0:T(128)S(1)} %add_rsqrt_fusion), kind=kLoop, calls=%fused_computation.43 | loop fusion | flops 524288 | bytes 532736 | tf_op jit(solution)/shard_map/convert_element_type | solution.py:38
  4.2 2.5 %collective-permute-start.1 = (bf16[64,2048]{1,0:T(8,128)(2,1)}, bf16[64,2048]{1,0:T(8,128)(2,1)}, u32[]{:S(2)}, u32[]{:S(2)}) collective-permute-start(bf16[64,2048]{1,0:T(8,128)(2,1)} %fusion.23), channel_id=1, source_target_pairs={{0,16},{8,24},{16,0},{24,8},{1,17},{9,25},{17,1},{25,9},{2,18},{10... | collective-permute-start | bytes 786440 | tf_op jit(solution)/shard_map/ppermute | solution.py:93
  8.2 1.8 %fusion.25 = bf16[1,64,2048]{2,1,0:T(8,128)(2,1)} fusion(bf16[1,64,2048]{2,1,0:T(8,128)(2,1)} %param.13, f32[2048]{0:T(1024)S(1)} %convert_element_type.101, f32[64]{0:T(128)S(1)} %add_rsqrt_fusion), kind=kLoop, calls=%fused_computation.45 | loop fusion | flops 524288 | bytes 532736 | tf_op jit(solution)/shard_map/convert_element_type | solution.py:38
  18.3 3.1 %fusion.111 = (bf16[1,16,128,256]{3,2,1,0:T(8,128)(2,1)}, bf16[16,128,256]{2,1,0:T(8,128)(2,1)}) fusion(bf16[2,16,128,256]{3,2,1,0:T(8,128)(2,1)} %param.20), kind=kLoop, calls=%fused_computation.209 | loop fusion | bytes 4194304 | tf_op jit(solution)/shard_map/slice | solution.py:279
  22.1 1.6 copy.146
  24.3 2.4 %pad_maximum_fusion.1 = bf16[4,64,2048]{2,1,0:T(8,128)(2,1)} fusion(bf16[1,64,2048]{2,1,0:T(8,128)(2,1)} %bitcast.5, bf16[1,64,2048]{2,1,0:T(8,128)(2,1)} %bitcast.4, bf16[1,64,2048]{2,1,0:T(8,128)(2,1)} %bitcast.3, bf16[1,64,2048]{2,1,0:T(8,128)(2,1)} %fusion.25), kind=kLoop, calls=%fused_computation.20 | loop fusion | flops 1572864 | bytes 2097152 | tf_op jit(solution)/shard_map/stack | solution.py:96
  26.7 2.8 %gather_fusion = bf16[4,64,2048]{2,1,0:T(8,128)(2,1)} fusion(bf16[4,64,2048]{2,1,0:T(8,128)(2,1)} %pad_maximum_fusion.1, s32[1024]{0:T(1024)S(1)} %pad_clamp_fusion.1), kind=kCustom, calls=%fused_computation | custom fusion | bytes 2097168 | tf_op jit(solution)/shard_map/jit(_take)/gather | solution.py:97
  30.9 3.8 %fusion.11 = f32[256,4,256]{2,0,1:T(8,128)S(1)} fusion(bf16[4,2048,256]{2,1,0:T(8,128)(2,1)} %param.17, bf16[256,2048]{1,0:T(8,128)(2,1)S(1)} %bitcast_select_fusion), kind=kOutput, calls=%fused_computation.26 | convolution fusion | flops 1073741824 | bytes 6291456 | tf_op jit(solution)/shard_map/nd,edc->nec/dot_general | solution.py:225
  35.9 2.1 %copy.110 = f32[256,2,256]{0,2,1:T(8,128)} copy(f32[256,2,256]{2,0,1:T(8,128)} %multiply_reduce_fusion) | data formatting | bytes 1048576 | tf_op jit(solution)/shard_map/reduce_sum | solution.py:226
  38.0 1.9 %fusion.112 = (f32[256,2,2,64]{0,3,2,1:T(8,128)}, f32[256,2,2,64]{0,3,2,1:T(8,128)}) fusion(f32[256,2,2,128]{0,3,2,1:T(8,128)} %bitcast.212), kind=kLoop, calls=%fused_computation.210 | loop fusion | bytes 1048576 | tf_op jit(solution)/shard_map/slice | solution.py:25
  39.8 2.0 %copy.143 = f32[256,2,2,64]{3,0,1,2:T(8,128)} copy(f32[256,2,2,64]{0,3,2,1:T(8,128)} %get-tuple-element.47) | data formatting | bytes 524288
  41.8 2.0 %copy.142 = f32[256,2,2,64]{3,0,1,2:T(8,128)} copy(f32[256,2,2,64]{0,3,2,1:T(8,128)} %get-tuple-element.48) | data formatting | bytes 524288
  43.8 1.4 multiply_subtract_fusion
  47.1 1.6 collective-permute-start.3
  51.1 1.7 copy.145
  52.8 1.7 copy.144
  57.9 1.5 collective-permute-start.7
  65.0 1.5 collective-permute-start.8
  66.5 2.0 %collective-permute-done.4 = bf16[512,256]{1,0:T(8,128)(2,1)S(1)} collective-permute-done((bf16[512,256]{1,0:T(8,128)(2,1)}, bf16[512,256]{1,0:T(8,128)(2,1)S(1)}, u32[]{:S(2)}, u32[]{:S(2)}) %collective-permute-start.4) | collective-permute-done | bytes 262176 | tf_op jit(solution)/shard_map/ppermute | solution.py:125
  72.2 1.5 collective-permute-start.9
  74.9 3.7 %collective-permute-done.9 = bf16[512,256]{1,0:T(8,128)(2,1)S(1)} collective-permute-done((bf16[512,256]{1,0:T(8,128)(2,1)S(1)}, bf16[512,256]{1,0:T(8,128)(2,1)S(1)}, u32[]{:S(2)}, u32[]{:S(2)}) %collective-permute-start.9) | collective-permute-done | bytes 262176 | tf_op jit(solution)/shard_map/ppermute | solution.py:121
  80.5 11.8 %shard_map.127 = (f32[8,2,1,512]{3,2,1,0:T(1,128)S(1)}, f32[8,2,1,512]{3,2,1,0:T(1,128)S(1)}, f32[8,2,128,512]{3,2,1,0:T(8,128)S(1)}) custom-call(s32[16]{0:T(128)S(1)} %get-tuple-element.59.offset_ref, s32[16]{0:T(128)S(1)} %broadcast_add_fusion.owner_ref, s32[16]{0:T(128)S(1)} %get-tuple-element.60.valid_ref, ...), custom_call_target="tpu_custom_call" | custom-call | tf_op jit(solution)/shard_map/pallas_call | solution.py:183
  93.5 1.5 pad_maximum_fusion
  95.0 5.9 %all-to-all-start = ((bf16[8,264,512]{2,1,0:T(8,128)(2,1)}), bf16[8,264,512]{2,1,0:T(8,128)(2,1)}, u32[]{:S(2)}, u32[]{:S(2)}) async-start(bf16[8,264,512]{2,1,0:T(8,128)(2,1)} %pad_maximum_fusion), calls=%async_computation | async-start | bytes 4325376 | tf_op jit(solution)/shard_map/all_to_all | solution.py:301
  101.5 45.5 %all-to-all-done = bf16[8,264,512]{2,1,0:T(8,128)(2,1)} async-done(((bf16[8,264,512]{2,1,0:T(8,128)(2,1)}), bf16[8,264,512]{2,1,0:T(8,128)(2,1)}, u32[]{:S(2)}, u32[]{:S(2)}) %all-to-all-start) | async-done | bytes 2162720 | tf_op jit(solution)/shard_map/all_to_all | solution.py:301
  148.7 2.9 %fusion = f32[256,512]{1,0:T(8,128)} fusion(bf16[8,264,512]{2,1,0:T(8,128)(2,1)} %all-to-all-done, f32[8,2,512]{2,1,0:T(2,128)S(1)} %get-tuple-element.35), kind=kLoop, calls=%fused_computation.5 | loop fusion | flops 3014656 | bytes 2654208 | tf_op jit(solution)/shard_map/reduce_sum | solution.py:316
  155.1 1.7 convolution_multiply_fusion.3
  156.9 1.9 %fusion.3 = f32[256,2048]{1,0:T(8,128)S(1)} fusion(f32[256,2048]{1,0:T(8,128)S(1)} %convolution_multiply_fusion.3, bf16[4,256,2048]{2,1,0:T(8,128)(2,1)} %param.19, f32[256]{0:T(256)S(1)} %get-tuple-element.21, pred[256]{0:T(512)(128)(4,1)S(1)} %get-tuple-element.26, pred[256]{0:T(512)(128)(4,1)S(1)} %get-tuple-element.24, ...), kind=kOutput, calls=%fused_computation.12 | convolution fusion | flops 269615104 | bytes 5506560 | tf_op jit(solution)/shard_map/dot_general | solution.py:338
  161.2 1.6 collective-permute-start.11
  163.0 3.9 %collective-permute-done.12 = bf16[64,2048]{1,0:T(8,128)(2,1)} collective-permute-done((bf16[64,2048]{1,0:T(8,128)(2,1)}, bf16[64,2048]{1,0:T(8,128)(2,1)}, u32[]{:S(2)}, u32[]{:S(2)}) %collective-permute-start.12) | collective-permute-done | bytes 262176 | tf_op jit(solution)/shard_map/ppermute | solution.py:107
  167.0 8.8 %collective-permute-done.11 = bf16[64,2048]{1,0:T(8,128)(2,1)} collective-permute-done((bf16[64,2048]{1,0:T(8,128)(2,1)}, bf16[64,2048]{1,0:T(8,128)(2,1)}, u32[]{:S(2)}, u32[]{:S(2)}) %collective-permute-start.11) | collective-permute-done | bytes 262176 | tf_op jit(solution)/shard_map/ppermute | solution.py:107
  175.8 1.9 %fusion.32 = bf16[1,64,2048]{2,1,0:T(8,128)(2,1)} fusion(bf16[64,2048]{1,0:T(8,128)(2,1)} %collective-permute-done.12, bf16[64,2048]{1,0:T(8,128)(2,1)} %collective-permute-done.11, bf16[64,2048]{1,0:T(8,128)(2,1)} %collective-permute-done.10, bf16[256,2048]{1,0:T(8,128)(2,1)S(1)} %fusion.4, s32[]{:T(128)S(6)} %select_n.178), kind=kLoop, calls=%fused_computation.56 | loop fusion | flops 1048576 | bytes 1310724 | tf_op jit(solution)/shard_map/convert_element_type | solution.py:342
  (125 shorter events, 45.2 us)
Async XLA Ops:
  0.0 49.2 %copy-start = (bf16[2,2048,256]{2,1,0:T(8,128)(2,1)S(1)}, bf16[2,2048,256]{2,1,0:T(8,128)(2,1)}, u32[]{:S(2)}) copy-start(bf16[2,2048,256]{2,1,0:T(8,128)(2,1)} %param.18) | copy-start | bytes 6291460
  0.0 17.6 %copy-start.13 = (s32[1,256,2]{1,2,0:T(2,128)S(1)}, s32[1,256,2]{1,2,0:T(2,128)}, u32[]{:S(2)}) copy-start(s32[1,256,2]{1,2,0:T(2,128)} %param.16) | copy-start | bytes 6148
  3.8 20.5 %collective-permute-start.2 = (bf16[64,2048]{1,0:T(8,128)(2,1)}, bf16[64,2048]{1,0:T(8,128)(2,1)}, u32[]{:S(2)}, u32[]{:S(2)}) collective-permute-start(bf16[64,2048]{1,0:T(8,128)(2,1)} %fusion.23), channel_id=1, source_target_pairs={{0,8},{8,16},{16,24},{24,0},{1,9},{9,17},{17,25},{25,1},{2,10},{10... | collective-permute-start | bytes 786440 | tf_op jit(solution)/shard_map/ppermute | solution.py:93
  4.2 20.1 %collective-permute-start.1 = (bf16[64,2048]{1,0:T(8,128)(2,1)}, bf16[64,2048]{1,0:T(8,128)(2,1)}, u32[]{:S(2)}, u32[]{:S(2)}) collective-permute-start(bf16[64,2048]{1,0:T(8,128)(2,1)} %fusion.23), channel_id=1, source_target_pairs={{0,16},{8,24},{16,0},{24,8},{1,17},{9,25},{17,1},{25,9},{2,18},{10... | collective-permute-start | bytes 786440 | tf_op jit(solution)/shard_map/ppermute | solution.py:93
  6.8 17.5 %collective-permute-start = (bf16[64,2048]{1,0:T(8,128)(2,1)}, bf16[64,2048]{1,0:T(8,128)(2,1)}, u32[]{:S(2)}, u32[]{:S(2)}) collective-permute-start(bf16[64,2048]{1,0:T(8,128)(2,1)} %fusion.23), channel_id=1, source_target_pairs={{0,24},{8,0},{16,8},{24,16},{1,25},{9,1},{17,9},{25,17},{2,26},{10... | collective-permute-start | bytes 786440 | tf_op jit(solution)/shard_map/ppermute | solution.py:93
  17.6 4.5 %copy-start.11 = (f32[256,2,4]{0,1,2:T(2,128)}, f32[256,2,4]{0,1,2:T(2,128)S(1)}, u32[]{:S(2)}) copy-start(f32[256,2,4]{0,1,2:T(2,128)S(1)} %fusion.82) | copy-start | bytes 24580
  24.3 19.5 %copy-start.9 = (f32[256,64]{1,0:T(8,128)}, f32[256,64]{1,0:T(8,128)S(1)}, u32[]{:S(2)}) copy-start(f32[256,64]{1,0:T(8,128)S(1)} %get-tuple-element.54) | copy-start | bytes 196612
  30.9 3.8 %copy-start.3 = (bf16[256,2048]{1,0:T(8,128)(2,1)}, bf16[256,2048]{1,0:T(8,128)(2,1)S(1)}, u32[]{:S(2)}) copy-start(bf16[256,2048]{1,0:T(8,128)(2,1)S(1)} %bitcast_select_fusion) | copy-start | bytes 3145732
  43.8 5.4 %copy-start.4 = (bf16[256,2048]{1,0:T(8,128)(2,1)S(1)}, bf16[256,2048]{1,0:T(8,128)(2,1)}, u32[]{:S(2)}) copy-start(bf16[256,2048]{1,0:T(8,128)(2,1)} %copy-done.3) | copy-start | bytes 3145732
  45.7 0.7 copy-start.7
  47.1 14.6 %collective-permute-start.3 = (bf16[512,256]{1,0:T(8,128)(2,1)}, bf16[512,256]{1,0:T(8,128)(2,1)}, u32[]{:S(2)}, u32[]{:S(2)}) collective-permute-start(bf16[512,256]{1,0:T(8,128)(2,1)} %bitcast.202), channel_id=1, source_target_pairs={{1,0},{3,1},{5,3},{7,5},{6,7},{4,6},{2,4},{0,2},{9,8},{11,9},{13,1... | collective-permute-start | bytes 786440 | tf_op jit(solution)/shard_map/ppermute | solution.py:125
  48.7 9.2 %collective-permute-start.6 = (bf16[512,256]{1,0:T(8,128)(2,1)}, bf16[512,256]{1,0:T(8,128)(2,1)}, u32[]{:S(2)}, u32[]{:S(2)}) collective-permute-start(bf16[512,256]{1,0:T(8,128)(2,1)} %bitcast.202), channel_id=1, source_target_pairs={{0,1},{1,3},{3,5},{5,7},{7,6},{6,4},{4,2},{2,0},{8,9},{9,11},{11,1... | collective-permute-start | bytes 786440 | tf_op jit(solution)/shard_map/ppermute | solution.py:121
  50.1 0.9 copy-start.10
  57.9 1.6 copy-start.2
  57.9 7.1 %collective-permute-start.7 = (bf16[512,256]{1,0:T(8,128)(2,1)}, bf16[512,256]{1,0:T(8,128)(2,1)}, u32[]{:S(2)}, u32[]{:S(2)}) collective-permute-start(bf16[512,256]{1,0:T(8,128)(2,1)} %collective-permute-done.6), channel_id=1, source_target_pairs={{0,1},{1,3},{3,5},{5,7},{7,6},{6,4},{4,2},{2,0},{8,9},{9,11},{11,1... | collective-permute-start | bytes 786440 | tf_op jit(solution)/shard_map/ppermute | solution.py:121
  61.7 6.7 %collective-permute-start.4 = (bf16[512,256]{1,0:T(8,128)(2,1)}, bf16[512,256]{1,0:T(8,128)(2,1)S(1)}, u32[]{:S(2)}, u32[]{:S(2)}) collective-permute-start(bf16[512,256]{1,0:T(8,128)(2,1)} %collective-permute-done.3), channel_id=1, source_target_pairs={{1,0},{3,1},{5,3},{7,5},{6,7},{4,6},{2,4},{0,2},{9,8},{11,9},{13,1... | collective-permute-start | bytes 786440 | tf_op jit(solution)/shard_map/ppermute | solution.py:125
  64.2 16.3 %copy-start.1 = (bf16[16,128,256]{2,1,0:T(8,128)(2,1)S(1)}, bf16[16,128,256]{2,1,0:T(8,128)(2,1)}, u32[]{:S(2)}) copy-start(bf16[16,128,256]{2,1,0:T(8,128)(2,1)} %get-tuple-element.39.k_ref) | copy-start | bytes 3145732
  65.0 7.2 %collective-permute-start.8 = (bf16[512,256]{1,0:T(8,128)(2,1)}, bf16[512,256]{1,0:T(8,128)(2,1)S(1)}, u32[]{:S(2)}, u32[]{:S(2)}) collective-permute-start(bf16[512,256]{1,0:T(8,128)(2,1)} %collective-permute-done.7), channel_id=1, source_target_pairs={{0,1},{1,3},{3,5},{5,7},{7,6},{6,4},{4,2},{2,0},{8,9},{9,11},{11,1... | collective-permute-start | bytes 786440 | tf_op jit(solution)/shard_map/ppermute | solution.py:121
  68.5 6.4 %collective-permute-start.5 = (bf16[512,256]{1,0:T(8,128)(2,1)S(1)}, bf16[512,256]{1,0:T(8,128)(2,1)S(1)}, u32[]{:S(2)}, u32[]{:S(2)}) collective-permute-start(bf16[512,256]{1,0:T(8,128)(2,1)S(1)} %collective-permute-done.4), channel_id=1, source_target_pairs={{1,0},{3,1},{5,3},{7,5},{6,7},{4,6},{2,4},{0,2},{9,8},{11,9},{13,1... | collective-permute-start | bytes 786440 | tf_op jit(solution)/shard_map/ppermute | solution.py:125
  72.2 6.4 %collective-permute-start.9 = (bf16[512,256]{1,0:T(8,128)(2,1)S(1)}, bf16[512,256]{1,0:T(8,128)(2,1)S(1)}, u32[]{:S(2)}, u32[]{:S(2)}) collective-permute-start(bf16[512,256]{1,0:T(8,128)(2,1)S(1)} %collective-permute-done.8), channel_id=1, source_target_pairs={{0,1},{1,3},{3,5},{5,7},{7,6},{6,4},{4,2},{2,0},{8,9},{9,11},{11,1... | collective-permute-start | bytes 786440 | tf_op jit(solution)/shard_map/ppermute | solution.py:121
  95.0 6.0 %copy-start.5 = (bf16[256,2048]{1,0:T(8,128)(2,1)S(1)}, bf16[256,2048]{1,0:T(8,128)(2,1)}, u32[]{:S(2)}) copy-start(bf16[256,2048]{1,0:T(8,128)(2,1)} %copy-done.3) | copy-start | bytes 3145732
  95.0 6.0 %copy-start.14 = (bf16[2048,4]{0,1:T(4,128)(2,1)S(1)}, bf16[2048,4]{0,1:T(4,128)(2,1)}, u32[]{:S(2)}) copy-start(bf16[2048,4]{0,1:T(4,128)(2,1)} %param.15) | copy-start | bytes 49156
  95.0 6.4 %copy-start.12 = (f32[256,2,4]{0,1,2:T(2,128)S(1)}, f32[256,2,4]{0,1,2:T(2,128)}, u32[]{:S(2)}) copy-start(f32[256,2,4]{0,1,2:T(2,128)} %copy-done.11) | copy-start | bytes 24580
  95.0 52.0 %all-to-all-start = ((bf16[8,264,512]{2,1,0:T(8,128)(2,1)}), bf16[8,264,512]{2,1,0:T(8,128)(2,1)}, u32[]{:S(2)}, u32[]{:S(2)}) async-start(bf16[8,264,512]{2,1,0:T(8,128)(2,1)} %pad_maximum_fusion), calls=%async_computation | async-start | bytes 4325376 | tf_op jit(solution)/shard_map/all_to_all | solution.py:301
  148.5 4.4 %copy-start.8 = (f32[2,256,2,128]{3,1,2,0:T(8,128)S(1)}, f32[2,256,2,128]{3,1,2,0:T(8,128)}, u32[]{:S(2)}) copy-start(f32[2,256,2,128]{3,1,2,0:T(8,128)} %fusion.26) | copy-start | bytes 1572868
  156.8 2.5 %copy-start.6 = (bf16[4,256,2048]{2,1,0:T(8,128)(2,1)S(1)}, bf16[4,256,2048]{2,1,0:T(8,128)(2,1)}, u32[]{:S(2)}) copy-start(bf16[4,256,2048]{2,1,0:T(8,128)(2,1)} %param.19) | copy-start | bytes 12582916
  161.2 5.8 %collective-permute-start.12 = (bf16[64,2048]{1,0:T(8,128)(2,1)}, bf16[64,2048]{1,0:T(8,128)(2,1)}, u32[]{:S(2)}, u32[]{:S(2)}) collective-permute-start(bf16[64,2048]{1,0:T(8,128)(2,1)} %get-tuple-element.43), channel_id=1, source_target_pairs={{0,24},{8,0},{16,8},{24,16},{1,25},{9,1},{17,9},{25,17},{2,26},{10... | collective-permute-start | bytes 786440 | tf_op jit(solution)/shard_map/ppermute | solution.py:107
  161.2 14.7 %collective-permute-start.11 = (bf16[64,2048]{1,0:T(8,128)(2,1)}, bf16[64,2048]{1,0:T(8,128)(2,1)}, u32[]{:S(2)}, u32[]{:S(2)}) collective-permute-start(bf16[64,2048]{1,0:T(8,128)(2,1)} %get-tuple-element.44), channel_id=1, source_target_pairs={{0,16},{8,24},{16,0},{24,8},{1,17},{9,25},{17,1},{25,9},{2,18},{10... | collective-permute-start | bytes 786440 | tf_op jit(solution)/shard_map/ppermute | solution.py:107
  162.8 13.0 %collective-permute-start.10 = (bf16[64,2048]{1,0:T(8,128)(2,1)S(1)}, bf16[64,2048]{1,0:T(8,128)(2,1)}, u32[]{:S(2)}, u32[]{:S(2)}) collective-permute-start(bf16[64,2048]{1,0:T(8,128)(2,1)S(1)} %get-tuple-element.42), channel_id=1, source_target_pairs={{0,8},{8,16},{16,24},{24,0},{1,9},{9,17},{17,25},{25,1},{2,10},{10... | collective-permute-start | bytes 786440 | tf_op jit(solution)/shard_map/ppermute | solution.py:107

commit v8 on v7

--- a/solution.py
+++ b/solution.py
@@ -93,18 +93,14 @@
         lax.ppermute(piece, axis_name, [(i, (i + s) % size) for i in range(size)])
         for s in range(1, size)
     ]
-    by_offset = jnp.stack(by_offset[:1] + by_offset[1:][::-1], axis=0)
-    return jnp.take(by_offset, (jnp.arange(size, dtype=jnp.int32) - rank) % size, axis=0)
-
-
-def shift_reduce_scatter(rows, axis_name):
+    return jnp.stack(by_offset[:1] + by_offset[1:][::-1], axis=0)
+
+
+def shift_reduce_scatter(blocks, axis_name):
     size = lax.axis_size(axis_name)
-    rank = lax.axis_index(axis_name)
-    share = rows.shape[0] // size
-    total = lax.dynamic_slice_in_dim(rows, rank * share, share, 0).astype(jnp.float32)
+    total = blocks[0].astype(jnp.float32)
     for s in range(1, size):
-        piece = lax.dynamic_slice_in_dim(rows, ((rank + s) % size) * share, share, 0)
-        moved = lax.ppermute(piece, axis_name, [(i, (i + s) % size) for i in range(size)])
+        moved = lax.ppermute(blocks[s], axis_name, [(i, (i + s) % size) for i in range(size)])
         total = total + moved.astype(jnp.float32)
     return total
 
@@ -218,9 +214,15 @@
     normed = normalize(hidden[0], norm_gain)
     gathered = shift_all_gather(normed, "heads").reshape(-1, normed.shape[1])
     new_count = gathered.shape[0]
-    chosen = att_experts[0]
+    rows_each = new_count // head_count
+    head_rank = lax.axis_index("heads")
+    token_ids = (
+        ((head_rank + jnp.arange(head_count, dtype=jnp.int32)[:, None]) % head_count) * rows_each
+        + jnp.arange(rows_each, dtype=jnp.int32)[None, :]
+    ).reshape(new_count)
+    chosen = jnp.take(att_experts[0], token_ids, axis=0)
     cached_len = cached_blocks * block_size - tail_trim
-    positions = cached_len[seq_rank] + jnp.arange(new_count, dtype=jnp.int32)
+    positions = cached_len[seq_rank] + token_ids
     onehot, gates = route(gathered, router_weight, chosen)
     every_q = jnp.einsum("nd,edc->nec", gathered, q_weight, preferred_element_type=jnp.float32)
     chosen_q = jnp.sum(onehot[:, :, :, None] * every_q[:, None, :, :], axis=2).reshape(
@@ -253,10 +255,7 @@
         jnp.einsum("nkhc,thc->hnkt", queries, new_keys, preferred_element_type=jnp.float32)
         * scale_q
     )
-    causal = (
-        jnp.arange(new_count, dtype=jnp.int32)[None, :]
-        <= jnp.arange(new_count, dtype=jnp.int32)[:, None]
-    )
+    causal = token_ids[None, :] <= token_ids[:, None]
     self_scores = jnp.where(causal[None, :, None, :], self_scores, NEG_FILL)
     self_best = jnp.max(self_scores, axis=-1)
     self_weights = jnp.exp(self_scores - self_best[..., None])
@@ -326,19 +325,24 @@
         jnp.transpose((numerator / denominator[..., None]).astype(jnp.bfloat16), (1, 2, 0, 3))
         .reshape(new_count, 2, local_heads * HD)
     )
-    rows_each = new_count // head_count
-    output = jnp.zeros((rows_each * lax.axis_size("heads"), o_weight.shape[2]), jnp.float32)
-    for expert in range(o_weight.shape[0]):
-        weight_expert = jnp.sum(onehot[:, :, expert] * gates, axis=1)
-        picked = jnp.where(
-            chosen[:, 0:1] == expert,
-            attended[:, 0],
-            jnp.where(chosen[:, 1:2] == expert, attended[:, 1], jnp.zeros_like(attended[:, 0])),
-        )
-        output = output + weight_expert[:, None] * jnp.dot(
-            picked, o_weight[expert], preferred_element_type=jnp.float32
-        )
-    summed = shift_reduce_scatter(output.astype(jnp.bfloat16), "heads")
+    output_blocks = []
+    for block in range(head_count):
+        rows = slice(block * rows_each, (block + 1) * rows_each)
+        block_out = jnp.zeros((rows_each, o_weight.shape[2]), jnp.float32)
+        for expert in range(o_weight.shape[0]):
+            weight_expert = jnp.sum(onehot[rows, :, expert] * gates[rows], axis=1)
+            picked = jnp.where(
+                chosen[rows, 0:1] == expert,
+                attended[rows, 0],
+                jnp.where(
+                    chosen[rows, 1:2] == expert, attended[rows, 1], jnp.zeros_like(attended[rows, 0])
+                ),
+            )
+            block_out = block_out + weight_expert[:, None] * jnp.dot(
+                picked, o_weight[expert], preferred_element_type=jnp.float32
+            )
+        output_blocks.append(block_out.astype(jnp.bfloat16))
+    summed = shift_reduce_scatter(output_blocks, "heads")
     return summed[None].astype(jnp.bfloat16)
 
 

time: 179 us -> 175 us (0.978)
  waiting for transfers between devices: 67.3 us -> 61.6 us
  matrix products: 12 us -> 16.4 us
    dot_general x4 -> x16, matrix products: 4.49 us -> 10.5 us  [per_device(): jnp.dot(picked, o_weight[expert], preferred_element_type=jnp.float32)]
    ppermute x3, waiting for transfers between devices: 12.8 us -> 8.12 us  [shift_reduce_scatter(): lax.ppermute(blocks[s], axis_name, [(i, (i + s) % size) for i in range(si...]
    dot_general x1, matrix products: 3.83 us -> 1.25 us  [per_device(): jnp.einsum('nd,edc->nec', gathered, q_weight, preferred_element_type=jnp....]
    ppermute x4, waiting for transfers between devices: 5.85 us -> 3.46 us  [ring_all_gather(): moving = lax.ppermute(moving, axis_name, forward)]
    ppermute x3, waiting for transfers between devices: 3.16 us -> 5.52 us  [ring_all_gather(): moving = lax.ppermute(moving, axis_name, backward)]
    gather x1, local copies, waits for them, and re-layouts: 2.82 us -> 0.73 us  [per_device(): chosen = jnp.take(att_experts[0], token_ids, axis=0)]
    convert_element_type x1 -> x0, other arithmetic: 1.94 us -> none  [per_device(): return summed[None].astype(jnp.bfloat16)]
    unnamed x44 -> x115, local copies, waits for them, and re-layouts: 13.3 us -> 14.1 us
  transfers between devices with their start and end apart: 14 -> 14, of which waited for: 8 -> 7; matrix products, arithmetic and copies ran while one was open for 17% -> 23% of each run, Pallas kernels for 0% -> 0%
where the time goes in v8:
time: 175 us; the launch traced here: 174 us
  waiting for transfers between devices  61.6 us (35%)
  local copies, waits for them, and re-layouts  36.4 us (21%)
  other arithmetic  27.5 us (16%)
  starting transfers between devices  19.4 us (11%)
  matrix products  16.4 us (9%)
  Pallas kernels  11.8 us (7%)
    all_to_all x1, waiting for transfers between devices, per_device(): received = lax.all_to_all(payload, 'seq', 0, 0, tiled=True)  44.5 us
    unnamed x115, local copies, waits for them, and re-layouts  14.1 us
    pallas_call x1, Pallas kernels, block_attention(): pl.pallas_call(kernel, grid_spec=grid_spec, out_shape=[jax.ShapeDtypeStru...  11.8 us
    dot_general x16, matrix products, per_device(): jnp.dot(picked, o_weight[expert], preferred_element_type=jnp.float32)  10.5 us
    ppermute x3, waiting for transfers between devices, shift_reduce_scatter(): lax.ppermute(blocks[s], axis_name, [(i, (i + s) % size) for i in range(si...  8.12 us
    ppermute x3, waiting for transfers between devices, ring_all_gather(): moving = lax.ppermute(moving, axis_name, backward)  5.52 us
    all_to_all x1, starting transfers between devices, per_device(): received = lax.all_to_all(payload, 'seq', 0, 0, tiled=True)  5.43 us
    ppermute x4, starting transfers between devices, ring_all_gather(): moving = lax.ppermute(moving, axis_name, forward)  5.07 us
  transfers between devices with their start and end apart: 14, of which 7 were waited for; matrix products, arithmetic and copies ran while one was open for 23% of the time, Pallas kernels for 0%

profile of v8, /device:TPU:0, one launch (start us, length us, event | category | flops | bytes accessed | tf_op | source)
XLA Modules:
  0.0 174.1 jit_solution(12482561188848130865)
XLA Ops:
  2.0 1.8 %fusion.57 = bf16[64,2048]{1,0:T(8,128)(2,1)} fusion(bf16[1,64,2048]{2,1,0:T(8,128)(2,1)} %param.13, f32[2048]{0:T(1024)S(1)} %convert_element_type.110, f32[64]{0:T(128)S(1)} %add_rsqrt_fusion), kind=kLoop, calls=%fused_computation.88 | loop fusion | flops 524288 | bytes 532736 | tf_op jit(solution)/shard_map/convert_element_type | solution.py:38
  4.2 2.5 %collective-permute-start.1 = (bf16[64,2048]{1,0:T(8,128)(2,1)}, bf16[64,2048]{1,0:T(8,128)(2,1)}, u32[]{:S(2)}, u32[]{:S(2)}) collective-permute-start(bf16[64,2048]{1,0:T(8,128)(2,1)} %fusion.57), channel_id=1, source_target_pairs={{0,16},{8,24},{16,0},{24,8},{1,17},{9,25},{17,1},{25,9},{2,18},{10... | collective-permute-start | bytes 786440 | tf_op jit(solution)/shard_map/ppermute | solution.py:93
  6.8 1.4 collective-permute-start
  16.1 1.8 %fusion.59 = bf16[1,64,2048]{2,1,0:T(8,128)(2,1)} fusion(bf16[1,64,2048]{2,1,0:T(8,128)(2,1)} %param.13, f32[2048]{0:T(1024)S(1)} %convert_element_type.110, f32[64]{0:T(128)S(1)} %add_rsqrt_fusion), kind=kLoop, calls=%fused_computation.90 | loop fusion | flops 524288 | bytes 532736 | tf_op jit(solution)/shard_map/convert_element_type | solution.py:38
  20.7 3.1 %fusion.278 = (bf16[1,16,128,256]{3,2,1,0:T(8,128)(2,1)}, bf16[16,128,256]{2,1,0:T(8,128)(2,1)}) fusion(bf16[2,16,128,256]{3,2,1,0:T(8,128)(2,1)} %param.20), kind=kLoop, calls=%fused_computation.417 | loop fusion | bytes 4194304 | tf_op jit(solution)/shard_map/slice | solution.py:278
  25.6 1.6 copy.200
  28.6 1.4 pad_maximum_fusion.1
  34.8 2.1 %copy.152 = f32[256,2,256]{0,2,1:T(8,128)} copy(f32[256,2,256]{2,0,1:T(8,128)} %multiply_reduce_fusion) | data formatting | bytes 1048576 | tf_op jit(solution)/shard_map/reduce_sum | solution.py:228
  36.8 1.9 %fusion.279 = (f32[256,2,2,64]{0,3,2,1:T(8,128)}, f32[256,2,2,64]{0,3,2,1:T(8,128)}) fusion(f32[256,2,2,128]{0,3,2,1:T(8,128)} %bitcast.371), kind=kLoop, calls=%fused_computation.418 | loop fusion | bytes 1048576 | tf_op jit(solution)/shard_map/slice | solution.py:25
  38.7 2.0 %copy.197 = f32[256,2,2,64]{3,0,1,2:T(8,128)} copy(f32[256,2,2,64]{0,3,2,1:T(8,128)} %get-tuple-element.80) | data formatting | bytes 524288
  40.7 2.0 %copy.196 = f32[256,2,2,64]{3,0,1,2:T(8,128)} copy(f32[256,2,2,64]{0,3,2,1:T(8,128)} %get-tuple-element.81) | data formatting | bytes 524288
  45.9 1.5 collective-permute-start.6
  47.9 1.7 fusion.280
  49.6 1.7 copy.199
  51.4 1.7 copy.198
  55.5 1.5 collective-permute-start.7
  57.1 2.1 %fusion.60 = f32[2,256,2,128]{3,1,2,0:T(8,128)} fusion(bf16[256,2,128,1]{0,2,3,1:T(8,128)(2,1)} %bitcast.374, f32[2,256,2,256]{1,3,2,0:T(8,128)S(1)} %get-tuple-element.104, f32[2,256,2]{1,2,0:T(2,128)S(1)} %get-tuple-element.16), kind=kOutput, calls=%fused_computation.91 | convolution fusion | flops 67633152 | bytes 1708032 | tf_op jit(solution)/shard_map/hnkt,thc->hnkc/dot_general | solution.py:263
  61.4 2.0 %fusion.36 = f32[2,256,2]{1,2,0:T(2,128)} fusion(f32[2,256,2,256]{1,3,2,0:T(8,128)} %copy-done.3, f32[2,256,2]{1,2,0:T(2,128)S(1)} %get-tuple-element.16), kind=kLoop, calls=%fused_computation.65 | loop fusion | flops 523264 | bytes 1056768 | tf_op jit(solution)/shard_map/reduce_sum | solution.py:262
  64.4 2.9 %collective-permute-done.4 = bf16[512,256]{1,0:T(8,128)(2,1)S(1)} collective-permute-done((bf16[512,256]{1,0:T(8,128)(2,1)}, bf16[512,256]{1,0:T(8,128)(2,1)S(1)}, u32[]{:S(2)}, u32[]{:S(2)}) %collective-permute-start.4) | collective-permute-done | bytes 262176 | tf_op jit(solution)/shard_map/ppermute | solution.py:121
  71.1 2.6 %collective-permute-done.5 = bf16[512,256]{1,0:T(8,128)(2,1)S(1)} collective-permute-done((bf16[512,256]{1,0:T(8,128)(2,1)S(1)}, bf16[512,256]{1,0:T(8,128)(2,1)S(1)}, u32[]{:S(2)}, u32[]{:S(2)}) %collective-permute-start.5) | collective-permute-done | bytes 262176 | tf_op jit(solution)/shard_map/ppermute | solution.py:121
  73.7 2.7 %collective-permute-done.9 = bf16[512,256]{1,0:T(8,128)(2,1)S(1)} collective-permute-done((bf16[512,256]{1,0:T(8,128)(2,1)S(1)}, bf16[512,256]{1,0:T(8,128)(2,1)S(1)}, u32[]{:S(2)}, u32[]{:S(2)}) %collective-permute-start.9) | collective-permute-done | bytes 262176 | tf_op jit(solution)/shard_map/ppermute | solution.py:117
  78.4 11.8 %shard_map.127 = (f32[8,2,1,512]{3,2,1,0:T(1,128)S(1)}, f32[8,2,1,512]{3,2,1,0:T(1,128)S(1)}, f32[8,2,128,512]{3,2,1,0:T(8,128)S(1)}) custom-call(s32[16]{0:T(128)S(1)} %and_select_fusion.offset_ref, s32[16]{0:T(128)S(1)} %broadcast_add_fusion.owner_ref, s32[16]{0:T(128)S(1)} %subtract_clamp_fusion.valid_ref, ...), custom_call_target="tpu_custom_call" | custom-call | tf_op jit(solution)/shard_map/pallas_call | solution.py:179
  91.4 1.5 pad_maximum_fusion
  93.0 5.4 %all-to-all-start = ((bf16[8,264,512]{2,1,0:T(8,128)(2,1)}), bf16[8,264,512]{2,1,0:T(8,128)(2,1)}, u32[]{:S(2)}, u32[]{:S(2)}) async-start(bf16[8,264,512]{2,1,0:T(8,128)(2,1)} %pad_maximum_fusion), calls=%async_computation | async-start | bytes 4325376 | tf_op jit(solution)/shard_map/all_to_all | solution.py:300
  100.4 44.5 %all-to-all-done = bf16[8,264,512]{2,1,0:T(8,128)(2,1)} async-done(((bf16[8,264,512]{2,1,0:T(8,128)(2,1)}), bf16[8,264,512]{2,1,0:T(8,128)(2,1)}, u32[]{:S(2)}, u32[]{:S(2)}) %all-to-all-start) | async-done | bytes 2162720 | tf_op jit(solution)/shard_map/all_to_all | solution.py:300
  146.1 2.9 %fusion = f32[256,512]{1,0:T(8,128)} fusion(bf16[8,264,512]{2,1,0:T(8,128)(2,1)} %all-to-all-done, f32[8,2,512]{2,1,0:T(2,128)S(1)} %get-tuple-element.71), kind=kLoop, calls=%fused_computation.5 | loop fusion | flops 3014656 | bytes 2654208 | tf_op jit(solution)/shard_map/reduce_sum | solution.py:315
  153.0 1.8 %convolution_multiply_fusion.1 = f32[64,2048]{1,0:T(8,128)S(1)} fusion(bf16[4,256,2048]{2,1,0:T(8,128)(2,1)} %param.19, f32[64]{0:T(128)S(1)} %get-tuple-element.53, pred[64]{0:T(512)(128)(4,1)S(1)} %copy-done.47, pred[64]{0:T(512)(128)(4,1)S(1)} %copy-done.48, bf16[256,2,256]{0,2,1:T(8,128)(2,1)S(1)} %bitcast.350), kind=kOutput, calls=%fused_computation.8 | convolution fusion | flops 67272704 | bytes 1705472 | tf_op jit(solution)/shard_map/dot_general | solution.py:341
  154.9 1.6 convolution_multiply_fusion
  156.5 1.6 convolution_multiply_fusion.2
  160.2 1.5 collective-permute-start.11
  164.9 6.4 %collective-permute-done.11 = bf16[64,2048]{1,0:T(8,128)(2,1)S(1)} collective-permute-done((bf16[64,2048]{1,0:T(8,128)(2,1)S(1)}, bf16[64,2048]{1,0:T(8,128)(2,1)S(1)}, u32[]{:S(2)}, u32[]{:S(2)}) %collective-permute-start.11) | collective-permute-done | bytes 262176 | tf_op jit(solution)/shard_map/ppermute | solution.py:103
  171.3 1.7 collective-permute-done.10
  (211 shorter events, 50.2 us)
Async XLA Ops:
  0.0 30.0 %copy-start = (bf16[2,2048,256]{2,1,0:T(8,128)(2,1)S(1)}, bf16[2,2048,256]{2,1,0:T(8,128)(2,1)}, u32[]{:S(2)}) copy-start(bf16[2,2048,256]{2,1,0:T(8,128)(2,1)} %param.18) | copy-start | bytes 6291460
  3.8 24.8 %collective-permute-start.2 = (bf16[64,2048]{1,0:T(8,128)(2,1)}, bf16[64,2048]{1,0:T(8,128)(2,1)}, u32[]{:S(2)}, u32[]{:S(2)}) collective-permute-start(bf16[64,2048]{1,0:T(8,128)(2,1)} %fusion.57), channel_id=1, source_target_pairs={{0,8},{8,16},{16,24},{24,0},{1,9},{9,17},{17,25},{25,1},{2,10},{10... | collective-permute-start | bytes 786440 | tf_op jit(solution)/shard_map/ppermute | solution.py:93
  4.2 24.4 %collective-permute-start.1 = (bf16[64,2048]{1,0:T(8,128)(2,1)}, bf16[64,2048]{1,0:T(8,128)(2,1)}, u32[]{:S(2)}, u32[]{:S(2)}) collective-permute-start(bf16[64,2048]{1,0:T(8,128)(2,1)} %fusion.57), channel_id=1, source_target_pairs={{0,16},{8,24},{16,0},{24,8},{1,17},{9,25},{17,1},{25,9},{2,18},{10... | collective-permute-start | bytes 786440 | tf_op jit(solution)/shard_map/ppermute | solution.py:93
  6.8 21.8 %collective-permute-start = (bf16[64,2048]{1,0:T(8,128)(2,1)}, bf16[64,2048]{1,0:T(8,128)(2,1)}, u32[]{:S(2)}, u32[]{:S(2)}) collective-permute-start(bf16[64,2048]{1,0:T(8,128)(2,1)} %fusion.57), channel_id=1, source_target_pairs={{0,24},{8,0},{16,8},{24,16},{1,25},{9,1},{17,9},{25,17},{2,26},{10... | collective-permute-start | bytes 786440 | tf_op jit(solution)/shard_map/ppermute | solution.py:93
  28.5 14.1 %copy-start.8 = (f32[256,64]{1,0:T(8,128)}, f32[256,64]{1,0:T(8,128)S(1)}, u32[]{:S(2)}) copy-start(f32[256,64]{1,0:T(8,128)S(1)} %get-tuple-element.99) | copy-start | bytes 196612
  28.5 14.1 %copy-start.9 = (f32[256,64]{1,0:T(8,128)}, f32[256,64]{1,0:T(8,128)S(1)}, u32[]{:S(2)}) copy-start(f32[256,64]{1,0:T(8,128)S(1)} %get-tuple-element.100) | copy-start | bytes 196612
  45.9 9.6 %collective-permute-start.6 = (bf16[512,256]{1,0:T(8,128)(2,1)}, bf16[512,256]{1,0:T(8,128)(2,1)}, u32[]{:S(2)}, u32[]{:S(2)}) collective-permute-start(bf16[512,256]{1,0:T(8,128)(2,1)} %bitcast.345), channel_id=1, source_target_pairs={{0,1},{1,3},{3,5},{5,7},{7,6},{6,4},{4,2},{2,0},{8,9},{9,11},{11,1... | collective-permute-start | bytes 786440 | tf_op jit(solution)/shard_map/ppermute | solution.py:117
  47.4 12.9 %collective-permute-start.3 = (bf16[512,256]{1,0:T(8,128)(2,1)}, bf16[512,256]{1,0:T(8,128)(2,1)}, u32[]{:S(2)}, u32[]{:S(2)}) collective-permute-start(bf16[512,256]{1,0:T(8,128)(2,1)} %bitcast.345), channel_id=1, source_target_pairs={{1,0},{3,1},{5,3},{7,5},{6,7},{4,6},{2,4},{0,2},{9,8},{11,9},{13,1... | collective-permute-start | bytes 786440 | tf_op jit(solution)/shard_map/ppermute | solution.py:121
  55.5 7.8 %collective-permute-start.7 = (bf16[512,256]{1,0:T(8,128)(2,1)}, bf16[512,256]{1,0:T(8,128)(2,1)}, u32[]{:S(2)}, u32[]{:S(2)}) collective-permute-start(bf16[512,256]{1,0:T(8,128)(2,1)} %collective-permute-done.6), channel_id=1, source_target_pairs={{0,1},{1,3},{3,5},{5,7},{7,6},{6,4},{4,2},{2,0},{8,9},{9,11},{11,1... | collective-permute-start | bytes 786440 | tf_op jit(solution)/shard_map/ppermute | solution.py:117
  60.3 18.1 %copy-start.1 = (bf16[16,128,256]{2,1,0:T(8,128)(2,1)S(1)}, bf16[16,128,256]{2,1,0:T(8,128)(2,1)}, u32[]{:S(2)}) copy-start(bf16[16,128,256]{2,1,0:T(8,128)(2,1)} %get-tuple-element.75.k_ref) | copy-start | bytes 3145732
  60.3 7.0 %collective-permute-start.4 = (bf16[512,256]{1,0:T(8,128)(2,1)}, bf16[512,256]{1,0:T(8,128)(2,1)S(1)}, u32[]{:S(2)}, u32[]{:S(2)}) collective-permute-start(bf16[512,256]{1,0:T(8,128)(2,1)} %collective-permute-done.3), channel_id=1, source_target_pairs={{1,0},{3,1},{5,3},{7,5},{6,7},{4,6},{2,4},{0,2},{9,8},{11,9},{13,1... | collective-permute-start | bytes 786440 | tf_op jit(solution)/shard_map/ppermute | solution.py:121
  63.4 6.7 %collective-permute-start.8 = (bf16[512,256]{1,0:T(8,128)(2,1)}, bf16[512,256]{1,0:T(8,128)(2,1)S(1)}, u32[]{:S(2)}, u32[]{:S(2)}) collective-permute-start(bf16[512,256]{1,0:T(8,128)(2,1)} %collective-permute-done.7), channel_id=1, source_target_pairs={{0,1},{1,3},{3,5},{5,7},{7,6},{6,4},{4,2},{2,0},{8,9},{9,11},{11,1... | collective-permute-start | bytes 786440 | tf_op jit(solution)/shard_map/ppermute | solution.py:117
  67.3 6.4 %collective-permute-start.5 = (bf16[512,256]{1,0:T(8,128)(2,1)S(1)}, bf16[512,256]{1,0:T(8,128)(2,1)S(1)}, u32[]{:S(2)}, u32[]{:S(2)}) collective-permute-start(bf16[512,256]{1,0:T(8,128)(2,1)S(1)} %collective-permute-done.4), channel_id=1, source_target_pairs={{1,0},{3,1},{5,3},{7,5},{6,7},{4,6},{2,4},{0,2},{9,8},{11,9},{13,1... | collective-permute-start | bytes 786440 | tf_op jit(solution)/shard_map/ppermute | solution.py:121
  70.1 6.4 %collective-permute-start.9 = (bf16[512,256]{1,0:T(8,128)(2,1)S(1)}, bf16[512,256]{1,0:T(8,128)(2,1)S(1)}, u32[]{:S(2)}, u32[]{:S(2)}) collective-permute-start(bf16[512,256]{1,0:T(8,128)(2,1)S(1)} %collective-permute-done.8), channel_id=1, source_target_pairs={{0,1},{1,3},{3,5},{5,7},{7,6},{6,4},{4,2},{2,0},{8,9},{9,11},{11,1... | collective-permute-start | bytes 786440 | tf_op jit(solution)/shard_map/ppermute | solution.py:117
  91.4 8.7 %copy-start.14 = (s32[256,2]{0,1:T(2,128)S(1)}, s32[256,2]{0,1:T(2,128)}, u32[]{:S(2)}) copy-start(s32[256,2]{0,1:T(2,128)} %copy-done.13) | copy-start | bytes 6148
  91.4 8.8 %copy-start.11 = (f32[256,2,4]{0,1,2:T(2,128)S(1)}, f32[256,2,4]{0,1,2:T(2,128)}, u32[]{:S(2)}) copy-start(f32[256,2,4]{0,1,2:T(2,128)} %copy-done.10) | copy-start | bytes 24580
  93.0 51.9 %all-to-all-start = ((bf16[8,264,512]{2,1,0:T(8,128)(2,1)}), bf16[8,264,512]{2,1,0:T(8,128)(2,1)}, u32[]{:S(2)}, u32[]{:S(2)}) async-start(bf16[8,264,512]{2,1,0:T(8,128)(2,1)} %pad_maximum_fusion), calls=%async_computation | async-start | bytes 4325376 | tf_op jit(solution)/shard_map/all_to_all | solution.py:300
  98.4 53.9 %copy-start.16 = (f32[2,256,2]{1,2,0:T(2,128)S(1)}, f32[2,256,2]{1,2,0:T(2,128)}, u32[]{:S(2)}) copy-start(f32[2,256,2]{1,2,0:T(2,128)} %fusion.36) | copy-start | bytes 12292
  99.7 53.3 %copy-start.47 = (pred[64]{0:T(512)(128)(4,1)S(1)}, pred[64]{0:T(512)(128)(4,1)}, u32[]{:S(2)}) copy-start(pred[64]{0:T(512)(128)(4,1)} %get-tuple-element.91) | copy-start | bytes 196
  99.7 53.3 %copy-start.48 = (pred[64]{0:T(512)(128)(4,1)S(1)}, pred[64]{0:T(512)(128)(4,1)}, u32[]{:S(2)}) copy-start(pred[64]{0:T(512)(128)(4,1)} %get-tuple-element.94) | copy-start | bytes 196
  100.1 52.3 %copy-start.7 = (f32[2,256,2,128]{3,1,2,0:T(8,128)S(1)}, f32[2,256,2,128]{3,1,2,0:T(8,128)}, u32[]{:S(2)}) copy-start(f32[2,256,2,128]{3,1,2,0:T(8,128)} %fusion.60) | copy-start | bytes 1572868
  145.9 9.0 %copy-start.45 = (pred[64]{0:T(512)(128)(4,1)S(1)}, pred[64]{0:T(512)(128)(4,1)}, u32[]{:S(2)}) copy-start(pred[64]{0:T(512)(128)(4,1)} %get-tuple-element.90) | copy-start | bytes 196
  145.9 9.0 %copy-start.46 = (pred[64]{0:T(512)(128)(4,1)S(1)}, pred[64]{0:T(512)(128)(4,1)}, u32[]{:S(2)}) copy-start(pred[64]{0:T(512)(128)(4,1)} %get-tuple-element.93) | copy-start | bytes 196
  146.1 10.4 %copy-start.43 = (pred[64]{0:T(512)(128)(4,1)S(1)}, pred[64]{0:T(512)(128)(4,1)}, u32[]{:S(2)}) copy-start(pred[64]{0:T(512)(128)(4,1)} %get-tuple-element.92) | copy-start | bytes 196
  146.1 10.4 %copy-start.44 = (pred[64]{0:T(512)(128)(4,1)S(1)}, pred[64]{0:T(512)(128)(4,1)}, u32[]{:S(2)}) copy-start(pred[64]{0:T(512)(128)(4,1)} %get-tuple-element.95) | copy-start | bytes 196
  149.0 9.2 %copy-start.41 = (pred[64]{0:T(512)(128)(4,1)S(1)}, pred[64]{0:T(512)(128)(4,1)}, u32[]{:S(2)}) copy-start(pred[64]{0:T(512)(128)(4,1)} %get-tuple-element.88) | copy-start | bytes 196
  149.0 9.3 %copy-start.42 = (pred[64]{0:T(512)(128)(4,1)S(1)}, pred[64]{0:T(512)(128)(4,1)}, u32[]{:S(2)}) copy-start(pred[64]{0:T(512)(128)(4,1)} %get-tuple-element.89) | copy-start | bytes 196
  158.7 6.2 %collective-permute-start.12 = (bf16[64,2048]{1,0:T(8,128)(2,1)S(1)}, bf16[64,2048]{1,0:T(8,128)(2,1)S(1)}, u32[]{:S(2)}, u32[]{:S(2)}) collective-permute-start(bf16[64,2048]{1,0:T(8,128)(2,1)S(1)} %fusion.13), channel_id=1, source_target_pairs={{0,24},{8,0},{16,8},{24,16},{1,25},{9,1},{17,9},{25,17},{2,26},{10... | collective-permute-start | bytes 786440 | tf_op jit(solution)/shard_map/ppermute | solution.py:103
  160.2 11.1 %collective-permute-start.11 = (bf16[64,2048]{1,0:T(8,128)(2,1)S(1)}, bf16[64,2048]{1,0:T(8,128)(2,1)S(1)}, u32[]{:S(2)}, u32[]{:S(2)}) collective-permute-start(bf16[64,2048]{1,0:T(8,128)(2,1)S(1)} %fusion.14), channel_id=1, source_target_pairs={{0,16},{8,24},{16,0},{24,8},{1,17},{9,25},{17,1},{25,9},{2,18},{10... | collective-permute-start | bytes 786440 | tf_op jit(solution)/shard_map/ppermute | solution.py:103
  163.1 9.9 %copy-start.17 = (pred[64]{0:T(512)(128)(4,1)S(1)}, pred[64]{0:T(512)(128)(4,1)}, u32[]{:S(2)}) copy-start(pred[64]{0:T(512)(128)(4,1)} %get-tuple-element.19) | copy-start | bytes 196
  163.1 9.9 %copy-start.18 = (pred[64]{0:T(512)(128)(4,1)S(1)}, pred[64]{0:T(512)(128)(4,1)}, u32[]{:S(2)}) copy-start(pred[64]{0:T(512)(128)(4,1)} %get-tuple-element.96) | copy-start | bytes 196
  163.6 9.4 %collective-permute-start.10 = (bf16[64,2048]{1,0:T(8,128)(2,1)S(1)}, bf16[64,2048]{1,0:T(8,128)(2,1)S(1)}, u32[]{:S(2)}, u32[]{:S(2)}) collective-permute-start(bf16[64,2048]{1,0:T(8,128)(2,1)S(1)} %fusion.15), channel_id=1, source_target_pairs={{0,8},{8,16},{16,24},{24,0},{1,9},{9,17},{17,25},{25,1},{2,10},{10... | collective-permute-start | bytes 786440 | tf_op jit(solution)/shard_map/ppermute | solution.py:103
  (32 other events, 111.1 us)

commit v9 on v8

--- a/solution.py
+++ b/solution.py
@@ -18,18 +18,13 @@
     half_dim = values.shape[-1] // 2
     inverse = 10000.0 ** (-2.0 * jnp.arange(half_dim, dtype=jnp.float32) / values.shape[-1])
     angles = positions.astype(jnp.float32)[:, None] * inverse[None, :]
-    target = (values.shape[0],) + (1,) * (values.ndim - 2) + (half_dim,)
-    cosine = jnp.cos(angles).reshape(target)
-    sine_part = jnp.sin(angles).reshape(target)
-    leading_part = values[..., :half_dim]
-    trailing_part = values[..., half_dim:]
-    return jnp.concatenate(
-        [
-            leading_part * cosine - trailing_part * sine_part,
-            trailing_part * cosine + leading_part * sine_part,
-        ],
-        axis=-1,
-    )
+    target = (values.shape[0],) + (1,) * (values.ndim - 2) + (2 * half_dim,)
+    cosine = jnp.cos(angles)
+    sine_part = jnp.sin(angles)
+    cosine = jnp.concatenate([cosine, cosine], axis=-1).reshape(target)
+    signed_sine = jnp.concatenate([-sine_part, sine_part], axis=-1).reshape(target)
+    swapped = jnp.concatenate([values[..., half_dim:], values[..., :half_dim]], axis=-1)
+    return values * cosine + swapped * signed_sine
 
 
 def normalize(rows, norm_gain):

time: 175 us -> 178 us (1.017)
  waiting for transfers between devices: 61.6 us -> 63.7 us
    unnamed x115 -> x110, local copies, waits for them, and re-layouts: 14.1 us -> 5.18 us
    ppermute x4, waiting for transfers between devices: 3.46 us -> 12.1 us  [ring_all_gather(): moving = lax.ppermute(moving, axis_name, forward)]
    mul x0 -> x4, local copies, waits for them, and re-layouts: none -> 5.66 us  [rotate(): return values * cosine + swapped * signed_sine]
    ppermute x3, waiting for transfers between devices: 5.52 us -> 0.01 us  [ring_all_gather(): moving = lax.ppermute(moving, axis_name, backward)]
    reshape x0 -> x2, local copies, waits for them, and re-layouts: none -> 4.43 us  [per_device(): jnp.sum(onehot[:, :, :, None] * every_q[:, None, :, :], axis=2)]
    convert_element_type x1 -> x2, other arithmetic: 0.15 us -> 4.14 us  [per_device(): queries = rotate(chosen_q, positions).astype(jnp.bfloat16)]
    slice x2, local copies, waits for them, and re-layouts: 3.56 us -> 1.2 us  [rotate(): values[..., half_dim:]]
  transfers between devices with their start and end apart: 14 -> 14, of which waited for: 7 -> 6; matrix products, arithmetic and copies ran while one was open for 23% -> 20% of each run, Pallas kernels for 0% -> 0%
where the time goes in v9:
time: 178 us; the launch traced here: 176 us
  waiting for transfers between devices  63.7 us (36%)
  local copies, waits for them, and re-layouts  36.8 us (21%)
  other arithmetic  27.3 us (15%)
  starting transfers between devices  19.9 us (11%)
  matrix products  15.7 us (9%)
  Pallas kernels  11.8 us (7%)
    all_to_all x1, waiting for transfers between devices, per_device(): received = lax.all_to_all(payload, 'seq', 0, 0, tiled=True)  43.5 us
    ppermute x4, waiting for transfers between devices, ring_all_gather(): moving = lax.ppermute(moving, axis_name, forward)  12.1 us
    pallas_call x1, Pallas kernels, block_attention(): pl.pallas_call(kernel, grid_spec=grid_spec, out_shape=[jax.ShapeDtypeStru...  11.8 us
    dot_general x16, matrix products, per_device(): jnp.dot(picked, o_weight[expert], preferred_element_type=jnp.float32)  10.5 us
    ppermute x3, waiting for transfers between devices, shift_reduce_scatter(): lax.ppermute(blocks[s], axis_name, [(i, (i + s) % size) for i in range(si...  8.12 us
    ppermute x4, starting transfers between devices, ring_all_gather(): moving = lax.ppermute(moving, axis_name, forward)  6.02 us
    all_to_all x1, starting transfers between devices, per_device(): received = lax.all_to_all(payload, 'seq', 0, 0, tiled=True)  5.8 us
    mul x4, local copies, waits for them, and re-layouts, rotate(): return values * cosine + swapped * signed_sine  5.66 us
  transfers between devices with their start and end apart: 14, of which 6 were waited for; matrix products, arithmetic and copies ran while one was open for 20% of the time, Pallas kernels for 0%

profile of v9, /device:TPU:0, one launch (start us, length us, event | category | flops | bytes accessed | tf_op | source)
XLA Modules:
  0.0 176.4 jit_solution(3588300577690737640)
XLA Ops:
  2.0 1.8 %fusion.57 = bf16[64,2048]{1,0:T(8,128)(2,1)} fusion(bf16[1,64,2048]{2,1,0:T(8,128)(2,1)} %param.13, f32[2048]{0:T(1024)S(1)} %convert_element_type.110, f32[64]{0:T(128)S(1)} %add_rsqrt_fusion), kind=kLoop, calls=%fused_computation.88 | loop fusion | flops 524288 | bytes 532736 | tf_op jit(solution)/shard_map/convert_element_type | solution.py:33
  4.2 2.5 %collective-permute-start.1 = (bf16[64,2048]{1,0:T(8,128)(2,1)}, bf16[64,2048]{1,0:T(8,128)(2,1)}, u32[]{:S(2)}, u32[]{:S(2)}) collective-permute-start(bf16[64,2048]{1,0:T(8,128)(2,1)} %fusion.57), channel_id=1, source_target_pairs={{0,16},{8,24},{16,0},{24,8},{1,17},{9,25},{17,1},{25,9},{2,18},{10... | collective-permute-start | bytes 786440 | tf_op jit(solution)/shard_map/ppermute | solution.py:88
  15.4 1.8 %fusion.59 = bf16[1,64,2048]{2,1,0:T(8,128)(2,1)} fusion(bf16[1,64,2048]{2,1,0:T(8,128)(2,1)} %param.13, f32[2048]{0:T(1024)S(1)} %convert_element_type.110, f32[64]{0:T(128)S(1)} %add_rsqrt_fusion), kind=kLoop, calls=%fused_computation.90 | loop fusion | flops 524288 | bytes 532736 | tf_op jit(solution)/shard_map/convert_element_type | solution.py:33
  20.2 3.1 %fusion.286 = (bf16[1,16,128,256]{3,2,1,0:T(8,128)(2,1)}, bf16[16,128,256]{2,1,0:T(8,128)(2,1)}) fusion(bf16[2,16,128,256]{3,2,1,0:T(8,128)(2,1)} %param.20), kind=kLoop, calls=%fused_computation.424 | loop fusion | bytes 4194304 | tf_op jit(solution)/shard_map/slice | solution.py:273
  27.0 1.6 copy.225
  29.4 1.7 pad_maximum_fusion.1
  37.2 2.0 %copy.175 = f32[256,2,256]{0,2,1:T(8,128)} copy(f32[256,2,256]{2,0,1:T(8,128)} %copy-done.4) | data formatting | bytes 1048576 | tf_op jit(solution)/shard_map/reduce_sum | solution.py:223
  39.2 2.2 %reshape.667 = f32[512,256]{1,0:T(8,128)} reshape(f32[256,2,256]{2,1,0:T(2,128)} %copy.173) | data formatting | bytes 1048576 | tf_op jit(solution)/shard_map/reshape | solution.py:223
  41.4 2.2 %reshape.665 = f32[1,512,256]{2,1,0:T(8,128)} reshape(f32[256,2,256]{2,1,0:T(2,128)} %copy.173) | data formatting | bytes 1048576 | tf_op jit(solution)/shard_map/reshape | solution.py:223
  44.7 2.0 %add_convert_fusion.1 = (bf16[256,2,2,128]{0,3,2,1:T(8,128)(2,1)}, f32[256,2,2,128]{0,3,2,1:T(8,128)}) fusion(f32[256,2,2,128]{0,3,2,1:T(8,128)} %bitcast.375, f32[256,128]{0,1:T(8,128)S(1)} %get-tuple-element.106, f32[256,128]{0,1:T(8,128)S(1)} %get-tuple-element.107, f32[256,2,2,64]{0,3,2,1:T(8,128)S(1)} %get-tuple-element.79, ...), kind=kLoop, calls=%fused_computation.101 | loop fusion | flops 655360 | bytes 2097152 | tf_op jit(solution)/shard_map/convert_element_type | solution.py:226
  46.7 2.0 %copy.176 = f32[256,2,2,128]{3,2,1,0:T(2,128)} copy(f32[256,2,2,128]{0,3,2,1:T(8,128)} %get-tuple-element.75) | data formatting | bytes 1048576 | tf_op jit(solution)/shard_map/mul | solution.py:27
  48.8 2.1 %fusion.62 = bf16[512,256]{1,0:T(8,128)(2,1)} fusion(f32[64,8,2,128]{3,2,1,0:T(2,128)} %bitcast.373, f32[512,256]{1,0:T(8,128)} %reshape.667, f32[64,8,2,128]{3,2,1,0:T(2,128)} %bitcast.372), kind=kLoop, calls=%fused_computation.93 | loop fusion | flops 393216 | bytes 1835008 | tf_op jit(solution)/shard_map/convert_element_type | solution.py:226
  50.9 1.5 collective-permute-start.6
  52.9 2.3 %mul.422 = f32[1,512,256]{2,1,0:T(8,128)} reshape(f32[256,2,2,128]{3,2,1,0:T(2,128)} %copy.176) | data formatting | bytes 1048576 | tf_op jit(solution)/shard_map/mul | solution.py:27
  57.9 1.5 fusion.67
  59.4 1.5 collective-permute-start.7
  62.7 3.7 %collective-permute-done.7 = bf16[512,256]{1,0:T(8,128)(2,1)S(1)} collective-permute-done((bf16[512,256]{1,0:T(8,128)(2,1)}, bf16[512,256]{1,0:T(8,128)(2,1)S(1)}, u32[]{:S(2)}, u32[]{:S(2)}) %collective-permute-start.7) | collective-permute-done | bytes 262176 | tf_op jit(solution)/shard_map/ppermute | solution.py:112
  66.4 1.5 collective-permute-start.8
  70.2 3.5 %collective-permute-done.8 = bf16[512,256]{1,0:T(8,128)(2,1)S(1)} collective-permute-done((bf16[512,256]{1,0:T(8,128)(2,1)S(1)}, bf16[512,256]{1,0:T(8,128)(2,1)S(1)}, u32[]{:S(2)}, u32[]{:S(2)}) %collective-permute-start.8) | collective-permute-done | bytes 262176 | tf_op jit(solution)/shard_map/ppermute | solution.py:112
  73.7 1.5 collective-permute-start.9
  75.2 4.8 %collective-permute-done.9 = bf16[512,256]{1,0:T(8,128)(2,1)S(1)} collective-permute-done((bf16[512,256]{1,0:T(8,128)(2,1)S(1)}, bf16[512,256]{1,0:T(8,128)(2,1)S(1)}, u32[]{:S(2)}, u32[]{:S(2)}) %collective-permute-start.9) | collective-permute-done | bytes 262176 | tf_op jit(solution)/shard_map/ppermute | solution.py:112
  81.1 11.8 %shard_map.127 = (f32[8,2,1,512]{3,2,1,0:T(1,128)S(1)}, f32[8,2,1,512]{3,2,1,0:T(1,128)S(1)}, f32[8,2,128,512]{3,2,1,0:T(8,128)S(1)}) custom-call(s32[16]{0:T(128)S(1)} %and_select_fusion.offset_ref, s32[16]{0:T(128)S(1)} %broadcast_add_fusion.owner_ref, s32[16]{0:T(128)S(1)} %subtract_clamp_fusion.valid_ref, ...), custom_call_target="tpu_custom_call" | custom-call | tf_op jit(solution)/shard_map/pallas_call | solution.py:174
  94.1 1.5 pad_maximum_fusion
  95.7 5.8 %all-to-all-start = ((bf16[8,264,512]{2,1,0:T(8,128)(2,1)}), bf16[8,264,512]{2,1,0:T(8,128)(2,1)}, u32[]{:S(2)}, u32[]{:S(2)}) async-start(bf16[8,264,512]{2,1,0:T(8,128)(2,1)} %pad_maximum_fusion), calls=%async_computation | async-start | bytes 4325376 | tf_op jit(solution)/shard_map/all_to_all | solution.py:295
  103.4 43.5 %all-to-all-done = bf16[8,264,512]{2,1,0:T(8,128)(2,1)} async-done(((bf16[8,264,512]{2,1,0:T(8,128)(2,1)}), bf16[8,264,512]{2,1,0:T(8,128)(2,1)}, u32[]{:S(2)}, u32[]{:S(2)}) %all-to-all-start) | async-done | bytes 2162720 | tf_op jit(solution)/shard_map/all_to_all | solution.py:295
  148.2 2.9 %fusion = f32[256,512]{1,0:T(8,128)} fusion(bf16[8,264,512]{2,1,0:T(8,128)(2,1)} %all-to-all-done, f32[8,2,512]{2,1,0:T(2,128)S(1)} %get-tuple-element.71), kind=kLoop, calls=%fused_computation.5 | loop fusion | flops 3014656 | bytes 2654208 | tf_op jit(solution)/shard_map/reduce_sum | solution.py:310
  155.2 1.8 %convolution_multiply_fusion.1 = f32[64,2048]{1,0:T(8,128)S(1)} fusion(bf16[4,256,2048]{2,1,0:T(8,128)(2,1)} %param.19, f32[64]{0:T(128)S(1)} %get-tuple-element.53, pred[64]{0:T(512)(128)(4,1)S(1)} %copy-done.47, pred[64]{0:T(512)(128)(4,1)S(1)} %copy-done.48, bf16[256,2,256]{0,2,1:T(8,128)(2,1)S(1)} %bitcast.356), kind=kOutput, calls=%fused_computation.8 | convolution fusion | flops 67272704 | bytes 1705472 | tf_op jit(solution)/shard_map/dot_general | solution.py:336
  157.0 1.6 convolution_multiply_fusion
  158.7 1.6 convolution_multiply_fusion.2
  162.4 1.7 collective-permute-start.11
  167.2 6.6 %collective-permute-done.11 = bf16[64,2048]{1,0:T(8,128)(2,1)S(1)} collective-permute-done((bf16[64,2048]{1,0:T(8,128)(2,1)S(1)}, bf16[64,2048]{1,0:T(8,128)(2,1)S(1)}, u32[]{:S(2)}, u32[]{:S(2)}) %collective-permute-start.11) | collective-permute-done | bytes 262176 | tf_op jit(solution)/shard_map/ppermute | solution.py:98
  173.8 1.5 collective-permute-done.10
  (214 shorter events, 47.8 us)
Async XLA Ops:
  0.0 31.1 %copy-start = (bf16[2,2048,256]{2,1,0:T(8,128)(2,1)S(1)}, bf16[2,2048,256]{2,1,0:T(8,128)(2,1)}, u32[]{:S(2)}) copy-start(bf16[2,2048,256]{2,1,0:T(8,128)(2,1)} %param.18) | copy-start | bytes 6291460
  3.8 25.6 %collective-permute-start.2 = (bf16[64,2048]{1,0:T(8,128)(2,1)}, bf16[64,2048]{1,0:T(8,128)(2,1)}, u32[]{:S(2)}, u32[]{:S(2)}) collective-permute-start(bf16[64,2048]{1,0:T(8,128)(2,1)} %fusion.57), channel_id=1, source_target_pairs={{0,8},{8,16},{16,24},{24,0},{1,9},{9,17},{17,25},{25,1},{2,10},{10... | collective-permute-start | bytes 786440 | tf_op jit(solution)/shard_map/ppermute | solution.py:88
  4.2 25.2 %collective-permute-start.1 = (bf16[64,2048]{1,0:T(8,128)(2,1)}, bf16[64,2048]{1,0:T(8,128)(2,1)}, u32[]{:S(2)}, u32[]{:S(2)}) collective-permute-start(bf16[64,2048]{1,0:T(8,128)(2,1)} %fusion.57), channel_id=1, source_target_pairs={{0,16},{8,24},{16,0},{24,8},{1,17},{9,25},{17,1},{25,9},{2,18},{10... | collective-permute-start | bytes 786440 | tf_op jit(solution)/shard_map/ppermute | solution.py:88
  6.8 22.7 %collective-permute-start = (bf16[64,2048]{1,0:T(8,128)(2,1)}, bf16[64,2048]{1,0:T(8,128)(2,1)}, u32[]{:S(2)}, u32[]{:S(2)}) collective-permute-start(bf16[64,2048]{1,0:T(8,128)(2,1)} %fusion.57), channel_id=1, source_target_pairs={{0,24},{8,0},{16,8},{24,16},{1,25},{9,1},{17,9},{25,17},{2,26},{10... | collective-permute-start | bytes 786440 | tf_op jit(solution)/shard_map/ppermute | solution.py:88
  50.9 8.5 %collective-permute-start.6 = (bf16[512,256]{1,0:T(8,128)(2,1)}, bf16[512,256]{1,0:T(8,128)(2,1)}, u32[]{:S(2)}, u32[]{:S(2)}) collective-permute-start(bf16[512,256]{1,0:T(8,128)(2,1)} %fusion.62), channel_id=1, source_target_pairs={{0,1},{1,3},{3,5},{5,7},{7,6},{6,4},{4,2},{2,0},{8,9},{9,11},{11,1... | collective-permute-start | bytes 786440 | tf_op jit(solution)/shard_map/ppermute | solution.py:112
  52.4 8.6 %collective-permute-start.3 = (bf16[512,256]{1,0:T(8,128)(2,1)}, bf16[512,256]{1,0:T(8,128)(2,1)}, u32[]{:S(2)}, u32[]{:S(2)}) collective-permute-start(bf16[512,256]{1,0:T(8,128)(2,1)} %fusion.62), channel_id=1, source_target_pairs={{1,0},{3,1},{5,3},{7,5},{6,7},{4,6},{2,4},{0,2},{9,8},{11,9},{13,1... | collective-permute-start | bytes 786440 | tf_op jit(solution)/shard_map/ppermute | solution.py:116
  57.9 23.2 %copy-start.1 = (bf16[16,128,256]{2,1,0:T(8,128)(2,1)S(1)}, bf16[16,128,256]{2,1,0:T(8,128)(2,1)}, u32[]{:S(2)}) copy-start(bf16[16,128,256]{2,1,0:T(8,128)(2,1)} %get-tuple-element.77.k_ref) | copy-start | bytes 3145732
  59.4 7.0 %collective-permute-start.7 = (bf16[512,256]{1,0:T(8,128)(2,1)}, bf16[512,256]{1,0:T(8,128)(2,1)S(1)}, u32[]{:S(2)}, u32[]{:S(2)}) collective-permute-start(bf16[512,256]{1,0:T(8,128)(2,1)} %collective-permute-done.6), channel_id=1, source_target_pairs={{0,1},{1,3},{3,5},{5,7},{7,6},{6,4},{4,2},{2,0},{8,9},{9,11},{11,1... | collective-permute-start | bytes 786440 | tf_op jit(solution)/shard_map/ppermute | solution.py:112
  61.0 7.7 %collective-permute-start.4 = (bf16[512,256]{1,0:T(8,128)(2,1)}, bf16[512,256]{1,0:T(8,128)(2,1)S(1)}, u32[]{:S(2)}, u32[]{:S(2)}) collective-permute-start(bf16[512,256]{1,0:T(8,128)(2,1)} %collective-permute-done.3), channel_id=1, source_target_pairs={{1,0},{3,1},{5,3},{7,5},{6,7},{4,6},{2,4},{0,2},{9,8},{11,9},{13,1... | collective-permute-start | bytes 786440 | tf_op jit(solution)/shard_map/ppermute | solution.py:116
  66.4 7.3 %collective-permute-start.8 = (bf16[512,256]{1,0:T(8,128)(2,1)S(1)}, bf16[512,256]{1,0:T(8,128)(2,1)S(1)}, u32[]{:S(2)}, u32[]{:S(2)}) collective-permute-start(bf16[512,256]{1,0:T(8,128)(2,1)S(1)} %collective-permute-done.7), channel_id=1, source_target_pairs={{0,1},{1,3},{3,5},{5,7},{7,6},{6,4},{4,2},{2,0},{8,9},{9,11},{11,1... | collective-permute-start | bytes 786440 | tf_op jit(solution)/shard_map/ppermute | solution.py:112
  68.7 6.5 %collective-permute-start.5 = (bf16[512,256]{1,0:T(8,128)(2,1)S(1)}, bf16[512,256]{1,0:T(8,128)(2,1)S(1)}, u32[]{:S(2)}, u32[]{:S(2)}) collective-permute-start(bf16[512,256]{1,0:T(8,128)(2,1)S(1)} %collective-permute-done.4), channel_id=1, source_target_pairs={{1,0},{3,1},{5,3},{7,5},{6,7},{4,6},{2,4},{0,2},{9,8},{11,9},{13,1... | collective-permute-start | bytes 786440 | tf_op jit(solution)/shard_map/ppermute | solution.py:116
  73.7 6.4 %collective-permute-start.9 = (bf16[512,256]{1,0:T(8,128)(2,1)S(1)}, bf16[512,256]{1,0:T(8,128)(2,1)S(1)}, u32[]{:S(2)}, u32[]{:S(2)}) collective-permute-start(bf16[512,256]{1,0:T(8,128)(2,1)S(1)} %collective-permute-done.8), channel_id=1, source_target_pairs={{0,1},{1,3},{3,5},{5,7},{7,6},{6,4},{4,2},{2,0},{8,9},{9,11},{11,1... | collective-permute-start | bytes 786440 | tf_op jit(solution)/shard_map/ppermute | solution.py:112
  94.1 8.7 %copy-start.6 = (bf16[4,64,2048]{2,1,0:T(8,128)(2,1)S(1)}, bf16[4,64,2048]{2,1,0:T(8,128)(2,1)}, u32[]{:S(2)}) copy-start(bf16[4,64,2048]{2,1,0:T(8,128)(2,1)} %copy-done.5) | copy-start | bytes 3145732
  94.1 8.7 %copy-start.15 = (bf16[2048,4]{0,1:T(4,128)(2,1)S(1)}, bf16[2048,4]{0,1:T(4,128)(2,1)}, u32[]{:S(2)}) copy-start(bf16[2048,4]{0,1:T(4,128)(2,1)} %param.15) | copy-start | bytes 49156
  94.1 9.0 %copy-start.14 = (s32[256,2]{0,1:T(2,128)S(1)}, s32[256,2]{0,1:T(2,128)}, u32[]{:S(2)}) copy-start(s32[256,2]{0,1:T(2,128)} %copy-done.13) | copy-start | bytes 6148
  94.1 9.1 %copy-start.11 = (f32[256,2,4]{0,1,2:T(2,128)S(1)}, f32[256,2,4]{0,1,2:T(2,128)}, u32[]{:S(2)}) copy-start(f32[256,2,4]{0,1,2:T(2,128)} %copy-done.10) | copy-start | bytes 24580
  95.7 51.3 %all-to-all-start = ((bf16[8,264,512]{2,1,0:T(8,128)(2,1)}), bf16[8,264,512]{2,1,0:T(8,128)(2,1)}, u32[]{:S(2)}, u32[]{:S(2)}) async-start(bf16[8,264,512]{2,1,0:T(8,128)(2,1)} %pad_maximum_fusion), calls=%async_computation | async-start | bytes 4325376 | tf_op jit(solution)/shard_map/all_to_all | solution.py:295
  101.5 53.0 %copy-start.16 = (f32[2,256,2]{1,2,0:T(2,128)S(1)}, f32[2,256,2]{1,2,0:T(2,128)}, u32[]{:S(2)}) copy-start(f32[2,256,2]{1,2,0:T(2,128)} %fusion.36) | copy-start | bytes 12292
  102.7 52.4 %copy-start.47 = (pred[64]{0:T(512)(128)(4,1)S(1)}, pred[64]{0:T(512)(128)(4,1)}, u32[]{:S(2)}) copy-start(pred[64]{0:T(512)(128)(4,1)} %get-tuple-element.89) | copy-start | bytes 196
  102.7 52.4 %copy-start.48 = (pred[64]{0:T(512)(128)(4,1)S(1)}, pred[64]{0:T(512)(128)(4,1)}, u32[]{:S(2)}) copy-start(pred[64]{0:T(512)(128)(4,1)} %get-tuple-element.92) | copy-start | bytes 196
  103.1 51.3 %copy-start.7 = (f32[2,256,2,128]{3,1,2,0:T(8,128)S(1)}, f32[2,256,2,128]{3,1,2,0:T(8,128)}, u32[]{:S(2)}) copy-start(f32[2,256,2,128]{3,1,2,0:T(8,128)} %fusion.60) | copy-start | bytes 1572868
  148.0 9.0 %copy-start.45 = (pred[64]{0:T(512)(128)(4,1)S(1)}, pred[64]{0:T(512)(128)(4,1)}, u32[]{:S(2)}) copy-start(pred[64]{0:T(512)(128)(4,1)} %get-tuple-element.88) | copy-start | bytes 196
  148.0 9.0 %copy-start.46 = (pred[64]{0:T(512)(128)(4,1)S(1)}, pred[64]{0:T(512)(128)(4,1)}, u32[]{:S(2)}) copy-start(pred[64]{0:T(512)(128)(4,1)} %get-tuple-element.91) | copy-start | bytes 196
  148.2 10.4 %copy-start.43 = (pred[64]{0:T(512)(128)(4,1)S(1)}, pred[64]{0:T(512)(128)(4,1)}, u32[]{:S(2)}) copy-start(pred[64]{0:T(512)(128)(4,1)} %get-tuple-element.90) | copy-start | bytes 196
  148.2 10.4 %copy-start.44 = (pred[64]{0:T(512)(128)(4,1)S(1)}, pred[64]{0:T(512)(128)(4,1)}, u32[]{:S(2)}) copy-start(pred[64]{0:T(512)(128)(4,1)} %get-tuple-element.93) | copy-start | bytes 196
  151.1 9.2 %copy-start.41 = (pred[64]{0:T(512)(128)(4,1)S(1)}, pred[64]{0:T(512)(128)(4,1)}, u32[]{:S(2)}) copy-start(pred[64]{0:T(512)(128)(4,1)} %get-tuple-element.86) | copy-start | bytes 196
  151.1 9.3 %copy-start.42 = (pred[64]{0:T(512)(128)(4,1)S(1)}, pred[64]{0:T(512)(128)(4,1)}, u32[]{:S(2)}) copy-start(pred[64]{0:T(512)(128)(4,1)} %get-tuple-element.87) | copy-start | bytes 196
  160.8 6.4 %collective-permute-start.12 = (bf16[64,2048]{1,0:T(8,128)(2,1)S(1)}, bf16[64,2048]{1,0:T(8,128)(2,1)S(1)}, u32[]{:S(2)}, u32[]{:S(2)}) collective-permute-start(bf16[64,2048]{1,0:T(8,128)(2,1)S(1)} %fusion.13), channel_id=1, source_target_pairs={{0,24},{8,0},{16,8},{24,16},{1,25},{9,1},{17,9},{25,17},{2,26},{10... | collective-permute-start | bytes 786440 | tf_op jit(solution)/shard_map/ppermute | solution.py:98
  162.4 11.5 %collective-permute-start.11 = (bf16[64,2048]{1,0:T(8,128)(2,1)S(1)}, bf16[64,2048]{1,0:T(8,128)(2,1)S(1)}, u32[]{:S(2)}, u32[]{:S(2)}) collective-permute-start(bf16[64,2048]{1,0:T(8,128)(2,1)S(1)} %fusion.14), channel_id=1, source_target_pairs={{0,16},{8,24},{16,0},{24,8},{1,17},{9,25},{17,1},{25,9},{2,18},{10... | collective-permute-start | bytes 786440 | tf_op jit(solution)/shard_map/ppermute | solution.py:98
  165.4 9.9 %copy-start.17 = (pred[64]{0:T(512)(128)(4,1)S(1)}, pred[64]{0:T(512)(128)(4,1)}, u32[]{:S(2)}) copy-start(pred[64]{0:T(512)(128)(4,1)} %get-tuple-element.19) | copy-start | bytes 196
  165.5 9.9 %copy-start.18 = (pred[64]{0:T(512)(128)(4,1)S(1)}, pred[64]{0:T(512)(128)(4,1)}, u32[]{:S(2)}) copy-start(pred[64]{0:T(512)(128)(4,1)} %get-tuple-element.94) | copy-start | bytes 196
  165.9 9.4 %collective-permute-start.10 = (bf16[64,2048]{1,0:T(8,128)(2,1)S(1)}, bf16[64,2048]{1,0:T(8,128)(2,1)S(1)}, u32[]{:S(2)}, u32[]{:S(2)}) collective-permute-start(bf16[64,2048]{1,0:T(8,128)(2,1)S(1)} %fusion.15), channel_id=1, source_target_pairs={{0,8},{8,16},{16,24},{24,0},{1,9},{9,17},{17,25},{25,1},{2,10},{10... | collective-permute-start | bytes 786440 | tf_op jit(solution)/shard_map/ppermute | solution.py:98
  (32 other events, 103.4 us)

commit v10 on v8

--- a/solution.py
+++ b/solution.py
@@ -224,10 +224,15 @@
     cached_len = cached_blocks * block_size - tail_trim
     positions = cached_len[seq_rank] + token_ids
     onehot, gates = route(gathered, router_weight, chosen)
-    every_q = jnp.einsum("nd,edc->nec", gathered, q_weight, preferred_element_type=jnp.float32)
-    chosen_q = jnp.sum(onehot[:, :, :, None] * every_q[:, None, :, :], axis=2).reshape(
-        new_count, 2, local_heads, HD
-    )
+    expert_ids = jnp.arange(q_weight.shape[0], dtype=jnp.int32)
+    slot_queries = []
+    for slot in range(chosen.shape[1]):
+        picks = chosen[:, slot][None, :, None] == expert_ids[:, None, None]
+        masked = jnp.where(picks, gathered[None], jnp.zeros_like(gathered[None]))
+        slot_queries.append(
+            jnp.einsum("end,edc->nc", masked, q_weight, preferred_element_type=jnp.float32)
+        )
+    chosen_q = jnp.stack(slot_queries, axis=1).reshape(new_count, 2, local_heads, HD)
     queries = rotate(chosen_q, positions).astype(jnp.bfloat16)
     fresh = jnp.einsum("nd,sdc->snc", gathered, kv_weight, preferred_element_type=jnp.float32)
     new_keys = rotate(fresh[0].reshape(new_count, local_heads, HD), positions).astype(jnp.bfloat16)

time: 175 us -> 180 us (1.029)
  matrix products: 16.4 us -> 26.6 us
  local copies, waits for them, and re-layouts: 36.4 us -> 29.9 us
  waiting for transfers between devices: 61.6 us -> 59 us
  starting transfers between devices: 19.4 us -> 21.8 us
    dot_general x1 -> x2, matrix products: 1.25 us -> 10.5 us  [per_device(): jnp.einsum('end,edc->nc', masked, q_weight, preferred_element_type=jnp.fl...]
    unnamed x115 -> x65, local copies, waits for them, and re-layouts: 14.1 us -> 9.57 us
    another operation x0 -> x2, local copies, waits for them, and re-layouts: none -> 3.6 us  [per_device(): jnp.stack(slot_queries, axis=1).reshape(new_count, 2, local_heads, HD)]
    slice x2 -> x1, local copies, waits for them, and re-layouts: 3.56 us -> 0.78 us  [rotate(): trailing_part = values[..., half_dim:]]
    ppermute x3, waiting for transfers between devices: 5.52 us -> 3.17 us  [ring_all_gather(): moving = lax.ppermute(moving, axis_name, backward)]
    reduce_sum x1 -> x0, local copies, waits for them, and re-layouts: 2.06 us -> none  [per_device(): jnp.sum(onehot[:, :, :, None] * every_q[:, None, :, :], axis=2)]
  transfers between devices with their start and end apart: 14 -> 14, of which waited for: 7 -> 8; matrix products, arithmetic and copies ran while one was open for 23% -> 24% of each run, Pallas kernels for 0% -> 0%
where the time goes in v10:
time: 180 us; the launch traced here: 179 us
  waiting for transfers between devices  59 us (33%)
  local copies, waits for them, and re-layouts  29.9 us (17%)
  other arithmetic  29 us (16%)
  matrix products  26.6 us (15%)
  starting transfers between devices  21.8 us (12%)
  Pallas kernels  11.8 us (7%)
    all_to_all x1, waiting for transfers between devices, per_device(): received = lax.all_to_all(payload, 'seq', 0, 0, tiled=True)  42.9 us
    pallas_call x1, Pallas kernels, block_attention(): pl.pallas_call(kernel, grid_spec=grid_spec, out_shape=[jax.ShapeDtypeStru...  11.8 us
    dot_general x16, matrix products, per_device(): jnp.dot(picked, o_weight[expert], preferred_element_type=jnp.float32)  11.2 us
    dot_general x2, matrix products, per_device(): jnp.einsum('end,edc->nc', masked, q_weight, preferred_element_type=jnp.fl...  10.5 us
    unnamed x65, local copies, waits for them, and re-layouts  9.57 us
    ppermute x3, waiting for transfers between devices, shift_reduce_scatter(): lax.ppermute(blocks[s], axis_name, [(i, (i + s) % size) for i in range(si...  8.27 us
    ppermute x4, starting transfers between devices, ring_all_gather(): moving = lax.ppermute(moving, axis_name, forward)  6.3 us
    all_to_all x1, starting transfers between devices, per_device(): received = lax.all_to_all(payload, 'seq', 0, 0, tiled=True)  6.09 us
  transfers between devices with their start and end apart: 14, of which 8 were waited for; matrix products, arithmetic and copies ran while one was open for 24% of the time, Pallas kernels for 0%

profile of v10, /device:TPU:0, one launch (start us, length us, event | category | flops | bytes accessed | tf_op | source)
XLA Modules:
  0.0 178.8 jit_solution(5867053320240731864)
XLA Ops:
  2.0 1.8 fusion.67
  4.2 2.5 %collective-permute-start.1 = (bf16[64,2048]{1,0:T(8,128)(2,1)}, bf16[64,2048]{1,0:T(8,128)(2,1)}, u32[]{:S(2)}, u32[]{:S(2)}) collective-permute-start(bf16[64,2048]{1,0:T(8,128)(2,1)} %fusion.67), channel_id=1, source_target_pairs={{0,16},{8,24},{16,0},{24,8},{1,17},{9,25},{17,1},{25,9},{2,18},{10... | collective-permute-start | bytes 786440 | tf_op jit(solution)/shard_map/ppermute | solution.py:93
  6.8 1.4 collective-permute-start
  16.2 1.8 %fusion.69 = bf16[1,64,2048]{2,1,0:T(8,128)(2,1)} fusion(bf16[1,64,2048]{2,1,0:T(8,128)(2,1)} %param.13, f32[2048]{0:T(1024)S(1)} %convert_element_type.106, f32[64]{0:T(128)S(1)} %add_rsqrt_fusion), kind=kLoop, calls=%fused_computation.99 | loop fusion | flops 524288 | bytes 532736 | tf_op jit(solution)/shard_map/convert_element_type | solution.py:38
  21.5 3.1 %fusion.290 = (bf16[1,16,128,256]{3,2,1,0:T(8,128)(2,1)}, bf16[16,128,256]{2,1,0:T(8,128)(2,1)}) fusion(bf16[2,16,128,256]{3,2,1,0:T(8,128)(2,1)} %param.20), kind=kLoop, calls=%fused_computation.434 | loop fusion | bytes 4194304 | tf_op jit(solution)/shard_map/slice | solution.py:283
  25.9 1.6 copy.202
  30.2 5.4 %fusion.1 = f32[256,256,1]{0,1,2:T(8,128)} fusion(bf16[4,2048,256]{2,1,0:T(8,128)(2,1)} %param.17, pred[4,256]{1,0:T(4,128)(4,1)} %iota_compare_fusion.1, bf16[256,2048]{1,0:T(8,128)(2,1)S(1)} %bitcast.371), kind=kOutput, calls=%fused_computation.7 | convolution fusion | flops 1075838976 | bytes 5506048 | tf_op jit(solution)/shard_map/end,edc->nc/dot_general | solution.py:233
  35.6 1.8 %copy.156 = f32[256,1,2,128]{3,0,1,2:T(8,128)} copy(f32[256,1,2,128]{0,3,2,1:T(8,128)} %bitcast.380) | data formatting | bytes 524288 | tf_op jit(solution)/shard_map/stack | solution.py:235
  37.4 5.1 %fusion.3 = f32[256,256,1]{0,1,2:T(8,128)} fusion(bf16[4,2048,256]{2,1,0:T(8,128)(2,1)} %param.17, pred[4,256]{1,0:T(4,128)(4,1)S(1)} %copy-done.25, bf16[256,2048]{1,0:T(8,128)(2,1)} %bitcast.372), kind=kOutput, calls=%fused_computation.9 | convolution fusion | flops 1075838976 | bytes 5506048 | tf_op jit(solution)/shard_map/end,edc->nc/dot_general | solution.py:233
  42.6 1.8 %copy.155 = f32[256,1,2,128]{3,0,1,2:T(8,128)} copy(f32[256,1,2,128]{0,3,2,1:T(8,128)} %bitcast.381) | data formatting | bytes 524288 | tf_op jit(solution)/shard_map/stack | solution.py:235
  44.4 1.6 multiply_subtract_fusion
  47.9 1.5 collective-permute-start.6
  49.9 2.2 %convolution_bitcast_fusion = f32[2,256,256]{1,2,0:T(8,128)S(1)} fusion(bf16[256,2048,1]{1,0,2:T(8,128)(2,1)} %bitcast.373, bf16[2,2048,256]{2,1,0:T(8,128)(2,1)S(1)} %copy-done), kind=kOutput, calls=%fused_computation.53 | convolution fusion | flops 536870912 | bytes 3670016 | tf_op jit(solution)/shard_map/nd,sdc->snc/dot_general | solution.py:237
  53.0 1.7 copy.201
  54.7 1.7 copy.200
  59.8 1.5 collective-permute-start.7
  64.8 2.0 %fusion.46 = f32[2,256,2]{1,2,0:T(2,128)} fusion(f32[2,256,2,256]{1,3,2,0:T(8,128)} %copy-done.3, f32[2,256,2]{1,2,0:T(2,128)S(1)} %get-tuple-element.16), kind=kLoop, calls=%fused_computation.74 | loop fusion | flops 523264 | bytes 1056768 | tf_op jit(solution)/shard_map/reduce_sum | solution.py:267
  66.9 1.5 collective-permute-start.8
  68.5 2.0 %collective-permute-done.4 = bf16[512,256]{1,0:T(8,128)(2,1)S(1)} collective-permute-done((bf16[512,256]{1,0:T(8,128)(2,1)}, bf16[512,256]{1,0:T(8,128)(2,1)S(1)}, u32[]{:S(2)}, u32[]{:S(2)}) %collective-permute-start.4) | collective-permute-done | bytes 262176 | tf_op jit(solution)/shard_map/ppermute | solution.py:121
  73.8 1.8 collective-permute-start.9
  76.8 3.4 %collective-permute-done.9 = bf16[512,256]{1,0:T(8,128)(2,1)S(1)} collective-permute-done((bf16[512,256]{1,0:T(8,128)(2,1)S(1)}, bf16[512,256]{1,0:T(8,128)(2,1)S(1)}, u32[]{:S(2)}, u32[]{:S(2)}) %collective-permute-start.9) | collective-permute-done | bytes 262176 | tf_op jit(solution)/shard_map/ppermute | solution.py:117
  82.2 11.8 %shard_map.127 = (f32[8,2,1,512]{3,2,1,0:T(1,128)S(1)}, f32[8,2,1,512]{3,2,1,0:T(1,128)S(1)}, f32[8,2,128,512]{3,2,1,0:T(8,128)S(1)}) custom-call(s32[16]{0:T(128)S(1)} %and_select_fusion.offset_ref, s32[16]{0:T(128)S(1)} %broadcast_add_fusion.owner_ref, s32[16]{0:T(128)S(1)} %subtract_clamp_fusion.valid_ref, ...), custom_call_target="tpu_custom_call" | custom-call | tf_op jit(solution)/shard_map/pallas_call | solution.py:179
  95.2 1.5 pad_maximum_fusion
  96.7 6.1 %all-to-all-start = ((bf16[8,264,512]{2,1,0:T(8,128)(2,1)}), bf16[8,264,512]{2,1,0:T(8,128)(2,1)}, u32[]{:S(2)}, u32[]{:S(2)}) async-start(bf16[8,264,512]{2,1,0:T(8,128)(2,1)} %pad_maximum_fusion), calls=%async_computation | async-start | bytes 4325376 | tf_op jit(solution)/shard_map/all_to_all | solution.py:305
  106.0 42.9 %all-to-all-done = bf16[8,264,512]{2,1,0:T(8,128)(2,1)} async-done(((bf16[8,264,512]{2,1,0:T(8,128)(2,1)}), bf16[8,264,512]{2,1,0:T(8,128)(2,1)}, u32[]{:S(2)}, u32[]{:S(2)}) %all-to-all-start) | async-done | bytes 2162720 | tf_op jit(solution)/shard_map/all_to_all | solution.py:305
  150.1 2.9 %fusion = f32[256,512]{1,0:T(8,128)} fusion(bf16[8,264,512]{2,1,0:T(8,128)(2,1)} %all-to-all-done, f32[8,2,512]{2,1,0:T(2,128)S(1)} %get-tuple-element.73), kind=kLoop, calls=%fused_computation.5 | loop fusion | flops 3014656 | bytes 2654208 | tf_op jit(solution)/shard_map/reduce_sum | solution.py:320
  157.0 1.8 %convolution_multiply_fusion.1 = f32[64,2048]{1,0:T(8,128)S(1)} fusion(bf16[4,256,2048]{2,1,0:T(8,128)(2,1)} %param.19, f32[64]{0:T(128)} %get-tuple-element.55, pred[64]{0:T(512)(128)(4,1)} %get-tuple-element.91, pred[64]{0:T(512)(128)(4,1)} %get-tuple-element.94, bf16[256,2,256]{0,2,1:T(8,128)(2,1)S(1)} %bitcast.355), kind=kOutput, calls=%fused_computation.14 | convolution fusion | flops 67272704 | bytes 1705472 | tf_op jit(solution)/shard_map/dot_general | solution.py:346
  158.8 1.6 convolution_multiply_fusion
  160.5 1.6 convolution_multiply_fusion.2
  164.7 1.7 collective-permute-start.11
  169.4 6.8 %collective-permute-done.11 = bf16[64,2048]{1,0:T(8,128)(2,1)S(1)} collective-permute-done((bf16[64,2048]{1,0:T(8,128)(2,1)S(1)}, bf16[64,2048]{1,0:T(8,128)(2,1)S(1)}, u32[]{:S(2)}, u32[]{:S(2)}) %collective-permute-start.11) | collective-permute-done | bytes 262176 | tf_op jit(solution)/shard_map/ppermute | solution.py:103
  176.3 1.4 collective-permute-done.10
  (163 shorter events, 50.5 us)
Async XLA Ops:
  0.0 49.9 %copy-start = (bf16[2,2048,256]{2,1,0:T(8,128)(2,1)S(1)}, bf16[2,2048,256]{2,1,0:T(8,128)(2,1)}, u32[]{:S(2)}) copy-start(bf16[2,2048,256]{2,1,0:T(8,128)(2,1)} %param.18) | copy-start | bytes 6291460
  3.8 25.1 %collective-permute-start.2 = (bf16[64,2048]{1,0:T(8,128)(2,1)}, bf16[64,2048]{1,0:T(8,128)(2,1)}, u32[]{:S(2)}, u32[]{:S(2)}) collective-permute-start(bf16[64,2048]{1,0:T(8,128)(2,1)} %fusion.67), channel_id=1, source_target_pairs={{0,8},{8,16},{16,24},{24,0},{1,9},{9,17},{17,25},{25,1},{2,10},{10... | collective-permute-start | bytes 786440 | tf_op jit(solution)/shard_map/ppermute | solution.py:93
  4.2 24.6 %collective-permute-start.1 = (bf16[64,2048]{1,0:T(8,128)(2,1)}, bf16[64,2048]{1,0:T(8,128)(2,1)}, u32[]{:S(2)}, u32[]{:S(2)}) collective-permute-start(bf16[64,2048]{1,0:T(8,128)(2,1)} %fusion.67), channel_id=1, source_target_pairs={{0,16},{8,24},{16,0},{24,8},{1,17},{9,25},{17,1},{25,9},{2,18},{10... | collective-permute-start | bytes 786440 | tf_op jit(solution)/shard_map/ppermute | solution.py:93
  6.8 22.1 %collective-permute-start = (bf16[64,2048]{1,0:T(8,128)(2,1)}, bf16[64,2048]{1,0:T(8,128)(2,1)}, u32[]{:S(2)}, u32[]{:S(2)}) collective-permute-start(bf16[64,2048]{1,0:T(8,128)(2,1)} %fusion.67), channel_id=1, source_target_pairs={{0,24},{8,0},{16,8},{24,16},{1,25},{9,1},{17,9},{25,17},{2,26},{10... | collective-permute-start | bytes 786440 | tf_op jit(solution)/shard_map/ppermute | solution.py:93
  28.8 15.6 %copy-start.8 = (f32[256,64]{1,0:T(8,128)}, f32[256,64]{1,0:T(8,128)S(1)}, u32[]{:S(2)}) copy-start(f32[256,64]{1,0:T(8,128)S(1)} %get-tuple-element.99) | copy-start | bytes 196612
  28.8 15.6 %copy-start.9 = (f32[256,64]{1,0:T(8,128)}, f32[256,64]{1,0:T(8,128)S(1)}, u32[]{:S(2)}) copy-start(f32[256,64]{1,0:T(8,128)S(1)} %get-tuple-element.100) | copy-start | bytes 196612
  30.2 5.4 %copy-start.4 = (bf16[4,64,2048]{2,1,0:T(8,128)(2,1)}, bf16[4,64,2048]{2,1,0:T(8,128)(2,1)S(1)}, u32[]{:S(2)}) copy-start(bf16[4,64,2048]{2,1,0:T(8,128)(2,1)S(1)} %pad_maximum_fusion.1) | copy-start | bytes 3145732
  30.2 7.2 %copy-start.25 = (pred[4,256]{1,0:T(4,128)(4,1)S(1)}, pred[4,256]{1,0:T(4,128)(4,1)}, u32[]{:S(2)}) copy-start(pred[4,256]{1,0:T(4,128)(4,1)} %iota_compare_fusion.2) | copy-start | bytes 3076
  47.9 11.9 %collective-permute-start.6 = (bf16[512,256]{1,0:T(8,128)(2,1)}, bf16[512,256]{1,0:T(8,128)(2,1)}, u32[]{:S(2)}, u32[]{:S(2)}) collective-permute-start(bf16[512,256]{1,0:T(8,128)(2,1)} %bitcast.350), channel_id=1, source_target_pairs={{0,1},{1,3},{3,5},{5,7},{7,6},{6,4},{4,2},{2,0},{8,9},{9,11},{11,1... | collective-permute-start | bytes 786440 | tf_op jit(solution)/shard_map/ppermute | solution.py:117
  49.4 14.3 %collective-permute-start.3 = (bf16[512,256]{1,0:T(8,128)(2,1)}, bf16[512,256]{1,0:T(8,128)(2,1)}, u32[]{:S(2)}, u32[]{:S(2)}) collective-permute-start(bf16[512,256]{1,0:T(8,128)(2,1)} %bitcast.350), channel_id=1, source_target_pairs={{1,0},{3,1},{5,3},{7,5},{6,7},{4,6},{2,4},{0,2},{9,8},{11,9},{13,1... | collective-permute-start | bytes 786440 | tf_op jit(solution)/shard_map/ppermute | solution.py:121
  59.8 7.1 %collective-permute-start.7 = (bf16[512,256]{1,0:T(8,128)(2,1)}, bf16[512,256]{1,0:T(8,128)(2,1)}, u32[]{:S(2)}, u32[]{:S(2)}) collective-permute-start(bf16[512,256]{1,0:T(8,128)(2,1)} %collective-permute-done.6), channel_id=1, source_target_pairs={{0,1},{1,3},{3,5},{5,7},{7,6},{6,4},{4,2},{2,0},{8,9},{9,11},{11,1... | collective-permute-start | bytes 786440 | tf_op jit(solution)/shard_map/ppermute | solution.py:117
  63.7 18.5 %copy-start.1 = (bf16[16,128,256]{2,1,0:T(8,128)(2,1)S(1)}, bf16[16,128,256]{2,1,0:T(8,128)(2,1)}, u32[]{:S(2)}) copy-start(bf16[16,128,256]{2,1,0:T(8,128)(2,1)} %get-tuple-element.77.k_ref) | copy-start | bytes 3145732
  63.7 6.7 %collective-permute-start.4 = (bf16[512,256]{1,0:T(8,128)(2,1)}, bf16[512,256]{1,0:T(8,128)(2,1)S(1)}, u32[]{:S(2)}, u32[]{:S(2)}) collective-permute-start(bf16[512,256]{1,0:T(8,128)(2,1)} %collective-permute-done.3), channel_id=1, source_target_pairs={{1,0},{3,1},{5,3},{7,5},{6,7},{4,6},{2,4},{0,2},{9,8},{11,9},{13,1... | collective-permute-start | bytes 786440 | tf_op jit(solution)/shard_map/ppermute | solution.py:121
  66.9 6.9 %collective-permute-start.8 = (bf16[512,256]{1,0:T(8,128)(2,1)}, bf16[512,256]{1,0:T(8,128)(2,1)S(1)}, u32[]{:S(2)}, u32[]{:S(2)}) collective-permute-start(bf16[512,256]{1,0:T(8,128)(2,1)} %collective-permute-done.7), channel_id=1, source_target_pairs={{0,1},{1,3},{3,5},{5,7},{7,6},{6,4},{4,2},{2,0},{8,9},{9,11},{11,1... | collective-permute-start | bytes 786440 | tf_op jit(solution)/shard_map/ppermute | solution.py:117
  70.4 6.4 %collective-permute-start.5 = (bf16[512,256]{1,0:T(8,128)(2,1)S(1)}, bf16[512,256]{1,0:T(8,128)(2,1)S(1)}, u32[]{:S(2)}, u32[]{:S(2)}) collective-permute-start(bf16[512,256]{1,0:T(8,128)(2,1)S(1)} %collective-permute-done.4), channel_id=1, source_target_pairs={{1,0},{3,1},{5,3},{7,5},{6,7},{4,6},{2,4},{0,2},{9,8},{11,9},{13,1... | collective-permute-start | bytes 786440 | tf_op jit(solution)/shard_map/ppermute | solution.py:121
  73.8 6.4 %collective-permute-start.9 = (bf16[512,256]{1,0:T(8,128)(2,1)S(1)}, bf16[512,256]{1,0:T(8,128)(2,1)S(1)}, u32[]{:S(2)}, u32[]{:S(2)}) collective-permute-start(bf16[512,256]{1,0:T(8,128)(2,1)S(1)} %collective-permute-done.8), channel_id=1, source_target_pairs={{0,1},{1,3},{3,5},{5,7},{7,6},{6,4},{4,2},{2,0},{8,9},{9,11},{11,1... | collective-permute-start | bytes 786440 | tf_op jit(solution)/shard_map/ppermute | solution.py:117
  95.1 9.0 %copy-start.5 = (bf16[4,64,2048]{2,1,0:T(8,128)(2,1)S(1)}, bf16[4,64,2048]{2,1,0:T(8,128)(2,1)}, u32[]{:S(2)}) copy-start(bf16[4,64,2048]{2,1,0:T(8,128)(2,1)} %copy-done.4) | copy-start | bytes 3145732
  95.2 9.0 %copy-start.11 = (bf16[2048,4]{0,1:T(4,128)(2,1)S(1)}, bf16[2048,4]{0,1:T(4,128)(2,1)}, u32[]{:S(2)}) copy-start(bf16[2048,4]{0,1:T(4,128)(2,1)} %param.15) | copy-start | bytes 49156
  96.7 52.2 %all-to-all-start = ((bf16[8,264,512]{2,1,0:T(8,128)(2,1)}), bf16[8,264,512]{2,1,0:T(8,128)(2,1)}, u32[]{:S(2)}, u32[]{:S(2)}) async-start(bf16[8,264,512]{2,1,0:T(8,128)(2,1)} %pad_maximum_fusion), calls=%async_computation | async-start | bytes 4325376 | tf_op jit(solution)/shard_map/all_to_all | solution.py:305
  102.8 53.5 %copy-start.12 = (f32[2,256,2]{1,2,0:T(2,128)S(1)}, f32[2,256,2]{1,2,0:T(2,128)}, u32[]{:S(2)}) copy-start(f32[2,256,2]{1,2,0:T(2,128)} %fusion.46) | copy-start | bytes 12292
  104.5 51.9 %copy-start.7 = (f32[2,256,2,128]{3,1,2,0:T(8,128)S(1)}, f32[2,256,2,128]{3,1,2,0:T(8,128)}, u32[]{:S(2)}) copy-start(f32[2,256,2,128]{3,1,2,0:T(8,128)} %fusion.70) | copy-start | bytes 1572868
  156.9 6.4 %copy-start.24 = (f32[64]{0:T(128)S(1)}, f32[64]{0:T(128)}, u32[]{:S(2)}) copy-start(f32[64]{0:T(128)} %get-tuple-element.59) | copy-start | bytes 772
  157.0 5.1 %copy-start.2 = (bf16[4,256,2048]{2,1,0:T(8,128)(2,1)S(1)}, bf16[4,256,2048]{2,1,0:T(8,128)(2,1)}, u32[]{:S(2)}) copy-start(bf16[4,256,2048]{2,1,0:T(8,128)(2,1)} %param.19) | copy-start | bytes 12582916
  158.8 4.8 %copy-start.23 = (f32[64]{0:T(128)S(1)}, f32[64]{0:T(128)}, u32[]{:S(2)}) copy-start(f32[64]{0:T(128)} %get-tuple-element.58) | copy-start | bytes 772
  160.5 3.5 %copy-start.22 = (f32[64]{0:T(128)S(1)}, f32[64]{0:T(128)}, u32[]{:S(2)}) copy-start(f32[64]{0:T(128)} %get-tuple-element.60) | copy-start | bytes 772
  163.2 6.2 %collective-permute-start.12 = (bf16[64,2048]{1,0:T(8,128)(2,1)S(1)}, bf16[64,2048]{1,0:T(8,128)(2,1)S(1)}, u32[]{:S(2)}, u32[]{:S(2)}) collective-permute-start(bf16[64,2048]{1,0:T(8,128)(2,1)S(1)} %fusion.19), channel_id=1, source_target_pairs={{0,24},{8,0},{16,8},{24,16},{1,25},{9,1},{17,9},{25,17},{2,26},{10... | collective-permute-start | bytes 786440 | tf_op jit(solution)/shard_map/ppermute | solution.py:103
  164.0 3.3 %copy-start.18 = (f32[64]{0:T(128)S(1)}, f32[64]{0:T(128)}, u32[]{:S(2)}) copy-start(f32[64]{0:T(128)} %get-tuple-element.65) | copy-start | bytes 772
  164.3 3.4 %copy-start.17 = (f32[64]{0:T(128)S(1)}, f32[64]{0:T(128)}, u32[]{:S(2)}) copy-start(f32[64]{0:T(128)} %get-tuple-element.66) | copy-start | bytes 772
  164.7 3.7 %copy-start.16 = (f32[64]{0:T(128)S(1)}, f32[64]{0:T(128)}, u32[]{:S(2)}) copy-start(f32[64]{0:T(128)} %get-tuple-element.68) | copy-start | bytes 772
  164.7 11.6 %collective-permute-start.11 = (bf16[64,2048]{1,0:T(8,128)(2,1)S(1)}, bf16[64,2048]{1,0:T(8,128)(2,1)S(1)}, u32[]{:S(2)}, u32[]{:S(2)}) collective-permute-start(bf16[64,2048]{1,0:T(8,128)(2,1)S(1)} %fusion.20), channel_id=1, source_target_pairs={{0,16},{8,24},{16,0},{24,8},{1,17},{9,25},{17,1},{25,9},{2,18},{10... | collective-permute-start | bytes 786440 | tf_op jit(solution)/shard_map/ppermute | solution.py:103
  167.7 10.0 %copy-start.13 = (f32[64]{0:T(128)S(1)}, f32[64]{0:T(128)}, u32[]{:S(2)}) copy-start(f32[64]{0:T(128)} %get-tuple-element.53) | copy-start | bytes 772
  168.2 9.6 %collective-permute-start.10 = (bf16[64,2048]{1,0:T(8,128)(2,1)S(1)}, bf16[64,2048]{1,0:T(8,128)(2,1)S(1)}, u32[]{:S(2)}, u32[]{:S(2)}) collective-permute-start(bf16[64,2048]{1,0:T(8,128)(2,1)S(1)} %fusion.21), channel_id=1, source_target_pairs={{0,8},{8,16},{16,24},{24,0},{1,9},{9,17},{17,25},{25,1},{2,10},{10... | collective-permute-start | bytes 786440 | tf_op jit(solution)/shard_map/ppermute | solution.py:103
  (8 other events, 15.5 us)

commit v11 on v8

--- a/solution.py
+++ b/solution.py
@@ -297,7 +297,15 @@
         ],
         axis=1,
     )
-    received = lax.all_to_all(payload, "seq", 0, 0, tiled=True)
+    cycle_arr = jnp.asarray(cycle, dtype=jnp.int32)
+    arrivals = [lax.dynamic_index_in_dim(payload, seq_rank, 0, keepdims=False)]
+    for s in range(1, ring_size):
+        target = cycle_arr[(position + s) % ring_size]
+        pairs = [(cycle[i], cycle[(i + s) % ring_size]) for i in range(ring_size)]
+        arrivals.append(
+            lax.ppermute(lax.dynamic_index_in_dim(payload, target, 0, keepdims=False), "seq", pairs)
+        )
+    received = jnp.stack(arrivals, axis=0)
     acc_rows = local_heads * HD
     sources = received.shape[0]
     part_accum = received[:, :acc_rows].astype(jnp.float32).reshape(

time: 175 us -> 187 us (1.069)
  between operations: 1.08 us -> 18.1 us
  waiting for transfers between devices: 61.6 us -> 46.5 us
  starting transfers between devices: 19.4 us -> 34.3 us
  other arithmetic: 27.5 us -> 23.2 us
    all_to_all x1 -> x0, waiting for transfers between devices: 44.5 us -> none  [per_device(): received = lax.all_to_all(payload, 'seq', 0, 0, tiled=True)]
    ppermute x0 -> x7, waiting for transfers between devices: none -> 26.6 us  [per_device(): lax.ppermute(lax.dynamic_index_in_dim(payload, target, 0, keepdims=False)...]
    ppermute x0 -> x7, starting transfers between devices: none -> 20.2 us  [per_device(): lax.ppermute(lax.dynamic_index_in_dim(payload, target, 0, keepdims=False)...]
    ppermute x4, waiting for transfers between devices: 3.46 us -> 10.9 us  [ring_all_gather(): moving = lax.ppermute(moving, axis_name, forward)]
    all_to_all x1 -> x0, starting transfers between devices: 5.43 us -> none  [per_device(): received = lax.all_to_all(payload, 'seq', 0, 0, tiled=True)]
    ppermute x3, waiting for transfers between devices: 5.52 us -> 0.79 us  [ring_all_gather(): moving = lax.ppermute(moving, axis_name, backward)]
    unnamed x115 -> x131, local copies, waits for them, and re-layouts: 14.1 us -> 15.8 us
  transfers between devices with their start and end apart: 14 -> 20, of which waited for: 7 -> 9; matrix products, arithmetic and copies ran while one was open for 23% -> 18% of each run, Pallas kernels for 0% -> 0%
where the time goes in v11:
time: 187 us; the launch traced here: 185 us
  waiting for transfers between devices  46.5 us (25%)
  local copies, waits for them, and re-layouts  35.9 us (19%)
  starting transfers between devices  34.3 us (18%)
  other arithmetic  23.2 us (12%)
  between operations  18.1 us (10%)
  matrix products  15.5 us (8%)
  Pallas kernels  11.8 us (6%)
    ppermute x7, waiting for transfers between devices, per_device(): lax.ppermute(lax.dynamic_index_in_dim(payload, target, 0, keepdims=False)...  26.6 us
    ppermute x7, starting transfers between devices, per_device(): lax.ppermute(lax.dynamic_index_in_dim(payload, target, 0, keepdims=False)...  20.2 us
    unnamed x131, local copies, waits for them, and re-layouts  15.8 us
    pallas_call x1, Pallas kernels, block_attention(): pl.pallas_call(kernel, grid_spec=grid_spec, out_shape=[jax.ShapeDtypeStru...  11.8 us
    ppermute x4, waiting for transfers between devices, ring_all_gather(): moving = lax.ppermute(moving, axis_name, forward)  10.9 us
    dot_general x16, matrix products, per_device(): jnp.dot(picked, o_weight[expert], preferred_element_type=jnp.float32)  10.5 us
    ppermute x3, waiting for transfers between devices, shift_reduce_scatter(): lax.ppermute(blocks[s], axis_name, [(i, (i + s) % size) for i in range(si...  8.11 us
    ppermute x4, starting transfers between devices, ring_all_gather(): moving = lax.ppermute(moving, axis_name, forward)  6.02 us
  transfers between devices with their start and end apart: 20, of which 9 were waited for; matrix products, arithmetic and copies ran while one was open for 18% of the time, Pallas kernels for 0%

profile of v11, /device:TPU:0, one launch (start us, length us, event | category | flops | bytes accessed | tf_op | source)
XLA Modules:
  0.0 185.2 jit_solution(17353662792711286892)
XLA Ops:
  2.0 1.8 fusion.57
  4.3 2.5 %collective-permute-start.1 = (bf16[64,2048]{1,0:T(8,128)(2,1)}, bf16[64,2048]{1,0:T(8,128)(2,1)}, u32[]{:S(2)}, u32[]{:S(2)}) collective-permute-start(bf16[64,2048]{1,0:T(8,128)(2,1)} %fusion.57), channel_id=1, source_target_pairs={{0,16},{8,24},{16,0},{24,8},{1,17},{9,25},{17,1},{25,9},{2,18},{10... | collective-permute-start | bytes 786440 | tf_op jit(solution)/shard_map/ppermute | solution.py:93
  19.3 3.1 %fusion.294 = (bf16[1,16,128,256]{3,2,1,0:T(8,128)(2,1)}, bf16[16,128,256]{2,1,0:T(8,128)(2,1)}) fusion(bf16[2,16,128,256]{3,2,1,0:T(8,128)(2,1)} %param.21), kind=kLoop, calls=%fused_computation.455 | loop fusion | bytes 4194304 | tf_op jit(solution)/shard_map/slice | solution.py:278
  36.3 1.6 copy.201
  49.4 2.1 %copy.153 = f32[256,2,256]{0,2,1:T(8,128)} copy(f32[256,2,256]{2,0,1:T(8,128)} %multiply_reduce_fusion) | data formatting | bytes 1048576 | tf_op jit(solution)/shard_map/reduce_sum | solution.py:228
  51.5 1.8 fusion.295
  53.3 2.0 %copy.198 = f32[256,2,2,64]{3,0,1,2:T(8,128)} copy(f32[256,2,2,64]{0,3,2,1:T(8,128)} %get-tuple-element.88) | data formatting | bytes 524288
  55.3 1.9 %copy.197 = f32[256,2,2,64]{3,0,1,2:T(8,128)} copy(f32[256,2,2,64]{0,3,2,1:T(8,128)} %get-tuple-element.89) | data formatting | bytes 524288
  59.9 1.5 collective-permute-start.6
  63.1 1.7 copy.200
  64.9 1.8 copy.199
  71.9 1.5 collective-permute-start.7
  76.5 2.4 %collective-permute-done.7 = bf16[512,256]{1,0:T(8,128)(2,1)} collective-permute-done((bf16[512,256]{1,0:T(8,128)(2,1)}, bf16[512,256]{1,0:T(8,128)(2,1)}, u32[]{:S(2)}, u32[]{:S(2)}) %collective-permute-start.7) | collective-permute-done | bytes 262176 | tf_op jit(solution)/shard_map/ppermute | solution.py:117
  79.0 1.5 collective-permute-start.8
  82.8 3.7 %collective-permute-done.8 = bf16[512,256]{1,0:T(8,128)(2,1)S(1)} collective-permute-done((bf16[512,256]{1,0:T(8,128)(2,1)}, bf16[512,256]{1,0:T(8,128)(2,1)S(1)}, u32[]{:S(2)}, u32[]{:S(2)}) %collective-permute-start.8) | collective-permute-done | bytes 262176 | tf_op jit(solution)/shard_map/ppermute | solution.py:117
  88.0 4.8 %collective-permute-done.9 = bf16[512,256]{1,0:T(8,128)(2,1)S(1)} collective-permute-done((bf16[512,256]{1,0:T(8,128)(2,1)S(1)}, bf16[512,256]{1,0:T(8,128)(2,1)S(1)}, u32[]{:S(2)}, u32[]{:S(2)}) %collective-permute-start.9) | collective-permute-done | bytes 262176 | tf_op jit(solution)/shard_map/ppermute | solution.py:117
  94.8 11.8 %shard_map.136 = (f32[8,2,1,512]{3,2,1,0:T(1,128)S(1)}, f32[8,2,1,512]{3,2,1,0:T(1,128)S(1)}, f32[8,2,128,512]{3,2,1,0:T(8,128)S(1)}) custom-call(s32[16]{0:T(128)S(1)} %get-tuple-element.120.offset_ref, s32[16]{0:T(128)S(1)} %broadcast_add_fusion.owner_ref, s32[16]{0:T(128)S(1)} %get-tuple-element.121.valid_ref, ...), custom_call_target="tpu_custom_call" | custom-call | tf_op jit(solution)/shard_map/pallas_call | solution.py:179
  107.9 1.5 collective-permute-start.10
  109.7 2.7 %collective-permute-start.11 = (bf16[264,512]{1,0:T(8,128)(2,1)S(1)}, bf16[264,512]{1,0:T(8,128)(2,1)S(1)}, u32[]{:S(2)}, u32[]{:S(2)}) collective-permute-start(bf16[264,512]{1,0:T(8,128)(2,1)S(1)} %get-tuple-element.77), channel_id=1, source_target_pairs={{0,3},{1,5},{3,7},{5,6},{7,4},{6,2},{4,0},{2,1},{8,11},{9,13},{11,... | collective-permute-start | bytes 811016 | tf_op jit(solution)/shard_map/ppermute | solution.py:306
  112.7 2.6 %collective-permute-start.14 = (bf16[264,512]{1,0:T(8,128)(2,1)S(1)}, bf16[264,512]{1,0:T(8,128)(2,1)S(1)}, u32[]{:S(2)}, u32[]{:S(2)}) collective-permute-start(bf16[264,512]{1,0:T(8,128)(2,1)S(1)} %get-tuple-element.81), channel_id=1, source_target_pairs={{0,6},{1,4},{3,2},{5,0},{7,1},{6,3},{4,5},{2,7},{8,14},{9,12},{11,... | collective-permute-start | bytes 811016 | tf_op jit(solution)/shard_map/ppermute | solution.py:306
  115.3 1.5 collective-permute-start.16
  117.6 9.2 %collective-permute-start.12 = (bf16[264,512]{1,0:T(8,128)(2,1)S(1)}, bf16[264,512]{1,0:T(8,128)(2,1)S(1)}, u32[]{:S(2)}, u32[]{:S(2)}) collective-permute-start(bf16[264,512]{1,0:T(8,128)(2,1)S(1)} %get-tuple-element.78), channel_id=1, source_target_pairs={{0,5},{1,7},{3,6},{5,4},{7,2},{6,0},{4,1},{2,3},{8,13},{9,15},{11,... | collective-permute-start | bytes 811016 | tf_op jit(solution)/shard_map/ppermute | solution.py:306
  126.8 19.0 %collective-permute-done.11 = bf16[264,512]{1,0:T(8,128)(2,1)S(1)} collective-permute-done((bf16[264,512]{1,0:T(8,128)(2,1)S(1)}, bf16[264,512]{1,0:T(8,128)(2,1)S(1)}, u32[]{:S(2)}, u32[]{:S(2)}) %collective-permute-start.11) | collective-permute-done | bytes 270368 | tf_op jit(solution)/shard_map/ppermute | solution.py:306
  145.8 2.3 %collective-permute-start.13 = (bf16[264,512]{1,0:T(8,128)(2,1)S(1)}, bf16[264,512]{1,0:T(8,128)(2,1)S(1)}, u32[]{:S(2)}, u32[]{:S(2)}) collective-permute-start(bf16[264,512]{1,0:T(8,128)(2,1)S(1)} %get-tuple-element.79), channel_id=1, source_target_pairs={{0,7},{1,6},{3,4},{5,2},{7,0},{6,1},{4,3},{2,5},{8,15},{9,14},{11,... | collective-permute-start | bytes 811016 | tf_op jit(solution)/shard_map/ppermute | solution.py:306
  148.1 6.9 %collective-permute-done.13 = bf16[264,512]{1,0:T(8,128)(2,1)S(1)} collective-permute-done((bf16[264,512]{1,0:T(8,128)(2,1)S(1)}, bf16[264,512]{1,0:T(8,128)(2,1)S(1)}, u32[]{:S(2)}, u32[]{:S(2)}) %collective-permute-start.13) | collective-permute-done | bytes 270368 | tf_op jit(solution)/shard_map/ppermute | solution.py:306
  157.0 2.9 %fusion = f32[256,512]{1,0:T(8,128)} fusion(bf16[8,264,512]{2,1,0:T(8,128)(2,1)} %copy-done.7, f32[8,2,512]{2,1,0:T(2,128)S(1)} %get-tuple-element.71), kind=kLoop, calls=%fused_computation.13 | loop fusion | flops 3014656 | bytes 2654208 | tf_op jit(solution)/shard_map/reduce_sum | solution.py:323
  164.0 1.8 convolution_multiply_fusion.1
  165.8 1.6 convolution_multiply_fusion
  167.5 1.6 convolution_multiply_fusion.2
  171.2 1.7 collective-permute-start.18
  176.0 6.6 %collective-permute-done.18 = bf16[64,2048]{1,0:T(8,128)(2,1)S(1)} collective-permute-done((bf16[64,2048]{1,0:T(8,128)(2,1)S(1)}, bf16[64,2048]{1,0:T(8,128)(2,1)S(1)}, u32[]{:S(2)}, u32[]{:S(2)}) %collective-permute-start.18) | collective-permute-done | bytes 262176 | tf_op jit(solution)/shard_map/ppermute | solution.py:103
  182.6 1.5 collective-permute-done.17
  (243 shorter events, 56.0 us)
Async XLA Ops:
  0.0 44.2 %copy-start = (bf16[2,2048,256]{2,1,0:T(8,128)(2,1)S(1)}, bf16[2,2048,256]{2,1,0:T(8,128)(2,1)}, u32[]{:S(2)}) copy-start(bf16[2,2048,256]{2,1,0:T(8,128)(2,1)} %param.19) | copy-start | bytes 6291460
  0.0 14.1 %copy-start.2 = (s32[8]{0:T(128)S(1)}, s32[8]{0:T(128)}, u32[]{:S(2)}) copy-start(s32[8]{0:T(128)} %constant.162.clone) | copy-start | bytes 100
  0.0 15.5 %copy-start.21 = (s32[1,256,2]{1,2,0:T(2,128)S(1)}, s32[1,256,2]{1,2,0:T(2,128)}, u32[]{:S(2)}) copy-start(s32[1,256,2]{1,2,0:T(2,128)} %param.17) | copy-start | bytes 6148
  1.3 16.6 %copy-start.8 = (bf16[1,64,2048]{2,1,0:T(8,128)(2,1)S(1)}, bf16[1,64,2048]{2,1,0:T(8,128)(2,1)}, u32[]{:S(2)}) copy-start(bf16[1,64,2048]{2,1,0:T(8,128)(2,1)} %param.14) | copy-start | bytes 786436
  3.8 39.0 %collective-permute-start.2 = (bf16[64,2048]{1,0:T(8,128)(2,1)}, bf16[64,2048]{1,0:T(8,128)(2,1)}, u32[]{:S(2)}, u32[]{:S(2)}) collective-permute-start(bf16[64,2048]{1,0:T(8,128)(2,1)} %fusion.57), channel_id=1, source_target_pairs={{0,8},{8,16},{16,24},{24,0},{1,9},{9,17},{17,25},{25,1},{2,10},{10... | collective-permute-start | bytes 786440 | tf_op jit(solution)/shard_map/ppermute | solution.py:93
  4.3 38.6 %collective-permute-start.1 = (bf16[64,2048]{1,0:T(8,128)(2,1)}, bf16[64,2048]{1,0:T(8,128)(2,1)}, u32[]{:S(2)}, u32[]{:S(2)}) collective-permute-start(bf16[64,2048]{1,0:T(8,128)(2,1)} %fusion.57), channel_id=1, source_target_pairs={{0,16},{8,24},{16,0},{24,8},{1,17},{9,25},{17,1},{25,9},{2,18},{10... | collective-permute-start | bytes 786440 | tf_op jit(solution)/shard_map/ppermute | solution.py:93
  6.8 36.0 %collective-permute-start = (bf16[64,2048]{1,0:T(8,128)(2,1)}, bf16[64,2048]{1,0:T(8,128)(2,1)}, u32[]{:S(2)}, u32[]{:S(2)}) collective-permute-start(bf16[64,2048]{1,0:T(8,128)(2,1)} %fusion.57), channel_id=1, source_target_pairs={{0,24},{8,0},{16,8},{24,16},{1,25},{9,1},{17,9},{25,17},{2,26},{10... | collective-permute-start | bytes 786440 | tf_op jit(solution)/shard_map/ppermute | solution.py:93
  16.6 5.9 %copy-start.17 = (s32[256,2]{0,1:T(2,128)}, s32[256,2]{0,1:T(2,128)S(1)}, u32[]{:S(2)}) copy-start(s32[256,2]{0,1:T(2,128)S(1)} %copy.151) | copy-start | bytes 6148
  19.3 17.0 %copy-start.14 = (f32[256,2,4]{0,1,2:T(2,128)}, f32[256,2,4]{0,1,2:T(2,128)S(1)}, u32[]{:S(2)}) copy-start(f32[256,2,4]{0,1,2:T(2,128)S(1)} %fusion.230) | copy-start | bytes 24580
  19.3 7.7 %copy-start.16 = (s32[8]{0:T(128)S(1)}, s32[8]{0:T(128)}, u32[]{:S(2)}) copy-start(s32[8]{0:T(128)} %constant.163.clone) | copy-start | bytes 100
  42.8 14.4 %copy-start.11 = (f32[256,64]{1,0:T(8,128)}, f32[256,64]{1,0:T(8,128)S(1)}, u32[]{:S(2)}) copy-start(f32[256,64]{1,0:T(8,128)S(1)} %get-tuple-element.108) | copy-start | bytes 196612
  59.9 11.9 %collective-permute-start.6 = (bf16[512,256]{1,0:T(8,128)(2,1)}, bf16[512,256]{1,0:T(8,128)(2,1)}, u32[]{:S(2)}, u32[]{:S(2)}) collective-permute-start(bf16[512,256]{1,0:T(8,128)(2,1)} %bitcast.380), channel_id=1, source_target_pairs={{0,1},{1,3},{3,5},{5,7},{7,6},{6,4},{4,2},{2,0},{8,9},{9,11},{11,1... | collective-permute-start | bytes 786440 | tf_op jit(solution)/shard_map/ppermute | solution.py:117
  61.4 13.1 %collective-permute-start.3 = (bf16[512,256]{1,0:T(8,128)(2,1)}, bf16[512,256]{1,0:T(8,128)(2,1)}, u32[]{:S(2)}, u32[]{:S(2)}) collective-permute-start(bf16[512,256]{1,0:T(8,128)(2,1)} %bitcast.380), channel_id=1, source_target_pairs={{1,0},{3,1},{5,3},{7,5},{6,7},{4,6},{2,4},{0,2},{9,8},{11,9},{13,1... | collective-permute-start | bytes 786440 | tf_op jit(solution)/shard_map/ppermute | solution.py:121
  71.9 7.1 %collective-permute-start.7 = (bf16[512,256]{1,0:T(8,128)(2,1)}, bf16[512,256]{1,0:T(8,128)(2,1)}, u32[]{:S(2)}, u32[]{:S(2)}) collective-permute-start(bf16[512,256]{1,0:T(8,128)(2,1)} %collective-permute-done.6), channel_id=1, source_target_pairs={{0,1},{1,3},{3,5},{5,7},{7,6},{6,4},{4,2},{2,0},{8,9},{9,11},{11,1... | collective-permute-start | bytes 786440 | tf_op jit(solution)/shard_map/ppermute | solution.py:117
  74.6 6.7 %collective-permute-start.4 = (bf16[512,256]{1,0:T(8,128)(2,1)}, bf16[512,256]{1,0:T(8,128)(2,1)S(1)}, u32[]{:S(2)}, u32[]{:S(2)}) collective-permute-start(bf16[512,256]{1,0:T(8,128)(2,1)} %collective-permute-done.3), channel_id=1, source_target_pairs={{1,0},{3,1},{5,3},{7,5},{6,7},{4,6},{2,4},{0,2},{9,8},{11,9},{13,1... | collective-permute-start | bytes 786440 | tf_op jit(solution)/shard_map/ppermute | solution.py:121
  76.5 18.3 %copy-start.1 = (bf16[16,128,256]{2,1,0:T(8,128)(2,1)S(1)}, bf16[16,128,256]{2,1,0:T(8,128)(2,1)}, u32[]{:S(2)}) copy-start(bf16[16,128,256]{2,1,0:T(8,128)(2,1)} %get-tuple-element.83.k_ref) | copy-start | bytes 3145732
  79.0 7.5 %collective-permute-start.8 = (bf16[512,256]{1,0:T(8,128)(2,1)}, bf16[512,256]{1,0:T(8,128)(2,1)S(1)}, u32[]{:S(2)}, u32[]{:S(2)}) collective-permute-start(bf16[512,256]{1,0:T(8,128)(2,1)} %collective-permute-done.7), channel_id=1, source_target_pairs={{0,1},{1,3},{3,5},{5,7},{7,6},{6,4},{4,2},{2,0},{8,9},{9,11},{11,1... | collective-permute-start | bytes 786440 | tf_op jit(solution)/shard_map/ppermute | solution.py:117
  81.3 6.7 %collective-permute-start.5 = (bf16[512,256]{1,0:T(8,128)(2,1)S(1)}, bf16[512,256]{1,0:T(8,128)(2,1)S(1)}, u32[]{:S(2)}, u32[]{:S(2)}) collective-permute-start(bf16[512,256]{1,0:T(8,128)(2,1)S(1)} %collective-permute-done.4), channel_id=1, source_target_pairs={{1,0},{3,1},{5,3},{7,5},{6,7},{4,6},{2,4},{0,2},{9,8},{11,9},{13,1... | collective-permute-start | bytes 786440 | tf_op jit(solution)/shard_map/ppermute | solution.py:121
  86.4 6.4 %collective-permute-start.9 = (bf16[512,256]{1,0:T(8,128)(2,1)S(1)}, bf16[512,256]{1,0:T(8,128)(2,1)S(1)}, u32[]{:S(2)}, u32[]{:S(2)}) collective-permute-start(bf16[512,256]{1,0:T(8,128)(2,1)S(1)} %collective-permute-done.8), channel_id=1, source_target_pairs={{0,1},{1,3},{3,5},{5,7},{7,6},{6,4},{4,2},{2,0},{8,9},{9,11},{11,1... | collective-permute-start | bytes 786440 | tf_op jit(solution)/shard_map/ppermute | solution.py:117
  107.9 9.6 %collective-permute-start.10 = (bf16[264,512]{1,0:T(8,128)(2,1)S(1)}, bf16[264,512]{1,0:T(8,128)(2,1)S(1)}, u32[]{:S(2)}, u32[]{:S(2)}) collective-permute-start(bf16[264,512]{1,0:T(8,128)(2,1)S(1)} %get-tuple-element.76), channel_id=1, source_target_pairs={{0,1},{1,3},{3,5},{5,7},{7,6},{6,4},{4,2},{2,0},{8,9},{9,11},{11,1... | collective-permute-start | bytes 811016 | tf_op jit(solution)/shard_map/ppermute | solution.py:306
  109.7 36.1 %collective-permute-start.11 = (bf16[264,512]{1,0:T(8,128)(2,1)S(1)}, bf16[264,512]{1,0:T(8,128)(2,1)S(1)}, u32[]{:S(2)}, u32[]{:S(2)}) collective-permute-start(bf16[264,512]{1,0:T(8,128)(2,1)S(1)} %get-tuple-element.77), channel_id=1, source_target_pairs={{0,3},{1,5},{3,7},{5,6},{7,4},{6,2},{4,0},{2,1},{8,11},{9,13},{11,... | collective-permute-start | bytes 811016 | tf_op jit(solution)/shard_map/ppermute | solution.py:306
  112.4 42.8 %collective-permute-start.15 = (bf16[264,512]{1,0:T(8,128)(2,1)S(1)}, bf16[264,512]{1,0:T(8,128)(2,1)S(1)}, u32[]{:S(2)}, u32[]{:S(2)}) collective-permute-start(bf16[264,512]{1,0:T(8,128)(2,1)S(1)} %get-tuple-element.80), channel_id=1, source_target_pairs={{0,4},{1,2},{3,0},{5,1},{7,3},{6,5},{4,7},{2,6},{8,12},{9,10},{11,... | collective-permute-start | bytes 811016 | tf_op jit(solution)/shard_map/ppermute | solution.py:306
  112.7 42.3 %collective-permute-start.14 = (bf16[264,512]{1,0:T(8,128)(2,1)S(1)}, bf16[264,512]{1,0:T(8,128)(2,1)S(1)}, u32[]{:S(2)}, u32[]{:S(2)}) collective-permute-start(bf16[264,512]{1,0:T(8,128)(2,1)S(1)} %get-tuple-element.81), channel_id=1, source_target_pairs={{0,6},{1,4},{3,2},{5,0},{7,1},{6,3},{4,5},{2,7},{8,14},{9,12},{11,... | collective-permute-start | bytes 811016 | tf_op jit(solution)/shard_map/ppermute | solution.py:306
  115.3 39.8 %collective-permute-start.16 = (bf16[264,512]{1,0:T(8,128)(2,1)S(1)}, bf16[264,512]{1,0:T(8,128)(2,1)S(1)}, u32[]{:S(2)}, u32[]{:S(2)}) collective-permute-start(bf16[264,512]{1,0:T(8,128)(2,1)S(1)} %get-tuple-element.74), channel_id=1, source_target_pairs={{0,2},{1,0},{3,1},{5,3},{7,5},{6,7},{4,6},{2,4},{8,10},{9,8},{11,9... | collective-permute-start | bytes 811016 | tf_op jit(solution)/shard_map/ppermute | solution.py:306
  117.6 30.5 %collective-permute-start.12 = (bf16[264,512]{1,0:T(8,128)(2,1)S(1)}, bf16[264,512]{1,0:T(8,128)(2,1)S(1)}, u32[]{:S(2)}, u32[]{:S(2)}) collective-permute-start(bf16[264,512]{1,0:T(8,128)(2,1)S(1)} %get-tuple-element.78), channel_id=1, source_target_pairs={{0,5},{1,7},{3,6},{5,4},{7,2},{6,0},{4,1},{2,3},{8,13},{9,15},{11,... | collective-permute-start | bytes 811016 | tf_op jit(solution)/shard_map/ppermute | solution.py:306
  145.8 9.3 %collective-permute-start.13 = (bf16[264,512]{1,0:T(8,128)(2,1)S(1)}, bf16[264,512]{1,0:T(8,128)(2,1)S(1)}, u32[]{:S(2)}, u32[]{:S(2)}) collective-permute-start(bf16[264,512]{1,0:T(8,128)(2,1)S(1)} %get-tuple-element.79), channel_id=1, source_target_pairs={{0,7},{1,6},{3,4},{5,2},{7,0},{6,1},{4,3},{2,5},{8,15},{9,14},{11,... | collective-permute-start | bytes 811016 | tf_op jit(solution)/shard_map/ppermute | solution.py:306
  156.9 6.3 %copy-start.10 = (f32[2,256,2,128]{3,1,2,0:T(8,128)S(1)}, f32[2,256,2,128]{3,1,2,0:T(8,128)}, u32[]{:S(2)}) copy-start(f32[2,256,2,128]{3,1,2,0:T(8,128)} %fusion.60) | copy-start | bytes 1572868
  169.6 6.4 %collective-permute-start.19 = (bf16[64,2048]{1,0:T(8,128)(2,1)S(1)}, bf16[64,2048]{1,0:T(8,128)(2,1)S(1)}, u32[]{:S(2)}, u32[]{:S(2)}) collective-permute-start(bf16[64,2048]{1,0:T(8,128)(2,1)S(1)} %fusion.13), channel_id=1, source_target_pairs={{0,24},{8,0},{16,8},{24,16},{1,25},{9,1},{17,9},{25,17},{2,26},{10... | collective-permute-start | bytes 786440 | tf_op jit(solution)/shard_map/ppermute | solution.py:103
  171.2 11.4 %collective-permute-start.18 = (bf16[64,2048]{1,0:T(8,128)(2,1)S(1)}, bf16[64,2048]{1,0:T(8,128)(2,1)S(1)}, u32[]{:S(2)}, u32[]{:S(2)}) collective-permute-start(bf16[64,2048]{1,0:T(8,128)(2,1)S(1)} %fusion.14), channel_id=1, source_target_pairs={{0,16},{8,24},{16,0},{24,8},{1,17},{9,25},{17,1},{25,9},{2,18},{10... | collective-permute-start | bytes 786440 | tf_op jit(solution)/shard_map/ppermute | solution.py:103
  174.7 9.4 %collective-permute-start.17 = (bf16[64,2048]{1,0:T(8,128)(2,1)S(1)}, bf16[64,2048]{1,0:T(8,128)(2,1)S(1)}, u32[]{:S(2)}, u32[]{:S(2)}) collective-permute-start(bf16[64,2048]{1,0:T(8,128)(2,1)S(1)} %fusion.15), channel_id=1, source_target_pairs={{0,8},{8,16},{16,24},{24,0},{1,9},{9,17},{17,25},{25,1},{2,10},{10... | collective-permute-start | bytes 786440 | tf_op jit(solution)/shard_map/ppermute | solution.py:103
  174.9 9.2 %copy-start.22 = (pred[64]{0:T(512)(128)(4,1)S(1)}, pred[64]{0:T(512)(128)(4,1)}, u32[]{:S(2)}) copy-start(pred[64]{0:T(512)(128)(4,1)} %get-tuple-element.19) | copy-start | bytes 196
  174.9 9.2 %copy-start.23 = (pred[64]{0:T(512)(128)(4,1)S(1)}, pred[64]{0:T(512)(128)(4,1)}, u32[]{:S(2)}) copy-start(pred[64]{0:T(512)(128)(4,1)} %get-tuple-element.104) | copy-start | bytes 196
  (44 other events, 117.1 us)

commit v12 on v8

--- a/solution.py
+++ b/solution.py
@@ -326,7 +326,7 @@
         .reshape(new_count, 2, local_heads * HD)
     )
     output_blocks = []
-    for block in range(head_count):
+    for block in list(range(1, head_count)) + [0]:
         rows = slice(block * rows_each, (block + 1) * rows_each)
         block_out = jnp.zeros((rows_each, o_weight.shape[2]), jnp.float32)
         for expert in range(o_weight.shape[0]):
@@ -341,8 +341,10 @@
             block_out = block_out + weight_expert[:, None] * jnp.dot(
                 picked, o_weight[expert], preferred_element_type=jnp.float32
             )
-        output_blocks.append(block_out.astype(jnp.bfloat16))
-    summed = shift_reduce_scatter(output_blocks, "heads")
+        block_out = block_out.astype(jnp.bfloat16)
+        block_out, attended = lax.optimization_barrier((block_out, attended))
+        output_blocks.append(block_out)
+    summed = shift_reduce_scatter(output_blocks[-1:] + output_blocks[:-1], "heads")
     return summed[None].astype(jnp.bfloat16)
 
 

time: 175 us -> 174 us (level)
  waiting for transfers between devices: 61.6 us -> 58.9 us
    ppermute x3, waiting for transfers between devices: 8.12 us -> 5.48 us  [shift_reduce_scatter(): lax.ppermute(blocks[s], axis_name, [(i, (i + s) % size) for i in range(si...]
where the time goes in v12:
time: 174 us; the launch traced here: 173 us
  waiting for transfers between devices  58.9 us (34%)
  local copies, waits for them, and re-layouts  36.4 us (21%)
  other arithmetic  28.3 us (16%)
  starting transfers between devices  20.6 us (12%)
  matrix products  15.6 us (9%)
  Pallas kernels  11.8 us (7%)
    all_to_all x1, waiting for transfers between devices, per_device(): received = lax.all_to_all(payload, 'seq', 0, 0, tiled=True)  44.5 us
    unnamed x115, local copies, waits for them, and re-layouts  14.1 us
    pallas_call x1, Pallas kernels, block_attention(): pl.pallas_call(kernel, grid_spec=grid_spec, out_shape=[jax.ShapeDtypeStru...  11.8 us
    dot_general x16, matrix products, per_device(): jnp.dot(picked, o_weight[expert], preferred_element_type=jnp.float32)  9.74 us
    ppermute x3, waiting for transfers between devices, ring_all_gather(): moving = lax.ppermute(moving, axis_name, backward)  5.52 us
    ppermute x3, waiting for transfers between devices, shift_reduce_scatter(): lax.ppermute(blocks[s], axis_name, [(i, (i + s) % size) for i in range(si...  5.48 us
    all_to_all x1, starting transfers between devices, per_device(): received = lax.all_to_all(payload, 'seq', 0, 0, tiled=True)  5.42 us
    ppermute x4, starting transfers between devices, ring_all_gather(): moving = lax.ppermute(moving, axis_name, forward)  5.07 us
  transfers between devices with their start and end apart: 14, of which 7 were waited for; matrix products, arithmetic and copies ran while one was open for 23% of the time, Pallas kernels for 0%

profile of v12, /device:TPU:0, one launch (start us, length us, event | category | flops | bytes accessed | tf_op | source)
XLA Modules:
  0.0 172.8 jit_solution(3523410203505463021)
XLA Ops:
  2.0 1.8 %fusion.56 = bf16[64,2048]{1,0:T(8,128)(2,1)} fusion(bf16[1,64,2048]{2,1,0:T(8,128)(2,1)} %param.13, f32[2048]{0:T(1024)S(1)} %convert_element_type.110, f32[64]{0:T(128)S(1)} %add_rsqrt_fusion), kind=kLoop, calls=%fused_computation.87 | loop fusion | flops 524288 | bytes 532736 | tf_op jit(solution)/shard_map/convert_element_type | solution.py:38
  4.2 2.5 %collective-permute-start.1 = (bf16[64,2048]{1,0:T(8,128)(2,1)}, bf16[64,2048]{1,0:T(8,128)(2,1)}, u32[]{:S(2)}, u32[]{:S(2)}) collective-permute-start(bf16[64,2048]{1,0:T(8,128)(2,1)} %fusion.56), channel_id=1, source_target_pairs={{0,16},{8,24},{16,0},{24,8},{1,17},{9,25},{17,1},{25,9},{2,18},{10... | collective-permute-start | bytes 786440 | tf_op jit(solution)/shard_map/ppermute | solution.py:93
  6.8 1.4 collective-permute-start
  16.1 1.8 %fusion.58 = bf16[1,64,2048]{2,1,0:T(8,128)(2,1)} fusion(bf16[1,64,2048]{2,1,0:T(8,128)(2,1)} %param.13, f32[2048]{0:T(1024)S(1)} %convert_element_type.110, f32[64]{0:T(128)S(1)} %add_rsqrt_fusion), kind=kLoop, calls=%fused_computation.89 | loop fusion | flops 524288 | bytes 532736 | tf_op jit(solution)/shard_map/convert_element_type | solution.py:38
  20.7 3.1 %fusion.275 = (bf16[1,16,128,256]{3,2,1,0:T(8,128)(2,1)}, bf16[16,128,256]{2,1,0:T(8,128)(2,1)}) fusion(bf16[2,16,128,256]{3,2,1,0:T(8,128)(2,1)} %param.20), kind=kLoop, calls=%fused_computation.416 | loop fusion | bytes 4194304 | tf_op jit(solution)/shard_map/slice | solution.py:278
  25.6 1.6 copy.200
  34.8 2.1 %copy.152 = f32[256,2,256]{0,2,1:T(8,128)} copy(f32[256,2,256]{2,0,1:T(8,128)} %multiply_reduce_fusion) | data formatting | bytes 1048576 | tf_op jit(solution)/shard_map/reduce_sum | solution.py:228
  36.8 1.9 %fusion.276 = (f32[256,2,2,64]{0,3,2,1:T(8,128)}, f32[256,2,2,64]{0,3,2,1:T(8,128)}) fusion(f32[256,2,2,128]{0,3,2,1:T(8,128)} %bitcast.369), kind=kLoop, calls=%fused_computation.417 | loop fusion | bytes 1048576 | tf_op jit(solution)/shard_map/slice | solution.py:25
  38.7 2.0 %copy.197 = f32[256,2,2,64]{3,0,1,2:T(8,128)} copy(f32[256,2,2,64]{0,3,2,1:T(8,128)} %get-tuple-element.94) | data formatting | bytes 524288
  40.7 2.0 %copy.196 = f32[256,2,2,64]{3,0,1,2:T(8,128)} copy(f32[256,2,2,64]{0,3,2,1:T(8,128)} %get-tuple-element.95) | data formatting | bytes 524288
  45.9 1.5 collective-permute-start.6
  47.9 1.7 fusion.277
  49.6 1.7 %copy.199 = f32[256,2,64]{2,0,1:T(8,128)} copy(f32[256,2,64]{0,2,1:T(8,128)} %get-tuple-element.96) | data formatting | bytes 262144
  51.4 1.7 %copy.198 = f32[256,2,64]{2,0,1:T(8,128)} copy(f32[256,2,64]{0,2,1:T(8,128)} %get-tuple-element.97) | data formatting | bytes 262144
  55.5 1.5 collective-permute-start.7
  57.1 2.1 %fusion.59 = f32[2,256,2,128]{3,1,2,0:T(8,128)} fusion(bf16[256,2,128,1]{0,2,3,1:T(8,128)(2,1)} %bitcast.372, f32[2,256,2,256]{1,3,2,0:T(8,128)S(1)} %get-tuple-element.118, f32[2,256,2]{1,2,0:T(2,128)S(1)} %get-tuple-element.23), kind=kOutput, calls=%fused_computation.90 | convolution fusion | flops 67633152 | bytes 1708032 | tf_op jit(solution)/shard_map/hnkt,thc->hnkc/dot_general | solution.py:263
  61.4 2.0 %fusion.35 = f32[2,256,2]{1,2,0:T(2,128)} fusion(f32[2,256,2,256]{1,3,2,0:T(8,128)} %copy-done.3, f32[2,256,2]{1,2,0:T(2,128)S(1)} %get-tuple-element.23), kind=kLoop, calls=%fused_computation.64 | loop fusion | flops 523264 | bytes 1056768 | tf_op jit(solution)/shard_map/reduce_sum | solution.py:262
  64.4 2.9 %collective-permute-done.4 = bf16[512,256]{1,0:T(8,128)(2,1)S(1)} collective-permute-done((bf16[512,256]{1,0:T(8,128)(2,1)}, bf16[512,256]{1,0:T(8,128)(2,1)S(1)}, u32[]{:S(2)}, u32[]{:S(2)}) %collective-permute-start.4) | collective-permute-done | bytes 262176 | tf_op jit(solution)/shard_map/ppermute | solution.py:121
  71.1 2.6 %collective-permute-done.5 = bf16[512,256]{1,0:T(8,128)(2,1)S(1)} collective-permute-done((bf16[512,256]{1,0:T(8,128)(2,1)S(1)}, bf16[512,256]{1,0:T(8,128)(2,1)S(1)}, u32[]{:S(2)}, u32[]{:S(2)}) %collective-permute-start.5) | collective-permute-done | bytes 262176 | tf_op jit(solution)/shard_map/ppermute | solution.py:121
  73.7 2.7 %collective-permute-done.9 = bf16[512,256]{1,0:T(8,128)(2,1)S(1)} collective-permute-done((bf16[512,256]{1,0:T(8,128)(2,1)S(1)}, bf16[512,256]{1,0:T(8,128)(2,1)S(1)}, u32[]{:S(2)}, u32[]{:S(2)}) %collective-permute-start.9) | collective-permute-done | bytes 262176 | tf_op jit(solution)/shard_map/ppermute | solution.py:117
  78.4 11.8 %shard_map.127 = (f32[8,2,1,512]{3,2,1,0:T(1,128)S(1)}, f32[8,2,1,512]{3,2,1,0:T(1,128)S(1)}, f32[8,2,128,512]{3,2,1,0:T(8,128)S(1)}) custom-call(s32[16]{0:T(128)S(1)} %and_select_fusion.offset_ref, s32[16]{0:T(128)S(1)} %broadcast_add_fusion.owner_ref, s32[16]{0:T(128)S(1)} %subtract_clamp_fusion.valid_ref, ...), custom_call_target="tpu_custom_call" | custom-call | tf_op jit(solution)/shard_map/pallas_call | solution.py:179
  91.4 1.5 pad_maximum_fusion
  92.9 5.4 %all-to-all-start = ((bf16[8,264,512]{2,1,0:T(8,128)(2,1)}), bf16[8,264,512]{2,1,0:T(8,128)(2,1)}, u32[]{:S(2)}, u32[]{:S(2)}) async-start(bf16[8,264,512]{2,1,0:T(8,128)(2,1)} %pad_maximum_fusion), calls=%async_computation | async-start | bytes 4325376 | tf_op jit(solution)/shard_map/all_to_all | solution.py:300
  100.3 44.5 %all-to-all-done = bf16[8,264,512]{2,1,0:T(8,128)(2,1)} async-done(((bf16[8,264,512]{2,1,0:T(8,128)(2,1)}), bf16[8,264,512]{2,1,0:T(8,128)(2,1)}, u32[]{:S(2)}, u32[]{:S(2)}) %all-to-all-start) | async-done | bytes 2162720 | tf_op jit(solution)/shard_map/all_to_all | solution.py:300
  146.1 2.9 %fusion = f32[256,512]{1,0:T(8,128)} fusion(bf16[8,264,512]{2,1,0:T(8,128)(2,1)} %all-to-all-done, f32[8,2,512]{2,1,0:T(2,128)S(1)} %get-tuple-element.85), kind=kLoop, calls=%fused_computation.5 | loop fusion | flops 3014656 | bytes 2654208 | tf_op jit(solution)/shard_map/reduce_sum | solution.py:315
  153.0 1.8 %convolution_multiply_fusion.13 = f32[64,2048]{1,0:T(8,128)S(1)} fusion(bf16[4,256,2048]{2,1,0:T(8,128)(2,1)} %param.19, f32[64]{0:T(128)S(1)} %get-tuple-element.77, pred[64]{0:T(512)(128)(4,1)S(1)} %copy-done.48, pred[64]{0:T(512)(128)(4,1)S(1)} %copy-done.47, bf16[256,2,256]{0,2,1:T(8,128)(2,1)S(1)} %bitcast.348), kind=kOutput, calls=%fused_computation.20 | convolution fusion | flops 67272704 | bytes 1705472 | tf_op jit(solution)/shard_map/dot_general | solution.py:341
  154.8 1.6 convolution_multiply_fusion.12
  156.5 1.6 convolution_multiply_fusion.14
  160.2 1.5 collective-permute-start.11
  163.6 1.5 collective-permute-start.12
  166.5 3.1 %collective-permute-done.11 = bf16[64,2048]{1,0:T(8,128)(2,1)S(1)} collective-permute-done((bf16[64,2048]{1,0:T(8,128)(2,1)S(1)}, bf16[64,2048]{1,0:T(8,128)(2,1)S(1)}, u32[]{:S(2)}, u32[]{:S(2)}) %collective-permute-start.11) | collective-permute-done | bytes 262176 | tf_op jit(solution)/shard_map/ppermute | solution.py:103
  169.5 2.4 %collective-permute-done.12 = bf16[64,2048]{1,0:T(8,128)(2,1)S(1)} collective-permute-done((bf16[64,2048]{1,0:T(8,128)(2,1)S(1)}, bf16[64,2048]{1,0:T(8,128)(2,1)S(1)}, u32[]{:S(2)}, u32[]{:S(2)}) %collective-permute-start.12) | collective-permute-done | bytes 262176 | tf_op jit(solution)/shard_map/ppermute | solution.py:103
  (212 shorter events, 51.4 us)
Async XLA Ops:
  0.0 30.0 %copy-start = (bf16[2,2048,256]{2,1,0:T(8,128)(2,1)S(1)}, bf16[2,2048,256]{2,1,0:T(8,128)(2,1)}, u32[]{:S(2)}) copy-start(bf16[2,2048,256]{2,1,0:T(8,128)(2,1)} %param.18) | copy-start | bytes 6291460
  3.8 24.8 %collective-permute-start.2 = (bf16[64,2048]{1,0:T(8,128)(2,1)}, bf16[64,2048]{1,0:T(8,128)(2,1)}, u32[]{:S(2)}, u32[]{:S(2)}) collective-permute-start(bf16[64,2048]{1,0:T(8,128)(2,1)} %fusion.56), channel_id=1, source_target_pairs={{0,8},{8,16},{16,24},{24,0},{1,9},{9,17},{17,25},{25,1},{2,10},{10... | collective-permute-start | bytes 786440 | tf_op jit(solution)/shard_map/ppermute | solution.py:93
  4.2 24.4 %collective-permute-start.1 = (bf16[64,2048]{1,0:T(8,128)(2,1)}, bf16[64,2048]{1,0:T(8,128)(2,1)}, u32[]{:S(2)}, u32[]{:S(2)}) collective-permute-start(bf16[64,2048]{1,0:T(8,128)(2,1)} %fusion.56), channel_id=1, source_target_pairs={{0,16},{8,24},{16,0},{24,8},{1,17},{9,25},{17,1},{25,9},{2,18},{10... | collective-permute-start | bytes 786440 | tf_op jit(solution)/shard_map/ppermute | solution.py:93
  6.8 21.8 %collective-permute-start = (bf16[64,2048]{1,0:T(8,128)(2,1)}, bf16[64,2048]{1,0:T(8,128)(2,1)}, u32[]{:S(2)}, u32[]{:S(2)}) collective-permute-start(bf16[64,2048]{1,0:T(8,128)(2,1)} %fusion.56), channel_id=1, source_target_pairs={{0,24},{8,0},{16,8},{24,16},{1,25},{9,1},{17,9},{25,17},{2,26},{10... | collective-permute-start | bytes 786440 | tf_op jit(solution)/shard_map/ppermute | solution.py:93
  28.5 14.1 %copy-start.8 = (f32[256,64]{1,0:T(8,128)}, f32[256,64]{1,0:T(8,128)S(1)}, u32[]{:S(2)}) copy-start(f32[256,64]{1,0:T(8,128)S(1)} %get-tuple-element.113) | copy-start | bytes 196612
  28.5 14.1 %copy-start.9 = (f32[256,64]{1,0:T(8,128)}, f32[256,64]{1,0:T(8,128)S(1)}, u32[]{:S(2)}) copy-start(f32[256,64]{1,0:T(8,128)S(1)} %get-tuple-element.114) | copy-start | bytes 196612
  45.9 9.6 %collective-permute-start.6 = (bf16[512,256]{1,0:T(8,128)(2,1)}, bf16[512,256]{1,0:T(8,128)(2,1)}, u32[]{:S(2)}, u32[]{:S(2)}) collective-permute-start(bf16[512,256]{1,0:T(8,128)(2,1)} %bitcast.343), channel_id=1, source_target_pairs={{0,1},{1,3},{3,5},{5,7},{7,6},{6,4},{4,2},{2,0},{8,9},{9,11},{11,1... | collective-permute-start | bytes 786440 | tf_op jit(solution)/shard_map/ppermute | solution.py:117
  47.4 12.9 %collective-permute-start.3 = (bf16[512,256]{1,0:T(8,128)(2,1)}, bf16[512,256]{1,0:T(8,128)(2,1)}, u32[]{:S(2)}, u32[]{:S(2)}) collective-permute-start(bf16[512,256]{1,0:T(8,128)(2,1)} %bitcast.343), channel_id=1, source_target_pairs={{1,0},{3,1},{5,3},{7,5},{6,7},{4,6},{2,4},{0,2},{9,8},{11,9},{13,1... | collective-permute-start | bytes 786440 | tf_op jit(solution)/shard_map/ppermute | solution.py:121
  55.5 7.8 %collective-permute-start.7 = (bf16[512,256]{1,0:T(8,128)(2,1)}, bf16[512,256]{1,0:T(8,128)(2,1)}, u32[]{:S(2)}, u32[]{:S(2)}) collective-permute-start(bf16[512,256]{1,0:T(8,128)(2,1)} %collective-permute-done.6), channel_id=1, source_target_pairs={{0,1},{1,3},{3,5},{5,7},{7,6},{6,4},{4,2},{2,0},{8,9},{9,11},{11,1... | collective-permute-start | bytes 786440 | tf_op jit(solution)/shard_map/ppermute | solution.py:117
  60.3 18.1 %copy-start.1 = (bf16[16,128,256]{2,1,0:T(8,128)(2,1)S(1)}, bf16[16,128,256]{2,1,0:T(8,128)(2,1)}, u32[]{:S(2)}) copy-start(bf16[16,128,256]{2,1,0:T(8,128)(2,1)} %get-tuple-element.89.k_ref) | copy-start | bytes 3145732
  60.3 7.0 %collective-permute-start.4 = (bf16[512,256]{1,0:T(8,128)(2,1)}, bf16[512,256]{1,0:T(8,128)(2,1)S(1)}, u32[]{:S(2)}, u32[]{:S(2)}) collective-permute-start(bf16[512,256]{1,0:T(8,128)(2,1)} %collective-permute-done.3), channel_id=1, source_target_pairs={{1,0},{3,1},{5,3},{7,5},{6,7},{4,6},{2,4},{0,2},{9,8},{11,9},{13,1... | collective-permute-start | bytes 786440 | tf_op jit(solution)/shard_map/ppermute | solution.py:121
  63.4 6.7 %collective-permute-start.8 = (bf16[512,256]{1,0:T(8,128)(2,1)}, bf16[512,256]{1,0:T(8,128)(2,1)S(1)}, u32[]{:S(2)}, u32[]{:S(2)}) collective-permute-start(bf16[512,256]{1,0:T(8,128)(2,1)} %collective-permute-done.7), channel_id=1, source_target_pairs={{0,1},{1,3},{3,5},{5,7},{7,6},{6,4},{4,2},{2,0},{8,9},{9,11},{11,1... | collective-permute-start | bytes 786440 | tf_op jit(solution)/shard_map/ppermute | solution.py:117
  67.3 6.4 %collective-permute-start.5 = (bf16[512,256]{1,0:T(8,128)(2,1)S(1)}, bf16[512,256]{1,0:T(8,128)(2,1)S(1)}, u32[]{:S(2)}, u32[]{:S(2)}) collective-permute-start(bf16[512,256]{1,0:T(8,128)(2,1)S(1)} %collective-permute-done.4), channel_id=1, source_target_pairs={{1,0},{3,1},{5,3},{7,5},{6,7},{4,6},{2,4},{0,2},{9,8},{11,9},{13,1... | collective-permute-start | bytes 786440 | tf_op jit(solution)/shard_map/ppermute | solution.py:121
  70.1 6.4 %collective-permute-start.9 = (bf16[512,256]{1,0:T(8,128)(2,1)S(1)}, bf16[512,256]{1,0:T(8,128)(2,1)S(1)}, u32[]{:S(2)}, u32[]{:S(2)}) collective-permute-start(bf16[512,256]{1,0:T(8,128)(2,1)S(1)} %collective-permute-done.8), channel_id=1, source_target_pairs={{0,1},{1,3},{3,5},{5,7},{7,6},{6,4},{4,2},{2,0},{8,9},{9,11},{11,1... | collective-permute-start | bytes 786440 | tf_op jit(solution)/shard_map/ppermute | solution.py:117
  91.4 8.3 %copy-start.5 = (bf16[4,64,2048]{2,1,0:T(8,128)(2,1)S(1)}, bf16[4,64,2048]{2,1,0:T(8,128)(2,1)}, u32[]{:S(2)}) copy-start(bf16[4,64,2048]{2,1,0:T(8,128)(2,1)} %copy-done.4) | copy-start | bytes 3145732
  91.4 8.3 %copy-start.15 = (bf16[2048,4]{0,1:T(4,128)(2,1)S(1)}, bf16[2048,4]{0,1:T(4,128)(2,1)}, u32[]{:S(2)}) copy-start(bf16[2048,4]{0,1:T(4,128)(2,1)} %param.15) | copy-start | bytes 49156
  91.4 8.7 %copy-start.14 = (s32[256,2]{0,1:T(2,128)S(1)}, s32[256,2]{0,1:T(2,128)}, u32[]{:S(2)}) copy-start(s32[256,2]{0,1:T(2,128)} %copy-done.13) | copy-start | bytes 6148
  91.4 8.8 %copy-start.11 = (f32[256,2,4]{0,1,2:T(2,128)S(1)}, f32[256,2,4]{0,1,2:T(2,128)}, u32[]{:S(2)}) copy-start(f32[256,2,4]{0,1,2:T(2,128)} %copy-done.10) | copy-start | bytes 24580
  92.9 51.9 %all-to-all-start = ((bf16[8,264,512]{2,1,0:T(8,128)(2,1)}), bf16[8,264,512]{2,1,0:T(8,128)(2,1)}, u32[]{:S(2)}, u32[]{:S(2)}) async-start(bf16[8,264,512]{2,1,0:T(8,128)(2,1)} %pad_maximum_fusion), calls=%async_computation | async-start | bytes 4325376 | tf_op jit(solution)/shard_map/all_to_all | solution.py:300
  98.4 53.9 %copy-start.16 = (f32[2,256,2]{1,2,0:T(2,128)S(1)}, f32[2,256,2]{1,2,0:T(2,128)}, u32[]{:S(2)}) copy-start(f32[2,256,2]{1,2,0:T(2,128)} %fusion.35) | copy-start | bytes 12292
  99.7 53.3 %copy-start.47 = (pred[64]{0:T(512)(128)(4,1)S(1)}, pred[64]{0:T(512)(128)(4,1)}, u32[]{:S(2)}) copy-start(pred[64]{0:T(512)(128)(4,1)} %get-tuple-element.44) | copy-start | bytes 196
  99.7 53.4 %copy-start.48 = (pred[64]{0:T(512)(128)(4,1)S(1)}, pred[64]{0:T(512)(128)(4,1)}, u32[]{:S(2)}) copy-start(pred[64]{0:T(512)(128)(4,1)} %get-tuple-element.47) | copy-start | bytes 196
  100.0 52.3 %copy-start.7 = (f32[2,256,2,128]{3,1,2,0:T(8,128)S(1)}, f32[2,256,2,128]{3,1,2,0:T(8,128)}, u32[]{:S(2)}) copy-start(f32[2,256,2,128]{3,1,2,0:T(8,128)} %fusion.59) | copy-start | bytes 1572868
  145.8 9.0 %copy-start.45 = (pred[64]{0:T(512)(128)(4,1)S(1)}, pred[64]{0:T(512)(128)(4,1)}, u32[]{:S(2)}) copy-start(pred[64]{0:T(512)(128)(4,1)} %get-tuple-element.45) | copy-start | bytes 196
  145.8 9.0 %copy-start.46 = (pred[64]{0:T(512)(128)(4,1)S(1)}, pred[64]{0:T(512)(128)(4,1)}, u32[]{:S(2)}) copy-start(pred[64]{0:T(512)(128)(4,1)} %get-tuple-element.48) | copy-start | bytes 196
  146.1 10.4 %copy-start.43 = (pred[64]{0:T(512)(128)(4,1)S(1)}, pred[64]{0:T(512)(128)(4,1)}, u32[]{:S(2)}) copy-start(pred[64]{0:T(512)(128)(4,1)} %get-tuple-element.43) | copy-start | bytes 196
  146.1 10.4 %copy-start.44 = (pred[64]{0:T(512)(128)(4,1)S(1)}, pred[64]{0:T(512)(128)(4,1)}, u32[]{:S(2)}) copy-start(pred[64]{0:T(512)(128)(4,1)} %get-tuple-element.46) | copy-start | bytes 196
  149.0 9.2 %copy-start.41 = (pred[64]{0:T(512)(128)(4,1)S(1)}, pred[64]{0:T(512)(128)(4,1)}, u32[]{:S(2)}) copy-start(pred[64]{0:T(512)(128)(4,1)} %get-tuple-element.100) | copy-start | bytes 196
  149.0 9.3 %copy-start.42 = (pred[64]{0:T(512)(128)(4,1)S(1)}, pred[64]{0:T(512)(128)(4,1)}, u32[]{:S(2)}) copy-start(pred[64]{0:T(512)(128)(4,1)} %get-tuple-element.101) | copy-start | bytes 196
  158.7 7.8 %collective-permute-start.10 = (bf16[64,2048]{1,0:T(8,128)(2,1)S(1)}, bf16[64,2048]{1,0:T(8,128)(2,1)S(1)}, u32[]{:S(2)}, u32[]{:S(2)}) collective-permute-start(bf16[64,2048]{1,0:T(8,128)(2,1)S(1)} %fusion.16), channel_id=1, source_target_pairs={{0,8},{8,16},{16,24},{24,0},{1,9},{9,17},{17,25},{25,1},{2,10},{10... | collective-permute-start | bytes 786440 | tf_op jit(solution)/shard_map/ppermute | solution.py:103
  160.2 9.3 %collective-permute-start.11 = (bf16[64,2048]{1,0:T(8,128)(2,1)S(1)}, bf16[64,2048]{1,0:T(8,128)(2,1)S(1)}, u32[]{:S(2)}, u32[]{:S(2)}) collective-permute-start(bf16[64,2048]{1,0:T(8,128)(2,1)S(1)} %fusion.15), channel_id=1, source_target_pairs={{0,16},{8,24},{16,0},{24,8},{1,17},{9,25},{17,1},{25,9},{2,18},{10... | collective-permute-start | bytes 786440 | tf_op jit(solution)/shard_map/ppermute | solution.py:103
  163.6 8.4 %collective-permute-start.12 = (bf16[64,2048]{1,0:T(8,128)(2,1)S(1)}, bf16[64,2048]{1,0:T(8,128)(2,1)S(1)}, u32[]{:S(2)}, u32[]{:S(2)}) collective-permute-start(bf16[64,2048]{1,0:T(8,128)(2,1)S(1)} %fusion.14), channel_id=1, source_target_pairs={{0,24},{8,0},{16,8},{24,16},{1,25},{9,1},{17,9},{25,17},{2,26},{10... | collective-permute-start | bytes 786440 | tf_op jit(solution)/shard_map/ppermute | solution.py:103
  (32 other events, 107.8 us)

commit v13 on v12

--- a/solution.py
+++ b/solution.py
@@ -232,10 +232,12 @@
     fresh = jnp.einsum("nd,sdc->snc", gathered, kv_weight, preferred_element_type=jnp.float32)
     new_keys = rotate(fresh[0].reshape(new_count, local_heads, HD), positions).astype(jnp.bfloat16)
     new_values = fresh[1].reshape(new_count, local_heads, HD).astype(jnp.bfloat16)
-    ring_queries = ring_all_gather(
-        queries.reshape(new_count * 2, local_heads * HD), "seq", cycle
-    )
-    request_count = ring_queries.shape[0]
+    query_table = queries.reshape(new_count * 2, local_heads * HD)
+    ring_by_head = [
+        ring_all_gather(query_table[:, h * HD:(h + 1) * HD], "seq", cycle)
+        for h in range(local_heads)
+    ]
+    request_count = ring_by_head[0].shape[0]
     ring_size = len(cycle)
     position_of = np.argsort(np.asarray(cycle))
     position = jnp.asarray(position_of, dtype=jnp.int32)[seq_rank]
@@ -266,55 +268,68 @@
         new_values,
         preferred_element_type=jnp.float32,
     )
-    ring_queries, self_best, self_total, self_accum = lax.optimization_barrier(
-        (ring_queries, self_best, self_total, self_accum)
-    )
+    first_ring, self_best, self_total, self_accum = lax.optimization_barrier(
+        (ring_by_head[0], self_best, self_total, self_accum)
+    )
+    ring_by_head = [first_ring] + ring_by_head[1:]
     owner_offset = (jnp.asarray(position_of, dtype=jnp.int32)[owner] - position) % ring_size
     valid = jnp.clip(cached_len[owner] - ordinal * block_size, 0, block_size).astype(jnp.int32)
     query_rows = new_count * 2
-    request_best, totals, accum = block_attention(
-        ring_queries,
-        kv_cache[0],
-        jnp.swapaxes(kv_cache[1], 1, 2),
-        owner_offset,
-        owner,
-        valid,
-        request_count,
-    )
-    request_best = request_best[:, :, 0]
-    best_hi, best_lo = split_bf16(request_best)
-    request_ref = best_hi + best_lo
-    present = request_best > 0.5 * NEG_FILL
-    adjust = jnp.exp(jnp.where(present, request_best - request_ref, 0.0))
-    totals = totals[:, :, 0] * adjust
-    accum = accum * adjust[:, :, None, :]
-    totals_hi, totals_lo = split_bf16(totals)
-    stats = jnp.stack([best_hi, best_lo, totals_hi, totals_lo], axis=1).astype(jnp.bfloat16)
-    payload = jnp.concatenate(
-        [
-            accum.astype(jnp.bfloat16).reshape(request_count, -1, query_rows),
-            stats.reshape(request_count, -1, query_rows),
-        ],
-        axis=1,
-    )
-    received = lax.all_to_all(payload, "seq", 0, 0, tiled=True)
-    acc_rows = local_heads * HD
-    sources = received.shape[0]
-    part_accum = received[:, :acc_rows].astype(jnp.float32).reshape(
-        sources, local_heads, HD, query_rows
-    )
-    part_stats = received[:, acc_rows:].astype(jnp.float32).reshape(
-        sources, 4, local_heads, query_rows
-    )
-    part_best = part_stats[:, 0] + part_stats[:, 1]
-    part_totals = part_stats[:, 2] + part_stats[:, 3]
-    cache_best = jnp.max(part_best, axis=0)
-    share = jnp.exp(part_best - cache_best[None])
-    cache_total = jnp.sum(part_totals * share, axis=0).reshape(local_heads, new_count, 2)
-    cache_accum = jnp.transpose(
-        jnp.sum(part_accum * share[:, :, None, :], axis=0), (0, 2, 1)
-    ).reshape(local_heads, new_count, 2, HD)
-    cache_best = cache_best.reshape(local_heads, new_count, 2)
+    values_t = jnp.swapaxes(kv_cache[1], 1, 2)
+
+    def head_payload(head, head_queries):
+        request_best, totals, accum = block_attention(
+            head_queries,
+            kv_cache[0][:, :, head * HD:(head + 1) * HD],
+            values_t[:, head * HD:(head + 1) * HD],
+            owner_offset,
+            owner,
+            valid,
+            request_count,
+        )
+        request_best = request_best[:, :, 0]
+        best_hi, best_lo = split_bf16(request_best)
+        request_ref = best_hi + best_lo
+        present = request_best > 0.5 * NEG_FILL
+        adjust = jnp.exp(jnp.where(present, request_best - request_ref, 0.0))
+        totals = totals[:, :, 0] * adjust
+        accum = accum * adjust[:, :, None, :]
+        totals_hi, totals_lo = split_bf16(totals)
+        stats = jnp.stack([best_hi, best_lo, totals_hi, totals_lo], axis=1).astype(jnp.bfloat16)
+        return jnp.concatenate(
+            [
+                accum.astype(jnp.bfloat16).reshape(request_count, -1, query_rows),
+                stats.reshape(request_count, -1, query_rows),
+            ],
+            axis=1,
+        )
+
+    def head_parts(received):
+        sources = received.shape[0]
+        part_accum = received[:, :HD].astype(jnp.float32)
+        part_stats = received[:, HD:].astype(jnp.float32).reshape(sources, 4, query_rows)
+        part_best = part_stats[:, 0] + part_stats[:, 1]
+        part_totals = part_stats[:, 2] + part_stats[:, 3]
+        best = jnp.max(part_best, axis=0)
+        share = jnp.exp(part_best - best[None])
+        total = jnp.sum(part_totals * share, axis=0)
+        accum = jnp.sum(part_accum * share[:, None, :], axis=0)
+        return best, total, accum
+
+    head_results = []
+    pending = ring_by_head
+    for head in range(local_heads):
+        payload = head_payload(head, pending[head])
+        if head + 1 < local_heads:
+            payload, next_queries = lax.optimization_barrier((payload, pending[head + 1]))
+            pending = pending[: head + 1] + [next_queries] + pending[head + 2:]
+        received = lax.all_to_all(payload, "seq", 0, 0, tiled=True)
+        head_results.append(head_parts(received))
+    cache_best = jnp.stack([r[0] for r in head_results]).reshape(local_heads, new_count, 2)
+    cache_total = jnp.stack([r[1] for r in head_results]).reshape(local_heads, new_count, 2)
+    cache_accum = jnp.transpose(jnp.stack([r[2] for r in head_results]), (0, 2, 1)).reshape(
+        local_heads, new_count, 2, HD
+    )
 
     peak = jnp.maximum(cache_best, self_best)
     cache_share = jnp.exp(cache_best - peak)

time: 174 us -> 191 us (1.098)
  local copies, waits for them, and re-layouts: 36.4 us -> 51.1 us
  waiting for transfers between devices: 58.9 us -> 44.2 us
  starting transfers between devices: 20.6 us -> 28.1 us
  other arithmetic: 28.3 us -> 32.1 us
  Pallas kernels: 11.8 us -> 14.8 us
    all_to_all x1 -> x2, waiting for transfers between devices: 44.5 us -> 30.3 us  [per_device(): received = lax.all_to_all(payload, 'seq', 0, 0, tiled=True)]
    concatenate x0 -> x2, local copies, waits for them, and re-layouts: none -> 9.39 us  [head_payload(): jnp.concatenate([accum.astype(jnp.bfloat16).reshape(request_count, -1, qu...]
    ppermute x3 -> x6, starting transfers between devices: 2.64 us -> 9.49 us  [ring_all_gather(): moving = lax.ppermute(moving, axis_name, backward)]
    ppermute x3 -> x6, waiting for transfers between devices: 5.52 us -> 0.02 us  [ring_all_gather(): moving = lax.ppermute(moving, axis_name, backward)]
    unnamed x115 -> x146, local copies, waits for them, and re-layouts: 14.1 us -> 19.4 us
    ppermute x4 -> x8, waiting for transfers between devices: 3.46 us -> 8.58 us  [ring_all_gather(): moving = lax.ppermute(moving, axis_name, forward)]
    all_to_all x1 -> x2, starting transfers between devices: 5.42 us -> 8.53 us  [per_device(): received = lax.all_to_all(payload, 'seq', 0, 0, tiled=True)]
    slice x1 -> x3, local copies, waits for them, and re-layouts: 3.13 us -> 6.21 us  [the longest x1 2.77 us: head_payload(): values_t[:, head * HD:(head + 1) * HD]]
  transfers between devices with their start and end apart: 14 -> 22, of which waited for: 7 -> 7; matrix products, arithmetic and copies ran while one was open for 23% -> 30% of each run, Pallas kernels for 0% -> 8%
where the time goes in v13:
time: 191 us; the launch traced here: 188 us
  local copies, waits for them, and re-layouts  51.1 us (27%)
  waiting for transfers between devices  44.2 us (23%)
  other arithmetic  32.1 us (17%)
  starting transfers between devices  28.1 us (15%)
  matrix products  16.9 us (9%)
  Pallas kernels  14.8 us (8%)
    all_to_all x2, waiting for transfers between devices, per_device(): received = lax.all_to_all(payload, 'seq', 0, 0, tiled=True)  30.3 us
    unnamed x146, local copies, waits for them, and re-layouts  19.4 us
    pallas_call x2, Pallas kernels, block_attention(): pl.pallas_call(kernel, grid_spec=grid_spec, out_shape=[jax.ShapeDtypeStru...  14.8 us
    dot_general x16, matrix products, per_device(): jnp.dot(picked, o_weight[expert], preferred_element_type=jnp.float32)  9.75 us
    ppermute x6, starting transfers between devices, ring_all_gather(): moving = lax.ppermute(moving, axis_name, backward)  9.49 us
    concatenate x2, local copies, waits for them, and re-layouts, head_payload(): jnp.concatenate([accum.astype(jnp.bfloat16).reshape(request_count, -1, qu...  9.39 us
    ppermute x8, waiting for transfers between devices, ring_all_gather(): moving = lax.ppermute(moving, axis_name, forward)  8.58 us
    all_to_all x2, starting transfers between devices, per_device(): received = lax.all_to_all(payload, 'seq', 0, 0, tiled=True)  8.53 us
  transfers between devices with their start and end apart: 22, of which 7 were waited for; matrix products, arithmetic and copies ran while one was open for 30% of the time, Pallas kernels for 8%

profile of v13, /device:TPU:0, one launch (start us, length us, event | category | flops | bytes accessed | tf_op | source)
XLA Modules:
  0.0 188.5 jit_solution(6011697243868155305)
XLA Ops:
  2.0 1.8 fusion.57
  4.2 2.5 %collective-permute-start.1 = (bf16[64,2048]{1,0:T(8,128)(2,1)}, bf16[64,2048]{1,0:T(8,128)(2,1)}, u32[]{:S(2)}, u32[]{:S(2)}) collective-permute-start(bf16[64,2048]{1,0:T(8,128)(2,1)} %fusion.57), channel_id=1, source_target_pairs={{0,16},{8,24},{16,0},{24,8},{1,17},{9,25},{17,1},{25,9},{2,18},{10... | collective-permute-start | bytes 786440 | tf_op jit(solution)/shard_map/ppermute | solution.py:93
  16.1 1.8 fusion.59
  20.3 2.7 %fusion.277 = (bf16[1,16,128,256]{3,2,1,0:T(8,128)(2,1)S(1)}, bf16[16,128,256]{2,1,0:T(8,128)(2,1)}) fusion(bf16[2,16,128,256]{3,2,1,0:T(8,128)(2,1)} %param.20), kind=kLoop, calls=%fused_computation.439 | loop fusion | bytes 4194304 | tf_op jit(solution)/shard_map/slice | solution.py:278
  25.0 2.8 %fusion.278 = (bf16[16,128,128]{2,1,0:T(8,128)(2,1)S(1)}, bf16[16,128,128]{2,1,0:T(8,128)(2,1)}, bf16[16,128,128]{2,1,0:T(8,128)(2,1)}, bf16[16,128,128]{2,1,0:T(8,128)(2,1)S(1)}) fusion(bf16[16,256,128]{2,1,0:T(8,128)(2,1)} %bitcast.373, bf16[16,128,256]{2,1,0:T(8,128)(2,1)} %get-tuple-element.99), kind=kLoop, calls=%fused_computation.440 | loop fusion | bytes 4194304 | tf_op jit(solution)/shard_map/slice | solution.py:284
  28.4 1.7 pad_maximum_fusion
  34.9 2.0 %copy.359 = f32[256,2,256]{0,2,1:T(8,128)} copy(f32[256,2,256]{2,0,1:T(8,128)} %multiply_reduce_fusion.2) | data formatting | bytes 1048576 | tf_op jit(solution)/shard_map/reduce_sum | solution.py:228
  37.0 1.9 fusion.280
  38.8 1.9 %copy.415 = f32[256,2,2,64]{3,0,1,2:T(8,128)} copy(f32[256,2,2,64]{0,3,2,1:T(8,128)} %get-tuple-element.108) | data formatting | bytes 524288
  40.8 2.0 %copy.414 = f32[256,2,2,64]{3,0,1,2:T(8,128)} copy(f32[256,2,2,64]{0,3,2,1:T(8,128)} %get-tuple-element.109) | data formatting | bytes 524288
  50.8 1.7 copy.417
  52.6 1.7 copy.416
  56.9 2.1 %fusion.60 = f32[2,256,2,128]{3,1,2,0:T(8,128)} fusion(bf16[256,2,128,1]{0,2,3,1:T(8,128)(2,1)} %bitcast.382, f32[2,256,2,256]{1,3,2,0:T(8,128)S(1)} %get-tuple-element.148, f32[2,256,2]{1,2,0:T(2,128)S(1)} %get-tuple-element.33), kind=kOutput, calls=%fused_computation.92 | convolution fusion | flops 67633152 | bytes 1708032 | tf_op jit(solution)/shard_map/hnkt,thc->hnkc/dot_general | solution.py:265
  59.7 1.6 collective-permute-start.11
  61.7 1.6 collective-permute-start.4
  66.2 1.6 collective-permute-start.12
  71.0 2.0 %collective-permute-done.15 = bf16[512,128]{1,0:T(8,128)(2,1)} collective-permute-done((bf16[512,128]{1,0:T(8,128)(2,1)S(1)}, bf16[512,128]{1,0:T(8,128)(2,1)}, u32[]{:S(2)}, u32[]{:S(2)}) %collective-permute-start.15) | collective-permute-done | bytes 131104 | tf_op jit(solution)/shard_map/ppermute | solution.py:117
  73.5 2.7 %collective-permute-done.8 = bf16[512,128]{1,0:T(8,128)(2,1)S(1)} collective-permute-done((bf16[512,128]{1,0:T(8,128)(2,1)S(1)}, bf16[512,128]{1,0:T(8,128)(2,1)S(1)}, u32[]{:S(2)}, u32[]{:S(2)}) %collective-permute-start.8) | collective-permute-done | bytes 131104 | tf_op jit(solution)/shard_map/ppermute | solution.py:117
  77.4 3.8 %collective-permute-done.9 = bf16[512,128]{1,0:T(8,128)(2,1)S(1)} collective-permute-done((bf16[512,128]{1,0:T(8,128)(2,1)S(1)}, bf16[512,128]{1,0:T(8,128)(2,1)S(1)}, u32[]{:S(2)}, u32[]{:S(2)}) %collective-permute-start.9) | collective-permute-done | bytes 131104 | tf_op jit(solution)/shard_map/ppermute | solution.py:117
  82.2 7.4 %shard_map.127 = (f32[8,1,1,512]{3,2,1,0:T(1,128)S(1)}, f32[8,1,1,512]{3,2,1,0:T(1,128)S(1)}, f32[8,1,128,512]{3,2,1,0:T(8,128)S(1)}) custom-call(s32[16]{0:T(128)S(1)} %and_select_fusion.offset_ref, s32[16]{0:T(128)S(1)} %broadcast_add_fusion.owner_ref, s32[16]{0:T(128)S(1)} %subtract_clamp_fusion.valid_ref, ...), custom_call_target="tpu_custom_call" | custom-call | tf_op jit(solution)/shard_map/pallas_call | solution.py:179
  91.0 5.9 %concatenate.27 = bf16[8,132,512]{2,1,0:T(8,128)(2,1)} concatenate(bf16[8,128,512]{2,1,0:T(8,128)(2,1)} %fusion.17, bf16[8,1,512]{2,1,0:T(2,128)(2,1)S(1)} %get-tuple-element.140, bf16[8,1,512]{2,1,0:T(2,128)(2,1)S(1)} %get-tuple-element.139, bf16[8,1,512]{2,1,0:T(2,128)(2,1)S(1)} %fusion.198, bf16[8,1,512]{2,1,0:T(2,128)(2,1)S(1)} %get-tuple-element.141), dimensions={1} | concatenate | bytes 2162688 | tf_op jit(solution)/shard_map/concatenate | solution.py:299
  102.3 4.8 %all-to-all-start = ((bf16[8,132,512]{2,1,0:T(8,128)(2,1)}), bf16[8,132,512]{2,1,0:T(8,128)(2,1)}, u32[]{:S(2)}, u32[]{:S(2)}) async-start(bf16[8,132,512]{2,1,0:T(8,128)(2,1)} %concatenate.27), calls=%async_computation | async-start | bytes 2228224 | tf_op jit(solution)/shard_map/all_to_all | solution.py:326
  108.3 7.4 %shard_map.128 = (f32[8,1,1,512]{3,2,1,0:T(1,128)S(1)}, f32[8,1,1,512]{3,2,1,0:T(1,128)S(1)}, f32[8,1,128,512]{3,2,1,0:T(8,128)S(1)}) custom-call(s32[16]{0:T(128)S(1)} %and_select_fusion.offset_ref, s32[16]{0:T(128)S(1)} %broadcast_add_fusion.owner_ref, s32[16]{0:T(128)S(1)} %subtract_clamp_fusion.valid_ref, bf16[8,512,128]{2,1,0:T(8,128)(2,1)S(1)} %copy-done.4, ...), custom_call_target="tpu_custom_call" | custom-call | tf_op jit(solution)/shard_map/pallas_call | solution.py:179
  116.1 3.5 %concatenate.28 = bf16[8,132,512]{2,1,0:T(8,128)(2,1)} concatenate(bf16[8,128,512]{2,1,0:T(8,128)(2,1)S(1)} %fusion.18, bf16[8,1,512]{2,1,0:T(2,128)(2,1)S(1)} %get-tuple-element.136, bf16[8,1,512]{2,1,0:T(2,128)(2,1)S(1)} %get-tuple-element.135, bf16[8,1,512]{2,1,0:T(2,128)(2,1)S(1)} %fusion.202, bf16[8,1,512]{2,1,0:T(2,128)(2,1)S(1)} %get-tuple-element.137), dimensions={1} | concatenate | bytes 2162688 | tf_op jit(solution)/shard_map/concatenate | solution.py:299
  119.6 11.3 %all-to-all-done = bf16[8,132,512]{2,1,0:T(8,128)(2,1)} async-done(((bf16[8,132,512]{2,1,0:T(8,128)(2,1)}), bf16[8,132,512]{2,1,0:T(8,128)(2,1)}, u32[]{:S(2)}, u32[]{:S(2)}) %all-to-all-start) | async-done | bytes 1081376 | tf_op jit(solution)/shard_map/all_to_all | solution.py:326
  130.9 3.7 %all-to-all-start.1 = ((bf16[8,132,512]{2,1,0:T(8,128)(2,1)}), bf16[8,132,512]{2,1,0:T(8,128)(2,1)S(1)}, u32[]{:S(2)}, u32[]{:S(2)}) async-start(bf16[8,132,512]{2,1,0:T(8,128)(2,1)} %concatenate.28), calls=%async_computation.1 | async-start | bytes 2228224 | tf_op jit(solution)/shard_map/all_to_all | solution.py:326
  136.0 1.6 fusion.286
  141.4 19.0 %all-to-all-done.1 = bf16[8,132,512]{2,1,0:T(8,128)(2,1)S(1)} async-done(((bf16[8,132,512]{2,1,0:T(8,128)(2,1)}), bf16[8,132,512]{2,1,0:T(8,128)(2,1)S(1)}, u32[]{:S(2)}, u32[]{:S(2)}) %all-to-all-start.1) | async-done | bytes 1081376 | tf_op jit(solution)/shard_map/all_to_all | solution.py:326
  169.7 1.8 convolution_multiply_fusion.13
  171.6 1.6 convolution_multiply_fusion.12
  173.3 1.6 convolution_multiply_fusion.14
  182.4 4.0 %collective-permute-done.18 = bf16[64,2048]{1,0:T(8,128)(2,1)S(1)} collective-permute-done((bf16[64,2048]{1,0:T(8,128)(2,1)S(1)}, bf16[64,2048]{1,0:T(8,128)(2,1)S(1)}, u32[]{:S(2)}, u32[]{:S(2)}) %collective-permute-start.18) | collective-permute-done | bytes 262176 | tf_op jit(solution)/shard_map/ppermute | solution.py:103
  (274 shorter events, 73.5 us)
Async XLA Ops:
  0.0 30.1 %copy-start = (bf16[2,2048,256]{2,1,0:T(8,128)(2,1)S(1)}, bf16[2,2048,256]{2,1,0:T(8,128)(2,1)}, u32[]{:S(2)}) copy-start(bf16[2,2048,256]{2,1,0:T(8,128)(2,1)} %param.18) | copy-start | bytes 6291460
  3.8 24.6 %collective-permute-start.2 = (bf16[64,2048]{1,0:T(8,128)(2,1)}, bf16[64,2048]{1,0:T(8,128)(2,1)}, u32[]{:S(2)}, u32[]{:S(2)}) collective-permute-start(bf16[64,2048]{1,0:T(8,128)(2,1)} %fusion.57), channel_id=1, source_target_pairs={{0,8},{8,16},{16,24},{24,0},{1,9},{9,17},{17,25},{25,1},{2,10},{10... | collective-permute-start | bytes 786440 | tf_op jit(solution)/shard_map/ppermute | solution.py:93
  4.2 24.2 %collective-permute-start.1 = (bf16[64,2048]{1,0:T(8,128)(2,1)}, bf16[64,2048]{1,0:T(8,128)(2,1)}, u32[]{:S(2)}, u32[]{:S(2)}) collective-permute-start(bf16[64,2048]{1,0:T(8,128)(2,1)} %fusion.57), channel_id=1, source_target_pairs={{0,16},{8,24},{16,0},{24,8},{1,17},{9,25},{17,1},{25,9},{2,18},{10... | collective-permute-start | bytes 786440 | tf_op jit(solution)/shard_map/ppermute | solution.py:93
  6.8 21.6 %collective-permute-start = (bf16[64,2048]{1,0:T(8,128)(2,1)}, bf16[64,2048]{1,0:T(8,128)(2,1)}, u32[]{:S(2)}, u32[]{:S(2)}) collective-permute-start(bf16[64,2048]{1,0:T(8,128)(2,1)} %fusion.57), channel_id=1, source_target_pairs={{0,24},{8,0},{16,8},{24,16},{1,25},{9,1},{17,9},{25,17},{2,26},{10... | collective-permute-start | bytes 786440 | tf_op jit(solution)/shard_map/ppermute | solution.py:93
  28.3 14.4 %copy-start.7 = (f32[256,64]{1,0:T(8,128)}, f32[256,64]{1,0:T(8,128)S(1)}, u32[]{:S(2)}) copy-start(f32[256,64]{1,0:T(8,128)S(1)} %get-tuple-element.143) | copy-start | bytes 196612
  28.3 14.4 %copy-start.8 = (f32[256,64]{1,0:T(8,128)}, f32[256,64]{1,0:T(8,128)S(1)}, u32[]{:S(2)}) copy-start(f32[256,64]{1,0:T(8,128)S(1)} %get-tuple-element.144) | copy-start | bytes 196612
  45.3 14.3 %collective-permute-start.10 = (bf16[512,128]{1,0:T(8,128)(2,1)}, bf16[512,128]{1,0:T(8,128)(2,1)}, u32[]{:S(2)}, u32[]{:S(2)}) collective-permute-start(bf16[512,128]{1,0:T(8,128)(2,1)} %get-tuple-element.110), channel_id=1, source_target_pairs={{1,0},{3,1},{5,3},{7,5},{6,7},{4,6},{2,4},{0,2},{9,8},{11,9},{13,1... | collective-permute-start | bytes 393224 | tf_op jit(solution)/shard_map/ppermute | solution.py:121
  46.9 14.3 %collective-permute-start.13 = (bf16[512,128]{1,0:T(8,128)(2,1)}, bf16[512,128]{1,0:T(8,128)(2,1)}, u32[]{:S(2)}, u32[]{:S(2)}) collective-permute-start(bf16[512,128]{1,0:T(8,128)(2,1)} %get-tuple-element.110), channel_id=1, source_target_pairs={{0,1},{1,3},{3,5},{5,7},{7,6},{6,4},{4,2},{2,0},{8,9},{9,11},{11,1... | collective-permute-start | bytes 393224 | tf_op jit(solution)/shard_map/ppermute | solution.py:117
  47.4 14.4 %collective-permute-start.3 = (bf16[512,128]{1,0:T(8,128)(2,1)}, bf16[512,128]{1,0:T(8,128)(2,1)}, u32[]{:S(2)}, u32[]{:S(2)}) collective-permute-start(bf16[512,128]{1,0:T(8,128)(2,1)} %get-tuple-element.111), channel_id=1, source_target_pairs={{1,0},{3,1},{5,3},{7,5},{6,7},{4,6},{2,4},{0,2},{9,8},{11,9},{13,1... | collective-permute-start | bytes 393224 | tf_op jit(solution)/shard_map/ppermute | solution.py:121
  48.9 14.4 %collective-permute-start.6 = (bf16[512,128]{1,0:T(8,128)(2,1)}, bf16[512,128]{1,0:T(8,128)(2,1)}, u32[]{:S(2)}, u32[]{:S(2)}) collective-permute-start(bf16[512,128]{1,0:T(8,128)(2,1)} %get-tuple-element.111), channel_id=1, source_target_pairs={{0,1},{1,3},{3,5},{5,7},{7,6},{6,4},{4,2},{2,0},{8,9},{9,11},{11,1... | collective-permute-start | bytes 393224 | tf_op jit(solution)/shard_map/ppermute | solution.py:117
  54.3 11.0 %copy-start.3 = (bf16[8,512,128]{2,1,0:T(8,128)(2,1)S(1)}, bf16[8,512,128]{2,1,0:T(8,128)(2,1)}, u32[]{:S(2)}) copy-start(bf16[8,512,128]{2,1,0:T(8,128)(2,1)} %get-tuple-element.113) | copy-start | bytes 3145732
  54.3 27.9 %copy-start.1 = (bf16[16,128,128]{2,1,0:T(8,128)(2,1)S(1)}, bf16[16,128,128]{2,1,0:T(8,128)(2,1)}, u32[]{:S(2)}) copy-start(bf16[16,128,128]{2,1,0:T(8,128)(2,1)} %get-tuple-element.103.v_ref) | copy-start | bytes 1572868
  54.3 27.9 %copy-start.2 = (bf16[16,128,128]{2,1,0:T(8,128)(2,1)S(1)}, bf16[16,128,128]{2,1,0:T(8,128)(2,1)}, u32[]{:S(2)}) copy-start(bf16[16,128,128]{2,1,0:T(8,128)(2,1)} %get-tuple-element.151.k_ref) | copy-start | bytes 1572868
  59.7 6.5 %collective-permute-start.11 = (bf16[512,128]{1,0:T(8,128)(2,1)}, bf16[512,128]{1,0:T(8,128)(2,1)S(1)}, u32[]{:S(2)}, u32[]{:S(2)}) collective-permute-start(bf16[512,128]{1,0:T(8,128)(2,1)} %collective-permute-done.10), channel_id=1, source_target_pairs={{1,0},{3,1},{5,3},{7,5},{6,7},{4,6},{2,4},{0,2},{9,8},{11,9},{13,1... | collective-permute-start | bytes 393224 | tf_op jit(solution)/shard_map/ppermute | solution.py:121
  61.3 6.6 %collective-permute-start.14 = (bf16[512,128]{1,0:T(8,128)(2,1)}, bf16[512,128]{1,0:T(8,128)(2,1)S(1)}, u32[]{:S(2)}, u32[]{:S(2)}) collective-permute-start(bf16[512,128]{1,0:T(8,128)(2,1)} %collective-permute-done.13), channel_id=1, source_target_pairs={{0,1},{1,3},{3,5},{5,7},{7,6},{6,4},{4,2},{2,0},{8,9},{9,11},{11,1... | collective-permute-start | bytes 393224 | tf_op jit(solution)/shard_map/ppermute | solution.py:117
  61.7 6.6 %collective-permute-start.4 = (bf16[512,128]{1,0:T(8,128)(2,1)}, bf16[512,128]{1,0:T(8,128)(2,1)S(1)}, u32[]{:S(2)}, u32[]{:S(2)}) collective-permute-start(bf16[512,128]{1,0:T(8,128)(2,1)} %collective-permute-done.3), channel_id=1, source_target_pairs={{1,0},{3,1},{5,3},{7,5},{6,7},{4,6},{2,4},{0,2},{9,8},{11,9},{13,1... | collective-permute-start | bytes 393224 | tf_op jit(solution)/shard_map/ppermute | solution.py:121
  63.3 6.6 %collective-permute-start.7 = (bf16[512,128]{1,0:T(8,128)(2,1)}, bf16[512,128]{1,0:T(8,128)(2,1)S(1)}, u32[]{:S(2)}, u32[]{:S(2)}) collective-permute-start(bf16[512,128]{1,0:T(8,128)(2,1)} %collective-permute-done.6), channel_id=1, source_target_pairs={{0,1},{1,3},{3,5},{5,7},{7,6},{6,4},{4,2},{2,0},{8,9},{9,11},{11,1... | collective-permute-start | bytes 393224 | tf_op jit(solution)/shard_map/ppermute | solution.py:117
  66.2 10.5 %collective-permute-start.12 = (bf16[512,128]{1,0:T(8,128)(2,1)S(1)}, bf16[512,128]{1,0:T(8,128)(2,1)S(1)}, u32[]{:S(2)}, u32[]{:S(2)}) collective-permute-start(bf16[512,128]{1,0:T(8,128)(2,1)S(1)} %collective-permute-done.11), channel_id=1, source_target_pairs={{1,0},{3,1},{5,3},{7,5},{6,7},{4,6},{2,4},{0,2},{9,8},{11,9},{13,1... | collective-permute-start | bytes 393224 | tf_op jit(solution)/shard_map/ppermute | solution.py:121
  67.9 5.2 %collective-permute-start.15 = (bf16[512,128]{1,0:T(8,128)(2,1)S(1)}, bf16[512,128]{1,0:T(8,128)(2,1)}, u32[]{:S(2)}, u32[]{:S(2)}) collective-permute-start(bf16[512,128]{1,0:T(8,128)(2,1)S(1)} %collective-permute-done.14), channel_id=1, source_target_pairs={{0,1},{1,3},{3,5},{5,7},{7,6},{6,4},{4,2},{2,0},{8,9},{9,11},{11,1... | collective-permute-start | bytes 393224 | tf_op jit(solution)/shard_map/ppermute | solution.py:117
  68.3 9.0 %collective-permute-start.5 = (bf16[512,128]{1,0:T(8,128)(2,1)S(1)}, bf16[512,128]{1,0:T(8,128)(2,1)S(1)}, u32[]{:S(2)}, u32[]{:S(2)}) collective-permute-start(bf16[512,128]{1,0:T(8,128)(2,1)S(1)} %collective-permute-done.4), channel_id=1, source_target_pairs={{1,0},{3,1},{5,3},{7,5},{6,7},{4,6},{2,4},{0,2},{9,8},{11,9},{13,1... | collective-permute-start | bytes 393224 | tf_op jit(solution)/shard_map/ppermute | solution.py:121
  69.9 6.3 %collective-permute-start.8 = (bf16[512,128]{1,0:T(8,128)(2,1)S(1)}, bf16[512,128]{1,0:T(8,128)(2,1)S(1)}, u32[]{:S(2)}, u32[]{:S(2)}) collective-permute-start(bf16[512,128]{1,0:T(8,128)(2,1)S(1)} %collective-permute-done.7), channel_id=1, source_target_pairs={{0,1},{1,3},{3,5},{5,7},{7,6},{6,4},{4,2},{2,0},{8,9},{9,11},{11,1... | collective-permute-start | bytes 393224 | tf_op jit(solution)/shard_map/ppermute | solution.py:117
  73.1 23.9 %collective-permute-start.16 = (bf16[512,128]{1,0:T(8,128)(2,1)}, bf16[512,128]{1,0:T(8,128)(2,1)}, u32[]{:S(2)}, u32[]{:S(2)}) collective-permute-start(bf16[512,128]{1,0:T(8,128)(2,1)} %collective-permute-done.15), channel_id=1, source_target_pairs={{0,1},{1,3},{3,5},{5,7},{7,6},{6,4},{4,2},{2,0},{8,9},{9,11},{11,1... | collective-permute-start | bytes 393224 | tf_op jit(solution)/shard_map/ppermute | solution.py:117
  76.2 5.0 %collective-permute-start.9 = (bf16[512,128]{1,0:T(8,128)(2,1)S(1)}, bf16[512,128]{1,0:T(8,128)(2,1)S(1)}, u32[]{:S(2)}, u32[]{:S(2)}) collective-permute-start(bf16[512,128]{1,0:T(8,128)(2,1)S(1)} %collective-permute-done.8), channel_id=1, source_target_pairs={{0,1},{1,3},{3,5},{5,7},{7,6},{6,4},{4,2},{2,0},{8,9},{9,11},{11,1... | collective-permute-start | bytes 393224 | tf_op jit(solution)/shard_map/ppermute | solution.py:117
  102.3 28.7 %all-to-all-start = ((bf16[8,132,512]{2,1,0:T(8,128)(2,1)}), bf16[8,132,512]{2,1,0:T(8,128)(2,1)}, u32[]{:S(2)}, u32[]{:S(2)}) async-start(bf16[8,132,512]{2,1,0:T(8,128)(2,1)} %concatenate.27), calls=%async_computation | async-start | bytes 2228224 | tf_op jit(solution)/shard_map/all_to_all | solution.py:326
  115.7 20.4 %copy-start.14 = (bf16[2048,4]{0,1:T(4,128)(2,1)S(1)}, bf16[2048,4]{0,1:T(4,128)(2,1)}, u32[]{:S(2)}) copy-start(bf16[2048,4]{0,1:T(4,128)(2,1)} %param.15) | copy-start | bytes 49156
  115.8 21.8 %copy-start.13 = (s32[256,2]{0,1:T(2,128)S(1)}, s32[256,2]{0,1:T(2,128)}, u32[]{:S(2)}) copy-start(s32[256,2]{0,1:T(2,128)} %copy-done.12) | copy-start | bytes 6148
  115.8 21.9 %copy-start.11 = (f32[256,2,4]{0,1,2:T(2,128)S(1)}, f32[256,2,4]{0,1,2:T(2,128)}, u32[]{:S(2)}) copy-start(f32[256,2,4]{0,1,2:T(2,128)} %copy-done.10) | copy-start | bytes 24580
  130.9 29.4 %all-to-all-start.1 = ((bf16[8,132,512]{2,1,0:T(8,128)(2,1)}), bf16[8,132,512]{2,1,0:T(8,128)(2,1)S(1)}, u32[]{:S(2)}, u32[]{:S(2)}) async-start(bf16[8,132,512]{2,1,0:T(8,128)(2,1)} %concatenate.28), calls=%async_computation.1 | async-start | bytes 2228224 | tf_op jit(solution)/shard_map/all_to_all | solution.py:326
  136.0 31.9 %copy-start.15 = (f32[2,256,2]{1,2,0:T(2,128)S(1)}, f32[2,256,2]{1,2,0:T(2,128)}, u32[]{:S(2)}) copy-start(f32[2,256,2]{1,2,0:T(2,128)} %fusion.36) | copy-start | bytes 12292
  175.4 6.9 %collective-permute-start.17 = (bf16[64,2048]{1,0:T(8,128)(2,1)S(1)}, bf16[64,2048]{1,0:T(8,128)(2,1)S(1)}, u32[]{:S(2)}, u32[]{:S(2)}) collective-permute-start(bf16[64,2048]{1,0:T(8,128)(2,1)S(1)} %fusion.15), channel_id=1, source_target_pairs={{0,8},{8,16},{16,24},{24,0},{1,9},{9,17},{17,25},{25,1},{2,10},{10... | collective-permute-start | bytes 786440 | tf_op jit(solution)/shard_map/ppermute | solution.py:103
  177.1 9.3 %collective-permute-start.18 = (bf16[64,2048]{1,0:T(8,128)(2,1)S(1)}, bf16[64,2048]{1,0:T(8,128)(2,1)S(1)}, u32[]{:S(2)}, u32[]{:S(2)}) collective-permute-start(bf16[64,2048]{1,0:T(8,128)(2,1)S(1)} %fusion.14), channel_id=1, source_target_pairs={{0,16},{8,24},{16,0},{24,8},{1,17},{9,25},{17,1},{25,9},{2,18},{10... | collective-permute-start | bytes 786440 | tf_op jit(solution)/shard_map/ppermute | solution.py:103
  179.4 8.2 %collective-permute-start.19 = (bf16[64,2048]{1,0:T(8,128)(2,1)S(1)}, bf16[64,2048]{1,0:T(8,128)(2,1)S(1)}, u32[]{:S(2)}, u32[]{:S(2)}) collective-permute-start(bf16[64,2048]{1,0:T(8,128)(2,1)S(1)} %fusion.13), channel_id=1, source_target_pairs={{0,24},{8,0},{16,8},{24,16},{1,25},{9,1},{17,9},{25,17},{2,26},{10... | collective-permute-start | bytes 786440 | tf_op jit(solution)/shard_map/ppermute | solution.py:103
  (52 other events, 212.5 us)

commit v14 on v12

--- a/solution.py
+++ b/solution.py
@@ -89,11 +89,9 @@
 def shift_all_gather(piece, axis_name):
     size = lax.axis_size(axis_name)
     rank = lax.axis_index(axis_name)
-    by_offset = [piece] + [
-        lax.ppermute(piece, axis_name, [(i, (i + s) % size) for i in range(size)])
-        for s in range(1, size)
-    ]
-    return jnp.stack(by_offset[:1] + by_offset[1:][::-1], axis=0)
+    copies = jnp.broadcast_to(piece[None], (size,) + piece.shape)
+    everyone = lax.all_to_all(copies, axis_name, 0, 0, tiled=True)
+    return jnp.take(everyone, (rank + jnp.arange(size, dtype=jnp.int32)) % size, axis=0)
 
 
 def shift_reduce_scatter(blocks, axis_name):

time: 174 us -> 176 us (1.011)
  other arithmetic: 28.3 us -> 24 us
  local copies, waits for them, and re-layouts: 36.4 us -> 38.5 us
  starting transfers between devices: 20.6 us -> 22.5 us
  waiting for transfers between devices: 58.9 us -> 60.7 us
    ppermute x3 -> x0, starting transfers between devices: 4.43 us -> none  [shift_all_gather(): lax.ppermute(piece, axis_name, [(i, (i + s) % size) for i in range(size)])]
    all_to_all x0 -> x1, starting transfers between devices: none -> 4.26 us  [shift_all_gather(): everyone = lax.all_to_all(copies, axis_name, 0, 0, tiled=True)]
    convert_element_type x3 -> x1, other arithmetic: 4.27 us -> 0.7 us  [normalize(): return (scaled * norm_gain.astype(jnp.float32)).astype(jnp.bfloat16)]
    gather x0 -> x1, local copies, waits for them, and re-layouts: none -> 2.82 us  [shift_all_gather(): jnp.take(everyone, (rank + jnp.arange(size, dtype=jnp.int32)) % size, axi...]
    ppermute x4, starting transfers between devices: 5.07 us -> 7.68 us  [ring_all_gather(): moving = lax.ppermute(moving, axis_name, forward)]
    another operation x5 -> x4, other arithmetic: 3.54 us -> 1.51 us
    broadcast_in_dim x0 -> x3, local copies, waits for them, and re-layouts: none -> 1.79 us  [the longest x1 1.11 us: shift_all_gather(): copies = jnp.broadcast_to(piece[None], (size,) + piece.shape)]
    unnamed x115 -> x125, local copies, waits for them, and re-layouts: 14.1 us -> 12.9 us
  transfers between devices with their start and end apart: 14 -> 12, of which waited for: 7 -> 9; matrix products, arithmetic and copies ran while one was open for 23% -> 20% of each run, Pallas kernels for 0% -> 0%
where the time goes in v14:
time: 176 us; the launch traced here: 174 us
  waiting for transfers between devices  60.7 us (34%)
  local copies, waits for them, and re-layouts  38.5 us (22%)
  other arithmetic  24 us (14%)
  starting transfers between devices  22.5 us (13%)
  matrix products  15.6 us (9%)
  Pallas kernels  11.8 us (7%)
    all_to_all x1, waiting for transfers between devices, per_device(): received = lax.all_to_all(payload, 'seq', 0, 0, tiled=True)  45.4 us
    unnamed x125, local copies, waits for them, and re-layouts  12.9 us
    pallas_call x1, Pallas kernels, block_attention(): pl.pallas_call(kernel, grid_spec=grid_spec, out_shape=[jax.ShapeDtypeStru...  11.8 us
    dot_general x16, matrix products, per_device(): jnp.dot(picked, o_weight[expert], preferred_element_type=jnp.float32)  9.74 us
    ppermute x4, starting transfers between devices, ring_all_gather(): moving = lax.ppermute(moving, axis_name, forward)  7.68 us
    ppermute x3, waiting for transfers between devices, shift_reduce_scatter(): lax.ppermute(blocks[s], axis_name, [(i, (i + s) % size) for i in range(si...  5.48 us
    all_to_all x1, starting transfers between devices, per_device(): received = lax.all_to_all(payload, 'seq', 0, 0, tiled=True)  5.41 us
    ppermute x3, waiting for transfers between devices, ring_all_gather(): moving = lax.ppermute(moving, axis_name, backward)  5.21 us
  transfers between devices with their start and end apart: 12, of which 9 were waited for; matrix products, arithmetic and copies ran while one was open for 20% of the time, Pallas kernels for 0%

profile of v14, /device:TPU:0, one launch (start us, length us, event | category | flops | bytes accessed | tf_op | source)
XLA Modules:
  0.0 174.3 jit_solution(6430861929478666503)
XLA Ops:
  4.2 4.3 %all-to-all-start = ((bf16[4,64,2048]{2,1,0:T(8,128)(2,1)}), bf16[4,64,2048]{2,1,0:T(8,128)(2,1)}, u32[]{:S(2)}, u32[]{:S(2)}) async-start(bf16[4,64,2048]{2,1,0:T(8,128)(2,1)} %broadcast_in_dim.279), calls=%async_computation | async-start | bytes 2097152 | tf_op jit(solution)/shard_map/all_to_all | solution.py:93
  16.0 3.1 %fusion.276 = (bf16[1,16,128,256]{3,2,1,0:T(8,128)(2,1)}, bf16[16,128,256]{2,1,0:T(8,128)(2,1)}) fusion(bf16[2,16,128,256]{3,2,1,0:T(8,128)(2,1)} %param.20), kind=kLoop, calls=%fused_computation.426 | loop fusion | bytes 4194304 | tf_op jit(solution)/shard_map/slice | solution.py:276
  19.1 1.6 copy.200
  23.6 2.8 %gather_fusion.1 = bf16[4,64,2048]{2,1,0:T(8,128)(2,1)} fusion(bf16[4,64,2048]{2,1,0:T(8,128)(2,1)} %all-to-all-done, s32[1024]{0:T(1024)S(1)} %pad_clamp_fusion.1), kind=kCustom, calls=%fused_computation.1 | custom fusion | bytes 2097168 | tf_op jit(solution)/shard_map/jit(_take)/gather | solution.py:94
  26.4 1.5 bitcast_select_fusion
  32.8 2.1 %copy.152 = f32[256,2,256]{0,2,1:T(8,128)} copy(f32[256,2,256]{2,0,1:T(8,128)} %multiply_reduce_fusion) | data formatting | bytes 1048576 | tf_op jit(solution)/shard_map/reduce_sum | solution.py:226
  34.9 1.9 %fusion.277 = (f32[256,2,2,64]{0,3,2,1:T(8,128)}, f32[256,2,2,64]{0,3,2,1:T(8,128)}) fusion(f32[256,2,2,128]{0,3,2,1:T(8,128)} %bitcast.357), kind=kLoop, calls=%fused_computation.427 | loop fusion | bytes 1048576 | tf_op jit(solution)/shard_map/slice | solution.py:25
  36.7 2.0 %copy.197 = f32[256,2,2,64]{3,0,1,2:T(8,128)} copy(f32[256,2,2,64]{0,3,2,1:T(8,128)} %get-tuple-element.94) | data formatting | bytes 524288
  38.7 2.0 %copy.196 = f32[256,2,2,64]{3,0,1,2:T(8,128)} copy(f32[256,2,2,64]{0,3,2,1:T(8,128)} %get-tuple-element.95) | data formatting | bytes 524288
  40.7 1.4 multiply_subtract_fusion
  43.9 2.7 %collective-permute-start.3 = (bf16[512,256]{1,0:T(8,128)(2,1)}, bf16[512,256]{1,0:T(8,128)(2,1)}, u32[]{:S(2)}, u32[]{:S(2)}) collective-permute-start(bf16[512,256]{1,0:T(8,128)(2,1)} %bitcast.334), channel_id=1, source_target_pairs={{0,1},{1,3},{3,5},{5,7},{7,6},{6,4},{4,2},{2,0},{8,9},{9,11},{11,1... | collective-permute-start | bytes 786440 | tf_op jit(solution)/shard_map/ppermute | solution.py:115
  46.7 1.7 fusion.278
  48.4 1.7 copy.199
  50.2 1.8 %copy.198 = f32[256,2,64]{2,0,1:T(8,128)} copy(f32[256,2,64]{0,2,1:T(8,128)} %get-tuple-element.97) | data formatting | bytes 262144
  54.3 2.0 %collective-permute-start.4 = (bf16[512,256]{1,0:T(8,128)(2,1)}, bf16[512,256]{1,0:T(8,128)(2,1)}, u32[]{:S(2)}, u32[]{:S(2)}) collective-permute-start(bf16[512,256]{1,0:T(8,128)(2,1)} %collective-permute-done.3), channel_id=1, source_target_pairs={{0,1},{1,3},{3,5},{5,7},{7,6},{6,4},{4,2},{2,0},{8,9},{9,11},{11,1... | collective-permute-start | bytes 786440 | tf_op jit(solution)/shard_map/ppermute | solution.py:115
  56.3 2.1 %fusion.58 = f32[2,256,2,128]{3,1,2,0:T(8,128)} fusion(bf16[256,2,128,1]{0,2,3,1:T(8,128)(2,1)} %bitcast.360, f32[2,256,2,256]{1,3,2,0:T(8,128)S(1)} %get-tuple-element.118, f32[2,256,2]{1,2,0:T(2,128)S(1)} %get-tuple-element.23), kind=kOutput, calls=%fused_computation.90 | convolution fusion | flops 67633152 | bytes 1708032 | tf_op jit(solution)/shard_map/hnkt,thc->hnkc/dot_general | solution.py:261
  60.7 2.0 %fusion.38 = f32[2,256,2]{1,2,0:T(2,128)} fusion(f32[2,256,2,256]{1,3,2,0:T(8,128)} %copy-done.4, f32[2,256,2]{1,2,0:T(2,128)S(1)} %get-tuple-element.23), kind=kLoop, calls=%fused_computation.68 | loop fusion | flops 523264 | bytes 1056768 | tf_op jit(solution)/shard_map/reduce_sum | solution.py:260
  63.1 1.6 collective-permute-start.5
  64.8 2.9 %collective-permute-done.1 = bf16[512,256]{1,0:T(8,128)(2,1)S(1)} collective-permute-done((bf16[512,256]{1,0:T(8,128)(2,1)}, bf16[512,256]{1,0:T(8,128)(2,1)S(1)}, u32[]{:S(2)}, u32[]{:S(2)}) %collective-permute-start.1) | collective-permute-done | bytes 262176 | tf_op jit(solution)/shard_map/ppermute | solution.py:119
  72.2 2.3 %collective-permute-done.2 = bf16[512,256]{1,0:T(8,128)(2,1)S(1)} collective-permute-done((bf16[512,256]{1,0:T(8,128)(2,1)S(1)}, bf16[512,256]{1,0:T(8,128)(2,1)S(1)}, u32[]{:S(2)}, u32[]{:S(2)}) %collective-permute-start.2) | collective-permute-done | bytes 262176 | tf_op jit(solution)/shard_map/ppermute | solution.py:119
  74.6 2.9 %collective-permute-done.6 = bf16[512,256]{1,0:T(8,128)(2,1)S(1)} collective-permute-done((bf16[512,256]{1,0:T(8,128)(2,1)S(1)}, bf16[512,256]{1,0:T(8,128)(2,1)S(1)}, u32[]{:S(2)}, u32[]{:S(2)}) %collective-permute-start.6) | collective-permute-done | bytes 262176 | tf_op jit(solution)/shard_map/ppermute | solution.py:115
  79.5 11.8 %shard_map.127 = (f32[8,2,1,512]{3,2,1,0:T(1,128)S(1)}, f32[8,2,1,512]{3,2,1,0:T(1,128)S(1)}, f32[8,2,128,512]{3,2,1,0:T(8,128)S(1)}) custom-call(s32[16]{0:T(128)S(1)} %and_select_fusion.offset_ref, s32[16]{0:T(128)S(1)} %broadcast_add_fusion.owner_ref, s32[16]{0:T(128)S(1)} %subtract_clamp_fusion.valid_ref, ...), custom_call_target="tpu_custom_call" | custom-call | tf_op jit(solution)/shard_map/pallas_call | solution.py:177
  92.4 1.5 pad_maximum_fusion
  94.0 5.4 %all-to-all-start.1 = ((bf16[8,264,512]{2,1,0:T(8,128)(2,1)}), bf16[8,264,512]{2,1,0:T(8,128)(2,1)}, u32[]{:S(2)}, u32[]{:S(2)}) async-start(bf16[8,264,512]{2,1,0:T(8,128)(2,1)} %pad_maximum_fusion), calls=%async_computation.1 | async-start | bytes 4325376 | tf_op jit(solution)/shard_map/all_to_all | solution.py:298
  101.4 45.4 %all-to-all-done.1 = bf16[8,264,512]{2,1,0:T(8,128)(2,1)} async-done(((bf16[8,264,512]{2,1,0:T(8,128)(2,1)}), bf16[8,264,512]{2,1,0:T(8,128)(2,1)}, u32[]{:S(2)}, u32[]{:S(2)}) %all-to-all-start.1) | async-done | bytes 2162720 | tf_op jit(solution)/shard_map/all_to_all | solution.py:298
  148.1 2.9 %fusion = f32[256,512]{1,0:T(8,128)} fusion(bf16[8,264,512]{2,1,0:T(8,128)(2,1)} %all-to-all-done.1, f32[8,2,512]{2,1,0:T(2,128)S(1)} %get-tuple-element.85), kind=kLoop, calls=%fused_computation.6 | loop fusion | flops 3014656 | bytes 2654208 | tf_op jit(solution)/shard_map/reduce_sum | solution.py:313
  155.0 1.8 %convolution_multiply_fusion.13 = f32[64,2048]{1,0:T(8,128)S(1)} fusion(bf16[4,256,2048]{2,1,0:T(8,128)(2,1)} %param.19, f32[64]{0:T(128)S(1)} %get-tuple-element.77, pred[64]{0:T(512)(128)(4,1)S(1)} %copy-done.50, pred[64]{0:T(512)(128)(4,1)S(1)} %copy-done.49, bf16[256,2,256]{0,2,1:T(8,128)(2,1)S(1)} %bitcast.339), kind=kOutput, calls=%fused_computation.21 | convolution fusion | flops 67272704 | bytes 1705472 | tf_op jit(solution)/shard_map/dot_general | solution.py:339
  156.8 1.6 convolution_multiply_fusion.12
  158.5 1.6 convolution_multiply_fusion.14
  165.1 1.5 collective-permute-start.9
  167.9 3.6 %collective-permute-done.8 = bf16[64,2048]{1,0:T(8,128)(2,1)S(1)} collective-permute-done((bf16[64,2048]{1,0:T(8,128)(2,1)S(1)}, bf16[64,2048]{1,0:T(8,128)(2,1)S(1)}, u32[]{:S(2)}, u32[]{:S(2)}) %collective-permute-start.8) | collective-permute-done | bytes 262176 | tf_op jit(solution)/shard_map/ppermute | solution.py:101
  171.5 1.9 %collective-permute-done.9 = bf16[64,2048]{1,0:T(8,128)(2,1)S(1)} collective-permute-done((bf16[64,2048]{1,0:T(8,128)(2,1)S(1)}, bf16[64,2048]{1,0:T(8,128)(2,1)S(1)}, u32[]{:S(2)}, u32[]{:S(2)}) %collective-permute-start.9) | collective-permute-done | bytes 262176 | tf_op jit(solution)/shard_map/ppermute | solution.py:101
  (224 shorter events, 47.8 us)
Async XLA Ops:
  0.0 28.0 %copy-start = (bf16[2,2048,256]{2,1,0:T(8,128)(2,1)S(1)}, bf16[2,2048,256]{2,1,0:T(8,128)(2,1)}, u32[]{:S(2)}) copy-start(bf16[2,2048,256]{2,1,0:T(8,128)(2,1)} %param.18) | copy-start | bytes 6291460
  0.0 11.2 %copy-start.2 = (s32[8]{0:T(128)S(1)}, s32[8]{0:T(128)}, u32[]{:S(2)}) copy-start(s32[8]{0:T(128)} %constant.125.clone) | copy-start | bytes 100
  0.0 8.7 %copy-start.54 = (s32[128]{0:T(128)S(1)}, s32[128]{0:T(128)}, u32[]{:S(2)}) copy-start(s32[128]{0:T(128)} %param.23) | copy-start | bytes 1540
  0.0 8.9 %copy-start.52 = (s32[8]{0:T(128)S(1)}, s32[8]{0:T(128)}, u32[]{:S(2)}) copy-start(s32[8]{0:T(128)} %param.22) | copy-start | bytes 100
  0.0 14.3 %copy-start.18 = (s32[1,256,2]{1,2,0:T(2,128)S(1)}, s32[1,256,2]{1,2,0:T(2,128)}, u32[]{:S(2)}) copy-start(s32[1,256,2]{1,2,0:T(2,128)} %param.16) | copy-start | bytes 6148
  4.2 19.4 %all-to-all-start = ((bf16[4,64,2048]{2,1,0:T(8,128)(2,1)}), bf16[4,64,2048]{2,1,0:T(8,128)(2,1)}, u32[]{:S(2)}, u32[]{:S(2)}) async-start(bf16[4,64,2048]{2,1,0:T(8,128)(2,1)} %broadcast_in_dim.279), calls=%async_computation | async-start | bytes 2097152 | tf_op jit(solution)/shard_map/all_to_all | solution.py:93
  23.3 17.4 %copy-start.9 = (f32[256,64]{1,0:T(8,128)}, f32[256,64]{1,0:T(8,128)S(1)}, u32[]{:S(2)}) copy-start(f32[256,64]{1,0:T(8,128)S(1)} %get-tuple-element.113) | copy-start | bytes 196612
  23.3 17.4 %copy-start.10 = (f32[256,64]{1,0:T(8,128)}, f32[256,64]{1,0:T(8,128)S(1)}, u32[]{:S(2)}) copy-start(f32[256,64]{1,0:T(8,128)S(1)} %get-tuple-element.114) | copy-start | bytes 196612
  43.9 10.4 %collective-permute-start.3 = (bf16[512,256]{1,0:T(8,128)(2,1)}, bf16[512,256]{1,0:T(8,128)(2,1)}, u32[]{:S(2)}, u32[]{:S(2)}) collective-permute-start(bf16[512,256]{1,0:T(8,128)(2,1)} %bitcast.334), channel_id=1, source_target_pairs={{0,1},{1,3},{3,5},{5,7},{7,6},{6,4},{4,2},{2,0},{8,9},{9,11},{11,1... | collective-permute-start | bytes 786440 | tf_op jit(solution)/shard_map/ppermute | solution.py:115
  46.6 12.9 %collective-permute-start = (bf16[512,256]{1,0:T(8,128)(2,1)}, bf16[512,256]{1,0:T(8,128)(2,1)}, u32[]{:S(2)}, u32[]{:S(2)}) collective-permute-start(bf16[512,256]{1,0:T(8,128)(2,1)} %bitcast.334), channel_id=1, source_target_pairs={{1,0},{3,1},{5,3},{7,5},{6,7},{4,6},{2,4},{0,2},{9,8},{11,9},{13,1... | collective-permute-start | bytes 786440 | tf_op jit(solution)/shard_map/ppermute | solution.py:119
  54.3 8.8 %collective-permute-start.4 = (bf16[512,256]{1,0:T(8,128)(2,1)}, bf16[512,256]{1,0:T(8,128)(2,1)}, u32[]{:S(2)}, u32[]{:S(2)}) collective-permute-start(bf16[512,256]{1,0:T(8,128)(2,1)} %collective-permute-done.3), channel_id=1, source_target_pairs={{0,1},{1,3},{3,5},{5,7},{7,6},{6,4},{4,2},{2,0},{8,9},{9,11},{11,1... | collective-permute-start | bytes 786440 | tf_op jit(solution)/shard_map/ppermute | solution.py:115
  59.5 20.0 %copy-start.1 = (bf16[16,128,256]{2,1,0:T(8,128)(2,1)S(1)}, bf16[16,128,256]{2,1,0:T(8,128)(2,1)}, u32[]{:S(2)}) copy-start(bf16[16,128,256]{2,1,0:T(8,128)(2,1)} %get-tuple-element.89.k_ref) | copy-start | bytes 3145732
  59.5 8.1 %collective-permute-start.1 = (bf16[512,256]{1,0:T(8,128)(2,1)}, bf16[512,256]{1,0:T(8,128)(2,1)S(1)}, u32[]{:S(2)}, u32[]{:S(2)}) collective-permute-start(bf16[512,256]{1,0:T(8,128)(2,1)} %collective-permute-done), channel_id=1, source_target_pairs={{1,0},{3,1},{5,3},{7,5},{6,7},{4,6},{2,4},{0,2},{9,8},{11,9},{13,1... | collective-permute-start | bytes 786440 | tf_op jit(solution)/shard_map/ppermute | solution.py:119
  63.1 7.8 %collective-permute-start.5 = (bf16[512,256]{1,0:T(8,128)(2,1)}, bf16[512,256]{1,0:T(8,128)(2,1)S(1)}, u32[]{:S(2)}, u32[]{:S(2)}) collective-permute-start(bf16[512,256]{1,0:T(8,128)(2,1)} %collective-permute-done.4), channel_id=1, source_target_pairs={{0,1},{1,3},{3,5},{5,7},{7,6},{6,4},{4,2},{2,0},{8,9},{9,11},{11,1... | collective-permute-start | bytes 786440 | tf_op jit(solution)/shard_map/ppermute | solution.py:115
  67.6 6.9 %collective-permute-start.2 = (bf16[512,256]{1,0:T(8,128)(2,1)S(1)}, bf16[512,256]{1,0:T(8,128)(2,1)S(1)}, u32[]{:S(2)}, u32[]{:S(2)}) collective-permute-start(bf16[512,256]{1,0:T(8,128)(2,1)S(1)} %collective-permute-done.1), channel_id=1, source_target_pairs={{1,0},{3,1},{5,3},{7,5},{6,7},{4,6},{2,4},{0,2},{9,8},{11,9},{13,1... | collective-permute-start | bytes 786440 | tf_op jit(solution)/shard_map/ppermute | solution.py:119
  70.9 6.6 %collective-permute-start.6 = (bf16[512,256]{1,0:T(8,128)(2,1)S(1)}, bf16[512,256]{1,0:T(8,128)(2,1)S(1)}, u32[]{:S(2)}, u32[]{:S(2)}) collective-permute-start(bf16[512,256]{1,0:T(8,128)(2,1)S(1)} %collective-permute-done.5), channel_id=1, source_target_pairs={{0,1},{1,3},{3,5},{5,7},{7,6},{6,4},{4,2},{2,0},{8,9},{9,11},{11,1... | collective-permute-start | bytes 786440 | tf_op jit(solution)/shard_map/ppermute | solution.py:115
  92.4 8.6 %copy-start.15 = (s32[256,2]{0,1:T(2,128)S(1)}, s32[256,2]{0,1:T(2,128)}, u32[]{:S(2)}) copy-start(s32[256,2]{0,1:T(2,128)} %copy-done.14) | copy-start | bytes 6148
  92.4 8.7 %copy-start.12 = (f32[256,2,4]{0,1,2:T(2,128)S(1)}, f32[256,2,4]{0,1,2:T(2,128)}, u32[]{:S(2)}) copy-start(f32[256,2,4]{0,1,2:T(2,128)} %copy-done.11) | copy-start | bytes 24580
  94.0 52.8 %all-to-all-start.1 = ((bf16[8,264,512]{2,1,0:T(8,128)(2,1)}), bf16[8,264,512]{2,1,0:T(8,128)(2,1)}, u32[]{:S(2)}, u32[]{:S(2)}) async-start(bf16[8,264,512]{2,1,0:T(8,128)(2,1)} %pad_maximum_fusion), calls=%async_computation.1 | async-start | bytes 4325376 | tf_op jit(solution)/shard_map/all_to_all | solution.py:298
  99.4 54.9 %copy-start.17 = (f32[2,256,2]{1,2,0:T(2,128)S(1)}, f32[2,256,2]{1,2,0:T(2,128)}, u32[]{:S(2)}) copy-start(f32[2,256,2]{1,2,0:T(2,128)} %fusion.38) | copy-start | bytes 12292
  100.7 54.3 %copy-start.49 = (pred[64]{0:T(512)(128)(4,1)S(1)}, pred[64]{0:T(512)(128)(4,1)}, u32[]{:S(2)}) copy-start(pred[64]{0:T(512)(128)(4,1)} %get-tuple-element.44) | copy-start | bytes 196
  100.7 54.3 %copy-start.50 = (pred[64]{0:T(512)(128)(4,1)S(1)}, pred[64]{0:T(512)(128)(4,1)}, u32[]{:S(2)}) copy-start(pred[64]{0:T(512)(128)(4,1)} %get-tuple-element.47) | copy-start | bytes 196
  101.1 53.2 %copy-start.8 = (f32[2,256,2,128]{3,1,2,0:T(8,128)S(1)}, f32[2,256,2,128]{3,1,2,0:T(8,128)}, u32[]{:S(2)}) copy-start(f32[2,256,2,128]{3,1,2,0:T(8,128)} %fusion.58) | copy-start | bytes 1572868
  147.8 9.0 %copy-start.47 = (pred[64]{0:T(512)(128)(4,1)S(1)}, pred[64]{0:T(512)(128)(4,1)}, u32[]{:S(2)}) copy-start(pred[64]{0:T(512)(128)(4,1)} %get-tuple-element.45) | copy-start | bytes 196
  147.8 9.0 %copy-start.48 = (pred[64]{0:T(512)(128)(4,1)S(1)}, pred[64]{0:T(512)(128)(4,1)}, u32[]{:S(2)}) copy-start(pred[64]{0:T(512)(128)(4,1)} %get-tuple-element.48) | copy-start | bytes 196
  148.0 10.4 %copy-start.45 = (pred[64]{0:T(512)(128)(4,1)S(1)}, pred[64]{0:T(512)(128)(4,1)}, u32[]{:S(2)}) copy-start(pred[64]{0:T(512)(128)(4,1)} %get-tuple-element.43) | copy-start | bytes 196
  148.0 10.4 %copy-start.46 = (pred[64]{0:T(512)(128)(4,1)S(1)}, pred[64]{0:T(512)(128)(4,1)}, u32[]{:S(2)}) copy-start(pred[64]{0:T(512)(128)(4,1)} %get-tuple-element.46) | copy-start | bytes 196
  150.9 9.2 %copy-start.43 = (pred[64]{0:T(512)(128)(4,1)S(1)}, pred[64]{0:T(512)(128)(4,1)}, u32[]{:S(2)}) copy-start(pred[64]{0:T(512)(128)(4,1)} %get-tuple-element.100) | copy-start | bytes 196
  150.9 9.3 %copy-start.44 = (pred[64]{0:T(512)(128)(4,1)S(1)}, pred[64]{0:T(512)(128)(4,1)}, u32[]{:S(2)}) copy-start(pred[64]{0:T(512)(128)(4,1)} %get-tuple-element.101) | copy-start | bytes 196
  160.6 7.3 %collective-permute-start.7 = (bf16[64,2048]{1,0:T(8,128)(2,1)S(1)}, bf16[64,2048]{1,0:T(8,128)(2,1)S(1)}, u32[]{:S(2)}, u32[]{:S(2)}) collective-permute-start(bf16[64,2048]{1,0:T(8,128)(2,1)S(1)} %fusion.16), channel_id=1, source_target_pairs={{0,8},{8,16},{16,24},{24,0},{1,9},{9,17},{17,25},{25,1},{2,10},{10... | collective-permute-start | bytes 786440 | tf_op jit(solution)/shard_map/ppermute | solution.py:101
  162.2 9.3 %collective-permute-start.8 = (bf16[64,2048]{1,0:T(8,128)(2,1)S(1)}, bf16[64,2048]{1,0:T(8,128)(2,1)S(1)}, u32[]{:S(2)}, u32[]{:S(2)}) collective-permute-start(bf16[64,2048]{1,0:T(8,128)(2,1)S(1)} %fusion.15), channel_id=1, source_target_pairs={{0,16},{8,24},{16,0},{24,8},{1,17},{9,25},{17,1},{25,9},{2,18},{10... | collective-permute-start | bytes 786440 | tf_op jit(solution)/shard_map/ppermute | solution.py:101
  165.1 8.4 %collective-permute-start.9 = (bf16[64,2048]{1,0:T(8,128)(2,1)S(1)}, bf16[64,2048]{1,0:T(8,128)(2,1)S(1)}, u32[]{:S(2)}, u32[]{:S(2)}) collective-permute-start(bf16[64,2048]{1,0:T(8,128)(2,1)S(1)} %fusion.14), channel_id=1, source_target_pairs={{0,24},{8,0},{16,8},{24,16},{1,25},{9,1},{17,9},{25,17},{2,26},{10... | collective-permute-start | bytes 786440 | tf_op jit(solution)/shard_map/ppermute | solution.py:101
  (35 other events, 129.4 us)

commit v15 on v11

--- a/solution.py
+++ b/solution.py
@@ -334,7 +334,7 @@
         .reshape(new_count, 2, local_heads * HD)
     )
     output_blocks = []
-    for block in range(head_count):
+    for block in list(range(1, head_count)) + [0]:
         rows = slice(block * rows_each, (block + 1) * rows_each)
         block_out = jnp.zeros((rows_each, o_weight.shape[2]), jnp.float32)
         for expert in range(o_weight.shape[0]):
@@ -349,8 +349,10 @@
             block_out = block_out + weight_expert[:, None] * jnp.dot(
                 picked, o_weight[expert], preferred_element_type=jnp.float32
             )
-        output_blocks.append(block_out.astype(jnp.bfloat16))
-    summed = shift_reduce_scatter(output_blocks, "heads")
+        block_out = block_out.astype(jnp.bfloat16)
+        block_out, attended = lax.optimization_barrier((block_out, attended))
+        output_blocks.append(block_out)
+    summed = shift_reduce_scatter(output_blocks[-1:] + output_blocks[:-1], "heads")
     return summed[None].astype(jnp.bfloat16)
 
 

time: 187 us -> 187 us (level)
  waiting for transfers between devices: 46.5 us -> 43.8 us
    ppermute x3, waiting for transfers between devices: 8.11 us -> 5.47 us  [shift_reduce_scatter(): lax.ppermute(blocks[s], axis_name, [(i, (i + s) % size) for i in range(si...]
  transfers between devices with their start and end apart: 20 -> 20, of which waited for: 9 -> 9; matrix products, arithmetic and copies ran while one was open for 18% -> 19% of each run, Pallas kernels for 0% -> 0%
where the time goes in v15:
time: 187 us; the launch traced here: 184 us
  waiting for transfers between devices  43.8 us (23%)
  local copies, waits for them, and re-layouts  35.9 us (19%)
  starting transfers between devices  35.6 us (19%)
  other arithmetic  24.1 us (13%)
  between operations  18.1 us (10%)
  matrix products  14.7 us (8%)
  Pallas kernels  11.8 us (6%)
    ppermute x7, waiting for transfers between devices, per_device(): lax.ppermute(lax.dynamic_index_in_dim(payload, target, 0, keepdims=False)...  26.6 us
    ppermute x7, starting transfers between devices, per_device(): lax.ppermute(lax.dynamic_index_in_dim(payload, target, 0, keepdims=False)...  20.2 us
    unnamed x131, local copies, waits for them, and re-layouts  15.8 us
    pallas_call x1, Pallas kernels, block_attention(): pl.pallas_call(kernel, grid_spec=grid_spec, out_shape=[jax.ShapeDtypeStru...  11.8 us
    ppermute x4, waiting for transfers between devices, ring_all_gather(): moving = lax.ppermute(moving, axis_name, forward)  10.9 us
    dot_general x16, matrix products, per_device(): jnp.dot(picked, o_weight[expert], preferred_element_type=jnp.float32)  9.73 us
    ppermute x4, starting transfers between devices, ring_all_gather(): moving = lax.ppermute(moving, axis_name, forward)  6.02 us
    ppermute x3, waiting for transfers between devices, shift_reduce_scatter(): lax.ppermute(blocks[s], axis_name, [(i, (i + s) % size) for i in range(si...  5.47 us
  transfers between devices with their start and end apart: 20, of which 9 were waited for; matrix products, arithmetic and copies ran while one was open for 19% of the time, Pallas kernels for 0%

profile of v15, /device:TPU:0, one launch (start us, length us, event | category | flops | bytes accessed | tf_op | source)
XLA Modules:
  0.0 183.9 jit_solution(11680381903942233293)
XLA Ops:
  2.0 1.8 fusion.56
  4.3 2.5 %collective-permute-start.1 = (bf16[64,2048]{1,0:T(8,128)(2,1)}, bf16[64,2048]{1,0:T(8,128)(2,1)}, u32[]{:S(2)}, u32[]{:S(2)}) collective-permute-start(bf16[64,2048]{1,0:T(8,128)(2,1)} %fusion.56), channel_id=1, source_target_pairs={{0,16},{8,24},{16,0},{24,8},{1,17},{9,25},{17,1},{25,9},{2,18},{10... | collective-permute-start | bytes 786440 | tf_op jit(solution)/shard_map/ppermute | solution.py:93
  19.3 3.1 %fusion.291 = (bf16[1,16,128,256]{3,2,1,0:T(8,128)(2,1)}, bf16[16,128,256]{2,1,0:T(8,128)(2,1)}) fusion(bf16[2,16,128,256]{3,2,1,0:T(8,128)(2,1)} %param.21), kind=kLoop, calls=%fused_computation.454 | loop fusion | bytes 4194304 | tf_op jit(solution)/shard_map/slice | solution.py:278
  36.3 1.6 copy.201
  49.4 2.1 %copy.153 = f32[256,2,256]{0,2,1:T(8,128)} copy(f32[256,2,256]{2,0,1:T(8,128)} %multiply_reduce_fusion) | data formatting | bytes 1048576 | tf_op jit(solution)/shard_map/reduce_sum | solution.py:228
  51.5 1.8 %fusion.292 = (f32[256,2,2,64]{0,3,2,1:T(8,128)}, f32[256,2,2,64]{0,3,2,1:T(8,128)}) fusion(f32[256,2,2,128]{0,3,2,1:T(8,128)} %bitcast.405), kind=kLoop, calls=%fused_computation.455 | loop fusion | bytes 1048576 | tf_op jit(solution)/shard_map/slice | solution.py:25
  53.3 2.0 %copy.198 = f32[256,2,2,64]{3,0,1,2:T(8,128)} copy(f32[256,2,2,64]{0,3,2,1:T(8,128)} %get-tuple-element.102) | data formatting | bytes 524288
  55.3 1.9 %copy.197 = f32[256,2,2,64]{3,0,1,2:T(8,128)} copy(f32[256,2,2,64]{0,3,2,1:T(8,128)} %get-tuple-element.103) | data formatting | bytes 524288
  59.9 1.5 collective-permute-start.6
  63.1 1.7 copy.200
  64.9 1.8 copy.199
  71.9 1.5 collective-permute-start.7
  76.5 2.4 %collective-permute-done.7 = bf16[512,256]{1,0:T(8,128)(2,1)} collective-permute-done((bf16[512,256]{1,0:T(8,128)(2,1)}, bf16[512,256]{1,0:T(8,128)(2,1)}, u32[]{:S(2)}, u32[]{:S(2)}) %collective-permute-start.7) | collective-permute-done | bytes 262176 | tf_op jit(solution)/shard_map/ppermute | solution.py:117
  79.0 1.5 collective-permute-start.8
  82.8 3.7 %collective-permute-done.8 = bf16[512,256]{1,0:T(8,128)(2,1)S(1)} collective-permute-done((bf16[512,256]{1,0:T(8,128)(2,1)}, bf16[512,256]{1,0:T(8,128)(2,1)S(1)}, u32[]{:S(2)}, u32[]{:S(2)}) %collective-permute-start.8) | collective-permute-done | bytes 262176 | tf_op jit(solution)/shard_map/ppermute | solution.py:117
  88.0 4.8 %collective-permute-done.9 = bf16[512,256]{1,0:T(8,128)(2,1)S(1)} collective-permute-done((bf16[512,256]{1,0:T(8,128)(2,1)S(1)}, bf16[512,256]{1,0:T(8,128)(2,1)S(1)}, u32[]{:S(2)}, u32[]{:S(2)}) %collective-permute-start.9) | collective-permute-done | bytes 262176 | tf_op jit(solution)/shard_map/ppermute | solution.py:117
  94.8 11.8 %shard_map.136 = (f32[8,2,1,512]{3,2,1,0:T(1,128)S(1)}, f32[8,2,1,512]{3,2,1,0:T(1,128)S(1)}, f32[8,2,128,512]{3,2,1,0:T(8,128)S(1)}) custom-call(s32[16]{0:T(128)S(1)} %get-tuple-element.134.offset_ref, s32[16]{0:T(128)S(1)} %broadcast_add_fusion.owner_ref, s32[16]{0:T(128)S(1)} %get-tuple-element.135.valid_ref, ...), custom_call_target="tpu_custom_call" | custom-call | tf_op jit(solution)/shard_map/pallas_call | solution.py:179
  107.9 1.6 collective-permute-start.10
  109.7 2.6 %collective-permute-start.11 = (bf16[264,512]{1,0:T(8,128)(2,1)S(1)}, bf16[264,512]{1,0:T(8,128)(2,1)S(1)}, u32[]{:S(2)}, u32[]{:S(2)}) collective-permute-start(bf16[264,512]{1,0:T(8,128)(2,1)S(1)} %get-tuple-element.91), channel_id=1, source_target_pairs={{0,3},{1,5},{3,7},{5,6},{7,4},{6,2},{4,0},{2,1},{8,11},{9,13},{11,... | collective-permute-start | bytes 811016 | tf_op jit(solution)/shard_map/ppermute | solution.py:306
  112.7 2.6 %collective-permute-start.14 = (bf16[264,512]{1,0:T(8,128)(2,1)S(1)}, bf16[264,512]{1,0:T(8,128)(2,1)S(1)}, u32[]{:S(2)}, u32[]{:S(2)}) collective-permute-start(bf16[264,512]{1,0:T(8,128)(2,1)S(1)} %get-tuple-element.95), channel_id=1, source_target_pairs={{0,6},{1,4},{3,2},{5,0},{7,1},{6,3},{4,5},{2,7},{8,14},{9,12},{11,... | collective-permute-start | bytes 811016 | tf_op jit(solution)/shard_map/ppermute | solution.py:306
  115.3 1.5 collective-permute-start.16
  117.6 9.2 %collective-permute-start.12 = (bf16[264,512]{1,0:T(8,128)(2,1)S(1)}, bf16[264,512]{1,0:T(8,128)(2,1)S(1)}, u32[]{:S(2)}, u32[]{:S(2)}) collective-permute-start(bf16[264,512]{1,0:T(8,128)(2,1)S(1)} %get-tuple-element.92), channel_id=1, source_target_pairs={{0,5},{1,7},{3,6},{5,4},{7,2},{6,0},{4,1},{2,3},{8,13},{9,15},{11,... | collective-permute-start | bytes 811016 | tf_op jit(solution)/shard_map/ppermute | solution.py:306
  126.8 19.0 %collective-permute-done.11 = bf16[264,512]{1,0:T(8,128)(2,1)S(1)} collective-permute-done((bf16[264,512]{1,0:T(8,128)(2,1)S(1)}, bf16[264,512]{1,0:T(8,128)(2,1)S(1)}, u32[]{:S(2)}, u32[]{:S(2)}) %collective-permute-start.11) | collective-permute-done | bytes 270368 | tf_op jit(solution)/shard_map/ppermute | solution.py:306
  145.8 2.3 %collective-permute-start.13 = (bf16[264,512]{1,0:T(8,128)(2,1)S(1)}, bf16[264,512]{1,0:T(8,128)(2,1)S(1)}, u32[]{:S(2)}, u32[]{:S(2)}) collective-permute-start(bf16[264,512]{1,0:T(8,128)(2,1)S(1)} %get-tuple-element.93), channel_id=1, source_target_pairs={{0,7},{1,6},{3,4},{5,2},{7,0},{6,1},{4,3},{2,5},{8,15},{9,14},{11,... | collective-permute-start | bytes 811016 | tf_op jit(solution)/shard_map/ppermute | solution.py:306
  148.1 6.9 %collective-permute-done.13 = bf16[264,512]{1,0:T(8,128)(2,1)S(1)} collective-permute-done((bf16[264,512]{1,0:T(8,128)(2,1)S(1)}, bf16[264,512]{1,0:T(8,128)(2,1)S(1)}, u32[]{:S(2)}, u32[]{:S(2)}) %collective-permute-start.13) | collective-permute-done | bytes 270368 | tf_op jit(solution)/shard_map/ppermute | solution.py:306
  156.9 2.9 %fusion = f32[256,512]{1,0:T(8,128)} fusion(bf16[8,264,512]{2,1,0:T(8,128)(2,1)} %copy-done.7, f32[8,2,512]{2,1,0:T(2,128)S(1)} %get-tuple-element.85), kind=kLoop, calls=%fused_computation.13 | loop fusion | flops 3014656 | bytes 2654208 | tf_op jit(solution)/shard_map/reduce_sum | solution.py:323
  164.0 1.8 convolution_multiply_fusion.13
  165.8 1.6 convolution_multiply_fusion.12
  167.5 1.6 convolution_multiply_fusion.14
  171.2 1.7 collective-permute-start.18
  177.6 2.9 %collective-permute-done.18 = bf16[64,2048]{1,0:T(8,128)(2,1)S(1)} collective-permute-done((bf16[64,2048]{1,0:T(8,128)(2,1)S(1)}, bf16[64,2048]{1,0:T(8,128)(2,1)S(1)}, u32[]{:S(2)}, u32[]{:S(2)}) %collective-permute-start.18) | collective-permute-done | bytes 262176 | tf_op jit(solution)/shard_map/ppermute | solution.py:103
  180.5 2.6 %collective-permute-done.19 = bf16[64,2048]{1,0:T(8,128)(2,1)S(1)} collective-permute-done((bf16[64,2048]{1,0:T(8,128)(2,1)S(1)}, bf16[64,2048]{1,0:T(8,128)(2,1)S(1)}, u32[]{:S(2)}, u32[]{:S(2)}) %collective-permute-start.19) | collective-permute-done | bytes 262176 | tf_op jit(solution)/shard_map/ppermute | solution.py:103
  (244 shorter events, 57.3 us)
Async XLA Ops:
  0.0 44.2 %copy-start = (bf16[2,2048,256]{2,1,0:T(8,128)(2,1)S(1)}, bf16[2,2048,256]{2,1,0:T(8,128)(2,1)}, u32[]{:S(2)}) copy-start(bf16[2,2048,256]{2,1,0:T(8,128)(2,1)} %param.19) | copy-start | bytes 6291460
  0.0 14.1 %copy-start.2 = (s32[8]{0:T(128)S(1)}, s32[8]{0:T(128)}, u32[]{:S(2)}) copy-start(s32[8]{0:T(128)} %constant.162.clone) | copy-start | bytes 100
  0.0 15.5 %copy-start.21 = (s32[1,256,2]{1,2,0:T(2,128)S(1)}, s32[1,256,2]{1,2,0:T(2,128)}, u32[]{:S(2)}) copy-start(s32[1,256,2]{1,2,0:T(2,128)} %param.17) | copy-start | bytes 6148
  1.3 16.6 %copy-start.8 = (bf16[1,64,2048]{2,1,0:T(8,128)(2,1)S(1)}, bf16[1,64,2048]{2,1,0:T(8,128)(2,1)}, u32[]{:S(2)}) copy-start(bf16[1,64,2048]{2,1,0:T(8,128)(2,1)} %param.14) | copy-start | bytes 786436
  3.8 39.0 %collective-permute-start.2 = (bf16[64,2048]{1,0:T(8,128)(2,1)}, bf16[64,2048]{1,0:T(8,128)(2,1)}, u32[]{:S(2)}, u32[]{:S(2)}) collective-permute-start(bf16[64,2048]{1,0:T(8,128)(2,1)} %fusion.56), channel_id=1, source_target_pairs={{0,8},{8,16},{16,24},{24,0},{1,9},{9,17},{17,25},{25,1},{2,10},{10... | collective-permute-start | bytes 786440 | tf_op jit(solution)/shard_map/ppermute | solution.py:93
  4.3 38.6 %collective-permute-start.1 = (bf16[64,2048]{1,0:T(8,128)(2,1)}, bf16[64,2048]{1,0:T(8,128)(2,1)}, u32[]{:S(2)}, u32[]{:S(2)}) collective-permute-start(bf16[64,2048]{1,0:T(8,128)(2,1)} %fusion.56), channel_id=1, source_target_pairs={{0,16},{8,24},{16,0},{24,8},{1,17},{9,25},{17,1},{25,9},{2,18},{10... | collective-permute-start | bytes 786440 | tf_op jit(solution)/shard_map/ppermute | solution.py:93
  6.8 36.0 %collective-permute-start = (bf16[64,2048]{1,0:T(8,128)(2,1)}, bf16[64,2048]{1,0:T(8,128)(2,1)}, u32[]{:S(2)}, u32[]{:S(2)}) collective-permute-start(bf16[64,2048]{1,0:T(8,128)(2,1)} %fusion.56), channel_id=1, source_target_pairs={{0,24},{8,0},{16,8},{24,16},{1,25},{9,1},{17,9},{25,17},{2,26},{10... | collective-permute-start | bytes 786440 | tf_op jit(solution)/shard_map/ppermute | solution.py:93
  16.6 5.9 %copy-start.17 = (s32[256,2]{0,1:T(2,128)}, s32[256,2]{0,1:T(2,128)S(1)}, u32[]{:S(2)}) copy-start(s32[256,2]{0,1:T(2,128)S(1)} %copy.151) | copy-start | bytes 6148
  19.3 17.0 %copy-start.14 = (f32[256,2,4]{0,1,2:T(2,128)}, f32[256,2,4]{0,1,2:T(2,128)S(1)}, u32[]{:S(2)}) copy-start(f32[256,2,4]{0,1,2:T(2,128)S(1)} %fusion.227) | copy-start | bytes 24580
  19.3 7.7 %copy-start.16 = (s32[8]{0:T(128)S(1)}, s32[8]{0:T(128)}, u32[]{:S(2)}) copy-start(s32[8]{0:T(128)} %constant.163.clone) | copy-start | bytes 100
  42.8 14.4 %copy-start.11 = (f32[256,64]{1,0:T(8,128)}, f32[256,64]{1,0:T(8,128)S(1)}, u32[]{:S(2)}) copy-start(f32[256,64]{1,0:T(8,128)S(1)} %get-tuple-element.122) | copy-start | bytes 196612
  59.9 11.9 %collective-permute-start.6 = (bf16[512,256]{1,0:T(8,128)(2,1)}, bf16[512,256]{1,0:T(8,128)(2,1)}, u32[]{:S(2)}, u32[]{:S(2)}) collective-permute-start(bf16[512,256]{1,0:T(8,128)(2,1)} %bitcast.378), channel_id=1, source_target_pairs={{0,1},{1,3},{3,5},{5,7},{7,6},{6,4},{4,2},{2,0},{8,9},{9,11},{11,1... | collective-permute-start | bytes 786440 | tf_op jit(solution)/shard_map/ppermute | solution.py:117
  61.4 13.1 %collective-permute-start.3 = (bf16[512,256]{1,0:T(8,128)(2,1)}, bf16[512,256]{1,0:T(8,128)(2,1)}, u32[]{:S(2)}, u32[]{:S(2)}) collective-permute-start(bf16[512,256]{1,0:T(8,128)(2,1)} %bitcast.378), channel_id=1, source_target_pairs={{1,0},{3,1},{5,3},{7,5},{6,7},{4,6},{2,4},{0,2},{9,8},{11,9},{13,1... | collective-permute-start | bytes 786440 | tf_op jit(solution)/shard_map/ppermute | solution.py:121
  71.9 7.1 %collective-permute-start.7 = (bf16[512,256]{1,0:T(8,128)(2,1)}, bf16[512,256]{1,0:T(8,128)(2,1)}, u32[]{:S(2)}, u32[]{:S(2)}) collective-permute-start(bf16[512,256]{1,0:T(8,128)(2,1)} %collective-permute-done.6), channel_id=1, source_target_pairs={{0,1},{1,3},{3,5},{5,7},{7,6},{6,4},{4,2},{2,0},{8,9},{9,11},{11,1... | collective-permute-start | bytes 786440 | tf_op jit(solution)/shard_map/ppermute | solution.py:117
  74.6 6.7 %collective-permute-start.4 = (bf16[512,256]{1,0:T(8,128)(2,1)}, bf16[512,256]{1,0:T(8,128)(2,1)S(1)}, u32[]{:S(2)}, u32[]{:S(2)}) collective-permute-start(bf16[512,256]{1,0:T(8,128)(2,1)} %collective-permute-done.3), channel_id=1, source_target_pairs={{1,0},{3,1},{5,3},{7,5},{6,7},{4,6},{2,4},{0,2},{9,8},{11,9},{13,1... | collective-permute-start | bytes 786440 | tf_op jit(solution)/shard_map/ppermute | solution.py:121
  76.5 18.3 %copy-start.1 = (bf16[16,128,256]{2,1,0:T(8,128)(2,1)S(1)}, bf16[16,128,256]{2,1,0:T(8,128)(2,1)}, u32[]{:S(2)}) copy-start(bf16[16,128,256]{2,1,0:T(8,128)(2,1)} %get-tuple-element.97.k_ref) | copy-start | bytes 3145732
  79.0 7.5 %collective-permute-start.8 = (bf16[512,256]{1,0:T(8,128)(2,1)}, bf16[512,256]{1,0:T(8,128)(2,1)S(1)}, u32[]{:S(2)}, u32[]{:S(2)}) collective-permute-start(bf16[512,256]{1,0:T(8,128)(2,1)} %collective-permute-done.7), channel_id=1, source_target_pairs={{0,1},{1,3},{3,5},{5,7},{7,6},{6,4},{4,2},{2,0},{8,9},{9,11},{11,1... | collective-permute-start | bytes 786440 | tf_op jit(solution)/shard_map/ppermute | solution.py:117
  81.3 6.7 %collective-permute-start.5 = (bf16[512,256]{1,0:T(8,128)(2,1)S(1)}, bf16[512,256]{1,0:T(8,128)(2,1)S(1)}, u32[]{:S(2)}, u32[]{:S(2)}) collective-permute-start(bf16[512,256]{1,0:T(8,128)(2,1)S(1)} %collective-permute-done.4), channel_id=1, source_target_pairs={{1,0},{3,1},{5,3},{7,5},{6,7},{4,6},{2,4},{0,2},{9,8},{11,9},{13,1... | collective-permute-start | bytes 786440 | tf_op jit(solution)/shard_map/ppermute | solution.py:121
  86.4 6.4 %collective-permute-start.9 = (bf16[512,256]{1,0:T(8,128)(2,1)S(1)}, bf16[512,256]{1,0:T(8,128)(2,1)S(1)}, u32[]{:S(2)}, u32[]{:S(2)}) collective-permute-start(bf16[512,256]{1,0:T(8,128)(2,1)S(1)} %collective-permute-done.8), channel_id=1, source_target_pairs={{0,1},{1,3},{3,5},{5,7},{7,6},{6,4},{4,2},{2,0},{8,9},{9,11},{11,1... | collective-permute-start | bytes 786440 | tf_op jit(solution)/shard_map/ppermute | solution.py:117
  107.9 9.7 %collective-permute-start.10 = (bf16[264,512]{1,0:T(8,128)(2,1)S(1)}, bf16[264,512]{1,0:T(8,128)(2,1)S(1)}, u32[]{:S(2)}, u32[]{:S(2)}) collective-permute-start(bf16[264,512]{1,0:T(8,128)(2,1)S(1)} %get-tuple-element.90), channel_id=1, source_target_pairs={{0,1},{1,3},{3,5},{5,7},{7,6},{6,4},{4,2},{2,0},{8,9},{9,11},{11,1... | collective-permute-start | bytes 811016 | tf_op jit(solution)/shard_map/ppermute | solution.py:306
  109.7 36.1 %collective-permute-start.11 = (bf16[264,512]{1,0:T(8,128)(2,1)S(1)}, bf16[264,512]{1,0:T(8,128)(2,1)S(1)}, u32[]{:S(2)}, u32[]{:S(2)}) collective-permute-start(bf16[264,512]{1,0:T(8,128)(2,1)S(1)} %get-tuple-element.91), channel_id=1, source_target_pairs={{0,3},{1,5},{3,7},{5,6},{7,4},{6,2},{4,0},{2,1},{8,11},{9,13},{11,... | collective-permute-start | bytes 811016 | tf_op jit(solution)/shard_map/ppermute | solution.py:306
  112.3 42.8 %collective-permute-start.15 = (bf16[264,512]{1,0:T(8,128)(2,1)S(1)}, bf16[264,512]{1,0:T(8,128)(2,1)S(1)}, u32[]{:S(2)}, u32[]{:S(2)}) collective-permute-start(bf16[264,512]{1,0:T(8,128)(2,1)S(1)} %get-tuple-element.94), channel_id=1, source_target_pairs={{0,4},{1,2},{3,0},{5,1},{7,3},{6,5},{4,7},{2,6},{8,12},{9,10},{11,... | collective-permute-start | bytes 811016 | tf_op jit(solution)/shard_map/ppermute | solution.py:306
  112.7 42.4 %collective-permute-start.14 = (bf16[264,512]{1,0:T(8,128)(2,1)S(1)}, bf16[264,512]{1,0:T(8,128)(2,1)S(1)}, u32[]{:S(2)}, u32[]{:S(2)}) collective-permute-start(bf16[264,512]{1,0:T(8,128)(2,1)S(1)} %get-tuple-element.95), channel_id=1, source_target_pairs={{0,6},{1,4},{3,2},{5,0},{7,1},{6,3},{4,5},{2,7},{8,14},{9,12},{11,... | collective-permute-start | bytes 811016 | tf_op jit(solution)/shard_map/ppermute | solution.py:306
  115.3 39.8 %collective-permute-start.16 = (bf16[264,512]{1,0:T(8,128)(2,1)S(1)}, bf16[264,512]{1,0:T(8,128)(2,1)S(1)}, u32[]{:S(2)}, u32[]{:S(2)}) collective-permute-start(bf16[264,512]{1,0:T(8,128)(2,1)S(1)} %get-tuple-element.88), channel_id=1, source_target_pairs={{0,2},{1,0},{3,1},{5,3},{7,5},{6,7},{4,6},{2,4},{8,10},{9,8},{11,9... | collective-permute-start | bytes 811016 | tf_op jit(solution)/shard_map/ppermute | solution.py:306
  117.6 30.5 %collective-permute-start.12 = (bf16[264,512]{1,0:T(8,128)(2,1)S(1)}, bf16[264,512]{1,0:T(8,128)(2,1)S(1)}, u32[]{:S(2)}, u32[]{:S(2)}) collective-permute-start(bf16[264,512]{1,0:T(8,128)(2,1)S(1)} %get-tuple-element.92), channel_id=1, source_target_pairs={{0,5},{1,7},{3,6},{5,4},{7,2},{6,0},{4,1},{2,3},{8,13},{9,15},{11,... | collective-permute-start | bytes 811016 | tf_op jit(solution)/shard_map/ppermute | solution.py:306
  145.8 9.3 %collective-permute-start.13 = (bf16[264,512]{1,0:T(8,128)(2,1)S(1)}, bf16[264,512]{1,0:T(8,128)(2,1)S(1)}, u32[]{:S(2)}, u32[]{:S(2)}) collective-permute-start(bf16[264,512]{1,0:T(8,128)(2,1)S(1)} %get-tuple-element.93), channel_id=1, source_target_pairs={{0,7},{1,6},{3,4},{5,2},{7,0},{6,1},{4,3},{2,5},{8,15},{9,14},{11,... | collective-permute-start | bytes 811016 | tf_op jit(solution)/shard_map/ppermute | solution.py:306
  156.9 6.3 %copy-start.10 = (f32[2,256,2,128]{3,1,2,0:T(8,128)S(1)}, f32[2,256,2,128]{3,1,2,0:T(8,128)}, u32[]{:S(2)}) copy-start(f32[2,256,2,128]{3,1,2,0:T(8,128)} %fusion.59) | copy-start | bytes 1572868
  164.0 5.2 %copy-start.3 = (bf16[4,256,2048]{2,1,0:T(8,128)(2,1)S(1)}, bf16[4,256,2048]{2,1,0:T(8,128)(2,1)}, u32[]{:S(2)}) copy-start(bf16[4,256,2048]{2,1,0:T(8,128)(2,1)} %param.20) | copy-start | bytes 12582916
  164.0 5.2 %copy-start.46 = (pred[64]{0:T(512)(128)(4,1)S(1)}, pred[64]{0:T(512)(128)(4,1)}, u32[]{:S(2)}) copy-start(pred[64]{0:T(512)(128)(4,1)} %get-tuple-element.108) | copy-start | bytes 196
  169.6 8.0 %collective-permute-start.17 = (bf16[64,2048]{1,0:T(8,128)(2,1)S(1)}, bf16[64,2048]{1,0:T(8,128)(2,1)S(1)}, u32[]{:S(2)}, u32[]{:S(2)}) collective-permute-start(bf16[64,2048]{1,0:T(8,128)(2,1)S(1)} %fusion.16), channel_id=1, source_target_pairs={{0,8},{8,16},{16,24},{24,0},{1,9},{9,17},{17,25},{25,1},{2,10},{10... | collective-permute-start | bytes 786440 | tf_op jit(solution)/shard_map/ppermute | solution.py:103
  171.2 9.3 %collective-permute-start.18 = (bf16[64,2048]{1,0:T(8,128)(2,1)S(1)}, bf16[64,2048]{1,0:T(8,128)(2,1)S(1)}, u32[]{:S(2)}, u32[]{:S(2)}) collective-permute-start(bf16[64,2048]{1,0:T(8,128)(2,1)S(1)} %fusion.15), channel_id=1, source_target_pairs={{0,16},{8,24},{16,0},{24,8},{1,17},{9,25},{17,1},{25,9},{2,18},{10... | collective-permute-start | bytes 786440 | tf_op jit(solution)/shard_map/ppermute | solution.py:103
  174.7 8.4 %collective-permute-start.19 = (bf16[64,2048]{1,0:T(8,128)(2,1)S(1)}, bf16[64,2048]{1,0:T(8,128)(2,1)S(1)}, u32[]{:S(2)}, u32[]{:S(2)}) collective-permute-start(bf16[64,2048]{1,0:T(8,128)(2,1)S(1)} %fusion.14), channel_id=1, source_target_pairs={{0,24},{8,0},{16,8},{24,16},{1,25},{9,1},{17,9},{25,17},{2,26},{10... | collective-permute-start | bytes 786440 | tf_op jit(solution)/shard_map/ppermute | solution.py:103
  (44 other events, 116.3 us)

commit v16 on v12

--- a/solution.py
+++ b/solution.py
@@ -224,17 +224,34 @@
     cached_len = cached_blocks * block_size - tail_trim
     positions = cached_len[seq_rank] + token_ids
     onehot, gates = route(gathered, router_weight, chosen)
-    every_q = jnp.einsum("nd,edc->nec", gathered, q_weight, preferred_element_type=jnp.float32)
-    chosen_q = jnp.sum(onehot[:, :, :, None] * every_q[:, None, :, :], axis=2).reshape(
-        new_count, 2, local_heads, HD
-    )
-    queries = rotate(chosen_q, positions).astype(jnp.bfloat16)
+    every_q = jnp.einsum("nd,edc->enc", gathered, q_weight, preferred_element_type=jnp.float32)
+    half_dim = HD // 2
+    inverse = 10000.0 ** (-2.0 * jnp.arange(half_dim, dtype=jnp.float32) / HD)
+    angles = positions.astype(jnp.float32)[:, None] * inverse[None, :]
+    cosine = jnp.tile(jnp.cos(angles), (1, 2 * local_heads))
+    signed_sine = jnp.tile(
+        jnp.concatenate([-jnp.sin(angles), jnp.sin(angles)], axis=-1), (1, local_heads)
+    )
+    slot_tables = []
+    for slot in range(chosen.shape[1]):
+        slot_q = jnp.sum(onehot[:, slot, :].T[:, :, None] * every_q, axis=0)
+        swapped = jnp.concatenate(
+            [
+                part
+                for h in range(local_heads)
+                for part in (
+                    slot_q[:, h * HD + half_dim:(h + 1) * HD],
+                    slot_q[:, h * HD:h * HD + half_dim],
+                )
+            ],
+            axis=-1,
+        )
+        slot_tables.append((slot_q * cosine + swapped * signed_sine).astype(jnp.bfloat16))
+    queries = jnp.stack(slot_tables, axis=1).reshape(new_count, 2, local_heads, HD)
     fresh = jnp.einsum("nd,sdc->snc", gathered, kv_weight, preferred_element_type=jnp.float32)
     new_keys = rotate(fresh[0].reshape(new_count, local_heads, HD), positions).astype(jnp.bfloat16)
     new_values = fresh[1].reshape(new_count, local_heads, HD).astype(jnp.bfloat16)
-    ring_queries = ring_all_gather(
-        queries.reshape(new_count * 2, local_heads * HD), "seq", cycle
-    )
+    ring_queries = ring_all_gather(jnp.concatenate(slot_tables, axis=0), "seq", cycle)
     request_count = ring_queries.shape[0]
     ring_size = len(cycle)
     position_of = np.argsort(np.asarray(cycle))
@@ -310,11 +327,14 @@
     part_totals = part_stats[:, 2] + part_stats[:, 3]
     cache_best = jnp.max(part_best, axis=0)
     share = jnp.exp(part_best - cache_best[None])
-    cache_total = jnp.sum(part_totals * share, axis=0).reshape(local_heads, new_count, 2)
+    cache_total = jnp.swapaxes(
+        jnp.sum(part_totals * share, axis=0).reshape(local_heads, 2, new_count), 1, 2
+    )
     cache_accum = jnp.transpose(
-        jnp.sum(part_accum * share[:, :, None, :], axis=0), (0, 2, 1)
-    ).reshape(local_heads, new_count, 2, HD)
-    cache_best = cache_best.reshape(local_heads, new_count, 2)
+        jnp.sum(part_accum * share[:, :, None, :], axis=0).reshape(local_heads, HD, 2, new_count),
+        (0, 3, 2, 1),
+    )
+    cache_best = jnp.swapaxes(cache_best.reshape(local_heads, 2, new_count), 1, 2)
 
     peak = jnp.maximum(cache_best, self_best)
     cache_share = jnp.exp(cache_best - peak)

time: 174 us -> 169 us (0.971)
  local copies, waits for them, and re-layouts: 36.4 us -> 30.9 us
  waiting for transfers between devices: 58.9 us -> 61.1 us
    ppermute x4, waiting for transfers between devices: 3.46 us -> 11.1 us  [ring_all_gather(): moving = lax.ppermute(moving, axis_name, forward)]
    unnamed x115 -> x123, local copies, waits for them, and re-layouts: 14.1 us -> 8.76 us
    ppermute x3, waiting for transfers between devices: 5.52 us -> 0.92 us  [ring_all_gather(): moving = lax.ppermute(moving, axis_name, backward)]
    convert_element_type x2 -> x3, other arithmetic: 0.69 us -> 3.96 us  [the longest x2 3.35 us: per_device(): (slot_q * cosine + swapped * signed_sine).astype(jnp.bfloat16)]
    concatenate x0 -> x2, local copies, waits for them, and re-layouts: none -> 3.1 us  [per_device(): jnp.concatenate([part for h in range(local_heads) for part in (slot_q[:,...]
    slice x2 -> x1, local copies, waits for them, and re-layouts: 3.56 us -> 0.67 us  [rotate(): trailing_part = values[..., half_dim:]]
    another operation x0 -> x4, local copies, waits for them, and re-layouts: none -> 2.71 us  [the longest x3 1.71 us: per_device(): cosine = jnp.tile(jnp.cos(angles), (1, 2 * local_heads))]
    convert_element_type x3 -> x0, local copies, waits for them, and re-layouts: 1.99 us -> none  [the longest x2 1.39 us: per_device(): queries = rotate(chosen_q, positions).astype(jnp.bfloat16)]
  transfers between devices with their start and end apart: 14 -> 14, of which waited for: 7 -> 7; matrix products, arithmetic and copies ran while one was open for 23% -> 22% of each run, Pallas kernels for 0% -> 0%
where the time goes in v16:
time: 169 us; the launch traced here: 168 us
  waiting for transfers between devices  61.1 us (36%)
  local copies, waits for them, and re-layouts  30.9 us (18%)
  other arithmetic  26.8 us (16%)
  starting transfers between devices  21.1 us (12%)
  matrix products  15.5 us (9%)
  Pallas kernels  11.8 us (7%)
    all_to_all x1, waiting for transfers between devices, per_device(): received = lax.all_to_all(payload, 'seq', 0, 0, tiled=True)  43.5 us
    pallas_call x1, Pallas kernels, block_attention(): pl.pallas_call(kernel, grid_spec=grid_spec, out_shape=[jax.ShapeDtypeStru...  11.8 us
    ppermute x4, waiting for transfers between devices, ring_all_gather(): moving = lax.ppermute(moving, axis_name, forward)  11.1 us
    dot_general x16, matrix products, per_device(): jnp.dot(picked, o_weight[expert], preferred_element_type=jnp.float32)  9.74 us
    unnamed x123, local copies, waits for them, and re-layouts  8.76 us
    all_to_all x1, starting transfers between devices, per_device(): received = lax.all_to_all(payload, 'seq', 0, 0, tiled=True)  5.79 us
    ppermute x3, waiting for transfers between devices, shift_reduce_scatter(): lax.ppermute(blocks[s], axis_name, [(i, (i + s) % size) for i in range(si...  5.48 us
    ppermute x4, starting transfers between devices, ring_all_gather(): moving = lax.ppermute(moving, axis_name, forward)  4.98 us
  transfers between devices with their start and end apart: 14, of which 7 were waited for; matrix products, arithmetic and copies ran while one was open for 22% of the time, Pallas kernels for 0%

profile of v16, /device:TPU:0, one launch (start us, length us, event | category | flops | bytes accessed | tf_op | source)
XLA Modules:
  0.0 168.3 jit_solution(13972228981299718416)
XLA Ops:
  2.0 1.8 %fusion.56 = bf16[64,2048]{1,0:T(8,128)(2,1)} fusion(bf16[1,64,2048]{2,1,0:T(8,128)(2,1)} %param.13, f32[2048]{0:T(1024)S(1)} %convert_element_type.115, f32[64]{0:T(128)S(1)} %add_rsqrt_fusion), kind=kLoop, calls=%fused_computation.89 | loop fusion | flops 524288 | bytes 532736 | tf_op jit(solution)/shard_map/convert_element_type | solution.py:38
  4.2 2.5 %collective-permute-start.1 = (bf16[64,2048]{1,0:T(8,128)(2,1)}, bf16[64,2048]{1,0:T(8,128)(2,1)}, u32[]{:S(2)}, u32[]{:S(2)}) collective-permute-start(bf16[64,2048]{1,0:T(8,128)(2,1)} %fusion.56), channel_id=1, source_target_pairs={{0,16},{8,24},{16,0},{24,8},{1,17},{9,25},{17,1},{25,9},{2,18},{10... | collective-permute-start | bytes 786440 | tf_op jit(solution)/shard_map/ppermute | solution.py:93
  6.8 1.4 collective-permute-start
  14.1 1.3 gather_fusion.1
  19.5 3.1 %fusion.288 = (bf16[1,16,128,256]{3,2,1,0:T(8,128)(2,1)}, bf16[16,128,256]{2,1,0:T(8,128)(2,1)}) fusion(bf16[2,16,128,256]{3,2,1,0:T(8,128)(2,1)} %param.20), kind=kLoop, calls=%fused_computation.447 | loop fusion | bytes 4194304 | tf_op jit(solution)/shard_map/slice | solution.py:295
  27.6 1.6 copy.117
  30.0 1.6 pad_maximum_fusion.1
  33.3 2.0 %multiply_reduce_fusion.1 = (f32[256,256]{1,0:T(8,128)S(1)}, f32[256,256]{1,0:T(8,128)}) fusion(f32[4,256]{1,0:T(4,128)S(1)} %bitcast.446, f32[4,256]{1,0:T(4,128)S(1)} %bitcast.445, bf16[256,2048,1]{1,0,2:T(8,128)(2,1)S(1)} %bitcast.435, bf16[4,2048,256]{2,1,0:T(8,128)(2,1)S(1)} %copy-done.54), kind=kOutput, calls=%fused_computation.64 | convolution fusion | flops 1074659328 | bytes 5775360 | tf_op jit(solution)/shard_map/nd,edc->enc/dot_general | solution.py:227
  37.2 1.8 %reduce_sum.250 = f32[256,1,2,128]{3,2,0,1:T(2,128)} reshape(f32[256,256]{1,0:T(8,128)} %get-tuple-element.34) | data formatting | bytes 524288 | tf_op jit(solution)/shard_map/reduce_sum | solution.py:237
  39.0 2.0 %slice_bitcast_fusion.22 = (f32[256,1,64]{2,0,1:T(8,128)}, f32[256,1,64]{2,0,1:T(8,128)}, f32[256,1,64]{2,0,1:T(8,128)}, f32[256,1,64]{2,0,1:T(8,128)}, f32[256,...) fusion(f32[256,256]{1,0:T(8,128)} %get-tuple-element.34), kind=kLoop, calls=%fused_computation.442 | loop fusion | bytes 786432 | tf_op jit(solution)/shard_map/concatenate | solution.py:238
  42.0 1.6 fusion.67
  45.0 1.6 collective-permute-start.3
  48.5 1.8 %copy.115 = f32[256,2,64]{2,0,1:T(8,128)} copy(f32[256,2,64]{0,2,1:T(8,128)} %get-tuple-element.99) | data formatting | bytes 262144
  50.3 1.8 %fusion.73 = (bf16[256,1,2,128]{3,0,1,2:T(8,128)(2,1)S(1)}, bf16[256,1,2,128]{3,0,1,2:T(8,128)(2,1)S(1)}) fusion(f32[256,1,2,128]{3,0,1,2:T(8,128)} %copy.73, f32[256,1,2,128]{3,2,0,1:T(2,128)} %reduce_sum.249, f32[256,128]{1,0:T(8,128)} %pad_maximum_fusion.3, f32[256,1,2,128]{3,2,0,1:T(2,128)} %reduce_sum.250, f32[256,1,64]{2,0,1:T(8,128)} %get-tuple-element.111, ...), kind=kLoop, calls=%fused_computation.111 | loop fusion | flops 917504 | bytes 1703936 | tf_op jit(solution)/shard_map/convert_element_type | solution.py:249
  54.6 1.5 collective-permute-start.7
  58.7 3.0 %collective-permute-done.7 = bf16[512,256]{1,0:T(8,128)(2,1)S(1)} collective-permute-done((bf16[512,256]{1,0:T(8,128)(2,1)}, bf16[512,256]{1,0:T(8,128)(2,1)S(1)}, u32[]{:S(2)}, u32[]{:S(2)}) %collective-permute-start.7) | collective-permute-done | bytes 262176 | tf_op jit(solution)/shard_map/ppermute | solution.py:117
  61.6 1.5 collective-permute-start.8
  65.6 3.3 %collective-permute-done.8 = bf16[512,256]{1,0:T(8,128)(2,1)S(1)} collective-permute-done((bf16[512,256]{1,0:T(8,128)(2,1)S(1)}, bf16[512,256]{1,0:T(8,128)(2,1)S(1)}, u32[]{:S(2)}, u32[]{:S(2)}) %collective-permute-start.8) | collective-permute-done | bytes 262176 | tf_op jit(solution)/shard_map/ppermute | solution.py:117
  68.9 1.5 collective-permute-start.9
  70.4 4.8 %collective-permute-done.9 = bf16[512,256]{1,0:T(8,128)(2,1)S(1)} collective-permute-done((bf16[512,256]{1,0:T(8,128)(2,1)S(1)}, bf16[512,256]{1,0:T(8,128)(2,1)S(1)}, u32[]{:S(2)}, u32[]{:S(2)}) %collective-permute-start.9) | collective-permute-done | bytes 262176 | tf_op jit(solution)/shard_map/ppermute | solution.py:117
  76.3 11.8 %shard_map.127 = (f32[8,2,1,512]{3,2,1,0:T(1,128)S(1)}, f32[8,2,1,512]{3,2,1,0:T(1,128)S(1)}, f32[8,2,128,512]{3,2,1,0:T(8,128)S(1)}) custom-call(s32[16]{0:T(128)S(1)} %and_select_fusion.offset_ref, s32[16]{0:T(128)S(1)} %broadcast_add_fusion.owner_ref, s32[16]{0:T(128)S(1)} %subtract_clamp_fusion.valid_ref, ...), custom_call_target="tpu_custom_call" | custom-call | tf_op jit(solution)/shard_map/pallas_call | solution.py:179
  89.3 1.5 pad_maximum_fusion
  90.8 5.8 %all-to-all-start = ((bf16[8,264,512]{2,1,0:T(8,128)(2,1)}), bf16[8,264,512]{2,1,0:T(8,128)(2,1)}, u32[]{:S(2)}, u32[]{:S(2)}) async-start(bf16[8,264,512]{2,1,0:T(8,128)(2,1)} %pad_maximum_fusion), calls=%async_computation | async-start | bytes 4325376 | tf_op jit(solution)/shard_map/all_to_all | solution.py:317
  98.6 43.5 %all-to-all-done = bf16[8,264,512]{2,1,0:T(8,128)(2,1)} async-done(((bf16[8,264,512]{2,1,0:T(8,128)(2,1)}), bf16[8,264,512]{2,1,0:T(8,128)(2,1)}, u32[]{:S(2)}, u32[]{:S(2)}) %all-to-all-start) | async-done | bytes 2162720 | tf_op jit(solution)/shard_map/all_to_all | solution.py:317
  143.2 2.1 %fusion = f32[256,512]{1,0:T(8,128)S(1)} fusion(bf16[8,264,512]{2,1,0:T(8,128)(2,1)} %all-to-all-done, f32[8,2,512]{2,1,0:T(2,128)S(1)} %get-tuple-element.87), kind=kLoop, calls=%fused_computation.5 | loop fusion | flops 3014656 | bytes 2654208 | tf_op jit(solution)/shard_map/reduce_sum | solution.py:334
  148.4 1.8 %convolution_multiply_fusion.13 = f32[64,2048]{1,0:T(8,128)S(1)} fusion(bf16[4,256,2048]{2,1,0:T(8,128)(2,1)} %param.19, f32[64]{0:T(128)S(1)} %get-tuple-element.79, pred[64]{0:T(512)(128)(4,1)S(1)} %copy-done.53, pred[64]{0:T(512)(128)(4,1)S(1)} %copy-done.52, bf16[256,2,256]{0,2,1:T(8,128)(2,1)S(1)} %bitcast.418), kind=kOutput, calls=%fused_computation.20 | convolution fusion | flops 67272704 | bytes 1705472 | tf_op jit(solution)/shard_map/dot_general | solution.py:361
  150.2 1.6 convolution_multiply_fusion.12
  151.9 1.6 convolution_multiply_fusion.14
  155.6 1.7 %collective-permute-start.11 = (bf16[64,2048]{1,0:T(8,128)(2,1)S(1)}, bf16[64,2048]{1,0:T(8,128)(2,1)S(1)}, u32[]{:S(2)}, u32[]{:S(2)}) collective-permute-start(bf16[64,2048]{1,0:T(8,128)(2,1)S(1)} %fusion.15), channel_id=1, source_target_pairs={{0,16},{8,24},{16,0},{24,8},{1,17},{9,25},{17,1},{25,9},{2,18},{10... | collective-permute-start | bytes 786440 | tf_op jit(solution)/shard_map/ppermute | solution.py:103
  159.1 1.5 collective-permute-start.12
  162.0 2.9 %collective-permute-done.11 = bf16[64,2048]{1,0:T(8,128)(2,1)S(1)} collective-permute-done((bf16[64,2048]{1,0:T(8,128)(2,1)S(1)}, bf16[64,2048]{1,0:T(8,128)(2,1)S(1)}, u32[]{:S(2)}, u32[]{:S(2)}) %collective-permute-start.11) | collective-permute-done | bytes 262176 | tf_op jit(solution)/shard_map/ppermute | solution.py:103
  164.9 2.6 %collective-permute-done.12 = bf16[64,2048]{1,0:T(8,128)(2,1)S(1)} collective-permute-done((bf16[64,2048]{1,0:T(8,128)(2,1)S(1)}, bf16[64,2048]{1,0:T(8,128)(2,1)S(1)}, u32[]{:S(2)}, u32[]{:S(2)}) %collective-permute-start.12) | collective-permute-done | bytes 262176 | tf_op jit(solution)/shard_map/ppermute | solution.py:103
  (227 shorter events, 47.2 us)
Async XLA Ops:
  0.0 31.6 %copy-start = (bf16[2,2048,256]{2,1,0:T(8,128)(2,1)S(1)}, bf16[2,2048,256]{2,1,0:T(8,128)(2,1)}, u32[]{:S(2)}) copy-start(bf16[2,2048,256]{2,1,0:T(8,128)(2,1)} %param.18) | copy-start | bytes 6291460
  3.8 26.2 %collective-permute-start.2 = (bf16[64,2048]{1,0:T(8,128)(2,1)}, bf16[64,2048]{1,0:T(8,128)(2,1)}, u32[]{:S(2)}, u32[]{:S(2)}) collective-permute-start(bf16[64,2048]{1,0:T(8,128)(2,1)} %fusion.56), channel_id=1, source_target_pairs={{0,8},{8,16},{16,24},{24,0},{1,9},{9,17},{17,25},{25,1},{2,10},{10... | collective-permute-start | bytes 786440 | tf_op jit(solution)/shard_map/ppermute | solution.py:93
  4.2 25.7 %collective-permute-start.1 = (bf16[64,2048]{1,0:T(8,128)(2,1)}, bf16[64,2048]{1,0:T(8,128)(2,1)}, u32[]{:S(2)}, u32[]{:S(2)}) collective-permute-start(bf16[64,2048]{1,0:T(8,128)(2,1)} %fusion.56), channel_id=1, source_target_pairs={{0,16},{8,24},{16,0},{24,8},{1,17},{9,25},{17,1},{25,9},{2,18},{10... | collective-permute-start | bytes 786440 | tf_op jit(solution)/shard_map/ppermute | solution.py:93
  6.8 23.2 %collective-permute-start = (bf16[64,2048]{1,0:T(8,128)(2,1)}, bf16[64,2048]{1,0:T(8,128)(2,1)}, u32[]{:S(2)}, u32[]{:S(2)}) collective-permute-start(bf16[64,2048]{1,0:T(8,128)(2,1)} %fusion.56), channel_id=1, source_target_pairs={{0,24},{8,0},{16,8},{24,16},{1,25},{9,1},{17,9},{25,17},{2,26},{10... | collective-permute-start | bytes 786440 | tf_op jit(solution)/shard_map/ppermute | solution.py:93
  39.0 8.0 %slice-start = ((f32[2,256,256]{1,2,0:T(8,128)}), f32[1,256,256]{1,2,0:T(8,128)S(1)}, s32[]{:S(2)}) async-start(f32[2,256,256]{1,2,0:T(8,128)} %copy-done.12), calls=%async_computation.1 | async-start | bytes 524288 | tf_op jit(solution)/shard_map/slice | solution.py:252
  45.0 12.4 %collective-permute-start.3 = (bf16[512,256]{1,0:T(8,128)(2,1)}, bf16[512,256]{1,0:T(8,128)(2,1)}, u32[]{:S(2)}, u32[]{:S(2)}) collective-permute-start(bf16[512,256]{1,0:T(8,128)(2,1)} %pad_maximum_fusion.2), channel_id=1, source_target_pairs={{1,0},{3,1},{5,3},{7,5},{6,7},{4,6},{2,4},{0,2},{9,8},{11,9},{13,1... | collective-permute-start | bytes 786440 | tf_op jit(solution)/shard_map/ppermute | solution.py:121
  46.6 8.1 %collective-permute-start.6 = (bf16[512,256]{1,0:T(8,128)(2,1)}, bf16[512,256]{1,0:T(8,128)(2,1)}, u32[]{:S(2)}, u32[]{:S(2)}) collective-permute-start(bf16[512,256]{1,0:T(8,128)(2,1)} %pad_maximum_fusion.2), channel_id=1, source_target_pairs={{0,1},{1,3},{3,5},{5,7},{7,6},{6,4},{4,2},{2,0},{8,9},{9,11},{11,1... | collective-permute-start | bytes 786440 | tf_op jit(solution)/shard_map/ppermute | solution.py:117
  48.5 14.6 %copy-start.7 = (bf16[256,256]{1,0:T(8,128)(2,1)S(1)}, bf16[256,256]{1,0:T(8,128)(2,1)}, u32[]{:S(2)}) copy-start(bf16[256,256]{1,0:T(8,128)(2,1)} %copy-done.6) | copy-start | bytes 393220
  48.5 14.6 %copy-start.9 = (bf16[256,256]{1,0:T(8,128)(2,1)S(1)}, bf16[256,256]{1,0:T(8,128)(2,1)}, u32[]{:S(2)}) copy-start(bf16[256,256]{1,0:T(8,128)(2,1)} %copy-done.8) | copy-start | bytes 393220
  53.3 23.0 %copy-start.1 = (bf16[16,128,256]{2,1,0:T(8,128)(2,1)S(1)}, bf16[16,128,256]{2,1,0:T(8,128)(2,1)}, u32[]{:S(2)}) copy-start(bf16[16,128,256]{2,1,0:T(8,128)(2,1)} %get-tuple-element.91.k_ref) | copy-start | bytes 3145732
  54.6 7.0 %collective-permute-start.7 = (bf16[512,256]{1,0:T(8,128)(2,1)}, bf16[512,256]{1,0:T(8,128)(2,1)S(1)}, u32[]{:S(2)}, u32[]{:S(2)}) collective-permute-start(bf16[512,256]{1,0:T(8,128)(2,1)} %collective-permute-done.6), channel_id=1, source_target_pairs={{0,1},{1,3},{3,5},{5,7},{7,6},{6,4},{4,2},{2,0},{8,9},{9,11},{11,1... | collective-permute-start | bytes 786440 | tf_op jit(solution)/shard_map/ppermute | solution.py:117
  57.4 6.7 %collective-permute-start.4 = (bf16[512,256]{1,0:T(8,128)(2,1)}, bf16[512,256]{1,0:T(8,128)(2,1)S(1)}, u32[]{:S(2)}, u32[]{:S(2)}) collective-permute-start(bf16[512,256]{1,0:T(8,128)(2,1)} %collective-permute-done.3), channel_id=1, source_target_pairs={{1,0},{3,1},{5,3},{7,5},{6,7},{4,6},{2,4},{0,2},{9,8},{11,9},{13,1... | collective-permute-start | bytes 786440 | tf_op jit(solution)/shard_map/ppermute | solution.py:121
  61.6 7.3 %collective-permute-start.8 = (bf16[512,256]{1,0:T(8,128)(2,1)S(1)}, bf16[512,256]{1,0:T(8,128)(2,1)S(1)}, u32[]{:S(2)}, u32[]{:S(2)}) collective-permute-start(bf16[512,256]{1,0:T(8,128)(2,1)S(1)} %collective-permute-done.7), channel_id=1, source_target_pairs={{0,1},{1,3},{3,5},{5,7},{7,6},{6,4},{4,2},{2,0},{8,9},{9,11},{11,1... | collective-permute-start | bytes 786440 | tf_op jit(solution)/shard_map/ppermute | solution.py:117
  64.0 6.4 %collective-permute-start.5 = (bf16[512,256]{1,0:T(8,128)(2,1)S(1)}, bf16[512,256]{1,0:T(8,128)(2,1)S(1)}, u32[]{:S(2)}, u32[]{:S(2)}) collective-permute-start(bf16[512,256]{1,0:T(8,128)(2,1)S(1)} %collective-permute-done.4), channel_id=1, source_target_pairs={{1,0},{3,1},{5,3},{7,5},{6,7},{4,6},{2,4},{0,2},{9,8},{11,9},{13,1... | collective-permute-start | bytes 786440 | tf_op jit(solution)/shard_map/ppermute | solution.py:121
  68.9 6.4 %collective-permute-start.9 = (bf16[512,256]{1,0:T(8,128)(2,1)S(1)}, bf16[512,256]{1,0:T(8,128)(2,1)S(1)}, u32[]{:S(2)}, u32[]{:S(2)}) collective-permute-start(bf16[512,256]{1,0:T(8,128)(2,1)S(1)} %collective-permute-done.8), channel_id=1, source_target_pairs={{0,1},{1,3},{3,5},{5,7},{7,6},{6,4},{4,2},{2,0},{8,9},{9,11},{11,1... | collective-permute-start | bytes 786440 | tf_op jit(solution)/shard_map/ppermute | solution.py:117
  89.3 8.7 %copy-start.4 = (bf16[4,64,2048]{2,1,0:T(8,128)(2,1)S(1)}, bf16[4,64,2048]{2,1,0:T(8,128)(2,1)}, u32[]{:S(2)}) copy-start(bf16[4,64,2048]{2,1,0:T(8,128)(2,1)} %copy-done.3) | copy-start | bytes 3145732
  89.3 8.7 %copy-start.18 = (bf16[2048,4]{0,1:T(4,128)(2,1)S(1)}, bf16[2048,4]{0,1:T(4,128)(2,1)}, u32[]{:S(2)}) copy-start(bf16[2048,4]{0,1:T(4,128)(2,1)} %param.15) | copy-start | bytes 49156
  89.3 9.0 %copy-start.17 = (s32[256,2]{0,1:T(2,128)S(1)}, s32[256,2]{0,1:T(2,128)}, u32[]{:S(2)}) copy-start(s32[256,2]{0,1:T(2,128)} %copy-done.16) | copy-start | bytes 6148
  89.3 9.1 %copy-start.15 = (f32[256,2,4]{0,1,2:T(2,128)S(1)}, f32[256,2,4]{0,1,2:T(2,128)}, u32[]{:S(2)}) copy-start(f32[256,2,4]{0,1,2:T(2,128)} %copy-done.14) | copy-start | bytes 24580
  90.8 51.3 %all-to-all-start = ((bf16[8,264,512]{2,1,0:T(8,128)(2,1)}), bf16[8,264,512]{2,1,0:T(8,128)(2,1)}, u32[]{:S(2)}, u32[]{:S(2)}) async-start(bf16[8,264,512]{2,1,0:T(8,128)(2,1)} %pad_maximum_fusion), calls=%async_computation | async-start | bytes 4325376 | tf_op jit(solution)/shard_map/all_to_all | solution.py:317
  96.6 51.0 %copy-start.19 = (f32[2,256,2]{1,2,0:T(2,128)S(1)}, f32[2,256,2]{1,2,0:T(2,128)}, u32[]{:S(2)}) copy-start(f32[2,256,2]{1,2,0:T(2,128)} %fusion.35) | copy-start | bytes 12292
  97.9 50.4 %copy-start.52 = (pred[64]{0:T(512)(128)(4,1)S(1)}, pred[64]{0:T(512)(128)(4,1)}, u32[]{:S(2)}) copy-start(pred[64]{0:T(512)(128)(4,1)} %get-tuple-element.46) | copy-start | bytes 196
  97.9 50.4 %copy-start.53 = (pred[64]{0:T(512)(128)(4,1)S(1)}, pred[64]{0:T(512)(128)(4,1)}, u32[]{:S(2)}) copy-start(pred[64]{0:T(512)(128)(4,1)} %get-tuple-element.49) | copy-start | bytes 196
  98.3 49.4 %copy-start.5 = (f32[2,256,2,128]{3,1,2,0:T(8,128)S(1)}, f32[2,256,2,128]{3,1,2,0:T(8,128)}, u32[]{:S(2)}) copy-start(f32[2,256,2,128]{3,1,2,0:T(8,128)} %fusion.59) | copy-start | bytes 1572868
  143.2 7.0 %copy-start.50 = (pred[64]{0:T(512)(128)(4,1)S(1)}, pred[64]{0:T(512)(128)(4,1)}, u32[]{:S(2)}) copy-start(pred[64]{0:T(512)(128)(4,1)} %get-tuple-element.47) | copy-start | bytes 196
  143.2 7.0 %copy-start.51 = (pred[64]{0:T(512)(128)(4,1)S(1)}, pred[64]{0:T(512)(128)(4,1)}, u32[]{:S(2)}) copy-start(pred[64]{0:T(512)(128)(4,1)} %get-tuple-element.50) | copy-start | bytes 196
  145.3 6.6 %copy-start.48 = (pred[64]{0:T(512)(128)(4,1)S(1)}, pred[64]{0:T(512)(128)(4,1)}, u32[]{:S(2)}) copy-start(pred[64]{0:T(512)(128)(4,1)} %get-tuple-element.45) | copy-start | bytes 196
  146.4 7.2 %copy-start.46 = (pred[64]{0:T(512)(128)(4,1)S(1)}, pred[64]{0:T(512)(128)(4,1)}, u32[]{:S(2)}) copy-start(pred[64]{0:T(512)(128)(4,1)} %get-tuple-element.118) | copy-start | bytes 196
  146.4 7.2 %copy-start.47 = (pred[64]{0:T(512)(128)(4,1)S(1)}, pred[64]{0:T(512)(128)(4,1)}, u32[]{:S(2)}) copy-start(pred[64]{0:T(512)(128)(4,1)} %get-tuple-element.119) | copy-start | bytes 196
  154.0 8.0 %collective-permute-start.10 = (bf16[64,2048]{1,0:T(8,128)(2,1)S(1)}, bf16[64,2048]{1,0:T(8,128)(2,1)S(1)}, u32[]{:S(2)}, u32[]{:S(2)}) collective-permute-start(bf16[64,2048]{1,0:T(8,128)(2,1)S(1)} %fusion.16), channel_id=1, source_target_pairs={{0,8},{8,16},{16,24},{24,0},{1,9},{9,17},{17,25},{25,1},{2,10},{10... | collective-permute-start | bytes 786440 | tf_op jit(solution)/shard_map/ppermute | solution.py:103
  155.6 9.3 %collective-permute-start.11 = (bf16[64,2048]{1,0:T(8,128)(2,1)S(1)}, bf16[64,2048]{1,0:T(8,128)(2,1)S(1)}, u32[]{:S(2)}, u32[]{:S(2)}) collective-permute-start(bf16[64,2048]{1,0:T(8,128)(2,1)S(1)} %fusion.15), channel_id=1, source_target_pairs={{0,16},{8,24},{16,0},{24,8},{1,17},{9,25},{17,1},{25,9},{2,18},{10... | collective-permute-start | bytes 786440 | tf_op jit(solution)/shard_map/ppermute | solution.py:103
  159.1 8.4 %collective-permute-start.12 = (bf16[64,2048]{1,0:T(8,128)(2,1)S(1)}, bf16[64,2048]{1,0:T(8,128)(2,1)S(1)}, u32[]{:S(2)}, u32[]{:S(2)}) collective-permute-start(bf16[64,2048]{1,0:T(8,128)(2,1)S(1)} %fusion.14), channel_id=1, source_target_pairs={{0,24},{8,0},{16,8},{24,16},{1,25},{9,1},{17,9},{25,17},{2,26},{10... | collective-permute-start | bytes 786440 | tf_op jit(solution)/shard_map/ppermute | solution.py:103
  (38 other events, 132.2 us)

commit v17 on v16

--- a/solution.py
+++ b/solution.py
@@ -234,7 +234,9 @@
     )
     slot_tables = []
     for slot in range(chosen.shape[1]):
-        slot_q = jnp.sum(onehot[:, slot, :].T[:, :, None] * every_q, axis=0)
+        slot_q = every_q[0]
+        for expert in range(1, every_q.shape[0]):
+            slot_q = jnp.where(chosen[:, slot, None] == expert, every_q[expert], slot_q)
         swapped = jnp.concatenate(
             [
                 part

time: 169 us -> 172 us (1.018)
  local copies, waits for them, and re-layouts: 30.9 us -> 33.9 us
    squeeze x0 -> x4, local copies, waits for them, and re-layouts: none -> 7.16 us  [the longest x3 5.37 us: per_device(): slot_q = jnp.where(chosen[:, slot, None] == expert, every_q[expert], slot_q)]
    reduce_sum x2 -> x0, local copies, waits for them, and re-layouts: 2.61 us -> none  [per_device(): slot_q = jnp.sum(onehot[:, slot, :].T[:, :, None] * every_q, axis=0)]
    unnamed x123 -> x75, local copies, waits for them, and re-layouts: 8.76 us -> 8.36 us
  transfers between devices with their start and end apart: 14 -> 14, of which waited for: 7 -> 7; matrix products, arithmetic and copies ran while one was open for 22% -> 27% of each run, Pallas kernels for 0% -> 0%
where the time goes in v17:
time: 172 us; the launch traced here: 171 us
  waiting for transfers between devices  61.1 us (36%)
  local copies, waits for them, and re-layouts  33.9 us (20%)
  other arithmetic  26.7 us (16%)
  starting transfers between devices  21.2 us (12%)
  matrix products  15.5 us (9%)
  Pallas kernels  11.8 us (7%)
    all_to_all x1, waiting for transfers between devices, per_device(): received = lax.all_to_all(payload, 'seq', 0, 0, tiled=True)  42.8 us
    pallas_call x1, Pallas kernels, block_attention(): pl.pallas_call(kernel, grid_spec=grid_spec, out_shape=[jax.ShapeDtypeStru...  11.8 us
    ppermute x4, waiting for transfers between devices, ring_all_gather(): moving = lax.ppermute(moving, axis_name, forward)  11.7 us
    dot_general x16, matrix products, per_device(): jnp.dot(picked, o_weight[expert], preferred_element_type=jnp.float32)  10.4 us
    unnamed x75, local copies, waits for them, and re-layouts  8.36 us
    all_to_all x1, starting transfers between devices, per_device(): received = lax.all_to_all(payload, 'seq', 0, 0, tiled=True)  5.8 us
    ppermute x3, waiting for transfers between devices, shift_reduce_scatter(): lax.ppermute(blocks[s], axis_name, [(i, (i + s) % size) for i in range(si...  5.64 us
    squeeze x3, local copies, waits for them, and re-layouts, per_device(): slot_q = jnp.where(chosen[:, slot, None] == expert, every_q[expert], slot_q)  5.37 us
  transfers between devices with their start and end apart: 14, of which 7 were waited for; matrix products, arithmetic and copies ran while one was open for 27% of the time, Pallas kernels for 0%

profile of v17, /device:TPU:0, one launch (start us, length us, event | category | flops | bytes accessed | tf_op | source)
XLA Modules:
  0.0 171.0 jit_solution(334290861274594784)
XLA Ops:
  2.0 1.8 %fusion.56 = bf16[64,2048]{1,0:T(8,128)(2,1)} fusion(bf16[1,64,2048]{2,1,0:T(8,128)(2,1)} %param.13, f32[2048]{0:T(1024)S(1)} %convert_element_type.115, f32[64]{0:T(128)S(1)} %add_rsqrt_fusion), kind=kLoop, calls=%fused_computation.87 | loop fusion | flops 524288 | bytes 532736 | tf_op jit(solution)/shard_map/convert_element_type | solution.py:38
  4.2 2.5 %collective-permute-start.1 = (bf16[64,2048]{1,0:T(8,128)(2,1)}, bf16[64,2048]{1,0:T(8,128)(2,1)}, u32[]{:S(2)}, u32[]{:S(2)}) collective-permute-start(bf16[64,2048]{1,0:T(8,128)(2,1)} %fusion.56), channel_id=1, source_target_pairs={{0,16},{8,24},{16,0},{24,8},{1,17},{9,25},{17,1},{25,9},{2,18},{10... | collective-permute-start | bytes 786440 | tf_op jit(solution)/shard_map/ppermute | solution.py:93
  15.4 1.8 %fusion.58 = bf16[1,64,2048]{2,1,0:T(8,128)(2,1)} fusion(bf16[1,64,2048]{2,1,0:T(8,128)(2,1)} %param.13, f32[2048]{0:T(1024)S(1)} %convert_element_type.115, f32[64]{0:T(128)S(1)} %add_rsqrt_fusion), kind=kLoop, calls=%fused_computation.89 | loop fusion | flops 524288 | bytes 532736 | tf_op jit(solution)/shard_map/convert_element_type | solution.py:38
  19.9 3.1 %fusion.292 = (bf16[1,16,128,256]{3,2,1,0:T(8,128)(2,1)}, bf16[16,128,256]{2,1,0:T(8,128)(2,1)}) fusion(bf16[2,16,128,256]{3,2,1,0:T(8,128)(2,1)} %param.20), kind=kLoop, calls=%fused_computation.453 | loop fusion | bytes 4194304 | tf_op jit(solution)/shard_map/slice | solution.py:297
  26.7 1.6 copy.141
  29.1 1.7 %pad_maximum_fusion.1 = bf16[4,64,2048]{2,1,0:T(8,128)(2,1)S(1)} fusion(bf16[1,64,2048]{2,1,0:T(8,128)(2,1)} %bitcast.6, bf16[1,64,2048]{2,1,0:T(8,128)(2,1)} %bitcast.5, bf16[1,64,2048]{2,1,0:T(8,128)(2,1)} %bitcast.4, bf16[1,64,2048]{2,1,0:T(8,128)(2,1)} %fusion.58), kind=kLoop, calls=%fused_computation.44 | loop fusion | flops 1572864 | bytes 2097152 | tf_op jit(solution)/shard_map/stack | solution.py:96
  38.7 1.6 collective-permute-start.3
  41.5 1.8 %copy.140 = f32[256,2,64]{2,0,1:T(8,128)} copy(f32[256,2,64]{0,2,1:T(8,128)} %get-tuple-element.108) | data formatting | bytes 262144
  43.2 1.8 %copy.139 = f32[256,2,64]{2,0,1:T(8,128)} copy(f32[256,2,64]{0,2,1:T(8,128)} %get-tuple-element.109) | data formatting | bytes 262144
  45.0 1.8 %squeeze.83 = f32[256,1,2,128]{3,2,0,1:T(2,128)} reshape(f32[1,256,256]{2,1,0:T(8,128)} %get-tuple-element.98) | data formatting | bytes 524288 | tf_op jit(solution)/shard_map/squeeze | solution.py:239
  46.8 1.8 %squeeze.168 = f32[256,1,2,128]{3,2,0,1:T(2,128)} reshape(f32[1,256,256]{2,1,0:T(8,128)} %get-tuple-element.99) | data formatting | bytes 524288 | tf_op jit(solution)/shard_map/squeeze | solution.py:237
  48.6 1.8 %squeeze.82 = f32[256,1,2,128]{3,2,0,1:T(2,128)} reshape(f32[1,256,256]{2,1,0:T(8,128)} %get-tuple-element.100) | data formatting | bytes 524288 | tf_op jit(solution)/shard_map/squeeze | solution.py:239
  50.4 1.8 %squeeze.81 = f32[256,1,2,128]{3,2,0,1:T(2,128)} reshape(f32[1,256,256]{2,1,0:T(8,128)} %get-tuple-element.101) | data formatting | bytes 524288 | tf_op jit(solution)/shard_map/squeeze | solution.py:239
  52.1 2.1 %fusion.73 = (bf16[256,1,2,128]{3,0,1,2:T(8,128)(2,1)S(1)}, bf16[256,1,2,128]{3,0,1,2:T(8,128)(2,1)S(1)}) fusion(f32[256,1,2,128]{3,0,1,2:T(8,128)} %copy.94, f32[256,1,2,128]{3,2,0,1:T(2,128)} %squeeze.81, f32[256,1,2,128]{3,2,0,1:T(2,128)} %squeeze.82, f32[256,1,2,128]{3,2,0,1:T(2,128)} %squeeze.168, f32[256,1,2,128]{3,2,0,1:T(2,128)} %squeeze.83, ...), kind=kLoop, calls=%fused_computation.109 | loop fusion | flops 1310720 | bytes 2229760 | tf_op jit(solution)/shard_map/convert_element_type | solution.py:251
  56.8 1.5 collective-permute-start.7
  60.2 3.6 %collective-permute-done.7 = bf16[512,256]{1,0:T(8,128)(2,1)S(1)} collective-permute-done((bf16[512,256]{1,0:T(8,128)(2,1)}, bf16[512,256]{1,0:T(8,128)(2,1)S(1)}, u32[]{:S(2)}, u32[]{:S(2)}) %collective-permute-start.7) | collective-permute-done | bytes 262176 | tf_op jit(solution)/shard_map/ppermute | solution.py:117
  63.8 1.5 collective-permute-start.8
  67.7 3.3 %collective-permute-done.8 = bf16[512,256]{1,0:T(8,128)(2,1)S(1)} collective-permute-done((bf16[512,256]{1,0:T(8,128)(2,1)S(1)}, bf16[512,256]{1,0:T(8,128)(2,1)S(1)}, u32[]{:S(2)}, u32[]{:S(2)}) %collective-permute-start.8) | collective-permute-done | bytes 262176 | tf_op jit(solution)/shard_map/ppermute | solution.py:117
  71.0 1.5 collective-permute-start.9
  72.6 4.8 %collective-permute-done.9 = bf16[512,256]{1,0:T(8,128)(2,1)S(1)} collective-permute-done((bf16[512,256]{1,0:T(8,128)(2,1)S(1)}, bf16[512,256]{1,0:T(8,128)(2,1)S(1)}, u32[]{:S(2)}, u32[]{:S(2)}) %collective-permute-start.9) | collective-permute-done | bytes 262176 | tf_op jit(solution)/shard_map/ppermute | solution.py:117
  78.5 11.8 %shard_map.127 = (f32[8,2,1,512]{3,2,1,0:T(1,128)S(1)}, f32[8,2,1,512]{3,2,1,0:T(1,128)S(1)}, f32[8,2,128,512]{3,2,1,0:T(8,128)S(1)}) custom-call(s32[16]{0:T(128)S(1)} %and_select_fusion.offset_ref, s32[16]{0:T(128)S(1)} %broadcast_add_fusion.owner_ref, s32[16]{0:T(128)S(1)} %subtract_clamp_fusion.valid_ref, ...), custom_call_target="tpu_custom_call" | custom-call | tf_op jit(solution)/shard_map/pallas_call | solution.py:179
  91.4 1.5 pad_maximum_fusion
  93.0 5.8 %all-to-all-start = ((bf16[8,264,512]{2,1,0:T(8,128)(2,1)}), bf16[8,264,512]{2,1,0:T(8,128)(2,1)}, u32[]{:S(2)}, u32[]{:S(2)}) async-start(bf16[8,264,512]{2,1,0:T(8,128)(2,1)} %pad_maximum_fusion), calls=%async_computation | async-start | bytes 4325376 | tf_op jit(solution)/shard_map/all_to_all | solution.py:319
  101.5 42.8 %all-to-all-done = bf16[8,264,512]{2,1,0:T(8,128)(2,1)} async-done(((bf16[8,264,512]{2,1,0:T(8,128)(2,1)}), bf16[8,264,512]{2,1,0:T(8,128)(2,1)}, u32[]{:S(2)}, u32[]{:S(2)}) %all-to-all-start) | async-done | bytes 2162720 | tf_op jit(solution)/shard_map/all_to_all | solution.py:319
  145.3 2.1 %fusion = f32[256,512]{1,0:T(8,128)S(1)} fusion(bf16[8,264,512]{2,1,0:T(8,128)(2,1)} %all-to-all-done, f32[8,2,512]{2,1,0:T(2,128)S(1)} %get-tuple-element.91), kind=kLoop, calls=%fused_computation.5 | loop fusion | flops 3014656 | bytes 2654208 | tf_op jit(solution)/shard_map/reduce_sum | solution.py:336
  150.5 1.8 %convolution_multiply_fusion.13 = f32[64,2048]{1,0:T(8,128)S(1)} fusion(bf16[4,256,2048]{2,1,0:T(8,128)(2,1)} %param.19, f32[64]{0:T(128)} %get-tuple-element.83, pred[64]{0:T(512)(128)(4,1)S(1)} %get-tuple-element.47, pred[64]{0:T(512)(128)(4,1)S(1)} %get-tuple-element.44, bf16[256,2,256]{0,2,1:T(8,128)(2,1)S(1)} %bitcast.428), kind=kOutput, calls=%fused_computation.20 | convolution fusion | flops 67272704 | bytes 1705472 | tf_op jit(solution)/shard_map/dot_general | solution.py:363
  152.3 1.6 convolution_multiply_fusion.12
  153.9 1.6 convolution_multiply_fusion.14
  158.2 1.7 %collective-permute-start.11 = (bf16[64,2048]{1,0:T(8,128)(2,1)S(1)}, bf16[64,2048]{1,0:T(8,128)(2,1)S(1)}, u32[]{:S(2)}, u32[]{:S(2)}) collective-permute-start(bf16[64,2048]{1,0:T(8,128)(2,1)S(1)} %fusion.15), channel_id=1, source_target_pairs={{0,16},{8,24},{16,0},{24,8},{1,17},{9,25},{17,1},{25,9},{2,18},{10... | collective-permute-start | bytes 786440 | tf_op jit(solution)/shard_map/ppermute | solution.py:103
  161.7 1.5 collective-permute-start.12
  164.5 3.0 %collective-permute-done.11 = bf16[64,2048]{1,0:T(8,128)(2,1)S(1)} collective-permute-done((bf16[64,2048]{1,0:T(8,128)(2,1)S(1)}, bf16[64,2048]{1,0:T(8,128)(2,1)S(1)}, u32[]{:S(2)}, u32[]{:S(2)}) %collective-permute-start.11) | collective-permute-done | bytes 262176 | tf_op jit(solution)/shard_map/ppermute | solution.py:103
  167.5 2.7 %collective-permute-done.12 = bf16[64,2048]{1,0:T(8,128)(2,1)S(1)} collective-permute-done((bf16[64,2048]{1,0:T(8,128)(2,1)S(1)}, bf16[64,2048]{1,0:T(8,128)(2,1)S(1)}, u32[]{:S(2)}, u32[]{:S(2)}) %collective-permute-start.12) | collective-permute-done | bytes 262176 | tf_op jit(solution)/shard_map/ppermute | solution.py:103
  (183 shorter events, 49.0 us)
Async XLA Ops:
  0.0 30.8 %copy-start = (bf16[2,2048,256]{2,1,0:T(8,128)(2,1)S(1)}, bf16[2,2048,256]{2,1,0:T(8,128)(2,1)}, u32[]{:S(2)}) copy-start(bf16[2,2048,256]{2,1,0:T(8,128)(2,1)} %param.18) | copy-start | bytes 6291460
  3.8 25.3 %collective-permute-start.2 = (bf16[64,2048]{1,0:T(8,128)(2,1)}, bf16[64,2048]{1,0:T(8,128)(2,1)}, u32[]{:S(2)}, u32[]{:S(2)}) collective-permute-start(bf16[64,2048]{1,0:T(8,128)(2,1)} %fusion.56), channel_id=1, source_target_pairs={{0,8},{8,16},{16,24},{24,0},{1,9},{9,17},{17,25},{25,1},{2,10},{10... | collective-permute-start | bytes 786440 | tf_op jit(solution)/shard_map/ppermute | solution.py:93
  4.2 24.9 %collective-permute-start.1 = (bf16[64,2048]{1,0:T(8,128)(2,1)}, bf16[64,2048]{1,0:T(8,128)(2,1)}, u32[]{:S(2)}, u32[]{:S(2)}) collective-permute-start(bf16[64,2048]{1,0:T(8,128)(2,1)} %fusion.56), channel_id=1, source_target_pairs={{0,16},{8,24},{16,0},{24,8},{1,17},{9,25},{17,1},{25,9},{2,18},{10... | collective-permute-start | bytes 786440 | tf_op jit(solution)/shard_map/ppermute | solution.py:93
  6.8 22.3 %collective-permute-start = (bf16[64,2048]{1,0:T(8,128)(2,1)}, bf16[64,2048]{1,0:T(8,128)(2,1)}, u32[]{:S(2)}, u32[]{:S(2)}) collective-permute-start(bf16[64,2048]{1,0:T(8,128)(2,1)} %fusion.56), channel_id=1, source_target_pairs={{0,24},{8,0},{16,8},{24,16},{1,25},{9,1},{17,9},{25,17},{2,26},{10... | collective-permute-start | bytes 786440 | tf_op jit(solution)/shard_map/ppermute | solution.py:93
  19.9 15.0 %copy-start.14 = (pred[256]{0:T(512)(128)(4,1)}, pred[256]{0:T(512)(128)(4,1)S(1)}, u32[]{:S(2)}) copy-start(pred[256]{0:T(512)(128)(4,1)S(1)} %get-tuple-element.66) | copy-start | bytes 772
  19.9 15.0 %copy-start.15 = (pred[256]{0:T(512)(128)(4,1)}, pred[256]{0:T(512)(128)(4,1)S(1)}, u32[]{:S(2)}) copy-start(pred[256]{0:T(512)(128)(4,1)S(1)} %get-tuple-element.67) | copy-start | bytes 772
  19.9 15.0 %copy-start.16 = (pred[256]{0:T(512)(128)(4,1)}, pred[256]{0:T(512)(128)(4,1)S(1)}, u32[]{:S(2)}) copy-start(pred[256]{0:T(512)(128)(4,1)S(1)} %get-tuple-element.68) | copy-start | bytes 772
  19.9 15.0 %copy-start.17 = (pred[256]{0:T(512)(128)(4,1)}, pred[256]{0:T(512)(128)(4,1)S(1)}, u32[]{:S(2)}) copy-start(pred[256]{0:T(512)(128)(4,1)S(1)} %get-tuple-element.69) | copy-start | bytes 772
  19.9 15.0 %copy-start.18 = (pred[256]{0:T(512)(128)(4,1)}, pred[256]{0:T(512)(128)(4,1)S(1)}, u32[]{:S(2)}) copy-start(pred[256]{0:T(512)(128)(4,1)S(1)} %get-tuple-element.70) | copy-start | bytes 772
  28.4 4.2 %copy-start.31 = (bf16[4,2048,256]{2,1,0:T(8,128)(2,1)S(1)}, bf16[4,2048,256]{2,1,0:T(8,128)(2,1)}, u32[]{:S(2)}) copy-start(bf16[4,2048,256]{2,1,0:T(8,128)(2,1)} %param.17) | copy-start | bytes 12582916
  34.8 5.9 %slice-start = ((f32[2,256,256]{1,2,0:T(8,128)}), f32[1,256,256]{1,2,0:T(8,128)S(1)}, s32[]{:S(2)}) async-start(f32[2,256,256]{1,2,0:T(8,128)} %copy-done.11), calls=%async_computation.1 | async-start | bytes 524288 | tf_op jit(solution)/shard_map/slice | solution.py:254
  38.7 20.8 %collective-permute-start.3 = (bf16[512,256]{1,0:T(8,128)(2,1)}, bf16[512,256]{1,0:T(8,128)(2,1)}, u32[]{:S(2)}, u32[]{:S(2)}) collective-permute-start(bf16[512,256]{1,0:T(8,128)(2,1)} %pad_maximum_fusion.2), channel_id=1, source_target_pairs={{1,0},{3,1},{5,3},{7,5},{6,7},{4,6},{2,4},{0,2},{9,8},{11,9},{13,1... | collective-permute-start | bytes 786440 | tf_op jit(solution)/shard_map/ppermute | solution.py:121
  40.3 16.5 %collective-permute-start.6 = (bf16[512,256]{1,0:T(8,128)(2,1)}, bf16[512,256]{1,0:T(8,128)(2,1)}, u32[]{:S(2)}, u32[]{:S(2)}) collective-permute-start(bf16[512,256]{1,0:T(8,128)(2,1)} %pad_maximum_fusion.2), channel_id=1, source_target_pairs={{0,1},{1,3},{3,5},{5,7},{7,6},{6,4},{4,2},{2,0},{8,9},{9,11},{11,1... | collective-permute-start | bytes 786440 | tf_op jit(solution)/shard_map/ppermute | solution.py:117
  52.1 6.2 %copy-start.12 = (bf16[1,256,256]{1,2,0:T(8,128)(2,1)S(1)}, bf16[1,256,256]{1,2,0:T(8,128)(2,1)}, u32[]{:S(2)}) copy-start(bf16[1,256,256]{1,2,0:T(8,128)(2,1)} %slice.777) | copy-start | bytes 393220
  52.1 13.1 %copy-start.7 = (bf16[256,256]{1,0:T(8,128)(2,1)S(1)}, bf16[256,256]{1,0:T(8,128)(2,1)}, u32[]{:S(2)}) copy-start(bf16[256,256]{1,0:T(8,128)(2,1)} %copy-done.6) | copy-start | bytes 393220
  55.5 23.0 %copy-start.1 = (bf16[16,128,256]{2,1,0:T(8,128)(2,1)S(1)}, bf16[16,128,256]{2,1,0:T(8,128)(2,1)}, u32[]{:S(2)}) copy-start(bf16[16,128,256]{2,1,0:T(8,128)(2,1)} %get-tuple-element.95.k_ref) | copy-start | bytes 3145732
  56.8 7.0 %collective-permute-start.7 = (bf16[512,256]{1,0:T(8,128)(2,1)}, bf16[512,256]{1,0:T(8,128)(2,1)S(1)}, u32[]{:S(2)}, u32[]{:S(2)}) collective-permute-start(bf16[512,256]{1,0:T(8,128)(2,1)} %collective-permute-done.6), channel_id=1, source_target_pairs={{0,1},{1,3},{3,5},{5,7},{7,6},{6,4},{4,2},{2,0},{8,9},{9,11},{11,1... | collective-permute-start | bytes 786440 | tf_op jit(solution)/shard_map/ppermute | solution.py:117
  59.5 6.7 %collective-permute-start.4 = (bf16[512,256]{1,0:T(8,128)(2,1)}, bf16[512,256]{1,0:T(8,128)(2,1)S(1)}, u32[]{:S(2)}, u32[]{:S(2)}) collective-permute-start(bf16[512,256]{1,0:T(8,128)(2,1)} %collective-permute-done.3), channel_id=1, source_target_pairs={{1,0},{3,1},{5,3},{7,5},{6,7},{4,6},{2,4},{0,2},{9,8},{11,9},{13,1... | collective-permute-start | bytes 786440 | tf_op jit(solution)/shard_map/ppermute | solution.py:121
  63.8 7.3 %collective-permute-start.8 = (bf16[512,256]{1,0:T(8,128)(2,1)S(1)}, bf16[512,256]{1,0:T(8,128)(2,1)S(1)}, u32[]{:S(2)}, u32[]{:S(2)}) collective-permute-start(bf16[512,256]{1,0:T(8,128)(2,1)S(1)} %collective-permute-done.7), channel_id=1, source_target_pairs={{0,1},{1,3},{3,5},{5,7},{7,6},{6,4},{4,2},{2,0},{8,9},{9,11},{11,1... | collective-permute-start | bytes 786440 | tf_op jit(solution)/shard_map/ppermute | solution.py:117
  66.2 6.4 %collective-permute-start.5 = (bf16[512,256]{1,0:T(8,128)(2,1)S(1)}, bf16[512,256]{1,0:T(8,128)(2,1)S(1)}, u32[]{:S(2)}, u32[]{:S(2)}) collective-permute-start(bf16[512,256]{1,0:T(8,128)(2,1)S(1)} %collective-permute-done.4), channel_id=1, source_target_pairs={{1,0},{3,1},{5,3},{7,5},{6,7},{4,6},{2,4},{0,2},{9,8},{11,9},{13,1... | collective-permute-start | bytes 786440 | tf_op jit(solution)/shard_map/ppermute | solution.py:121
  71.0 6.4 %collective-permute-start.9 = (bf16[512,256]{1,0:T(8,128)(2,1)S(1)}, bf16[512,256]{1,0:T(8,128)(2,1)S(1)}, u32[]{:S(2)}, u32[]{:S(2)}) collective-permute-start(bf16[512,256]{1,0:T(8,128)(2,1)S(1)} %collective-permute-done.8), channel_id=1, source_target_pairs={{0,1},{1,3},{3,5},{5,7},{7,6},{6,4},{4,2},{2,0},{8,9},{9,11},{11,1... | collective-permute-start | bytes 786440 | tf_op jit(solution)/shard_map/ppermute | solution.py:117
  91.4 8.2 %copy-start.4 = (bf16[4,64,2048]{2,1,0:T(8,128)(2,1)S(1)}, bf16[4,64,2048]{2,1,0:T(8,128)(2,1)}, u32[]{:S(2)}) copy-start(bf16[4,64,2048]{2,1,0:T(8,128)(2,1)} %copy-done.3) | copy-start | bytes 3145732
  91.4 8.2 %copy-start.13 = (bf16[2048,4]{0,1:T(4,128)(2,1)S(1)}, bf16[2048,4]{0,1:T(4,128)(2,1)}, u32[]{:S(2)}) copy-start(bf16[2048,4]{0,1:T(4,128)(2,1)} %param.15) | copy-start | bytes 49156
  93.0 51.3 %all-to-all-start = ((bf16[8,264,512]{2,1,0:T(8,128)(2,1)}), bf16[8,264,512]{2,1,0:T(8,128)(2,1)}, u32[]{:S(2)}, u32[]{:S(2)}) async-start(bf16[8,264,512]{2,1,0:T(8,128)(2,1)} %pad_maximum_fusion), calls=%async_computation | async-start | bytes 4325376 | tf_op jit(solution)/shard_map/all_to_all | solution.py:319
  100.0 49.8 %copy-start.5 = (f32[2,256,2,128]{3,1,2,0:T(8,128)S(1)}, f32[2,256,2,128]{3,1,2,0:T(8,128)}, u32[]{:S(2)}) copy-start(f32[2,256,2,128]{3,1,2,0:T(8,128)} %fusion.59) | copy-start | bytes 1572868
  150.3 6.5 %copy-start.30 = (f32[64]{0:T(128)S(1)}, f32[64]{0:T(128)}, u32[]{:S(2)}) copy-start(f32[64]{0:T(128)} %get-tuple-element.79) | copy-start | bytes 772
  150.4 5.1 %copy-start.2 = (bf16[4,256,2048]{2,1,0:T(8,128)(2,1)S(1)}, bf16[4,256,2048]{2,1,0:T(8,128)(2,1)}, u32[]{:S(2)}) copy-start(bf16[4,256,2048]{2,1,0:T(8,128)(2,1)} %param.19) | copy-start | bytes 12582916
  152.2 4.9 %copy-start.29 = (f32[64]{0:T(128)S(1)}, f32[64]{0:T(128)}, u32[]{:S(2)}) copy-start(f32[64]{0:T(128)} %get-tuple-element.78) | copy-start | bytes 772
  156.7 7.8 %collective-permute-start.10 = (bf16[64,2048]{1,0:T(8,128)(2,1)S(1)}, bf16[64,2048]{1,0:T(8,128)(2,1)S(1)}, u32[]{:S(2)}, u32[]{:S(2)}) collective-permute-start(bf16[64,2048]{1,0:T(8,128)(2,1)S(1)} %fusion.16), channel_id=1, source_target_pairs={{0,8},{8,16},{16,24},{24,0},{1,9},{9,17},{17,25},{25,1},{2,10},{10... | collective-permute-start | bytes 786440 | tf_op jit(solution)/shard_map/ppermute | solution.py:103
  158.2 5.0 %copy-start.25 = (f32[64]{0:T(128)S(1)}, f32[64]{0:T(128)}, u32[]{:S(2)}) copy-start(f32[64]{0:T(128)} %get-tuple-element.73) | copy-start | bytes 772
  158.2 9.3 %collective-permute-start.11 = (bf16[64,2048]{1,0:T(8,128)(2,1)S(1)}, bf16[64,2048]{1,0:T(8,128)(2,1)S(1)}, u32[]{:S(2)}, u32[]{:S(2)}) collective-permute-start(bf16[64,2048]{1,0:T(8,128)(2,1)S(1)} %fusion.15), channel_id=1, source_target_pairs={{0,16},{8,24},{16,0},{24,8},{1,17},{9,25},{17,1},{25,9},{2,18},{10... | collective-permute-start | bytes 786440 | tf_op jit(solution)/shard_map/ppermute | solution.py:103
  161.7 8.5 %collective-permute-start.12 = (bf16[64,2048]{1,0:T(8,128)(2,1)S(1)}, bf16[64,2048]{1,0:T(8,128)(2,1)S(1)}, u32[]{:S(2)}, u32[]{:S(2)}) collective-permute-start(bf16[64,2048]{1,0:T(8,128)(2,1)S(1)} %fusion.14), channel_id=1, source_target_pairs={{0,24},{8,0},{16,8},{24,16},{1,25},{9,1},{17,9},{25,17},{2,26},{10... | collective-permute-start | bytes 786440 | tf_op jit(solution)/shard_map/ppermute | solution.py:103
  (15 other events, 39.4 us)

commit v18 on v16

--- a/solution.py
+++ b/solution.py
@@ -283,6 +283,9 @@
         new_values,
         preferred_element_type=jnp.float32,
     )
+    self_best = jnp.transpose(self_best, (0, 2, 1))
+    self_total = jnp.transpose(self_total, (0, 2, 1))
+    self_accum = jnp.transpose(self_accum, (0, 3, 2, 1))
     ring_queries, self_best, self_total, self_accum = lax.optimization_barrier(
         (ring_queries, self_best, self_total, self_accum)
     )
@@ -327,24 +330,20 @@
     part_totals = part_stats[:, 2] + part_stats[:, 3]
     cache_best = jnp.max(part_best, axis=0)
     share = jnp.exp(part_best - cache_best[None])
-    cache_total = jnp.swapaxes(
-        jnp.sum(part_totals * share, axis=0).reshape(local_heads, 2, new_count), 1, 2
-    )
-    cache_accum = jnp.transpose(
-        jnp.sum(part_accum * share[:, :, None, :], axis=0).reshape(local_heads, HD, 2, new_count),
-        (0, 3, 2, 1),
-    )
-    cache_best = jnp.swapaxes(cache_best.reshape(local_heads, 2, new_count), 1, 2)
+    cache_total = jnp.sum(part_totals * share, axis=0).reshape(local_heads, 2, new_count)
+    cache_accum = jnp.sum(part_accum * share[:, :, None, :], axis=0).reshape(
+        local_heads, HD, 2, new_count
+    )
+    cache_best = cache_best.reshape(local_heads, 2, new_count)
 
     peak = jnp.maximum(cache_best, self_best)
     cache_share = jnp.exp(cache_best - peak)
     self_share = jnp.exp(self_best - peak)
-    numerator = cache_accum * cache_share[..., None] + self_accum * self_share[..., None]
+    numerator = cache_accum * cache_share[:, None] + self_accum * self_share[:, None]
     denominator = cache_total * cache_share + self_total * self_share
-    attended = (
-        jnp.transpose((numerator / denominator[..., None]).astype(jnp.bfloat16), (1, 2, 0, 3))
-        .reshape(new_count, 2, local_heads * HD)
-    )
+    attended = jnp.transpose(
+        (numerator / denominator[:, None]).astype(jnp.bfloat16), (3, 2, 0, 1)
+    ).reshape(new_count, 2, local_heads * HD)
     output_blocks = []
     for block in list(range(1, head_count)) + [0]:
         rows = slice(block * rows_each, (block + 1) * rows_each)

time: 169 us -> 169 us (level)
  no operation moved by 1% of the time
where the time goes in v18:
time: 169 us; the launch traced here: 168 us
  waiting for transfers between devices  61.1 us (36%)
  local copies, waits for them, and re-layouts  30.8 us (18%)
  other arithmetic  26.8 us (16%)
  starting transfers between devices  21.1 us (12%)
  matrix products  15.5 us (9%)
  Pallas kernels  11.8 us (7%)
    all_to_all x1, waiting for transfers between devices, per_device(): received = lax.all_to_all(payload, 'seq', 0, 0, tiled=True)  43.5 us
    pallas_call x1, Pallas kernels, block_attention(): pl.pallas_call(kernel, grid_spec=grid_spec, out_shape=[jax.ShapeDtypeStru...  11.8 us
    ppermute x4, waiting for transfers between devices, ring_all_gather(): moving = lax.ppermute(moving, axis_name, forward)  11.1 us
    dot_general x16, matrix products, per_device(): jnp.dot(picked, o_weight[expert], preferred_element_type=jnp.float32)  9.73 us
    unnamed x123, local copies, waits for them, and re-layouts  8.74 us
    all_to_all x1, starting transfers between devices, per_device(): received = lax.all_to_all(payload, 'seq', 0, 0, tiled=True)  5.8 us
    ppermute x3, waiting for transfers between devices, shift_reduce_scatter(): lax.ppermute(blocks[s], axis_name, [(i, (i + s) % size) for i in range(si...  5.48 us
    ppermute x4, starting transfers between devices, ring_all_gather(): moving = lax.ppermute(moving, axis_name, forward)  4.96 us
  transfers between devices with their start and end apart: 14, of which 7 were waited for; matrix products, arithmetic and copies ran while one was open for 22% of the time, Pallas kernels for 0%

profile of v18, /device:TPU:0, one launch (start us, length us, event | category | flops | bytes accessed | tf_op | source)
XLA Modules:
  0.0 168.3 jit_solution(10162390221318542973)
XLA Ops:
  2.0 1.8 %fusion.56 = bf16[64,2048]{1,0:T(8,128)(2,1)} fusion(bf16[1,64,2048]{2,1,0:T(8,128)(2,1)} %param.13, f32[2048]{0:T(1024)S(1)} %convert_element_type.115, f32[64]{0:T(128)S(1)} %add_rsqrt_fusion), kind=kLoop, calls=%fused_computation.90 | loop fusion | flops 524288 | bytes 532736 | tf_op jit(solution)/shard_map/convert_element_type | solution.py:38
  4.2 2.5 %collective-permute-start.1 = (bf16[64,2048]{1,0:T(8,128)(2,1)}, bf16[64,2048]{1,0:T(8,128)(2,1)}, u32[]{:S(2)}, u32[]{:S(2)}) collective-permute-start(bf16[64,2048]{1,0:T(8,128)(2,1)} %fusion.56), channel_id=1, source_target_pairs={{0,16},{8,24},{16,0},{24,8},{1,17},{9,25},{17,1},{25,9},{2,18},{10... | collective-permute-start | bytes 786440 | tf_op jit(solution)/shard_map/ppermute | solution.py:93
  6.8 1.4 collective-permute-start
  14.1 1.3 gather_fusion.1
  19.5 3.1 %fusion.283 = (bf16[1,16,128,256]{3,2,1,0:T(8,128)(2,1)}, bf16[16,128,256]{2,1,0:T(8,128)(2,1)}) fusion(bf16[2,16,128,256]{3,2,1,0:T(8,128)(2,1)} %param.20), kind=kLoop, calls=%fused_computation.443 | loop fusion | bytes 4194304 | tf_op jit(solution)/shard_map/slice | solution.py:298
  27.6 1.6 copy.117
  30.0 1.6 pad_maximum_fusion.1
  33.3 2.0 %multiply_reduce_fusion.1 = (f32[256,256]{1,0:T(8,128)S(1)}, f32[256,256]{1,0:T(8,128)}) fusion(f32[4,256]{1,0:T(4,128)S(1)} %bitcast.433, f32[4,256]{1,0:T(4,128)S(1)} %bitcast.432, bf16[256,2048,1]{1,0,2:T(8,128)(2,1)S(1)} %bitcast.420, bf16[4,2048,256]{2,1,0:T(8,128)(2,1)S(1)} %copy-done.54), kind=kOutput, calls=%fused_computation.65 | convolution fusion | flops 1074659328 | bytes 5775360 | tf_op jit(solution)/shard_map/nd,edc->enc/dot_general | solution.py:227
  37.2 1.8 %reduce_sum.250 = f32[256,1,2,128]{3,2,0,1:T(2,128)} reshape(f32[256,256]{1,0:T(8,128)} %get-tuple-element.34) | data formatting | bytes 524288 | tf_op jit(solution)/shard_map/reduce_sum | solution.py:237
  39.0 2.0 %slice_bitcast_fusion.22 = (f32[256,1,64]{2,0,1:T(8,128)}, f32[256,1,64]{2,0,1:T(8,128)}, f32[256,1,64]{2,0,1:T(8,128)}, f32[256,1,64]{2,0,1:T(8,128)}, f32[256,...) fusion(f32[256,256]{1,0:T(8,128)} %get-tuple-element.34), kind=kLoop, calls=%fused_computation.438 | loop fusion | bytes 786432 | tf_op jit(solution)/shard_map/concatenate | solution.py:238
  42.0 1.6 fusion.63
  45.0 1.6 collective-permute-start.3
  48.5 1.8 %copy.115 = f32[256,2,64]{2,0,1:T(8,128)} copy(f32[256,2,64]{0,2,1:T(8,128)} %get-tuple-element.99) | data formatting | bytes 262144
  50.3 1.8 %fusion.69 = (bf16[256,1,2,128]{3,0,1,2:T(8,128)(2,1)S(1)}, bf16[256,1,2,128]{3,0,1,2:T(8,128)(2,1)S(1)}) fusion(f32[256,1,2,128]{3,0,1,2:T(8,128)} %copy.73, f32[256,1,2,128]{3,2,0,1:T(2,128)} %reduce_sum.249, f32[256,128]{1,0:T(8,128)} %pad_maximum_fusion.3, f32[256,1,2,128]{3,2,0,1:T(2,128)} %reduce_sum.250, f32[256,1,64]{2,0,1:T(8,128)} %get-tuple-element.111, ...), kind=kLoop, calls=%fused_computation.108 | loop fusion | flops 917504 | bytes 1703936 | tf_op jit(solution)/shard_map/convert_element_type | solution.py:249
  54.6 1.5 collective-permute-start.7
  58.6 3.0 %collective-permute-done.7 = bf16[512,256]{1,0:T(8,128)(2,1)S(1)} collective-permute-done((bf16[512,256]{1,0:T(8,128)(2,1)}, bf16[512,256]{1,0:T(8,128)(2,1)S(1)}, u32[]{:S(2)}, u32[]{:S(2)}) %collective-permute-start.7) | collective-permute-done | bytes 262176 | tf_op jit(solution)/shard_map/ppermute | solution.py:117
  61.6 1.5 collective-permute-start.8
  65.5 3.3 %collective-permute-done.8 = bf16[512,256]{1,0:T(8,128)(2,1)S(1)} collective-permute-done((bf16[512,256]{1,0:T(8,128)(2,1)S(1)}, bf16[512,256]{1,0:T(8,128)(2,1)S(1)}, u32[]{:S(2)}, u32[]{:S(2)}) %collective-permute-start.8) | collective-permute-done | bytes 262176 | tf_op jit(solution)/shard_map/ppermute | solution.py:117
  68.8 1.5 collective-permute-start.9
  70.4 4.8 %collective-permute-done.9 = bf16[512,256]{1,0:T(8,128)(2,1)S(1)} collective-permute-done((bf16[512,256]{1,0:T(8,128)(2,1)S(1)}, bf16[512,256]{1,0:T(8,128)(2,1)S(1)}, u32[]{:S(2)}, u32[]{:S(2)}) %collective-permute-start.9) | collective-permute-done | bytes 262176 | tf_op jit(solution)/shard_map/ppermute | solution.py:117
  76.3 11.8 %shard_map.127 = (f32[8,2,1,512]{3,2,1,0:T(1,128)S(1)}, f32[8,2,1,512]{3,2,1,0:T(1,128)S(1)}, f32[8,2,128,512]{3,2,1,0:T(8,128)S(1)}) custom-call(s32[16]{0:T(128)S(1)} %and_select_fusion.offset_ref, s32[16]{0:T(128)S(1)} %broadcast_add_fusion.owner_ref, s32[16]{0:T(128)S(1)} %subtract_clamp_fusion.valid_ref, ...), custom_call_target="tpu_custom_call" | custom-call | tf_op jit(solution)/shard_map/pallas_call | solution.py:179
  89.2 1.5 pad_maximum_fusion
  90.8 5.8 %all-to-all-start = ((bf16[8,264,512]{2,1,0:T(8,128)(2,1)}), bf16[8,264,512]{2,1,0:T(8,128)(2,1)}, u32[]{:S(2)}, u32[]{:S(2)}) async-start(bf16[8,264,512]{2,1,0:T(8,128)(2,1)} %pad_maximum_fusion), calls=%async_computation | async-start | bytes 4325376 | tf_op jit(solution)/shard_map/all_to_all | solution.py:320
  98.6 43.5 %all-to-all-done = bf16[8,264,512]{2,1,0:T(8,128)(2,1)} async-done(((bf16[8,264,512]{2,1,0:T(8,128)(2,1)}), bf16[8,264,512]{2,1,0:T(8,128)(2,1)}, u32[]{:S(2)}, u32[]{:S(2)}) %all-to-all-start) | async-done | bytes 2162720 | tf_op jit(solution)/shard_map/all_to_all | solution.py:320
  143.2 2.1 %fusion = f32[256,512]{1,0:T(8,128)S(1)} fusion(bf16[8,264,512]{2,1,0:T(8,128)(2,1)} %all-to-all-done, f32[8,2,512]{2,1,0:T(2,128)S(1)} %get-tuple-element.87), kind=kLoop, calls=%fused_computation.5 | loop fusion | flops 3014656 | bytes 2654208 | tf_op jit(solution)/shard_map/reduce_sum | solution.py:334
  148.3 1.8 %convolution_multiply_fusion.13 = f32[64,2048]{1,0:T(8,128)S(1)} fusion(bf16[4,256,2048]{2,1,0:T(8,128)(2,1)} %param.19, f32[64]{0:T(128)S(1)} %get-tuple-element.79, pred[64]{0:T(512)(128)(4,1)S(1)} %copy-done.53, pred[64]{0:T(512)(128)(4,1)S(1)} %copy-done.52, bf16[256,2,256]{0,2,1:T(8,128)(2,1)S(1)} %bitcast.403), kind=kOutput, calls=%fused_computation.20 | convolution fusion | flops 67272704 | bytes 1705472 | tf_op jit(solution)/shard_map/dot_general | solution.py:360
  150.2 1.6 convolution_multiply_fusion.12
  151.9 1.6 convolution_multiply_fusion.14
  155.6 1.7 %collective-permute-start.11 = (bf16[64,2048]{1,0:T(8,128)(2,1)S(1)}, bf16[64,2048]{1,0:T(8,128)(2,1)S(1)}, u32[]{:S(2)}, u32[]{:S(2)}) collective-permute-start(bf16[64,2048]{1,0:T(8,128)(2,1)S(1)} %fusion.15), channel_id=1, source_target_pairs={{0,16},{8,24},{16,0},{24,8},{1,17},{9,25},{17,1},{25,9},{2,18},{10... | collective-permute-start | bytes 786440 | tf_op jit(solution)/shard_map/ppermute | solution.py:103
  159.1 1.5 collective-permute-start.12
  162.0 2.9 %collective-permute-done.11 = bf16[64,2048]{1,0:T(8,128)(2,1)S(1)} collective-permute-done((bf16[64,2048]{1,0:T(8,128)(2,1)S(1)}, bf16[64,2048]{1,0:T(8,128)(2,1)S(1)}, u32[]{:S(2)}, u32[]{:S(2)}) %collective-permute-start.11) | collective-permute-done | bytes 262176 | tf_op jit(solution)/shard_map/ppermute | solution.py:103
  164.9 2.6 %collective-permute-done.12 = bf16[64,2048]{1,0:T(8,128)(2,1)S(1)} collective-permute-done((bf16[64,2048]{1,0:T(8,128)(2,1)S(1)}, bf16[64,2048]{1,0:T(8,128)(2,1)S(1)}, u32[]{:S(2)}, u32[]{:S(2)}) %collective-permute-start.12) | collective-permute-done | bytes 262176 | tf_op jit(solution)/shard_map/ppermute | solution.py:103
  (227 shorter events, 47.1 us)
Async XLA Ops:
  0.0 31.6 %copy-start = (bf16[2,2048,256]{2,1,0:T(8,128)(2,1)S(1)}, bf16[2,2048,256]{2,1,0:T(8,128)(2,1)}, u32[]{:S(2)}) copy-start(bf16[2,2048,256]{2,1,0:T(8,128)(2,1)} %param.18) | copy-start | bytes 6291460
  3.8 26.2 %collective-permute-start.2 = (bf16[64,2048]{1,0:T(8,128)(2,1)}, bf16[64,2048]{1,0:T(8,128)(2,1)}, u32[]{:S(2)}, u32[]{:S(2)}) collective-permute-start(bf16[64,2048]{1,0:T(8,128)(2,1)} %fusion.56), channel_id=1, source_target_pairs={{0,8},{8,16},{16,24},{24,0},{1,9},{9,17},{17,25},{25,1},{2,10},{10... | collective-permute-start | bytes 786440 | tf_op jit(solution)/shard_map/ppermute | solution.py:93
  4.2 25.7 %collective-permute-start.1 = (bf16[64,2048]{1,0:T(8,128)(2,1)}, bf16[64,2048]{1,0:T(8,128)(2,1)}, u32[]{:S(2)}, u32[]{:S(2)}) collective-permute-start(bf16[64,2048]{1,0:T(8,128)(2,1)} %fusion.56), channel_id=1, source_target_pairs={{0,16},{8,24},{16,0},{24,8},{1,17},{9,25},{17,1},{25,9},{2,18},{10... | collective-permute-start | bytes 786440 | tf_op jit(solution)/shard_map/ppermute | solution.py:93
  6.8 23.2 %collective-permute-start = (bf16[64,2048]{1,0:T(8,128)(2,1)}, bf16[64,2048]{1,0:T(8,128)(2,1)}, u32[]{:S(2)}, u32[]{:S(2)}) collective-permute-start(bf16[64,2048]{1,0:T(8,128)(2,1)} %fusion.56), channel_id=1, source_target_pairs={{0,24},{8,0},{16,8},{24,16},{1,25},{9,1},{17,9},{25,17},{2,26},{10... | collective-permute-start | bytes 786440 | tf_op jit(solution)/shard_map/ppermute | solution.py:93
  39.0 8.0 %slice-start = ((f32[2,256,256]{1,2,0:T(8,128)}), f32[1,256,256]{1,2,0:T(8,128)S(1)}, s32[]{:S(2)}) async-start(f32[2,256,256]{1,2,0:T(8,128)} %copy-done.12), calls=%async_computation.1 | async-start | bytes 524288 | tf_op jit(solution)/shard_map/slice | solution.py:252
  45.0 12.3 %collective-permute-start.3 = (bf16[512,256]{1,0:T(8,128)(2,1)}, bf16[512,256]{1,0:T(8,128)(2,1)}, u32[]{:S(2)}, u32[]{:S(2)}) collective-permute-start(bf16[512,256]{1,0:T(8,128)(2,1)} %pad_maximum_fusion.2), channel_id=1, source_target_pairs={{1,0},{3,1},{5,3},{7,5},{6,7},{4,6},{2,4},{0,2},{9,8},{11,9},{13,1... | collective-permute-start | bytes 786440 | tf_op jit(solution)/shard_map/ppermute | solution.py:121
  46.5 8.0 %collective-permute-start.6 = (bf16[512,256]{1,0:T(8,128)(2,1)}, bf16[512,256]{1,0:T(8,128)(2,1)}, u32[]{:S(2)}, u32[]{:S(2)}) collective-permute-start(bf16[512,256]{1,0:T(8,128)(2,1)} %pad_maximum_fusion.2), channel_id=1, source_target_pairs={{0,1},{1,3},{3,5},{5,7},{7,6},{6,4},{4,2},{2,0},{8,9},{9,11},{11,1... | collective-permute-start | bytes 786440 | tf_op jit(solution)/shard_map/ppermute | solution.py:117
  48.5 14.6 %copy-start.7 = (bf16[256,256]{1,0:T(8,128)(2,1)S(1)}, bf16[256,256]{1,0:T(8,128)(2,1)}, u32[]{:S(2)}) copy-start(bf16[256,256]{1,0:T(8,128)(2,1)} %copy-done.6) | copy-start | bytes 393220
  48.5 14.6 %copy-start.9 = (bf16[256,256]{1,0:T(8,128)(2,1)S(1)}, bf16[256,256]{1,0:T(8,128)(2,1)}, u32[]{:S(2)}) copy-start(bf16[256,256]{1,0:T(8,128)(2,1)} %copy-done.8) | copy-start | bytes 393220
  53.2 23.0 %copy-start.1 = (bf16[16,128,256]{2,1,0:T(8,128)(2,1)S(1)}, bf16[16,128,256]{2,1,0:T(8,128)(2,1)}, u32[]{:S(2)}) copy-start(bf16[16,128,256]{2,1,0:T(8,128)(2,1)} %get-tuple-element.91.k_ref) | copy-start | bytes 3145732
  54.6 7.0 %collective-permute-start.7 = (bf16[512,256]{1,0:T(8,128)(2,1)}, bf16[512,256]{1,0:T(8,128)(2,1)S(1)}, u32[]{:S(2)}, u32[]{:S(2)}) collective-permute-start(bf16[512,256]{1,0:T(8,128)(2,1)} %collective-permute-done.6), channel_id=1, source_target_pairs={{0,1},{1,3},{3,5},{5,7},{7,6},{6,4},{4,2},{2,0},{8,9},{9,11},{11,1... | collective-permute-start | bytes 786440 | tf_op jit(solution)/shard_map/ppermute | solution.py:117
  57.3 6.7 %collective-permute-start.4 = (bf16[512,256]{1,0:T(8,128)(2,1)}, bf16[512,256]{1,0:T(8,128)(2,1)S(1)}, u32[]{:S(2)}, u32[]{:S(2)}) collective-permute-start(bf16[512,256]{1,0:T(8,128)(2,1)} %collective-permute-done.3), channel_id=1, source_target_pairs={{1,0},{3,1},{5,3},{7,5},{6,7},{4,6},{2,4},{0,2},{9,8},{11,9},{13,1... | collective-permute-start | bytes 786440 | tf_op jit(solution)/shard_map/ppermute | solution.py:121
  61.6 7.3 %collective-permute-start.8 = (bf16[512,256]{1,0:T(8,128)(2,1)S(1)}, bf16[512,256]{1,0:T(8,128)(2,1)S(1)}, u32[]{:S(2)}, u32[]{:S(2)}) collective-permute-start(bf16[512,256]{1,0:T(8,128)(2,1)S(1)} %collective-permute-done.7), channel_id=1, source_target_pairs={{0,1},{1,3},{3,5},{5,7},{7,6},{6,4},{4,2},{2,0},{8,9},{9,11},{11,1... | collective-permute-start | bytes 786440 | tf_op jit(solution)/shard_map/ppermute | solution.py:117
  64.0 6.4 %collective-permute-start.5 = (bf16[512,256]{1,0:T(8,128)(2,1)S(1)}, bf16[512,256]{1,0:T(8,128)(2,1)S(1)}, u32[]{:S(2)}, u32[]{:S(2)}) collective-permute-start(bf16[512,256]{1,0:T(8,128)(2,1)S(1)} %collective-permute-done.4), channel_id=1, source_target_pairs={{1,0},{3,1},{5,3},{7,5},{6,7},{4,6},{2,4},{0,2},{9,8},{11,9},{13,1... | collective-permute-start | bytes 786440 | tf_op jit(solution)/shard_map/ppermute | solution.py:121
  68.8 6.4 %collective-permute-start.9 = (bf16[512,256]{1,0:T(8,128)(2,1)S(1)}, bf16[512,256]{1,0:T(8,128)(2,1)S(1)}, u32[]{:S(2)}, u32[]{:S(2)}) collective-permute-start(bf16[512,256]{1,0:T(8,128)(2,1)S(1)} %collective-permute-done.8), channel_id=1, source_target_pairs={{0,1},{1,3},{3,5},{5,7},{7,6},{6,4},{4,2},{2,0},{8,9},{9,11},{11,1... | collective-permute-start | bytes 786440 | tf_op jit(solution)/shard_map/ppermute | solution.py:117
  89.2 8.7 %copy-start.4 = (bf16[4,64,2048]{2,1,0:T(8,128)(2,1)S(1)}, bf16[4,64,2048]{2,1,0:T(8,128)(2,1)}, u32[]{:S(2)}) copy-start(bf16[4,64,2048]{2,1,0:T(8,128)(2,1)} %copy-done.3) | copy-start | bytes 3145732
  89.2 8.7 %copy-start.18 = (bf16[2048,4]{0,1:T(4,128)(2,1)S(1)}, bf16[2048,4]{0,1:T(4,128)(2,1)}, u32[]{:S(2)}) copy-start(bf16[2048,4]{0,1:T(4,128)(2,1)} %param.15) | copy-start | bytes 49156
  89.2 9.0 %copy-start.17 = (s32[256,2]{0,1:T(2,128)S(1)}, s32[256,2]{0,1:T(2,128)}, u32[]{:S(2)}) copy-start(s32[256,2]{0,1:T(2,128)} %copy-done.16) | copy-start | bytes 6148
  89.2 9.1 %copy-start.15 = (f32[256,2,4]{0,1,2:T(2,128)S(1)}, f32[256,2,4]{0,1,2:T(2,128)}, u32[]{:S(2)}) copy-start(f32[256,2,4]{0,1,2:T(2,128)} %copy-done.14) | copy-start | bytes 24580
  90.8 51.3 %all-to-all-start = ((bf16[8,264,512]{2,1,0:T(8,128)(2,1)}), bf16[8,264,512]{2,1,0:T(8,128)(2,1)}, u32[]{:S(2)}, u32[]{:S(2)}) async-start(bf16[8,264,512]{2,1,0:T(8,128)(2,1)} %pad_maximum_fusion), calls=%async_computation | async-start | bytes 4325376 | tf_op jit(solution)/shard_map/all_to_all | solution.py:320
  96.6 51.0 %copy-start.19 = (f32[2,256,2]{1,2,0:T(2,128)S(1)}, f32[2,256,2]{1,2,0:T(2,128)}, u32[]{:S(2)}) copy-start(f32[2,256,2]{1,2,0:T(2,128)} %fusion.35) | copy-start | bytes 12292
  97.9 50.5 %copy-start.52 = (pred[64]{0:T(512)(128)(4,1)S(1)}, pred[64]{0:T(512)(128)(4,1)}, u32[]{:S(2)}) copy-start(pred[64]{0:T(512)(128)(4,1)} %get-tuple-element.46) | copy-start | bytes 196
  97.9 50.5 %copy-start.53 = (pred[64]{0:T(512)(128)(4,1)S(1)}, pred[64]{0:T(512)(128)(4,1)}, u32[]{:S(2)}) copy-start(pred[64]{0:T(512)(128)(4,1)} %get-tuple-element.49) | copy-start | bytes 196
  98.3 49.4 %copy-start.5 = (f32[2,128,2,256]{1,3,2,0:T(8,128)S(1)}, f32[2,128,2,256]{1,3,2,0:T(8,128)}, u32[]{:S(2)}) copy-start(f32[2,128,2,256]{1,3,2,0:T(8,128)} %convolution_bitcast_fusion.1) | copy-start | bytes 1572868
  143.1 7.0 %copy-start.50 = (pred[64]{0:T(512)(128)(4,1)S(1)}, pred[64]{0:T(512)(128)(4,1)}, u32[]{:S(2)}) copy-start(pred[64]{0:T(512)(128)(4,1)} %get-tuple-element.47) | copy-start | bytes 196
  143.1 7.0 %copy-start.51 = (pred[64]{0:T(512)(128)(4,1)S(1)}, pred[64]{0:T(512)(128)(4,1)}, u32[]{:S(2)}) copy-start(pred[64]{0:T(512)(128)(4,1)} %get-tuple-element.50) | copy-start | bytes 196
  145.2 6.6 %copy-start.48 = (pred[64]{0:T(512)(128)(4,1)S(1)}, pred[64]{0:T(512)(128)(4,1)}, u32[]{:S(2)}) copy-start(pred[64]{0:T(512)(128)(4,1)} %get-tuple-element.45) | copy-start | bytes 196
  146.4 7.2 %copy-start.46 = (pred[64]{0:T(512)(128)(4,1)S(1)}, pred[64]{0:T(512)(128)(4,1)}, u32[]{:S(2)}) copy-start(pred[64]{0:T(512)(128)(4,1)} %get-tuple-element.118) | copy-start | bytes 196
  146.4 7.2 %copy-start.47 = (pred[64]{0:T(512)(128)(4,1)S(1)}, pred[64]{0:T(512)(128)(4,1)}, u32[]{:S(2)}) copy-start(pred[64]{0:T(512)(128)(4,1)} %get-tuple-element.119) | copy-start | bytes 196
  154.0 8.0 %collective-permute-start.10 = (bf16[64,2048]{1,0:T(8,128)(2,1)S(1)}, bf16[64,2048]{1,0:T(8,128)(2,1)S(1)}, u32[]{:S(2)}, u32[]{:S(2)}) collective-permute-start(bf16[64,2048]{1,0:T(8,128)(2,1)S(1)} %fusion.16), channel_id=1, source_target_pairs={{0,8},{8,16},{16,24},{24,0},{1,9},{9,17},{17,25},{25,1},{2,10},{10... | collective-permute-start | bytes 786440 | tf_op jit(solution)/shard_map/ppermute | solution.py:103
  155.6 9.3 %collective-permute-start.11 = (bf16[64,2048]{1,0:T(8,128)(2,1)S(1)}, bf16[64,2048]{1,0:T(8,128)(2,1)S(1)}, u32[]{:S(2)}, u32[]{:S(2)}) collective-permute-start(bf16[64,2048]{1,0:T(8,128)(2,1)S(1)} %fusion.15), channel_id=1, source_target_pairs={{0,16},{8,24},{16,0},{24,8},{1,17},{9,25},{17,1},{25,9},{2,18},{10... | collective-permute-start | bytes 786440 | tf_op jit(solution)/shard_map/ppermute | solution.py:103
  159.1 8.4 %collective-permute-start.12 = (bf16[64,2048]{1,0:T(8,128)(2,1)S(1)}, bf16[64,2048]{1,0:T(8,128)(2,1)S(1)}, u32[]{:S(2)}, u32[]{:S(2)}) collective-permute-start(bf16[64,2048]{1,0:T(8,128)(2,1)S(1)} %fusion.14), channel_id=1, source_target_pairs={{0,24},{8,0},{16,8},{24,16},{1,25},{9,1},{17,9},{25,17},{2,26},{10... | collective-permute-start | bytes 786440 | tf_op jit(solution)/shard_map/ppermute | solution.py:103
  (38 other events, 132.2 us)

commit v19 on v16

--- a/solution.py
+++ b/solution.py
@@ -248,7 +248,8 @@
         )
         slot_tables.append((slot_q * cosine + swapped * signed_sine).astype(jnp.bfloat16))
     queries = jnp.stack(slot_tables, axis=1).reshape(new_count, 2, local_heads, HD)
-    fresh = jnp.einsum("nd,sdc->snc", gathered, kv_weight, preferred_element_type=jnp.float32)
+    kv_input, slot_tables = lax.optimization_barrier((gathered, slot_tables))
+    fresh = jnp.einsum("nd,sdc->snc", kv_input, kv_weight, preferred_element_type=jnp.float32)
     new_keys = rotate(fresh[0].reshape(new_count, local_heads, HD), positions).astype(jnp.bfloat16)
     new_values = fresh[1].reshape(new_count, local_heads, HD).astype(jnp.bfloat16)
     ring_queries = ring_all_gather(jnp.concatenate(slot_tables, axis=0), "seq", cycle)

time: 169 us -> 173 us (1.024)
  local copies, waits for them, and re-layouts: 30.9 us -> 33.8 us
  matrix products: 15.5 us -> 18.1 us
    dot_general x1, matrix products: 1.98 us -> 4.59 us  [per_device(): jnp.einsum('nd,edc->enc', gathered, q_weight, preferred_element_type=jnp....]
    unnamed x123 -> x115, local copies, waits for them, and re-layouts: 8.76 us -> 10.6 us
  transfers between devices with their start and end apart: 14 -> 14, of which waited for: 7 -> 7; matrix products, arithmetic and copies ran while one was open for 22% -> 24% of each run, Pallas kernels for 0% -> 0%
where the time goes in v19:
time: 173 us; the launch traced here: 172 us
  waiting for transfers between devices  60.2 us (35%)
  local copies, waits for them, and re-layouts  33.8 us (20%)
  other arithmetic  25.6 us (15%)
  starting transfers between devices  21.1 us (12%)
  matrix products  18.1 us (10%)
  Pallas kernels  11.8 us (7%)
    all_to_all x1, waiting for transfers between devices, per_device(): received = lax.all_to_all(payload, 'seq', 0, 0, tiled=True)  43.5 us
    pallas_call x1, Pallas kernels, block_attention(): pl.pallas_call(kernel, grid_spec=grid_spec, out_shape=[jax.ShapeDtypeStru...  11.8 us
    ppermute x4, waiting for transfers between devices, ring_all_gather(): moving = lax.ppermute(moving, axis_name, forward)  10.9 us
    unnamed x115, local copies, waits for them, and re-layouts  10.6 us
    dot_general x16, matrix products, per_device(): jnp.dot(picked, o_weight[expert], preferred_element_type=jnp.float32)  9.73 us
    ppermute x4, starting transfers between devices, ring_all_gather(): moving = lax.ppermute(moving, axis_name, forward)  6.03 us
    all_to_all x1, starting transfers between devices, per_device(): received = lax.all_to_all(payload, 'seq', 0, 0, tiled=True)  5.8 us
    ppermute x3, waiting for transfers between devices, shift_reduce_scatter(): lax.ppermute(blocks[s], axis_name, [(i, (i + s) % size) for i in range(si...  5.48 us
  transfers between devices with their start and end apart: 14, of which 7 were waited for; matrix products, arithmetic and copies ran while one was open for 24% of the time, Pallas kernels for 0%

profile of v19, /device:TPU:0, one launch (start us, length us, event | category | flops | bytes accessed | tf_op | source)
XLA Modules:
  0.0 171.8 jit_solution(18155871379869264620)
XLA Ops:
  2.0 1.8 %fusion.57 = bf16[64,2048]{1,0:T(8,128)(2,1)} fusion(bf16[1,64,2048]{2,1,0:T(8,128)(2,1)} %param.13, f32[2048]{0:T(1024)S(1)} %convert_element_type.115, f32[64]{0:T(128)S(1)} %add_rsqrt_fusion), kind=kLoop, calls=%fused_computation.90 | loop fusion | flops 524288 | bytes 532736 | tf_op jit(solution)/shard_map/convert_element_type | solution.py:38
  4.2 2.5 %collective-permute-start.1 = (bf16[64,2048]{1,0:T(8,128)(2,1)}, bf16[64,2048]{1,0:T(8,128)(2,1)}, u32[]{:S(2)}, u32[]{:S(2)}) collective-permute-start(bf16[64,2048]{1,0:T(8,128)(2,1)} %fusion.57), channel_id=1, source_target_pairs={{0,16},{8,24},{16,0},{24,8},{1,17},{9,25},{17,1},{25,9},{2,18},{10... | collective-permute-start | bytes 786440 | tf_op jit(solution)/shard_map/ppermute | solution.py:93
  6.8 1.4 collective-permute-start
  14.1 1.3 gather_fusion.1
  19.5 3.1 %fusion.289 = (bf16[1,16,128,256]{3,2,1,0:T(8,128)(2,1)}, bf16[16,128,256]{2,1,0:T(8,128)(2,1)}) fusion(bf16[2,16,128,256]{3,2,1,0:T(8,128)(2,1)} %param.20), kind=kLoop, calls=%fused_computation.449 | loop fusion | bytes 4194304 | tf_op jit(solution)/shard_map/slice | solution.py:296
  27.6 1.6 copy.117
  31.2 4.6 %multiply_reduce_fusion = (f32[256,256]{1,0:T(8,128)S(1)}, f32[256,256]{1,0:T(8,128)}) fusion(f32[4,256]{1,0:T(4,128)} %bitcast.448, f32[4,256]{1,0:T(4,128)} %bitcast.447, bf16[256,2048,1]{1,0,2:T(8,128)(2,1)S(1)} %bitcast.436, bf16[4,2048,256]{2,1,0:T(8,128)(2,1)} %param.17), kind=kOutput, calls=%fused_computation.64 | convolution fusion | flops 1074659328 | bytes 5775360 | tf_op jit(solution)/shard_map/nd,edc->enc/dot_general | solution.py:227
  37.7 1.8 %reduce_sum.249 = f32[256,1,2,128]{3,2,0,1:T(2,128)} reshape(f32[256,256]{1,0:T(8,128)} %get-tuple-element.40) | data formatting | bytes 524288 | tf_op jit(solution)/shard_map/reduce_sum | solution.py:237
  39.5 2.0 %slice_bitcast_fusion.26 = (f32[256,1,64]{2,0,1:T(8,128)}, f32[256,1,64]{2,0,1:T(8,128)}, f32[256,1,64]{2,0,1:T(8,128)}, f32[256,1,64]{2,0,1:T(8,128)}, f32[256,...) fusion(f32[256,256]{1,0:T(8,128)} %get-tuple-element.40), kind=kLoop, calls=%fused_computation.448 | loop fusion | bytes 786432 | tf_op jit(solution)/shard_map/concatenate | solution.py:238
  42.5 1.6 fusion.70
  45.4 1.5 collective-permute-start.6
  49.3 1.8 %copy.116 = f32[256,2,64]{2,0,1:T(8,128)} copy(f32[256,2,64]{0,2,1:T(8,128)} %get-tuple-element.104) | data formatting | bytes 262144
  51.1 1.8 %copy.115 = f32[256,2,64]{2,0,1:T(8,128)} copy(f32[256,2,64]{0,2,1:T(8,128)} %get-tuple-element.105) | data formatting | bytes 262144
  52.8 1.7 %fusion.74 = (bf16[256,1,2,128]{3,0,1,2:T(8,128)(2,1)S(1)}, bf16[256,1,2,128]{3,0,1,2:T(8,128)(2,1)S(1)}) fusion(f32[256,1,2,128]{3,0,1,2:T(8,128)} %copy.73, f32[256,1,2,128]{3,2,0,1:T(2,128)} %reduce_sum.249, f32[256,128]{1,0:T(8,128)S(1)} %copy-done.7, f32[256,1,2,128]{3,2,0,1:T(2,128)} %reduce_sum.250, f32[256,1,64]{2,0,1:T(8,128)} %get-tuple-element.117, ...), kind=kLoop, calls=%fused_computation.112 | loop fusion | flops 917504 | bytes 1703936 | tf_op jit(solution)/shard_map/convert_element_type | solution.py:249
  58.0 1.5 collective-permute-start.7
  62.3 2.8 %collective-permute-done.7 = bf16[512,256]{1,0:T(8,128)(2,1)S(1)} collective-permute-done((bf16[512,256]{1,0:T(8,128)(2,1)}, bf16[512,256]{1,0:T(8,128)(2,1)S(1)}, u32[]{:S(2)}, u32[]{:S(2)}) %collective-permute-start.7) | collective-permute-done | bytes 262176 | tf_op jit(solution)/shard_map/ppermute | solution.py:117
  65.0 1.5 collective-permute-start.8
  69.0 3.3 %collective-permute-done.8 = bf16[512,256]{1,0:T(8,128)(2,1)S(1)} collective-permute-done((bf16[512,256]{1,0:T(8,128)(2,1)S(1)}, bf16[512,256]{1,0:T(8,128)(2,1)S(1)}, u32[]{:S(2)}, u32[]{:S(2)}) %collective-permute-start.8) | collective-permute-done | bytes 262176 | tf_op jit(solution)/shard_map/ppermute | solution.py:117
  72.3 1.5 collective-permute-start.9
  73.9 4.8 %collective-permute-done.9 = bf16[512,256]{1,0:T(8,128)(2,1)S(1)} collective-permute-done((bf16[512,256]{1,0:T(8,128)(2,1)S(1)}, bf16[512,256]{1,0:T(8,128)(2,1)S(1)}, u32[]{:S(2)}, u32[]{:S(2)}) %collective-permute-start.9) | collective-permute-done | bytes 262176 | tf_op jit(solution)/shard_map/ppermute | solution.py:117
  79.7 11.8 %shard_map.127 = (f32[8,2,1,512]{3,2,1,0:T(1,128)S(1)}, f32[8,2,1,512]{3,2,1,0:T(1,128)S(1)}, f32[8,2,128,512]{3,2,1,0:T(8,128)S(1)}) custom-call(s32[16]{0:T(128)S(1)} %and_select_fusion.offset_ref, s32[16]{0:T(128)S(1)} %broadcast_add_fusion.owner_ref, s32[16]{0:T(128)S(1)} %subtract_clamp_fusion.valid_ref, ...), custom_call_target="tpu_custom_call" | custom-call | tf_op jit(solution)/shard_map/pallas_call | solution.py:179
  92.7 1.5 pad_maximum_fusion
  94.3 5.8 %all-to-all-start = ((bf16[8,264,512]{2,1,0:T(8,128)(2,1)}), bf16[8,264,512]{2,1,0:T(8,128)(2,1)}, u32[]{:S(2)}, u32[]{:S(2)}) async-start(bf16[8,264,512]{2,1,0:T(8,128)(2,1)} %pad_maximum_fusion), calls=%async_computation | async-start | bytes 4325376 | tf_op jit(solution)/shard_map/all_to_all | solution.py:318
  102.0 43.5 %all-to-all-done = bf16[8,264,512]{2,1,0:T(8,128)(2,1)} async-done(((bf16[8,264,512]{2,1,0:T(8,128)(2,1)}), bf16[8,264,512]{2,1,0:T(8,128)(2,1)}, u32[]{:S(2)}, u32[]{:S(2)}) %all-to-all-start) | async-done | bytes 2162720 | tf_op jit(solution)/shard_map/all_to_all | solution.py:318
  146.7 2.1 %fusion = f32[256,512]{1,0:T(8,128)S(1)} fusion(bf16[8,264,512]{2,1,0:T(8,128)(2,1)} %all-to-all-done, f32[8,2,512]{2,1,0:T(2,128)S(1)} %get-tuple-element.93), kind=kLoop, calls=%fused_computation.5 | loop fusion | flops 3014656 | bytes 2654208 | tf_op jit(solution)/shard_map/reduce_sum | solution.py:335
  151.8 1.8 %convolution_multiply_fusion.13 = f32[64,2048]{1,0:T(8,128)S(1)} fusion(bf16[4,256,2048]{2,1,0:T(8,128)(2,1)} %param.19, f32[64]{0:T(128)S(1)} %get-tuple-element.85, pred[64]{0:T(512)(128)(4,1)S(1)} %copy-done.49, pred[64]{0:T(512)(128)(4,1)S(1)} %copy-done.48, bf16[256,2,256]{0,2,1:T(8,128)(2,1)S(1)} %bitcast.420), kind=kOutput, calls=%fused_computation.20 | convolution fusion | flops 67272704 | bytes 1705472 | tf_op jit(solution)/shard_map/dot_general | solution.py:362
  153.7 1.6 convolution_multiply_fusion.12
  155.4 1.6 convolution_multiply_fusion.14
  159.0 1.7 %collective-permute-start.11 = (bf16[64,2048]{1,0:T(8,128)(2,1)S(1)}, bf16[64,2048]{1,0:T(8,128)(2,1)S(1)}, u32[]{:S(2)}, u32[]{:S(2)}) collective-permute-start(bf16[64,2048]{1,0:T(8,128)(2,1)S(1)} %fusion.15), channel_id=1, source_target_pairs={{0,16},{8,24},{16,0},{24,8},{1,17},{9,25},{17,1},{25,9},{2,18},{10... | collective-permute-start | bytes 786440 | tf_op jit(solution)/shard_map/ppermute | solution.py:103
  162.6 1.5 collective-permute-start.12
  165.5 2.9 %collective-permute-done.11 = bf16[64,2048]{1,0:T(8,128)(2,1)S(1)} collective-permute-done((bf16[64,2048]{1,0:T(8,128)(2,1)S(1)}, bf16[64,2048]{1,0:T(8,128)(2,1)S(1)}, u32[]{:S(2)}, u32[]{:S(2)}) %collective-permute-start.11) | collective-permute-done | bytes 262176 | tf_op jit(solution)/shard_map/ppermute | solution.py:103
  168.4 2.6 %collective-permute-done.12 = bf16[64,2048]{1,0:T(8,128)(2,1)S(1)} collective-permute-done((bf16[64,2048]{1,0:T(8,128)(2,1)S(1)}, bf16[64,2048]{1,0:T(8,128)(2,1)S(1)}, u32[]{:S(2)}, u32[]{:S(2)}) %collective-permute-start.12) | collective-permute-done | bytes 262176 | tf_op jit(solution)/shard_map/ppermute | solution.py:103
  (217 shorter events, 48.2 us)
Async XLA Ops:
  0.0 47.5 %copy-start = (bf16[2,2048,256]{2,1,0:T(8,128)(2,1)S(1)}, bf16[2,2048,256]{2,1,0:T(8,128)(2,1)}, u32[]{:S(2)}) copy-start(bf16[2,2048,256]{2,1,0:T(8,128)(2,1)} %param.18) | copy-start | bytes 6291460
  3.8 26.2 %collective-permute-start.2 = (bf16[64,2048]{1,0:T(8,128)(2,1)}, bf16[64,2048]{1,0:T(8,128)(2,1)}, u32[]{:S(2)}, u32[]{:S(2)}) collective-permute-start(bf16[64,2048]{1,0:T(8,128)(2,1)} %fusion.57), channel_id=1, source_target_pairs={{0,8},{8,16},{16,24},{24,0},{1,9},{9,17},{17,25},{25,1},{2,10},{10... | collective-permute-start | bytes 786440 | tf_op jit(solution)/shard_map/ppermute | solution.py:93
  4.2 25.7 %collective-permute-start.1 = (bf16[64,2048]{1,0:T(8,128)(2,1)}, bf16[64,2048]{1,0:T(8,128)(2,1)}, u32[]{:S(2)}, u32[]{:S(2)}) collective-permute-start(bf16[64,2048]{1,0:T(8,128)(2,1)} %fusion.57), channel_id=1, source_target_pairs={{0,16},{8,24},{16,0},{24,8},{1,17},{9,25},{17,1},{25,9},{2,18},{10... | collective-permute-start | bytes 786440 | tf_op jit(solution)/shard_map/ppermute | solution.py:93
  6.8 23.2 %collective-permute-start = (bf16[64,2048]{1,0:T(8,128)(2,1)}, bf16[64,2048]{1,0:T(8,128)(2,1)}, u32[]{:S(2)}, u32[]{:S(2)}) collective-permute-start(bf16[64,2048]{1,0:T(8,128)(2,1)} %fusion.57), channel_id=1, source_target_pairs={{0,24},{8,0},{16,8},{24,16},{1,25},{9,1},{17,9},{25,17},{2,26},{10... | collective-permute-start | bytes 786440 | tf_op jit(solution)/shard_map/ppermute | solution.py:93
  39.5 8.0 %copy-start.4 = (bf16[4,64,2048]{2,1,0:T(8,128)(2,1)S(1)}, bf16[4,64,2048]{2,1,0:T(8,128)(2,1)}, u32[]{:S(2)}) copy-start(bf16[4,64,2048]{2,1,0:T(8,128)(2,1)} %copy-done.3) | copy-start | bytes 3145732
  44.1 8.8 %copy-start.7 = (f32[256,128]{1,0:T(8,128)S(1)}, f32[256,128]{1,0:T(8,128)}, u32[]{:S(2)}) copy-start(f32[256,128]{1,0:T(8,128)} %pad_maximum_fusion.2) | copy-start | bytes 393220
  44.1 10.5 %copy-start.9 = (f32[256,64]{1,0:T(8,128)S(1)}, f32[256,64]{1,0:T(8,128)}, u32[]{:S(2)}) copy-start(f32[256,64]{1,0:T(8,128)} %copy-done.8) | copy-start | bytes 196612
  45.4 12.6 %collective-permute-start.6 = (bf16[512,256]{1,0:T(8,128)(2,1)}, bf16[512,256]{1,0:T(8,128)(2,1)}, u32[]{:S(2)}, u32[]{:S(2)}) collective-permute-start(bf16[512,256]{1,0:T(8,128)(2,1)} %constant_dynamic-update-slice_fusion), channel_id=1, source_target_pairs={{0,1},{1,3},{3,5},{5,7},{7,6},{6,4},{4,2},{2,0},{8,9},{9,11},{11,1... | collective-permute-start | bytes 786440 | tf_op jit(solution)/shard_map/ppermute | solution.py:117
  46.9 13.8 %collective-permute-start.3 = (bf16[512,256]{1,0:T(8,128)(2,1)}, bf16[512,256]{1,0:T(8,128)(2,1)}, u32[]{:S(2)}, u32[]{:S(2)}) collective-permute-start(bf16[512,256]{1,0:T(8,128)(2,1)} %constant_dynamic-update-slice_fusion), channel_id=1, source_target_pairs={{1,0},{3,1},{5,3},{7,5},{6,7},{4,6},{2,4},{0,2},{9,8},{11,9},{13,1... | collective-permute-start | bytes 786440 | tf_op jit(solution)/shard_map/ppermute | solution.py:121
  56.7 23.0 %copy-start.1 = (bf16[16,128,256]{2,1,0:T(8,128)(2,1)S(1)}, bf16[16,128,256]{2,1,0:T(8,128)(2,1)}, u32[]{:S(2)}) copy-start(bf16[16,128,256]{2,1,0:T(8,128)(2,1)} %get-tuple-element.97.k_ref) | copy-start | bytes 3145732
  58.0 7.0 %collective-permute-start.7 = (bf16[512,256]{1,0:T(8,128)(2,1)}, bf16[512,256]{1,0:T(8,128)(2,1)S(1)}, u32[]{:S(2)}, u32[]{:S(2)}) collective-permute-start(bf16[512,256]{1,0:T(8,128)(2,1)} %collective-permute-done.6), channel_id=1, source_target_pairs={{0,1},{1,3},{3,5},{5,7},{7,6},{6,4},{4,2},{2,0},{8,9},{9,11},{11,1... | collective-permute-start | bytes 786440 | tf_op jit(solution)/shard_map/ppermute | solution.py:117
  60.8 6.7 %collective-permute-start.4 = (bf16[512,256]{1,0:T(8,128)(2,1)}, bf16[512,256]{1,0:T(8,128)(2,1)S(1)}, u32[]{:S(2)}, u32[]{:S(2)}) collective-permute-start(bf16[512,256]{1,0:T(8,128)(2,1)} %collective-permute-done.3), channel_id=1, source_target_pairs={{1,0},{3,1},{5,3},{7,5},{6,7},{4,6},{2,4},{0,2},{9,8},{11,9},{13,1... | collective-permute-start | bytes 786440 | tf_op jit(solution)/shard_map/ppermute | solution.py:121
  65.0 7.3 %collective-permute-start.8 = (bf16[512,256]{1,0:T(8,128)(2,1)S(1)}, bf16[512,256]{1,0:T(8,128)(2,1)S(1)}, u32[]{:S(2)}, u32[]{:S(2)}) collective-permute-start(bf16[512,256]{1,0:T(8,128)(2,1)S(1)} %collective-permute-done.7), channel_id=1, source_target_pairs={{0,1},{1,3},{3,5},{5,7},{7,6},{6,4},{4,2},{2,0},{8,9},{9,11},{11,1... | collective-permute-start | bytes 786440 | tf_op jit(solution)/shard_map/ppermute | solution.py:117
  67.5 6.4 %collective-permute-start.5 = (bf16[512,256]{1,0:T(8,128)(2,1)S(1)}, bf16[512,256]{1,0:T(8,128)(2,1)S(1)}, u32[]{:S(2)}, u32[]{:S(2)}) collective-permute-start(bf16[512,256]{1,0:T(8,128)(2,1)S(1)} %collective-permute-done.4), channel_id=1, source_target_pairs={{1,0},{3,1},{5,3},{7,5},{6,7},{4,6},{2,4},{0,2},{9,8},{11,9},{13,1... | collective-permute-start | bytes 786440 | tf_op jit(solution)/shard_map/ppermute | solution.py:121
  72.3 6.4 %collective-permute-start.9 = (bf16[512,256]{1,0:T(8,128)(2,1)S(1)}, bf16[512,256]{1,0:T(8,128)(2,1)S(1)}, u32[]{:S(2)}, u32[]{:S(2)}) collective-permute-start(bf16[512,256]{1,0:T(8,128)(2,1)S(1)} %collective-permute-done.8), channel_id=1, source_target_pairs={{0,1},{1,3},{3,5},{5,7},{7,6},{6,4},{4,2},{2,0},{8,9},{9,11},{11,1... | collective-permute-start | bytes 786440 | tf_op jit(solution)/shard_map/ppermute | solution.py:117
  92.7 8.7 %copy-start.5 = (bf16[4,64,2048]{2,1,0:T(8,128)(2,1)S(1)}, bf16[4,64,2048]{2,1,0:T(8,128)(2,1)}, u32[]{:S(2)}) copy-start(bf16[4,64,2048]{2,1,0:T(8,128)(2,1)} %copy-done.3) | copy-start | bytes 3145732
  92.7 8.7 %copy-start.16 = (bf16[2048,4]{0,1:T(4,128)(2,1)S(1)}, bf16[2048,4]{0,1:T(4,128)(2,1)}, u32[]{:S(2)}) copy-start(bf16[2048,4]{0,1:T(4,128)(2,1)} %param.15) | copy-start | bytes 49156
  92.7 9.0 %copy-start.15 = (s32[256,2]{0,1:T(2,128)S(1)}, s32[256,2]{0,1:T(2,128)}, u32[]{:S(2)}) copy-start(s32[256,2]{0,1:T(2,128)} %copy-done.14) | copy-start | bytes 6148
  92.7 9.1 %copy-start.13 = (f32[256,2,4]{0,1,2:T(2,128)S(1)}, f32[256,2,4]{0,1,2:T(2,128)}, u32[]{:S(2)}) copy-start(f32[256,2,4]{0,1,2:T(2,128)} %copy-done.12) | copy-start | bytes 24580
  94.3 51.3 %all-to-all-start = ((bf16[8,264,512]{2,1,0:T(8,128)(2,1)}), bf16[8,264,512]{2,1,0:T(8,128)(2,1)}, u32[]{:S(2)}, u32[]{:S(2)}) async-start(bf16[8,264,512]{2,1,0:T(8,128)(2,1)} %pad_maximum_fusion), calls=%async_computation | async-start | bytes 4325376 | tf_op jit(solution)/shard_map/all_to_all | solution.py:318
  100.1 51.0 %copy-start.17 = (f32[2,256,2]{1,2,0:T(2,128)S(1)}, f32[2,256,2]{1,2,0:T(2,128)}, u32[]{:S(2)}) copy-start(f32[2,256,2]{1,2,0:T(2,128)} %fusion.36) | copy-start | bytes 12292
  101.4 50.5 %copy-start.48 = (pred[64]{0:T(512)(128)(4,1)S(1)}, pred[64]{0:T(512)(128)(4,1)}, u32[]{:S(2)}) copy-start(pred[64]{0:T(512)(128)(4,1)} %get-tuple-element.52) | copy-start | bytes 196
  101.4 50.5 %copy-start.49 = (pred[64]{0:T(512)(128)(4,1)S(1)}, pred[64]{0:T(512)(128)(4,1)}, u32[]{:S(2)}) copy-start(pred[64]{0:T(512)(128)(4,1)} %get-tuple-element.55) | copy-start | bytes 196
  101.7 49.4 %copy-start.6 = (f32[2,256,2,128]{3,1,2,0:T(8,128)S(1)}, f32[2,256,2,128]{3,1,2,0:T(8,128)}, u32[]{:S(2)}) copy-start(f32[2,256,2,128]{3,1,2,0:T(8,128)} %fusion.60) | copy-start | bytes 1572868
  146.6 7.0 %copy-start.46 = (pred[64]{0:T(512)(128)(4,1)S(1)}, pred[64]{0:T(512)(128)(4,1)}, u32[]{:S(2)}) copy-start(pred[64]{0:T(512)(128)(4,1)} %get-tuple-element.53) | copy-start | bytes 196
  146.6 7.0 %copy-start.47 = (pred[64]{0:T(512)(128)(4,1)S(1)}, pred[64]{0:T(512)(128)(4,1)}, u32[]{:S(2)}) copy-start(pred[64]{0:T(512)(128)(4,1)} %get-tuple-element.56) | copy-start | bytes 196
  148.7 6.6 %copy-start.44 = (pred[64]{0:T(512)(128)(4,1)S(1)}, pred[64]{0:T(512)(128)(4,1)}, u32[]{:S(2)}) copy-start(pred[64]{0:T(512)(128)(4,1)} %get-tuple-element.51) | copy-start | bytes 196
  149.9 7.2 %copy-start.42 = (pred[64]{0:T(512)(128)(4,1)S(1)}, pred[64]{0:T(512)(128)(4,1)}, u32[]{:S(2)}) copy-start(pred[64]{0:T(512)(128)(4,1)} %get-tuple-element.124) | copy-start | bytes 196
  149.9 7.2 %copy-start.43 = (pred[64]{0:T(512)(128)(4,1)S(1)}, pred[64]{0:T(512)(128)(4,1)}, u32[]{:S(2)}) copy-start(pred[64]{0:T(512)(128)(4,1)} %get-tuple-element.125) | copy-start | bytes 196
  157.5 8.0 %collective-permute-start.10 = (bf16[64,2048]{1,0:T(8,128)(2,1)S(1)}, bf16[64,2048]{1,0:T(8,128)(2,1)S(1)}, u32[]{:S(2)}, u32[]{:S(2)}) collective-permute-start(bf16[64,2048]{1,0:T(8,128)(2,1)S(1)} %fusion.16), channel_id=1, source_target_pairs={{0,8},{8,16},{16,24},{24,0},{1,9},{9,17},{17,25},{25,1},{2,10},{10... | collective-permute-start | bytes 786440 | tf_op jit(solution)/shard_map/ppermute | solution.py:103
  159.0 9.3 %collective-permute-start.11 = (bf16[64,2048]{1,0:T(8,128)(2,1)S(1)}, bf16[64,2048]{1,0:T(8,128)(2,1)S(1)}, u32[]{:S(2)}, u32[]{:S(2)}) collective-permute-start(bf16[64,2048]{1,0:T(8,128)(2,1)S(1)} %fusion.15), channel_id=1, source_target_pairs={{0,16},{8,24},{16,0},{24,8},{1,17},{9,25},{17,1},{25,9},{2,18},{10... | collective-permute-start | bytes 786440 | tf_op jit(solution)/shard_map/ppermute | solution.py:103
  162.6 8.4 %collective-permute-start.12 = (bf16[64,2048]{1,0:T(8,128)(2,1)S(1)}, bf16[64,2048]{1,0:T(8,128)(2,1)S(1)}, u32[]{:S(2)}, u32[]{:S(2)}) collective-permute-start(bf16[64,2048]{1,0:T(8,128)(2,1)S(1)} %fusion.14), channel_id=1, source_target_pairs={{0,24},{8,0},{16,8},{24,16},{1,25},{9,1},{17,9},{25,17},{2,26},{10... | collective-permute-start | bytes 786440 | tf_op jit(solution)/shard_map/ppermute | solution.py:103
  (32 other events, 111.0 us)

commit v20 on v16

--- a/solution.py
+++ b/solution.py
@@ -89,11 +89,9 @@
 def shift_all_gather(piece, axis_name):
     size = lax.axis_size(axis_name)
     rank = lax.axis_index(axis_name)
-    by_offset = [piece] + [
-        lax.ppermute(piece, axis_name, [(i, (i + s) % size) for i in range(size)])
-        for s in range(1, size)
-    ]
-    return jnp.stack(by_offset[:1] + by_offset[1:][::-1], axis=0)
+    copies = jnp.broadcast_to(piece[None], (size,) + piece.shape)
+    everyone = lax.all_to_all(copies, axis_name, 0, 0, tiled=True)
+    return jnp.take(everyone, (rank + jnp.arange(size, dtype=jnp.int32)) % size, axis=0)
 
 
 def shift_reduce_scatter(blocks, axis_name):

time: 169 us -> 172 us (1.018)
  other arithmetic: 26.8 us -> 23.1 us
  waiting for transfers between devices: 61.1 us -> 63.3 us
    ppermute x3 -> x0, starting transfers between devices: 4.43 us -> none  [shift_all_gather(): lax.ppermute(piece, axis_name, [(i, (i + s) % size) for i in range(size)])]
    all_to_all x0 -> x1, starting transfers between devices: none -> 4.26 us  [shift_all_gather(): everyone = lax.all_to_all(copies, axis_name, 0, 0, tiled=True)]
    convert_element_type x3 -> x1, other arithmetic: 3.56 us -> 0.7 us  [normalize(): return (scaled * norm_gain.astype(jnp.float32)).astype(jnp.bfloat16)]
    gather x0 -> x1, local copies, waits for them, and re-layouts: none -> 2.82 us  [shift_all_gather(): jnp.take(everyone, (rank + jnp.arange(size, dtype=jnp.int32)) % size, axi...]
    another operation x5 -> x4, other arithmetic: 3.8 us -> 1.52 us
    ppermute x3, starting transfers between devices: 2.65 us -> 4.71 us  [ring_all_gather(): moving = lax.ppermute(moving, axis_name, backward)]
    unnamed x123 -> x129, local copies, waits for them, and re-layouts: 8.76 us -> 7.52 us
  transfers between devices with their start and end apart: 14 -> 12, of which waited for: 7 -> 9; matrix products, arithmetic and copies ran while one was open for 22% -> 19% of each run, Pallas kernels for 0% -> 0%
where the time goes in v20:
time: 172 us; the launch traced here: 170 us
  waiting for transfers between devices  63.3 us (37%)
  local copies, waits for them, and re-layouts  32.3 us (19%)
  other arithmetic  23.1 us (13%)
  starting transfers between devices  22.4 us (13%)
  matrix products  16.3 us (9%)
  Pallas kernels  11.8 us (7%)
    all_to_all x1, waiting for transfers between devices, per_device(): received = lax.all_to_all(payload, 'seq', 0, 0, tiled=True)  45.1 us
    pallas_call x1, Pallas kernels, block_attention(): pl.pallas_call(kernel, grid_spec=grid_spec, out_shape=[jax.ShapeDtypeStru...  11.8 us
    ppermute x4, waiting for transfers between devices, ring_all_gather(): moving = lax.ppermute(moving, axis_name, forward)  11.3 us
    dot_general x16, matrix products, per_device(): jnp.dot(picked, o_weight[expert], preferred_element_type=jnp.float32)  9.74 us
    unnamed x129, local copies, waits for them, and re-layouts  7.52 us
    all_to_all x1, starting transfers between devices, per_device(): received = lax.all_to_all(payload, 'seq', 0, 0, tiled=True)  6.38 us
    ppermute x3, waiting for transfers between devices, shift_reduce_scatter(): lax.ppermute(blocks[s], axis_name, [(i, (i + s) % size) for i in range(si...  5.48 us
    ppermute x3, starting transfers between devices, ring_all_gather(): moving = lax.ppermute(moving, axis_name, backward)  4.71 us
  transfers between devices with their start and end apart: 12, of which 9 were waited for; matrix products, arithmetic and copies ran while one was open for 19% of the time, Pallas kernels for 0%

profile of v20, /device:TPU:0, one launch (start us, length us, event | category | flops | bytes accessed | tf_op | source)
XLA Modules:
  0.0 170.5 jit_solution(14608660620365402520)
XLA Ops:
  0.0 1.2 fusion.54
  4.2 4.3 %all-to-all-start = ((bf16[4,64,2048]{2,1,0:T(8,128)(2,1)}), bf16[4,64,2048]{2,1,0:T(8,128)(2,1)}, u32[]{:S(2)}, u32[]{:S(2)}) async-start(bf16[4,64,2048]{2,1,0:T(8,128)(2,1)} %broadcast_in_dim.279), calls=%async_computation | async-start | bytes 2097152 | tf_op jit(solution)/shard_map/all_to_all | solution.py:93
  16.3 3.1 %fusion.288 = (bf16[1,16,128,256]{3,2,1,0:T(8,128)(2,1)}, bf16[16,128,256]{2,1,0:T(8,128)(2,1)}) fusion(bf16[2,16,128,256]{3,2,1,0:T(8,128)(2,1)} %param.20), kind=kLoop, calls=%fused_computation.456 | loop fusion | bytes 4194304 | tf_op jit(solution)/shard_map/slice | solution.py:293
  21.9 1.6 copy.117
  24.9 2.8 %gather_fusion.1 = bf16[4,64,2048]{2,1,0:T(8,128)(2,1)} fusion(bf16[4,64,2048]{2,1,0:T(8,128)(2,1)} %all-to-all-done, s32[1024]{0:T(1024)S(1)} %pad_clamp_fusion.1), kind=kCustom, calls=%fused_computation.1 | custom fusion | bytes 2097168 | tf_op jit(solution)/shard_map/jit(_take)/gather | solution.py:94
  27.8 1.5 bitcast_select_fusion
  31.0 2.7 %multiply_reduce_fusion.1 = (f32[256,256]{1,0:T(8,128)S(1)}, f32[256,256]{1,0:T(8,128)}) fusion(f32[4,256]{1,0:T(4,128)} %bitcast.436, f32[4,256]{1,0:T(4,128)S(1)} %bitcast.435, bf16[4,2048,256]{2,1,0:T(8,128)(2,1)S(1)} %copy-done.56, bf16[256,2048]{1,0:T(8,128)(2,1)S(1)} %bitcast_select_fusion), kind=kOutput, calls=%fused_computation.67 | convolution fusion | flops 1074659328 | bytes 5775360 | tf_op jit(solution)/shard_map/nd,edc->enc/dot_general | solution.py:225
  35.6 1.8 %reduce_sum.250 = f32[256,1,2,128]{3,2,0,1:T(2,128)} reshape(f32[256,256]{1,0:T(8,128)} %get-tuple-element.34) | data formatting | bytes 524288 | tf_op jit(solution)/shard_map/reduce_sum | solution.py:235
  37.4 2.0 %slice_bitcast_fusion.22 = (f32[256,1,64]{2,0,1:T(8,128)}, f32[256,1,64]{2,0,1:T(8,128)}, f32[256,1,64]{2,0,1:T(8,128)}, f32[256,1,64]{2,0,1:T(8,128)}, f32[256,...) fusion(f32[256,256]{1,0:T(8,128)} %get-tuple-element.34), kind=kLoop, calls=%fused_computation.451 | loop fusion | bytes 786432 | tf_op jit(solution)/shard_map/concatenate | solution.py:236
  40.4 1.6 fusion.66
  43.4 3.0 %collective-permute-start = (bf16[512,256]{1,0:T(8,128)(2,1)}, bf16[512,256]{1,0:T(8,128)(2,1)}, u32[]{:S(2)}, u32[]{:S(2)}) collective-permute-start(bf16[512,256]{1,0:T(8,128)(2,1)} %pad_maximum_fusion.1), channel_id=1, source_target_pairs={{1,0},{3,1},{5,3},{7,5},{6,7},{4,6},{2,4},{0,2},{9,8},{11,9},{13,1... | collective-permute-start | bytes 786440 | tf_op jit(solution)/shard_map/ppermute | solution.py:119
  47.9 1.8 %copy.115 = f32[256,2,64]{2,0,1:T(8,128)} copy(f32[256,2,64]{0,2,1:T(8,128)} %get-tuple-element.99) | data formatting | bytes 262144
  49.7 1.8 %fusion.72 = (bf16[256,1,2,128]{3,0,1,2:T(8,128)(2,1)S(1)}, bf16[256,1,2,128]{3,0,1,2:T(8,128)(2,1)S(1)}) fusion(f32[256,1,2,128]{3,0,1,2:T(8,128)} %copy.73, f32[256,1,2,128]{3,2,0,1:T(2,128)} %reduce_sum.249, f32[256,128]{1,0:T(8,128)} %pad_maximum_fusion.2, f32[256,1,2,128]{3,2,0,1:T(2,128)} %reduce_sum.250, f32[256,1,64]{2,0,1:T(8,128)} %get-tuple-element.111, ...), kind=kLoop, calls=%fused_computation.111 | loop fusion | flops 917504 | bytes 1703936 | tf_op jit(solution)/shard_map/convert_element_type | solution.py:247
  52.7 1.3 fusion.291
  59.1 3.8 %collective-permute-done.4 = bf16[512,256]{1,0:T(8,128)(2,1)S(1)} collective-permute-done((bf16[512,256]{1,0:T(8,128)(2,1)}, bf16[512,256]{1,0:T(8,128)(2,1)S(1)}, u32[]{:S(2)}, u32[]{:S(2)}) %collective-permute-start.4) | collective-permute-done | bytes 262176 | tf_op jit(solution)/shard_map/ppermute | solution.py:115
  62.9 1.5 collective-permute-start.5
  66.7 2.7 %collective-permute-done.5 = bf16[512,256]{1,0:T(8,128)(2,1)S(1)} collective-permute-done((bf16[512,256]{1,0:T(8,128)(2,1)S(1)}, bf16[512,256]{1,0:T(8,128)(2,1)S(1)}, u32[]{:S(2)}, u32[]{:S(2)}) %collective-permute-start.5) | collective-permute-done | bytes 262176 | tf_op jit(solution)/shard_map/ppermute | solution.py:115
  69.5 2.1 %collective-permute-start.6 = (bf16[512,256]{1,0:T(8,128)(2,1)S(1)}, bf16[512,256]{1,0:T(8,128)(2,1)S(1)}, u32[]{:S(2)}, u32[]{:S(2)}) collective-permute-start(bf16[512,256]{1,0:T(8,128)(2,1)S(1)} %collective-permute-done.5), channel_id=1, source_target_pairs={{0,1},{1,3},{3,5},{5,7},{7,6},{6,4},{4,2},{2,0},{8,9},{9,11},{11,1... | collective-permute-start | bytes 786440 | tf_op jit(solution)/shard_map/ppermute | solution.py:115
  72.2 3.7 %collective-permute-done.6 = bf16[512,256]{1,0:T(8,128)(2,1)S(1)} collective-permute-done((bf16[512,256]{1,0:T(8,128)(2,1)S(1)}, bf16[512,256]{1,0:T(8,128)(2,1)S(1)}, u32[]{:S(2)}, u32[]{:S(2)}) %collective-permute-start.6) | collective-permute-done | bytes 262176 | tf_op jit(solution)/shard_map/ppermute | solution.py:115
  76.9 11.8 %shard_map.127 = (f32[8,2,1,512]{3,2,1,0:T(1,128)S(1)}, f32[8,2,1,512]{3,2,1,0:T(1,128)S(1)}, f32[8,2,128,512]{3,2,1,0:T(8,128)S(1)}) custom-call(s32[16]{0:T(128)S(1)} %and_select_fusion.offset_ref, s32[16]{0:T(128)S(1)} %broadcast_add_fusion.owner_ref, s32[16]{0:T(128)S(1)} %subtract_clamp_fusion.valid_ref, ...), custom_call_target="tpu_custom_call" | custom-call | tf_op jit(solution)/shard_map/pallas_call | solution.py:177
  89.9 1.5 pad_maximum_fusion
  91.4 6.4 %all-to-all-start.1 = ((bf16[8,264,512]{2,1,0:T(8,128)(2,1)}), bf16[8,264,512]{2,1,0:T(8,128)(2,1)}, u32[]{:S(2)}, u32[]{:S(2)}) async-start(bf16[8,264,512]{2,1,0:T(8,128)(2,1)} %pad_maximum_fusion), calls=%async_computation.1 | async-start | bytes 4325376 | tf_op jit(solution)/shard_map/all_to_all | solution.py:315
  97.8 1.3 compare_reduce_fusion.31
  99.8 45.1 %all-to-all-done.1 = bf16[8,264,512]{2,1,0:T(8,128)(2,1)} async-done(((bf16[8,264,512]{2,1,0:T(8,128)(2,1)}), bf16[8,264,512]{2,1,0:T(8,128)(2,1)}, u32[]{:S(2)}, u32[]{:S(2)}) %all-to-all-start.1) | async-done | bytes 2162720 | tf_op jit(solution)/shard_map/all_to_all | solution.py:315
  146.0 2.1 %fusion = f32[256,512]{1,0:T(8,128)S(1)} fusion(bf16[8,264,512]{2,1,0:T(8,128)(2,1)} %all-to-all-done.1, f32[8,2,512]{2,1,0:T(2,128)S(1)} %get-tuple-element.87), kind=kLoop, calls=%fused_computation.6 | loop fusion | flops 3014656 | bytes 2654208 | tf_op jit(solution)/shard_map/reduce_sum | solution.py:332
  149.2 1.2 copy.88
  151.2 1.8 %convolution_multiply_fusion.13 = f32[64,2048]{1,0:T(8,128)S(1)} fusion(bf16[4,256,2048]{2,1,0:T(8,128)(2,1)} %param.19, f32[64]{0:T(128)S(1)} %get-tuple-element.79, pred[64]{0:T(512)(128)(4,1)S(1)} %copy-done.53, pred[64]{0:T(512)(128)(4,1)S(1)} %copy-done.52, bf16[256,2,256]{0,2,1:T(8,128)(2,1)S(1)} %bitcast.411), kind=kOutput, calls=%fused_computation.21 | convolution fusion | flops 67272704 | bytes 1705472 | tf_op jit(solution)/shard_map/dot_general | solution.py:359
  153.0 1.6 convolution_multiply_fusion.12
  154.7 1.6 convolution_multiply_fusion.14
  161.2 1.5 collective-permute-start.9
  164.1 3.6 %collective-permute-done.8 = bf16[64,2048]{1,0:T(8,128)(2,1)S(1)} collective-permute-done((bf16[64,2048]{1,0:T(8,128)(2,1)S(1)}, bf16[64,2048]{1,0:T(8,128)(2,1)S(1)}, u32[]{:S(2)}, u32[]{:S(2)}) %collective-permute-start.8) | collective-permute-done | bytes 262176 | tf_op jit(solution)/shard_map/ppermute | solution.py:101
  167.7 1.9 %collective-permute-done.9 = bf16[64,2048]{1,0:T(8,128)(2,1)S(1)} collective-permute-done((bf16[64,2048]{1,0:T(8,128)(2,1)S(1)}, bf16[64,2048]{1,0:T(8,128)(2,1)S(1)}, u32[]{:S(2)}, u32[]{:S(2)}) %collective-permute-start.9) | collective-permute-done | bytes 262176 | tf_op jit(solution)/shard_map/ppermute | solution.py:101
  (235 shorter events, 43.5 us)
Async XLA Ops:
  0.0 29.3 %copy-start = (bf16[2,2048,256]{2,1,0:T(8,128)(2,1)S(1)}, bf16[2,2048,256]{2,1,0:T(8,128)(2,1)}, u32[]{:S(2)}) copy-start(bf16[2,2048,256]{2,1,0:T(8,128)(2,1)} %param.18) | copy-start | bytes 6291460
  0.0 11.3 %copy-start.2 = (s32[8]{0:T(128)S(1)}, s32[8]{0:T(128)}, u32[]{:S(2)}) copy-start(s32[8]{0:T(128)} %constant.125.clone) | copy-start | bytes 100
  0.0 8.5 %copy-start.55 = (s32[8]{0:T(128)S(1)}, s32[8]{0:T(128)}, u32[]{:S(2)}) copy-start(s32[8]{0:T(128)} %param.21) | copy-start | bytes 100
  0.0 8.7 %copy-start.57 = (s32[128]{0:T(128)S(1)}, s32[128]{0:T(128)}, u32[]{:S(2)}) copy-start(s32[128]{0:T(128)} %param.23) | copy-start | bytes 1540
  0.0 8.9 %copy-start.54 = (s32[8]{0:T(128)S(1)}, s32[8]{0:T(128)}, u32[]{:S(2)}) copy-start(s32[8]{0:T(128)} %param.22) | copy-start | bytes 100
  0.0 13.4 %copy-start.21 = (s32[1,256,2]{1,2,0:T(2,128)S(1)}, s32[1,256,2]{1,2,0:T(2,128)}, u32[]{:S(2)}) copy-start(s32[1,256,2]{1,2,0:T(2,128)} %param.16) | copy-start | bytes 6148
  4.2 20.8 %all-to-all-start = ((bf16[4,64,2048]{2,1,0:T(8,128)(2,1)}), bf16[4,64,2048]{2,1,0:T(8,128)(2,1)}, u32[]{:S(2)}, u32[]{:S(2)}) async-start(bf16[4,64,2048]{2,1,0:T(8,128)(2,1)} %broadcast_in_dim.279), calls=%async_computation | async-start | bytes 2097152 | tf_op jit(solution)/shard_map/all_to_all | solution.py:93
  37.4 9.0 %slice-start = ((f32[2,256,256]{1,2,0:T(8,128)}), f32[1,256,256]{1,2,0:T(8,128)S(1)}, s32[]{:S(2)}) async-start(f32[2,256,256]{1,2,0:T(8,128)} %copy-done.13), calls=%async_computation.2 | async-start | bytes 524288 | tf_op jit(solution)/shard_map/slice | solution.py:250
  43.4 13.8 %collective-permute-start = (bf16[512,256]{1,0:T(8,128)(2,1)}, bf16[512,256]{1,0:T(8,128)(2,1)}, u32[]{:S(2)}, u32[]{:S(2)}) collective-permute-start(bf16[512,256]{1,0:T(8,128)(2,1)} %pad_maximum_fusion.1), channel_id=1, source_target_pairs={{1,0},{3,1},{5,3},{7,5},{6,7},{4,6},{2,4},{0,2},{9,8},{11,9},{13,1... | collective-permute-start | bytes 786440 | tf_op jit(solution)/shard_map/ppermute | solution.py:119
  46.4 8.7 %collective-permute-start.3 = (bf16[512,256]{1,0:T(8,128)(2,1)}, bf16[512,256]{1,0:T(8,128)(2,1)}, u32[]{:S(2)}, u32[]{:S(2)}) collective-permute-start(bf16[512,256]{1,0:T(8,128)(2,1)} %pad_maximum_fusion.1), channel_id=1, source_target_pairs={{0,1},{1,3},{3,5},{5,7},{7,6},{6,4},{4,2},{2,0},{8,9},{9,11},{11,1... | collective-permute-start | bytes 786440 | tf_op jit(solution)/shard_map/ppermute | solution.py:115
  47.9 16.4 %copy-start.8 = (bf16[256,256]{1,0:T(8,128)(2,1)S(1)}, bf16[256,256]{1,0:T(8,128)(2,1)}, u32[]{:S(2)}) copy-start(bf16[256,256]{1,0:T(8,128)(2,1)} %copy-done.7) | copy-start | bytes 393220
  47.9 16.4 %copy-start.10 = (bf16[256,256]{1,0:T(8,128)(2,1)S(1)}, bf16[256,256]{1,0:T(8,128)(2,1)}, u32[]{:S(2)}) copy-start(bf16[256,256]{1,0:T(8,128)(2,1)} %copy-done.9) | copy-start | bytes 393220
  52.7 24.2 %copy-start.1 = (bf16[16,128,256]{2,1,0:T(8,128)(2,1)S(1)}, bf16[16,128,256]{2,1,0:T(8,128)(2,1)}, u32[]{:S(2)}) copy-start(bf16[16,128,256]{2,1,0:T(8,128)(2,1)} %get-tuple-element.91.k_ref) | copy-start | bytes 3145732
  55.1 7.8 %collective-permute-start.4 = (bf16[512,256]{1,0:T(8,128)(2,1)}, bf16[512,256]{1,0:T(8,128)(2,1)S(1)}, u32[]{:S(2)}, u32[]{:S(2)}) collective-permute-start(bf16[512,256]{1,0:T(8,128)(2,1)} %collective-permute-done.3), channel_id=1, source_target_pairs={{0,1},{1,3},{3,5},{5,7},{7,6},{6,4},{4,2},{2,0},{8,9},{9,11},{11,1... | collective-permute-start | bytes 786440 | tf_op jit(solution)/shard_map/ppermute | solution.py:115
  57.2 8.0 %collective-permute-start.1 = (bf16[512,256]{1,0:T(8,128)(2,1)}, bf16[512,256]{1,0:T(8,128)(2,1)S(1)}, u32[]{:S(2)}, u32[]{:S(2)}) collective-permute-start(bf16[512,256]{1,0:T(8,128)(2,1)} %collective-permute-done), channel_id=1, source_target_pairs={{1,0},{3,1},{5,3},{7,5},{6,7},{4,6},{2,4},{0,2},{9,8},{11,9},{13,1... | collective-permute-start | bytes 786440 | tf_op jit(solution)/shard_map/ppermute | solution.py:119
  62.9 6.6 %collective-permute-start.5 = (bf16[512,256]{1,0:T(8,128)(2,1)S(1)}, bf16[512,256]{1,0:T(8,128)(2,1)S(1)}, u32[]{:S(2)}, u32[]{:S(2)}) collective-permute-start(bf16[512,256]{1,0:T(8,128)(2,1)S(1)} %collective-permute-done.4), channel_id=1, source_target_pairs={{0,1},{1,3},{3,5},{5,7},{7,6},{6,4},{4,2},{2,0},{8,9},{9,11},{11,1... | collective-permute-start | bytes 786440 | tf_op jit(solution)/shard_map/ppermute | solution.py:115
  65.2 6.9 %collective-permute-start.2 = (bf16[512,256]{1,0:T(8,128)(2,1)S(1)}, bf16[512,256]{1,0:T(8,128)(2,1)S(1)}, u32[]{:S(2)}, u32[]{:S(2)}) collective-permute-start(bf16[512,256]{1,0:T(8,128)(2,1)S(1)} %collective-permute-done.1), channel_id=1, source_target_pairs={{1,0},{3,1},{5,3},{7,5},{6,7},{4,6},{2,4},{0,2},{9,8},{11,9},{13,1... | collective-permute-start | bytes 786440 | tf_op jit(solution)/shard_map/ppermute | solution.py:119
  69.5 6.4 %collective-permute-start.6 = (bf16[512,256]{1,0:T(8,128)(2,1)S(1)}, bf16[512,256]{1,0:T(8,128)(2,1)S(1)}, u32[]{:S(2)}, u32[]{:S(2)}) collective-permute-start(bf16[512,256]{1,0:T(8,128)(2,1)S(1)} %collective-permute-done.5), channel_id=1, source_target_pairs={{0,1},{1,3},{3,5},{5,7},{7,6},{6,4},{4,2},{2,0},{8,9},{9,11},{11,1... | collective-permute-start | bytes 786440 | tf_op jit(solution)/shard_map/ppermute | solution.py:115
  89.9 9.3 %copy-start.5 = (bf16[256,2048]{1,0:T(8,128)(2,1)S(1)}, bf16[256,2048]{1,0:T(8,128)(2,1)}, u32[]{:S(2)}) copy-start(bf16[256,2048]{1,0:T(8,128)(2,1)} %copy-done.4) | copy-start | bytes 3145732
  89.9 9.2 %copy-start.19 = (bf16[2048,4]{0,1:T(4,128)(2,1)S(1)}, bf16[2048,4]{0,1:T(4,128)(2,1)}, u32[]{:S(2)}) copy-start(bf16[2048,4]{0,1:T(4,128)(2,1)} %param.15) | copy-start | bytes 49156
  89.9 9.6 %copy-start.18 = (s32[256,2]{0,1:T(2,128)S(1)}, s32[256,2]{0,1:T(2,128)}, u32[]{:S(2)}) copy-start(s32[256,2]{0,1:T(2,128)} %copy-done.17) | copy-start | bytes 6148
  89.9 9.7 %copy-start.16 = (f32[256,2,4]{0,1,2:T(2,128)S(1)}, f32[256,2,4]{0,1,2:T(2,128)}, u32[]{:S(2)}) copy-start(f32[256,2,4]{0,1,2:T(2,128)} %copy-done.15) | copy-start | bytes 24580
  91.4 53.5 %all-to-all-start.1 = ((bf16[8,264,512]{2,1,0:T(8,128)(2,1)}), bf16[8,264,512]{2,1,0:T(8,128)(2,1)}, u32[]{:S(2)}, u32[]{:S(2)}) async-start(bf16[8,264,512]{2,1,0:T(8,128)(2,1)} %pad_maximum_fusion), calls=%async_computation.1 | async-start | bytes 4325376 | tf_op jit(solution)/shard_map/all_to_all | solution.py:315
  97.8 52.6 %copy-start.20 = (f32[2,256,2]{1,2,0:T(2,128)S(1)}, f32[2,256,2]{1,2,0:T(2,128)}, u32[]{:S(2)}) copy-start(f32[2,256,2]{1,2,0:T(2,128)} %fusion.37) | copy-start | bytes 12292
  99.1 52.0 %copy-start.52 = (pred[64]{0:T(512)(128)(4,1)S(1)}, pred[64]{0:T(512)(128)(4,1)}, u32[]{:S(2)}) copy-start(pred[64]{0:T(512)(128)(4,1)} %get-tuple-element.46) | copy-start | bytes 196
  99.1 52.0 %copy-start.53 = (pred[64]{0:T(512)(128)(4,1)S(1)}, pred[64]{0:T(512)(128)(4,1)}, u32[]{:S(2)}) copy-start(pred[64]{0:T(512)(128)(4,1)} %get-tuple-element.49) | copy-start | bytes 196
  99.5 51.0 %copy-start.6 = (f32[2,256,2,128]{3,1,2,0:T(8,128)S(1)}, f32[2,256,2,128]{3,1,2,0:T(8,128)}, u32[]{:S(2)}) copy-start(f32[2,256,2,128]{3,1,2,0:T(8,128)} %fusion.57) | copy-start | bytes 1572868
  149.2 7.2 %copy-start.46 = (pred[64]{0:T(512)(128)(4,1)S(1)}, pred[64]{0:T(512)(128)(4,1)}, u32[]{:S(2)}) copy-start(pred[64]{0:T(512)(128)(4,1)} %get-tuple-element.118) | copy-start | bytes 196
  149.2 7.2 %copy-start.47 = (pred[64]{0:T(512)(128)(4,1)S(1)}, pred[64]{0:T(512)(128)(4,1)}, u32[]{:S(2)}) copy-start(pred[64]{0:T(512)(128)(4,1)} %get-tuple-element.119) | copy-start | bytes 196
  156.8 7.3 %collective-permute-start.7 = (bf16[64,2048]{1,0:T(8,128)(2,1)S(1)}, bf16[64,2048]{1,0:T(8,128)(2,1)S(1)}, u32[]{:S(2)}, u32[]{:S(2)}) collective-permute-start(bf16[64,2048]{1,0:T(8,128)(2,1)S(1)} %fusion.16), channel_id=1, source_target_pairs={{0,8},{8,16},{16,24},{24,0},{1,9},{9,17},{17,25},{25,1},{2,10},{10... | collective-permute-start | bytes 786440 | tf_op jit(solution)/shard_map/ppermute | solution.py:101
  158.4 9.3 %collective-permute-start.8 = (bf16[64,2048]{1,0:T(8,128)(2,1)S(1)}, bf16[64,2048]{1,0:T(8,128)(2,1)S(1)}, u32[]{:S(2)}, u32[]{:S(2)}) collective-permute-start(bf16[64,2048]{1,0:T(8,128)(2,1)S(1)} %fusion.15), channel_id=1, source_target_pairs={{0,16},{8,24},{16,0},{24,8},{1,17},{9,25},{17,1},{25,9},{2,18},{10... | collective-permute-start | bytes 786440 | tf_op jit(solution)/shard_map/ppermute | solution.py:101
  161.2 8.4 %collective-permute-start.9 = (bf16[64,2048]{1,0:T(8,128)(2,1)S(1)}, bf16[64,2048]{1,0:T(8,128)(2,1)S(1)}, u32[]{:S(2)}, u32[]{:S(2)}) collective-permute-start(bf16[64,2048]{1,0:T(8,128)(2,1)S(1)} %fusion.14), channel_id=1, source_target_pairs={{0,24},{8,0},{16,8},{24,16},{1,25},{9,1},{17,9},{25,17},{2,26},{10... | collective-permute-start | bytes 786440 | tf_op jit(solution)/shard_map/ppermute | solution.py:101
  (39 other events, 138.3 us)
